TPU v7x, 32 devices: a whole 2x2x4 slice. The times are simulated.
32 devices in a mesh: groups: 2 (over y), seq: 4 (over z), row: 2 (over x), col: 2 (over core).
Axes of the slice: x: 2, y: 2, z: 4, core: 2. Of those that a mesh axis runs over, the one named last changes fastest.
Arguments:
- acts: bfloat16 [3072, 4096], P(('groups', 'seq', 'row'), 'col'), parts along dimension 0, may hold values from -9 to 9
- w_query: bfloat16 [4096, 2048], P('seq', ('row', 'col')), may hold values from -0.1875 to 0.1875
- w_key: bfloat16 [4096, 2048], P('seq', ('row', 'col')), may hold values from -0.1875 to 0.1875
- w_value: bfloat16 [4096, 2048], P('seq', ('row', 'col')), may hold values from -0.09375 to 0.09375
Outputs:
- attended: bfloat16 [3072, 2048], P(('groups', 'seq'), ('row', 'col')), parts along dimension 0
There are 2 independent parts, one for each index of `groups`. A program takes and returns all parts, laid end to end along the dimension named above; an argument that names none is the same for every part. Nothing has to cross between parts.
All inputs are finite; a program needn't handle non-finite values.
Results may differ from a plain program's by a relative error of at most 0.0055.
The roundings to bfloat16 on the way count: a program that leaves them out, or rounds other values in their place, can miss the bound.
Values may be sent and summed in bfloat16 or wider, within the bound.
No kernel may reach another device: no remote copies, remote signals or barrier semaphores. Data moves between devices by JAX's collectives and lax.ppermute only.
A program may use at most 64 MiB of HBM per device.

v0:
```python
import jax
import jax.numpy as jnp
from jax import lax
from jax.sharding import PartitionSpec as P

HD = 128
SPAN = 4


def passed_along(block, axis, distance):
    devices = range(lax.axis_size(axis))
    route = [((i - distance) % len(devices), i) for i in devices]
    return lax.ppermute(block, axis, route)


def per_device(acts, w_query, w_key, w_value):
    block = lax.all_gather(acts, "row", axis=0, tiled=True)
    block = lax.all_gather(block, "col", axis=1, tiled=True)
    tokens_here = block.shape[0]
    width = w_query.shape[1]
    heads_here = width // HD
    pieces = (
        lax.all_gather(w_query, "seq", axis=0, tiled=True),
        lax.all_gather(w_key, "seq", axis=0, tiled=True),
        lax.all_gather(w_value, "seq", axis=0, tiled=True),
    )
    query_sum, key_sum, value_sum = tuple(
        (jnp.dot(block, piece, preferred_element_type=jnp.float32) for piece in pieces)
    )
    query = query_sum.astype(jnp.bfloat16).reshape(tokens_here, heads_here, HD)
    packed = jnp.stack([key_sum.astype(jnp.bfloat16), value_sum.astype(jnp.bfloat16)])
    blocks_seen = [packed]
    current = packed
    for step in range(1, SPAN):
        current = passed_along(current, "seq", 1)
        blocks_seen.append(current)
    scale = 1.0 / jnp.sqrt(jnp.float32(HD))
    score_list = []
    for seen in blocks_seen:
        seen_keys = seen[0].reshape(-1, heads_here, HD)
        score_list.append(
            jnp.einsum("qhd,khd->hqk", query, seen_keys, preferred_element_type=jnp.float32) * scale
        )
    largest = score_list[0].max(axis=-1, keepdims=True)
    for scores in score_list[1:]:
        largest = jnp.maximum(largest, scores.max(axis=-1, keepdims=True))
    running_total = jnp.zeros((heads_here, tokens_here), jnp.float32)
    summed = jnp.zeros((tokens_here, heads_here, HD), jnp.float32)
    for scores, seen in zip(score_list, blocks_seen):
        expos = jnp.exp(scores - largest)
        running_total = running_total + jnp.sum(expos, axis=-1)
        seen_values = seen[1].reshape(-1, heads_here, HD)
        summed = summed + jnp.einsum(
            "hqk,khd->qhd",
            expos.astype(jnp.bfloat16),
            seen_values,
            preferred_element_type=jnp.float32,
        )
    attended = summed / jnp.transpose(running_total)[:, :, None]
    return attended.astype(jnp.bfloat16).reshape(tokens_here, width)


def solution(mesh):
    in_specs = (
        P(("groups", "seq", "row"), "col"),
        P("seq", ("row", "col")),
        P("seq", ("row", "col")),
        P("seq", ("row", "col")),
    )
    out_specs = P(("groups", "seq"), ("row", "col"))
    return jax.shard_map(
        per_device, mesh=mesh, in_specs=in_specs, out_specs=out_specs, check_vma=False
    )
```

profile of v0, /device:TPU:0, one launch (start us, length us, event | category | flops | bytes accessed | tf_op | source)
XLA Modules:
  0.0 381.3 jit_solution(7910305317543473265)
XLA Ops:
  7.3 31.5 %all-gather.6.cloned.1.call-done = bf16[384,2048]{1,0:T(8,128)(2,1)} async-done(((bf16[192,2048]{1,0:T(8,128)(2,1)}), bf16[384,2048]{1,0:T(8,128)(2,1)}) %all-gather.6.cloned.1.call-update) | async-done | bytes 1572880 | tf_op jit(solution)/shard_map/all_gather | solution.py:17
  40.8 11.8 %all-gather.8.cloned.1.call-done = bf16[384,4096]{1,0:T(8,128)(2,1)} async-done(((bf16[384,2048]{1,0:T(8,128)(2,1)}), bf16[384,4096]{1,0:T(8,128)(2,1)}) %all-gather.8.cloned.1.call-update) | async-done | bytes 3145744 | tf_op jit(solution)/shard_map/all_gather | solution.py:18
  52.5 83.5 %all-gather.10.cloned.1.call-done = bf16[4096,512]{1,0:T(8,128)(2,1)} async-done(((bf16[1024,512]{1,0:T(8,128)(2,1)}), bf16[4096,512]{1,0:T(8,128)(2,1)}) %all-gather.10.cloned.1.call-update) | async-done | bytes 4194320 | tf_op jit(solution)/shard_map/all_gather | solution.py:25
  136.1 4.9 %convolution_convert_fusion.2 = bf16[384,512]{1,0:T(8,128)(2,1)S(1)} fusion(bf16[384,4096]{1,0:T(8,128)(2,1)} %all-gather.8.cloned.1.call-done, bf16[4096,512]{1,0:T(8,128)(2,1)} %all-gather.10.cloned.1.call-done), kind=kOutput, calls=%fused_computation.24 | convolution fusion | flops 1610809344 | bytes 7733248 | tf_op jit(solution)/shard_map/dot_general | solution.py:28
  141.0 75.8 %all-gather.14.cloned.1.call-done = bf16[4096,512]{1,0:T(8,128)(2,1)} async-done(((bf16[1024,512]{1,0:T(8,128)(2,1)}), bf16[4096,512]{1,0:T(8,128)(2,1)}) %all-gather.14.cloned.1.call-update) | async-done | bytes 4194320 | tf_op jit(solution)/shard_map/all_gather | solution.py:24
  216.8 4.9 %convolution_convert_fusion = bf16[384,512]{1,0:T(8,128)(2,1)S(1)} fusion(bf16[384,4096]{1,0:T(8,128)(2,1)} %all-gather.8.cloned.1.call-done, bf16[4096,512]{1,0:T(8,128)(2,1)} %all-gather.14.cloned.1.call-done), kind=kOutput, calls=%fused_computation.22 | convolution fusion | flops 1610809344 | bytes 7733248 | tf_op jit(solution)/shard_map/dot_general | solution.py:28
  221.9 35.7 %collective-permute-done = bf16[2,384,512]{2,1,0:T(8,128)(2,1)} collective-permute-done((bf16[2,384,512]{2,1,0:T(8,128)(2,1)S(1)}, bf16[2,384,512]{2,1,0:T(8,128)(2,1)}, u32[]{:S(2)}, u32[]{:S(2)}) %collective-permute-start) | collective-permute-done | bytes 786464 | tf_op jit(solution)/shard_map/ppermute | solution.py:13
  257.6 10.9 %collective-permute-start.1 = (bf16[2,384,512]{2,1,0:T(8,128)(2,1)}, bf16[2,384,512]{2,1,0:T(8,128)(2,1)}, u32[]{:S(2)}, u32[]{:S(2)}) collective-permute-start(bf16[2,384,512]{2,1,0:T(8,128)(2,1)} %collective-permute-done), channel_id=1, source_target_pairs={{12,0},{0,4},{4,8},{8,12},{13,1},{1,5},{5,9},{9,13},{14,2},{2,6},{... | collective-permute-start | bytes 2359304 | tf_op jit(solution)/shard_map/ppermute | solution.py:13
  268.5 59.4 %all-gather.12.cloned.1.call-done = bf16[4096,512]{1,0:T(8,128)(2,1)} async-done(((bf16[1024,512]{1,0:T(8,128)(2,1)}), bf16[4096,512]{1,0:T(8,128)(2,1)}) %all-gather.12.cloned.1.call-update) | async-done | bytes 4194320 | tf_op jit(solution)/shard_map/all_gather | solution.py:23
  327.9 4.9 %fusion.11 = bf16[48,4,8,128]{3,2,1,0:T(8,128)(2,1)S(1)} fusion(bf16[384,4096]{1,0:T(8,128)(2,1)} %all-gather.8.cloned.1.call-done, bf16[4096,512]{1,0:T(8,128)(2,1)} %all-gather.12.cloned.1.call-done), kind=kOutput, calls=%fused_computation.25 | convolution fusion | flops 1610809344 | bytes 7733248 | tf_op jit(solution)/shard_map/dot_general | solution.py:28
  334.2 1.2 fusion.48
  336.5 2.9 multiply_reduce_fusion.2
  339.4 1.9 fusion.47
  342.1 1.2 copy.28
  343.3 3.5 multiply_reduce_fusion.1
  346.8 11.3 %collective-permute-done.2 = bf16[2,384,512]{2,1,0:T(8,128)(2,1)} collective-permute-done((bf16[2,384,512]{2,1,0:T(8,128)(2,1)}, bf16[2,384,512]{2,1,0:T(8,128)(2,1)}, u32[]{:S(2)}, u32[]{:S(2)}) %collective-permute-start.2) | collective-permute-done | bytes 786464 | tf_op jit(solution)/shard_map/ppermute | solution.py:13
  358.1 2.1 fusion.46
  360.2 1.8 reshape_squeeze.20
  362.0 3.5 multiply_reduce_fusion
  365.5 1.2 copy.29
  367.6 1.7 fusion.15
  369.9 1.1 copy-done.1
  371.0 1.6 fusion.2
  373.9 0.9 copy.21
  (29 shorter events, 8.8 us)
Async XLA Ops:
  6.5 32.3 %all-gather.6.cloned.1.call-start = ((), (), s32[]{:S(2)}) async-start(), calls=%async_computation | async-start | bytes 2359296 | tf_op jit(solution)/shard_map/all_gather | solution.py:17
  7.3 45.3 %all-gather.8.cloned.1.call-start = ((), (), s32[]{:S(2)}) async-start(), calls=%async_computation.1 | async-start | bytes 4718592 | tf_op jit(solution)/shard_map/all_gather | solution.py:18
  38.9 97.2 %all-gather.10.cloned.1.call-start = ((), (), s32[]{:S(2)}) async-start(), calls=%async_computation.2 | async-start | bytes 5242880 | tf_op jit(solution)/shard_map/all_gather | solution.py:25
  39.6 177.2 %all-gather.14.cloned.1.call-start = ((), (), s32[]{:S(2)}) async-start(), calls=%async_computation.4 | async-start | bytes 5242880 | tf_op jit(solution)/shard_map/all_gather | solution.py:24
  40.2 287.7 %all-gather.12.cloned.1.call-start = ((), (), s32[]{:S(2)}) async-start(), calls=%async_computation.3 | async-start | bytes 5242880 | tf_op jit(solution)/shard_map/all_gather | solution.py:23
  221.8 35.7 %collective-permute-start = (bf16[2,384,512]{2,1,0:T(8,128)(2,1)S(1)}, bf16[2,384,512]{2,1,0:T(8,128)(2,1)}, u32[]{:S(2)}, u32[]{:S(2)}) collective-permute-start(bf16[2,384,512]{2,1,0:T(8,128)(2,1)S(1)} %pad_maximum_fusion), channel_id=1, source_target_pairs={{12,0},{0,4},{4,8},{8,12},{13,1},{1,5},{5,9},{9,13},{14,2},{2,6},{... | collective-permute-start | bytes 2359304 | tf_op jit(solution)/shard_map/ppermute | solution.py:13
  257.6 78.8 %collective-permute-start.1 = (bf16[2,384,512]{2,1,0:T(8,128)(2,1)}, bf16[2,384,512]{2,1,0:T(8,128)(2,1)}, u32[]{:S(2)}, u32[]{:S(2)}) collective-permute-start(bf16[2,384,512]{2,1,0:T(8,128)(2,1)} %collective-permute-done), channel_id=1, source_target_pairs={{12,0},{0,4},{4,8},{8,12},{13,1},{1,5},{5,9},{9,13},{14,2},{2,6},{... | collective-permute-start | bytes 2359304 | tf_op jit(solution)/shard_map/ppermute | solution.py:13
  336.4 21.7 %collective-permute-start.2 = (bf16[2,384,512]{2,1,0:T(8,128)(2,1)}, bf16[2,384,512]{2,1,0:T(8,128)(2,1)}, u32[]{:S(2)}, u32[]{:S(2)}) collective-permute-start(bf16[2,384,512]{2,1,0:T(8,128)(2,1)} %collective-permute-done.1), channel_id=1, source_target_pairs={{12,0},{0,4},{4,8},{8,12},{13,1},{1,5},{5,9},{9,13},{14,2},{2,6},{... | collective-permute-start | bytes 2359304 | tf_op jit(solution)/shard_map/ppermute | solution.py:13
  366.7 2.6 copy-start
  367.6 2.3 copy-start.2
  369.3 1.7 copy-start.1
Sparse Core Ops, SparseCore 0:
  8.9 29.8 all-gather.5
  40.4 12.1 all-gather.7
  54.1 81.9 all-gather.9
  137.5 79.2 all-gather.13
  218.2 109.5 all-gather.11
where the time goes:
time: 382 us; the launch traced here: 381 us
  waiting for transfers between devices  311 us (81%)
  matrix products  28.6 us (7%)
  local copies, waits for them, and re-layouts  14.2 us (4%)
  between operations  13.3 us (3%)
  starting transfers between devices  11.2 us (3%)
    all_gather x1, waiting for transfers between devices, per_device(): lax.all_gather(w_value, 'seq', axis=0, tiled=True)  83.5 us
    all_gather x1, waiting for transfers between devices, per_device(): lax.all_gather(w_key, 'seq', axis=0, tiled=True)  75.8 us
    all_gather x1, waiting for transfers between devices, per_device(): lax.all_gather(w_query, 'seq', axis=0, tiled=True)  59.4 us
    ppermute x3, waiting for transfers between devices, passed_along(): return lax.ppermute(block, axis, route)  47 us
    all_gather x1, waiting for transfers between devices, per_device(): block = lax.all_gather(acts, 'row', axis=0, tiled=True)  31.5 us
    dot_general x3, matrix products, per_device(): jnp.dot(block, piece, preferred_element_type=jnp.float32)  14.8 us
    all_gather x1, waiting for transfers between devices, per_device(): block = lax.all_gather(block, 'col', axis=1, tiled=True)  11.8 us
    ppermute x3, starting transfers between devices, passed_along(): return lax.ppermute(block, axis, route)  11 us
  transfers between devices with their start and end apart: 8, of which 7 were waited for; matrix products, arithmetic and copies ran while one was open for 8% of the time, Pallas kernels for 0%

commit v1 on v0

--- a/solution.py
+++ b/solution.py
@@ -13,18 +13,35 @@
     return lax.ppermute(block, axis, route)
 
 
+def swap_gather(piece, axis, dim):
+    if lax.axis_size(axis) != 2:
+        return lax.all_gather(piece, axis, axis=dim, tiled=True)
+    first = lax.axis_index(axis) == 0
+    other = lax.ppermute(piece, axis, [(0, 1), (1, 0)])
+    low = jnp.where(first, piece, other)
+    high = jnp.where(first, other, piece)
+    return jnp.concatenate([low, high], axis=dim)
+
+
+def full_columns(weight, shared):
+    if not shared:
+        return lax.all_gather(weight, "seq", axis=0, tiled=True)
+    half = weight.shape[1] // 2
+    own = lax.dynamic_slice_in_dim(weight, lax.axis_index("groups") * half, half, axis=1)
+    own = lax.all_gather(own, "seq", axis=0, tiled=True)
+    other = lax.ppermute(own, "groups", [(0, 1), (1, 0)])
+    return jnp.concatenate([own, other], axis=1)
+
+
 def per_device(acts, w_query, w_key, w_value):
-    block = lax.all_gather(acts, "row", axis=0, tiled=True)
-    block = lax.all_gather(block, "col", axis=1, tiled=True)
+    block = swap_gather(acts, "row", 0)
+    block = swap_gather(block, "col", 1)
     tokens_here = block.shape[0]
     width = w_query.shape[1]
     heads_here = width // HD
-    pieces = (
-        lax.all_gather(w_query, "seq", axis=0, tiled=True),
-        lax.all_gather(w_key, "seq", axis=0, tiled=True),
-        lax.all_gather(w_value, "seq", axis=0, tiled=True),
-    )
-    query_sum, key_sum, value_sum = tuple(
+    shared = lax.axis_size("groups") == 2 and width % (2 * HD) == 0
+    pieces = tuple(full_columns(w, shared) for w in (w_key, w_value, w_query))
+    key_sum, value_sum, query_sum = tuple(
         (jnp.dot(block, piece, preferred_element_type=jnp.float32) for piece in pieces)
     )
     query = query_sum.astype(jnp.bfloat16).reshape(tokens_here, heads_here, HD)
@@ -57,7 +74,10 @@
             preferred_element_type=jnp.float32,
         )
     attended = summed / jnp.transpose(running_total)[:, :, None]
-    return attended.astype(jnp.bfloat16).reshape(tokens_here, width)
+    attended = attended.astype(jnp.bfloat16).reshape(tokens_here, width)
+    if shared:
+        attended = jnp.roll(attended, lax.axis_index("groups") * (width // 2), axis=1)
+    return attended
 
 
 def solution(mesh):

time: 382 us -> 253 us (0.66)
  waiting for transfers between devices: 311 us -> 172 us
  local copies, waits for them, and re-layouts: 14.2 us -> 25.9 us
  other arithmetic: 2.54 us -> 8.14 us
    all_gather x5 -> x3, waiting for transfers between devices: 262 us -> 113 us  [full_columns(): own = lax.all_gather(own, 'seq', axis=0, tiled=True)]
    ppermute x0 -> x5, waiting for transfers between devices: none -> 30 us  [the longest x2 16.8 us: swap_gather(): other = lax.ppermute(piece, axis, [(0, 1), (1, 0)])]
    ppermute x3, waiting for transfers between devices: 47 us -> 28.8 us  [passed_along(): return lax.ppermute(block, axis, route)]
    ppermute x3, starting transfers between devices: 11 us -> 0.01 us  [passed_along(): return lax.ppermute(block, axis, route)]
    ppermute x0 -> x5, starting transfers between devices: none -> 7.43 us  [the longest x3 4.42 us: full_columns(): other = lax.ppermute(own, 'groups', [(0, 1), (1, 0)])]
  transfers between devices with their start and end apart: 8 -> 11, of which waited for: 7 -> 7; matrix products, arithmetic and copies ran while one was open for 8% -> 16% of each run, Pallas kernels for 0% -> 0%
where the time goes in v1:
time: 253 us
  waiting for transfers between devices  172 us (68%)
  local copies, waits for them, and re-layouts  25.9 us (10%)
  matrix products  25.5 us (10%)
  between operations  13.4 us (5%)
  other arithmetic  8.14 us (3%)
  starting transfers between devices  7.52 us (3%)
    all_gather x3, waiting for transfers between devices, full_columns(): own = lax.all_gather(own, 'seq', axis=0, tiled=True)  113 us
    ppermute x3, waiting for transfers between devices, passed_along(): return lax.ppermute(block, axis, route)  28.8 us
    ppermute x2, waiting for transfers between devices, swap_gather(): other = lax.ppermute(piece, axis, [(0, 1), (1, 0)])  16.8 us
    ppermute x3, waiting for transfers between devices, full_columns(): other = lax.ppermute(own, 'groups', [(0, 1), (1, 0)])  13.2 us
    dot_general x3, matrix products, per_device(): jnp.dot(block, piece, preferred_element_type=jnp.float32)  12.4 us
    dot_general x4, matrix products, per_device(): jnp.einsum('qhd,khd->hqk', query, seen_keys, preferred_element_type=jnp.f...  9.53 us
    another operation x4, local copies, waits for them, and re-layouts, per_device(): seen_values = seen[1].reshape(-1, heads_here, HD)  6.71 us
    slice x3, local copies, waits for them, and re-layouts, per_device(): seen_values = seen[1].reshape(-1, heads_here, HD)  6.24 us
  transfers between devices with their start and end apart: 11, of which 7 were waited for; matrix products, arithmetic and copies ran while one was open for 16% of the time, Pallas kernels for 0%

profile of v1, /device:TPU:0, one launch (start us, length us, event | category | flops | bytes accessed | tf_op | source)
XLA Modules:
  0.0 252.6 jit_solution(11105573697930698816)
XLA Ops:
  8.6 1.9 constant_dynamic-slice_fusion
  10.6 3.0 %collective-permute-start = (bf16[192,2048]{1,0:T(8,128)(2,1)S(1)}, bf16[192,2048]{1,0:T(8,128)(2,1)}, u32[]{:S(2)}, u32[]{:S(2)}) collective-permute-start(bf16[192,2048]{1,0:T(8,128)(2,1)S(1)} %copy-done.12), channel_id=1, source_target_pairs={{0,2},{2,0},{1,3},{3,1},{4,6},{6,4},{5,7},{7,5},{8,10},{10,8},{9,1... | collective-permute-start | bytes 2359304 | tf_op jit(solution)/shard_map/ppermute | solution.py:20
  14.5 16.8 %collective-permute-done = bf16[192,2048]{1,0:T(8,128)(2,1)} collective-permute-done((bf16[192,2048]{1,0:T(8,128)(2,1)S(1)}, bf16[192,2048]{1,0:T(8,128)(2,1)}, u32[]{:S(2)}, u32[]{:S(2)}) %collective-permute-start) | collective-permute-done | bytes 786464 | tf_op jit(solution)/shard_map/ppermute | solution.py:20
  33.8 23.8 %all-gather.4.cloned.1.call-done = bf16[4096,256]{1,0:T(8,128)(2,1)} async-done(((bf16[1024,256]{1,0:T(8,128)(2,1)}), bf16[4096,256]{1,0:T(8,128)(2,1)}) %all-gather.4.cloned.1.call-update) | async-done | bytes 2097168 | tf_op jit(solution)/shard_map/all_gather | solution.py:31
  59.1 44.8 %all-gather.8.cloned.1.call-done = bf16[4096,256]{1,0:T(8,128)(2,1)} async-done(((bf16[1024,256]{1,0:T(8,128)(2,1)}), bf16[4096,256]{1,0:T(8,128)(2,1)}) %all-gather.8.cloned.1.call-update) | async-done | bytes 2097168 | tf_op jit(solution)/shard_map/all_gather | solution.py:31
  105.3 44.8 %all-gather.6.cloned.1.call-done = bf16[4096,256]{1,0:T(8,128)(2,1)} async-done(((bf16[1024,256]{1,0:T(8,128)(2,1)}), bf16[4096,256]{1,0:T(8,128)(2,1)}) %all-gather.6.cloned.1.call-update) | async-done | bytes 2097168 | tf_op jit(solution)/shard_map/all_gather | solution.py:31
  151.6 2.2 broadcast_select_fusion.1
  153.8 4.6 %fusion.29 = bf16[384,512]{1,0:T(8,128)(2,1)S(1)} fusion(bf16[4096,256]{1,0:T(8,128)(2,1)} %collective-permute-done.2, bf16[4096,256]{1,0:T(8,128)(2,1)S(1)} %copy-done.15, bf16[384,2048]{1,0:T(8,128)(2,1)S(1)} %get-tuple-element.10, bf16[384,2048]{1,0:T(8,128)(2,1)S(1)} %get-tuple-element.9), kind=kOutput, calls=%fused_computation.40 | convolution fusion | flops 1625489408 | bytes 7733248 | tf_op jit(solution)/shard_map/dot_general | solution.py:45
  158.4 3.4 %fusion.23 = bf16[384,512]{1,0:T(8,128)(2,1)S(1)} fusion(bf16[4096,256]{1,0:T(8,128)(2,1)} %collective-permute-done.4, bf16[4096,256]{1,0:T(8,128)(2,1)S(1)} %copy-done.16, bf16[384,2048]{1,0:T(8,128)(2,1)S(1)} %get-tuple-element.10, bf16[384,2048]{1,0:T(8,128)(2,1)S(1)} %get-tuple-element.9), kind=kOutput, calls=%fused_computation.38 | convolution fusion | flops 1625489408 | bytes 7733248 | tf_op jit(solution)/shard_map/dot_general | solution.py:45
  164.5 20.2 %collective-permute-done.5 = bf16[2,384,512]{2,1,0:T(8,128)(2,1)} collective-permute-done((bf16[2,384,512]{2,1,0:T(8,128)(2,1)}, bf16[2,384,512]{2,1,0:T(8,128)(2,1)}, u32[]{:S(2)}, u32[]{:S(2)}) %collective-permute-start.5) | collective-permute-done | bytes 786464 | tf_op jit(solution)/shard_map/ppermute | solution.py:13
  184.6 13.2 %collective-permute-done.3 = bf16[4096,256]{1,0:T(8,128)(2,1)} collective-permute-done((bf16[4096,256]{1,0:T(8,128)(2,1)}, bf16[4096,256]{1,0:T(8,128)(2,1)}, u32[]{:S(2)}, u32[]{:S(2)}) %collective-permute-start.3) | collective-permute-done | bytes 2097184 | tf_op jit(solution)/shard_map/ppermute | solution.py:32
  197.8 4.5 %fusion.32 = bf16[48,4,8,128]{3,2,1,0:T(8,128)(2,1)S(1)} fusion(bf16[4096,256]{1,0:T(8,128)(2,1)} %collective-permute-done.3, bf16[4096,256]{1,0:T(8,128)(2,1)} %all-gather.6.cloned.1.call-done, bf16[384,2048]{1,0:T(8,128)(2,1)} %copy-done.9, bf16[384,2048]{1,0:T(8,128)(2,1)S(1)} %copy-done.8), kind=kOutput, calls=%fused_computation.41 | convolution fusion | flops 1625489408 | bytes 7733248 | tf_op jit(solution)/shard_map/dot_general | solution.py:45
  202.8 2.1 fusion.75
  204.9 1.8 reshape_squeeze.18
  206.8 1.9 copy.28
  208.7 3.0 %multiply_reduce_fusion.2 = (f32[4,384]{1,0:T(4,128)S(1)}, f32[4,384,384]{1,2,0:T(8,128)}) fusion(bf16[384,4,128]{2,1,0:T(4,128)(2,1)} %reshape_squeeze.18, bf16[48,4,8,128]{3,2,1,0:T(8,128)(2,1)} %copy-done.4), kind=kOutput, calls=%fused_computation.19 | convolution fusion | flops 152173056 | bytes 3151872 | tf_op jit(solution)/shard_map/qhd,khd->hqk/dot_general | solution.py:59
  211.7 2.1 fusion.74
  215.6 2.0 copy.29
  217.6 3.0 %multiply_reduce_fusion.1 = (f32[4,384]{1,0:T(4,128)S(1)}, f32[4,384,384]{1,2,0:T(8,128)}) fusion(bf16[384,4,128]{2,1,0:T(4,128)(2,1)} %reshape_squeeze.19, bf16[48,4,8,128]{3,2,1,0:T(8,128)(2,1)} %copy-done.4), kind=kOutput, calls=%fused_computation.18 | convolution fusion | flops 152173056 | bytes 3151872 | tf_op jit(solution)/shard_map/qhd,khd->hqk/dot_general | solution.py:59
  220.6 8.6 %collective-permute-done.7 = bf16[2,384,512]{2,1,0:T(8,128)(2,1)} collective-permute-done((bf16[2,384,512]{2,1,0:T(8,128)(2,1)}, bf16[2,384,512]{2,1,0:T(8,128)(2,1)}, u32[]{:S(2)}, u32[]{:S(2)}) %collective-permute-start.7) | collective-permute-done | bytes 786464 | tf_op jit(solution)/shard_map/ppermute | solution.py:13
  229.2 2.1 fusion.73
  231.3 1.9 reshape_squeeze.20
  233.2 3.0 %multiply_reduce_fusion = (f32[4,384]{1,0:T(4,128)S(1)}, f32[4,384,384]{1,2,0:T(8,128)}) fusion(bf16[384,4,128]{2,1,0:T(4,128)(2,1)} %reshape_squeeze.20, bf16[48,4,8,128]{3,2,1,0:T(8,128)(2,1)} %copy-done.4), kind=kOutput, calls=%fused_computation.17 | convolution fusion | flops 152173056 | bytes 3151872 | tf_op jit(solution)/shard_map/qhd,khd->hqk/dot_general | solution.py:59
  236.2 1.9 copy.30
  (68 shorter events, 22.8 us)
Async XLA Ops:
  6.5 4.1 %copy-start.12 = (bf16[192,2048]{1,0:T(8,128)(2,1)S(1)}, bf16[192,2048]{1,0:T(8,128)(2,1)}, u32[]{:S(2)}) copy-start(bf16[192,2048]{1,0:T(8,128)(2,1)} %param.4) | copy-start | bytes 2359300
  6.5 7.1 %copy-start.14 = (bf16[1024,512]{1,0:T(8,128)(2,1)S(1)}, bf16[1024,512]{1,0:T(8,128)(2,1)}, u32[]{:S(2)}) copy-start(bf16[1024,512]{1,0:T(8,128)(2,1)} %param.5) | copy-start | bytes 3145732
  6.5 51.1 %all-gather.4.cloned.1.call-start = ((), (), s32[]{:S(2)}) async-start(), calls=%async_computation | async-start | bytes 2621440 | tf_op jit(solution)/shard_map/all_gather | solution.py:31
  8.6 95.3 %all-gather.8.cloned.1.call-start = ((), (), s32[]{:S(2)}) async-start(), calls=%async_computation.2 | async-start | bytes 2621440 | tf_op jit(solution)/shard_map/all_gather | solution.py:31
  10.6 139.5 %all-gather.6.cloned.1.call-start = ((), (), s32[]{:S(2)}) async-start(), calls=%async_computation.1 | async-start | bytes 2621440 | tf_op jit(solution)/shard_map/all_gather | solution.py:31
  10.6 20.7 %collective-permute-start = (bf16[192,2048]{1,0:T(8,128)(2,1)S(1)}, bf16[192,2048]{1,0:T(8,128)(2,1)}, u32[]{:S(2)}, u32[]{:S(2)}) collective-permute-start(bf16[192,2048]{1,0:T(8,128)(2,1)S(1)} %copy-done.12), channel_id=1, source_target_pairs={{0,2},{2,0},{1,3},{3,1},{4,6},{6,4},{5,7},{7,5},{8,10},{10,8},{9,1... | collective-permute-start | bytes 2359304 | tf_op jit(solution)/shard_map/ppermute | solution.py:20
  33.8 117.8 %collective-permute-start.1 = (bf16[384,2048]{1,0:T(8,128)(2,1)}, bf16[384,2048]{1,0:T(8,128)(2,1)}, u32[]{:S(2)}, u32[]{:S(2)}) collective-permute-start(bf16[384,2048]{1,0:T(8,128)(2,1)} %pad_maximum_fusion.1), channel_id=1, source_target_pairs={{0,1},{1,0},{2,3},{3,2},{4,5},{5,4},{6,7},{7,6},{8,9},{9,8},{10,11... | collective-permute-start | bytes 4718600 | tf_op jit(solution)/shard_map/ppermute | solution.py:20
  57.6 96.2 %collective-permute-start.2 = (bf16[4096,256]{1,0:T(8,128)(2,1)}, bf16[4096,256]{1,0:T(8,128)(2,1)}, u32[]{:S(2)}, u32[]{:S(2)}) collective-permute-start(bf16[4096,256]{1,0:T(8,128)(2,1)} %all-gather.4.cloned.1.call-done), channel_id=1, source_target_pairs={{0,16},{16,0},{1,17},{17,1},{2,18},{18,2},{3,19},{19,3},{4,20},{20... | collective-permute-start | bytes 6291464 | tf_op jit(solution)/shard_map/ppermute | solution.py:32
  103.9 54.5 %collective-permute-start.4 = (bf16[4096,256]{1,0:T(8,128)(2,1)}, bf16[4096,256]{1,0:T(8,128)(2,1)}, u32[]{:S(2)}, u32[]{:S(2)}) collective-permute-start(bf16[4096,256]{1,0:T(8,128)(2,1)} %all-gather.8.cloned.1.call-done), channel_id=1, source_target_pairs={{0,16},{16,0},{1,17},{17,1},{2,18},{18,2},{3,19},{19,3},{4,20},{20... | collective-permute-start | bytes 6291464 | tf_op jit(solution)/shard_map/ppermute | solution.py:32
  150.1 3.7 %copy-start.15 = (bf16[4096,256]{1,0:T(8,128)(2,1)S(1)}, bf16[4096,256]{1,0:T(8,128)(2,1)}, u32[]{:S(2)}) copy-start(bf16[4096,256]{1,0:T(8,128)(2,1)} %all-gather.4.cloned.1.call-done) | copy-start | bytes 6291460
  150.1 47.7 %collective-permute-start.3 = (bf16[4096,256]{1,0:T(8,128)(2,1)}, bf16[4096,256]{1,0:T(8,128)(2,1)}, u32[]{:S(2)}, u32[]{:S(2)}) collective-permute-start(bf16[4096,256]{1,0:T(8,128)(2,1)} %all-gather.6.cloned.1.call-done), channel_id=1, source_target_pairs={{0,16},{16,0},{1,17},{17,1},{2,18},{18,2},{3,19},{19,3},{4,20},{20... | collective-permute-start | bytes 6291464 | tf_op jit(solution)/shard_map/ppermute | solution.py:32
  153.8 4.6 %copy-start.7 = (bf16[384,2048]{1,0:T(8,128)(2,1)}, bf16[384,2048]{1,0:T(8,128)(2,1)S(1)}, u32[]{:S(2)}) copy-start(bf16[384,2048]{1,0:T(8,128)(2,1)S(1)} %get-tuple-element.9) | copy-start | bytes 4718596
  153.8 4.6 %copy-start.9 = (bf16[384,2048]{1,0:T(8,128)(2,1)}, bf16[384,2048]{1,0:T(8,128)(2,1)S(1)}, u32[]{:S(2)}) copy-start(bf16[384,2048]{1,0:T(8,128)(2,1)S(1)} %get-tuple-element.10) | copy-start | bytes 4718596
  153.8 4.6 %copy-start.16 = (bf16[4096,256]{1,0:T(8,128)(2,1)S(1)}, bf16[4096,256]{1,0:T(8,128)(2,1)}, u32[]{:S(2)}) copy-start(bf16[4096,256]{1,0:T(8,128)(2,1)} %all-gather.8.cloned.1.call-done) | copy-start | bytes 6291460
  161.8 36.0 %copy-start.8 = (bf16[384,2048]{1,0:T(8,128)(2,1)S(1)}, bf16[384,2048]{1,0:T(8,128)(2,1)}, u32[]{:S(2)}) copy-start(bf16[384,2048]{1,0:T(8,128)(2,1)} %copy-done.7) | copy-start | bytes 4718596
  163.5 21.1 %collective-permute-start.5 = (bf16[2,384,512]{2,1,0:T(8,128)(2,1)}, bf16[2,384,512]{2,1,0:T(8,128)(2,1)}, u32[]{:S(2)}, u32[]{:S(2)}) collective-permute-start(bf16[2,384,512]{2,1,0:T(8,128)(2,1)} %pad_maximum_fusion.5), channel_id=1, source_target_pairs={{12,0},{0,4},{4,8},{8,12},{13,1},{1,5},{5,9},{9,13},{14,2},{2,6},{... | collective-permute-start | bytes 2359304 | tf_op jit(solution)/shard_map/ppermute | solution.py:13
  164.4 37.9 %copy-start.11 = (bf16[384,512]{1,0:T(8,128)(2,1)S(1)}, bf16[384,512]{1,0:T(8,128)(2,1)}, u32[]{:S(2)}) copy-start(bf16[384,512]{1,0:T(8,128)(2,1)} %copy-done.10) | copy-start | bytes 1179652
  184.6 24.0 %collective-permute-start.6 = (bf16[2,384,512]{2,1,0:T(8,128)(2,1)}, bf16[2,384,512]{2,1,0:T(8,128)(2,1)}, u32[]{:S(2)}, u32[]{:S(2)}) collective-permute-start(bf16[2,384,512]{2,1,0:T(8,128)(2,1)} %collective-permute-done.5), channel_id=1, source_target_pairs={{12,0},{0,4},{4,8},{8,12},{13,1},{1,5},{5,9},{9,13},{14,2},{2,6},{... | collective-permute-start | bytes 2359304 | tf_op jit(solution)/shard_map/ppermute | solution.py:13
  202.3 2.6 %copy-start.4 = (bf16[48,4,8,128]{3,2,1,0:T(8,128)(2,1)}, bf16[48,4,8,128]{3,2,1,0:T(8,128)(2,1)S(1)}, u32[]{:S(2)}) copy-start(bf16[48,4,8,128]{3,2,1,0:T(8,128)(2,1)S(1)} %fusion.32) | copy-start | bytes 1179652
  208.7 20.5 %collective-permute-start.7 = (bf16[2,384,512]{2,1,0:T(8,128)(2,1)}, bf16[2,384,512]{2,1,0:T(8,128)(2,1)}, u32[]{:S(2)}, u32[]{:S(2)}) collective-permute-start(bf16[2,384,512]{2,1,0:T(8,128)(2,1)} %collective-permute-done.6), channel_id=1, source_target_pairs={{12,0},{0,4},{4,8},{8,12},{13,1},{1,5},{5,9},{9,13},{14,2},{2,6},{... | collective-permute-start | bytes 2359304 | tf_op jit(solution)/shard_map/ppermute | solution.py:13
  238.1 1.8 copy-start.1
  238.1 1.8 copy-start.5
  238.1 2.6 %copy-start.3 = (f32[4,384,384]{1,2,0:T(8,128)S(1)}, f32[4,384,384]{1,2,0:T(8,128)}, u32[]{:S(2)}) copy-start(f32[4,384,384]{1,2,0:T(8,128)} %get-tuple-element.20) | copy-start | bytes 7077892
  239.9 1.9 copy-start.2
  (4 other events, 4.6 us)
Sparse Core Ops, SparseCore 0:
  8.9 48.6 all-gather.3
  59.2 44.6 all-gather.7
  105.4 44.6 all-gather.5

commit v2 on v1

--- a/solution.py
+++ b/solution.py
@@ -46,33 +46,25 @@
     )
     query = query_sum.astype(jnp.bfloat16).reshape(tokens_here, heads_here, HD)
     packed = jnp.stack([key_sum.astype(jnp.bfloat16), value_sum.astype(jnp.bfloat16)])
-    blocks_seen = [packed]
-    current = packed
-    for step in range(1, SPAN):
-        current = passed_along(current, "seq", 1)
-        blocks_seen.append(current)
+    if lax.axis_size("seq") == SPAN:
+        seen = lax.all_gather(packed, "seq", axis=1, tiled=True)
+    else:
+        blocks_seen = [packed]
+        current = packed
+        for step in range(1, SPAN):
+            current = passed_along(current, "seq", 1)
+            blocks_seen.append(current)
+        seen = jnp.concatenate(blocks_seen, axis=1)
+    seen_keys = seen[0].reshape(-1, heads_here, HD)
+    seen_values = seen[1].reshape(-1, heads_here, HD)
     scale = 1.0 / jnp.sqrt(jnp.float32(HD))
-    score_list = []
-    for seen in blocks_seen:
-        seen_keys = seen[0].reshape(-1, heads_here, HD)
-        score_list.append(
-            jnp.einsum("qhd,khd->hqk", query, seen_keys, preferred_element_type=jnp.float32) * scale
-        )
-    largest = score_list[0].max(axis=-1, keepdims=True)
-    for scores in score_list[1:]:
-        largest = jnp.maximum(largest, scores.max(axis=-1, keepdims=True))
-    running_total = jnp.zeros((heads_here, tokens_here), jnp.float32)
-    summed = jnp.zeros((tokens_here, heads_here, HD), jnp.float32)
-    for scores, seen in zip(score_list, blocks_seen):
-        expos = jnp.exp(scores - largest)
-        running_total = running_total + jnp.sum(expos, axis=-1)
-        seen_values = seen[1].reshape(-1, heads_here, HD)
-        summed = summed + jnp.einsum(
-            "hqk,khd->qhd",
-            expos.astype(jnp.bfloat16),
-            seen_values,
-            preferred_element_type=jnp.float32,
-        )
+    scores = jnp.einsum("qhd,khd->hqk", query, seen_keys, preferred_element_type=jnp.float32) * scale
+    largest = scores.max(axis=-1, keepdims=True)
+    expos = jnp.exp(scores - largest)
+    running_total = jnp.sum(expos, axis=-1)
+    summed = jnp.einsum(
+        "hqk,khd->qhd", expos.astype(jnp.bfloat16), seen_values, preferred_element_type=jnp.float32
+    )
     attended = summed / jnp.transpose(running_total)[:, :, None]
     attended = attended.astype(jnp.bfloat16).reshape(tokens_here, width)
     if shared:

time: 253 us -> 242 us (0.957)
  local copies, waits for them, and re-layouts: 25.9 us -> 13.3 us
  waiting for transfers between devices: 172 us -> 181 us
  matrix products: 25.5 us -> 17.9 us
    ppermute x3, waiting for transfers between devices: 13.2 us -> 84.6 us  [full_columns(): other = lax.ppermute(own, 'groups', [(0, 1), (1, 0)])]
    all_gather x3, waiting for transfers between devices: 113 us -> 68.5 us  [full_columns(): own = lax.all_gather(own, 'seq', axis=0, tiled=True)]
    ppermute x3 -> x0, waiting for transfers between devices: 28.8 us -> none  [passed_along(): return lax.ppermute(block, axis, route)]
    all_gather x0 -> x1, waiting for transfers between devices: none -> 10.7 us  [per_device(): seen = lax.all_gather(packed, 'seq', axis=1, tiled=True)]
    dot_general x4 -> x1, matrix products: 9.53 us -> 2.88 us  [per_device(): jnp.einsum('qhd,khd->hqk', query, seen_keys, preferred_element_type=jnp.f...]
    another operation x4 -> x1, local copies, waits for them, and re-layouts: 6.71 us -> 1.57 us  [per_device(): seen_values = seen[1].reshape(-1, heads_here, HD)]
    slice x3 -> x1, local copies, waits for them, and re-layouts: 6.24 us -> 3.25 us  [per_device(): seen_keys = seen[0].reshape(-1, heads_here, HD)]
    another operation x3 -> x1, local copies, waits for them, and re-layouts: 5.56 us -> 3.5 us  [per_device(): seen_keys = seen[0].reshape(-1, heads_here, HD)]
  transfers between devices with their start and end apart: 11 -> 9, of which waited for: 7 -> 6; matrix products, arithmetic and copies ran while one was open for 16% -> 9% of each run, Pallas kernels for 0% -> 0%
where the time goes in v2:
time: 242 us; the launch traced here: 241 us
  waiting for transfers between devices  181 us (75%)
  matrix products  17.9 us (7%)
  local copies, waits for them, and re-layouts  13.3 us (5%)
  between operations  13.3 us (5%)
  other arithmetic  8.47 us (4%)
  starting transfers between devices  7.62 us (3%)
    ppermute x3, waiting for transfers between devices, full_columns(): other = lax.ppermute(own, 'groups', [(0, 1), (1, 0)])  84.6 us
    all_gather x3, waiting for transfers between devices, full_columns(): own = lax.all_gather(own, 'seq', axis=0, tiled=True)  68.5 us
    ppermute x2, waiting for transfers between devices, swap_gather(): other = lax.ppermute(piece, axis, [(0, 1), (1, 0)])  16.7 us
    dot_general x3, matrix products, per_device(): jnp.dot(block, piece, preferred_element_type=jnp.float32)  12.9 us
    all_gather x1, waiting for transfers between devices, per_device(): seen = lax.all_gather(packed, 'seq', axis=1, tiled=True)  10.7 us
  transfers between devices with their start and end apart: 9, of which 6 were waited for; matrix products, arithmetic and copies ran while one was open for 9% of the time, Pallas kernels for 0%

profile of v2, /device:TPU:0, one launch (start us, length us, event | category | flops | bytes accessed | tf_op | source)
XLA Modules:
  0.0 241.2 jit_solution(16787921971046270781)
XLA Ops:
  6.6 1.2 copy-done
  8.7 1.9 constant_dynamic-slice_fusion.2
  10.6 3.0 %collective-permute-start = (bf16[192,2048]{1,0:T(8,128)(2,1)S(1)}, bf16[192,2048]{1,0:T(8,128)(2,1)}, u32[]{:S(2)}, u32[]{:S(2)}) collective-permute-start(bf16[192,2048]{1,0:T(8,128)(2,1)S(1)} %copy-done.4), channel_id=1, source_target_pairs={{0,2},{2,0},{1,3},{3,1},{4,6},{6,4},{5,7},{7,5},{8,10},{10,8},{9,1... | collective-permute-start | bytes 2359304 | tf_op jit(solution)/shard_map/ppermute | solution.py:20
  14.5 16.7 %collective-permute-done = bf16[192,2048]{1,0:T(8,128)(2,1)} collective-permute-done((bf16[192,2048]{1,0:T(8,128)(2,1)S(1)}, bf16[192,2048]{1,0:T(8,128)(2,1)}, u32[]{:S(2)}, u32[]{:S(2)}) %collective-permute-start) | collective-permute-done | bytes 786464 | tf_op jit(solution)/shard_map/ppermute | solution.py:20
  31.3 1.2 broadcast_select_fusion.3
  32.5 1.3 pad_maximum_fusion.1
  33.9 23.7 %all-gather.7.cloned.1.call-done = bf16[4096,256]{1,0:T(8,128)(2,1)} async-done(((bf16[1024,256]{1,0:T(8,128)(2,1)}), bf16[4096,256]{1,0:T(8,128)(2,1)}) %all-gather.7.cloned.1.call-update) | async-done | bytes 2097168 | tf_op jit(solution)/shard_map/all_gather | solution.py:31
  57.6 1.5 collective-permute-start.3
  59.1 44.8 %all-gather.5.cloned.1.call-done = bf16[4096,256]{1,0:T(8,128)(2,1)} async-done(((bf16[1024,256]{1,0:T(8,128)(2,1)}), bf16[4096,256]{1,0:T(8,128)(2,1)}) %all-gather.5.cloned.1.call-update) | async-done | bytes 2097168 | tf_op jit(solution)/shard_map/all_gather | solution.py:31
  103.9 1.5 collective-permute-start.2
  105.3 2.3 broadcast_select_fusion.1
  107.7 4.6 %fusion.35 = bf16[1,384,512]{2,1,0:T(8,128)(2,1)S(1)} fusion(bf16[4096,256]{1,0:T(8,128)(2,1)} %collective-permute-done.3, bf16[4096,256]{1,0:T(8,128)(2,1)S(1)} %copy-done.6, bf16[384,2048]{1,0:T(8,128)(2,1)S(1)} %get-tuple-element.8, bf16[384,2048]{1,0:T(8,128)(2,1)S(1)} %get-tuple-element.7), kind=kOutput, calls=%fused_computation.30 | convolution fusion | flops 1625489408 | bytes 7733248 | tf_op jit(solution)/shard_map/dot_general | solution.py:45
  112.3 39.3 %collective-permute-done.2 = bf16[4096,256]{1,0:T(8,128)(2,1)} collective-permute-done((bf16[4096,256]{1,0:T(8,128)(2,1)}, bf16[4096,256]{1,0:T(8,128)(2,1)}, u32[]{:S(2)}, u32[]{:S(2)}) %collective-permute-start.2) | collective-permute-done | bytes 2097184 | tf_op jit(solution)/shard_map/ppermute | solution.py:32
  151.6 3.4 %fusion.32 = bf16[1,384,512]{2,1,0:T(8,128)(2,1)S(1)} fusion(bf16[4096,256]{1,0:T(8,128)(2,1)} %collective-permute-done.2, bf16[4096,256]{1,0:T(8,128)(2,1)S(1)} %copy-done.7, bf16[384,2048]{1,0:T(8,128)(2,1)S(1)} %get-tuple-element.8, bf16[384,2048]{1,0:T(8,128)(2,1)S(1)} %get-tuple-element.7), kind=kOutput, calls=%fused_computation.29 | convolution fusion | flops 1625489408 | bytes 7733248 | tf_op jit(solution)/shard_map/dot_general | solution.py:45
  156.0 1.5 collective-permute-start.4
  157.6 45.3 %collective-permute-done.4 = bf16[4096,256]{1,0:T(8,128)(2,1)} collective-permute-done((bf16[4096,256]{1,0:T(8,128)(2,1)}, bf16[4096,256]{1,0:T(8,128)(2,1)}, u32[]{:S(2)}, u32[]{:S(2)}) %collective-permute-start.4) | collective-permute-done | bytes 2097184 | tf_op jit(solution)/shard_map/ppermute | solution.py:32
  202.9 5.0 %fusion.38 = bf16[48,4,8,128]{3,2,1,0:T(8,128)(2,1)S(1)} fusion(bf16[4096,256]{1,0:T(8,128)(2,1)} %collective-permute-done.4, bf16[4096,256]{1,0:T(8,128)(2,1)} %all-gather.11.cloned.1.call-done, bf16[384,2048]{1,0:T(8,128)(2,1)} %copy-done.3, bf16[384,2048]{1,0:T(8,128)(2,1)} %copy-done.2), kind=kOutput, calls=%fused_computation.31 | convolution fusion | flops 1625489408 | bytes 7733248 | tf_op jit(solution)/shard_map/dot_general | solution.py:45
  207.9 10.7 %all-gather.9.cloned.1.call-done = bf16[2,1536,512]{2,1,0:T(8,128)(2,1)} async-done(((bf16[2,384,512]{2,1,0:T(8,128)(2,1)}), bf16[2,1536,512]{2,1,0:T(8,128)(2,1)}) %all-gather.9.cloned.1.call-update) | async-done | bytes 3145744 | tf_op jit(solution)/shard_map/all_gather | solution.py:50
  218.5 3.2 %fusion.54 = (bf16[1,1536,512]{2,1,0:T(8,128)(2,1)}, bf16[1,1536,512]{2,1,0:T(8,128)(2,1)S(1)}) fusion(bf16[2,1536,512]{2,1,0:T(8,128)(2,1)} %all-gather.9.cloned.1.call-done), kind=kLoop, calls=%fused_computation.49 | loop fusion | bytes 6291456 | tf_op jit(solution)/shard_map/slice | solution.py:58
  221.8 3.5 %reshape_squeeze.7 = bf16[1536,4,128]{2,1,0:T(4,128)(2,1)} reshape(bf16[1,1536,512]{2,1,0:T(8,128)(2,1)} %get-tuple-element.5) | data formatting | bytes 3145728 | tf_op jit(solution)/shard_map/reshape;squeeze | solution.py:58
  225.3 1.6 copy.10
  226.9 2.9 %multiply_reduce_fusion = (f32[4,384]{1,0:T(4,128)S(1)}, f32[4,384,1536]{2,1,0:T(8,128)S(1)}) fusion(bf16[1536,4,128]{2,1,0:T(4,128)(2,1)} %reshape_squeeze.7, bf16[48,4,8,128]{3,2,1,0:T(8,128)(2,1)S(1)} %fusion.38), kind=kOutput, calls=%fused_computation.1 | convolution fusion | flops 608696832 | bytes 11409408 | tf_op jit(solution)/shard_map/qhd,khd->hqk/dot_general | solution.py:61
  229.7 1.7 fusion
  231.4 2.1 fusion.44
  (32 shorter events, 4.0 us)
Async XLA Ops:
  6.5 1.2 copy-start
  6.5 4.1 %copy-start.4 = (bf16[192,2048]{1,0:T(8,128)(2,1)S(1)}, bf16[192,2048]{1,0:T(8,128)(2,1)}, u32[]{:S(2)}) copy-start(bf16[192,2048]{1,0:T(8,128)(2,1)} %param.4) | copy-start | bytes 2359300
  6.5 7.1 %copy-start.5 = (bf16[1024,512]{1,0:T(8,128)(2,1)S(1)}, bf16[1024,512]{1,0:T(8,128)(2,1)}, u32[]{:S(2)}) copy-start(bf16[1024,512]{1,0:T(8,128)(2,1)} %param.5) | copy-start | bytes 3145732
  6.5 51.1 %all-gather.7.cloned.1.call-start = ((), (), s32[]{:S(2)}) async-start(), calls=%async_computation.1 | async-start | bytes 2621440 | tf_op jit(solution)/shard_map/all_gather | solution.py:31
  8.6 95.3 %all-gather.5.cloned.1.call-start = ((), (), s32[]{:S(2)}) async-start(), calls=%async_computation | async-start | bytes 2621440 | tf_op jit(solution)/shard_map/all_gather | solution.py:31
  10.6 145.4 %all-gather.11.cloned.1.call-start = ((), (), s32[]{:S(2)}) async-start(), calls=%async_computation.3 | async-start | bytes 2621440 | tf_op jit(solution)/shard_map/all_gather | solution.py:31
  10.6 20.7 %collective-permute-start = (bf16[192,2048]{1,0:T(8,128)(2,1)S(1)}, bf16[192,2048]{1,0:T(8,128)(2,1)}, u32[]{:S(2)}, u32[]{:S(2)}) collective-permute-start(bf16[192,2048]{1,0:T(8,128)(2,1)S(1)} %copy-done.4), channel_id=1, source_target_pairs={{0,2},{2,0},{1,3},{3,1},{4,6},{6,4},{5,7},{7,5},{8,10},{10,8},{9,1... | collective-permute-start | bytes 2359304 | tf_op jit(solution)/shard_map/ppermute | solution.py:20
  14.5 204.1 %all-gather.9.cloned.1.call-start = ((), (), s32[]{:S(2)}) async-start(), calls=%async_computation.2 | async-start | bytes 3932160 | tf_op jit(solution)/shard_map/all_gather | solution.py:50
  33.9 71.5 %collective-permute-start.1 = (bf16[384,2048]{1,0:T(8,128)(2,1)}, bf16[384,2048]{1,0:T(8,128)(2,1)}, u32[]{:S(2)}, u32[]{:S(2)}) collective-permute-start(bf16[384,2048]{1,0:T(8,128)(2,1)} %pad_maximum_fusion.1), channel_id=1, source_target_pairs={{0,1},{1,0},{2,3},{3,2},{4,5},{5,4},{6,7},{7,6},{8,9},{9,8},{10,11... | collective-permute-start | bytes 4718600 | tf_op jit(solution)/shard_map/ppermute | solution.py:20
  57.6 50.1 %collective-permute-start.3 = (bf16[4096,256]{1,0:T(8,128)(2,1)}, bf16[4096,256]{1,0:T(8,128)(2,1)}, u32[]{:S(2)}, u32[]{:S(2)}) collective-permute-start(bf16[4096,256]{1,0:T(8,128)(2,1)} %all-gather.7.cloned.1.call-done), channel_id=1, source_target_pairs={{0,16},{16,0},{1,17},{17,1},{2,18},{18,2},{3,19},{19,3},{4,20},{20... | collective-permute-start | bytes 6291464 | tf_op jit(solution)/shard_map/ppermute | solution.py:32
  103.9 47.7 %collective-permute-start.2 = (bf16[4096,256]{1,0:T(8,128)(2,1)}, bf16[4096,256]{1,0:T(8,128)(2,1)}, u32[]{:S(2)}, u32[]{:S(2)}) collective-permute-start(bf16[4096,256]{1,0:T(8,128)(2,1)} %all-gather.5.cloned.1.call-done), channel_id=1, source_target_pairs={{0,16},{16,0},{1,17},{17,1},{2,18},{18,2},{3,19},{19,3},{4,20},{20... | collective-permute-start | bytes 6291464 | tf_op jit(solution)/shard_map/ppermute | solution.py:32
  105.3 2.3 copy-start.6
  107.6 43.9 %copy-start.2 = (bf16[384,2048]{1,0:T(8,128)(2,1)}, bf16[384,2048]{1,0:T(8,128)(2,1)S(1)}, u32[]{:S(2)}) copy-start(bf16[384,2048]{1,0:T(8,128)(2,1)S(1)} %get-tuple-element.7) | copy-start | bytes 4718596
  107.7 43.9 %copy-start.3 = (bf16[384,2048]{1,0:T(8,128)(2,1)}, bf16[384,2048]{1,0:T(8,128)(2,1)S(1)}, u32[]{:S(2)}) copy-start(bf16[384,2048]{1,0:T(8,128)(2,1)S(1)} %get-tuple-element.8) | copy-start | bytes 4718596
  107.7 43.9 %copy-start.7 = (bf16[4096,256]{1,0:T(8,128)(2,1)S(1)}, bf16[4096,256]{1,0:T(8,128)(2,1)}, u32[]{:S(2)}) copy-start(bf16[4096,256]{1,0:T(8,128)(2,1)} %all-gather.5.cloned.1.call-done) | copy-start | bytes 6291460
  156.0 46.9 %collective-permute-start.4 = (bf16[4096,256]{1,0:T(8,128)(2,1)}, bf16[4096,256]{1,0:T(8,128)(2,1)}, u32[]{:S(2)}, u32[]{:S(2)}) collective-permute-start(bf16[4096,256]{1,0:T(8,128)(2,1)} %all-gather.11.cloned.1.call-done), channel_id=1, source_target_pairs={{0,16},{16,0},{1,17},{17,1},{2,18},{18,2},{3,19},{19,3},{4,20},{20... | collective-permute-start | bytes 6291464 | tf_op jit(solution)/shard_map/ppermute | solution.py:32
  229.7 1.7 copy-start.1
Sparse Core Ops, SparseCore 0:
  8.9 48.6 all-gather.6
  59.2 44.6 all-gather.4
  105.4 44.4 all-gather.10
  156.1 62.3 all-gather.8

commit v3 on v2

--- a/solution.py
+++ b/solution.py
@@ -11,6 +11,20 @@
     devices = range(lax.axis_size(axis))
     route = [((i - distance) % len(devices), i) for i in devices]
     return lax.ppermute(block, axis, route)
+
+
+def line_gather(piece):
+    n = lax.axis_size("seq")
+    here = lax.axis_index("seq")
+    from_right = [piece]
+    from_left = [piece]
+    for k in range(1, n):
+        from_right.append(lax.ppermute(from_right[-1], "seq", [(j, j - 1) for j in range(1, n - k + 1)]))
+        from_left.append(lax.ppermute(from_left[-1], "seq", [(j, j + 1) for j in range(k - 1, n - 1)]))
+    slots = [piece]
+    for m in range(1, n):
+        slots.append(jnp.where(here + m < n, from_right[m], from_left[n - m]))
+    return jnp.concatenate(slots, axis=0)
 
 
 def swap_gather(piece, axis, dim):
@@ -45,10 +59,12 @@
         (jnp.dot(block, piece, preferred_element_type=jnp.float32) for piece in pieces)
     )
     query = query_sum.astype(jnp.bfloat16).reshape(tokens_here, heads_here, HD)
-    packed = jnp.stack([key_sum.astype(jnp.bfloat16), value_sum.astype(jnp.bfloat16)])
     if lax.axis_size("seq") == SPAN:
-        seen = lax.all_gather(packed, "seq", axis=1, tiled=True)
+        seen = jnp.stack(
+            [line_gather(key_sum.astype(jnp.bfloat16)), line_gather(value_sum.astype(jnp.bfloat16))]
+        )
     else:
+        packed = jnp.stack([key_sum.astype(jnp.bfloat16), value_sum.astype(jnp.bfloat16)])
         blocks_seen = [packed]
         current = packed
         for step in range(1, SPAN):

time: 242 us -> 241 us (level)
  starting transfers between devices: 7.62 us -> 25.9 us
  waiting for transfers between devices: 181 us -> 165 us
  local copies, waits for them, and re-layouts: 13.3 us -> 6.64 us
    ppermute x3, waiting for transfers between devices: 84.6 us -> 12.9 us  [full_columns(): other = lax.ppermute(own, 'groups', [(0, 1), (1, 0)])]
    all_gather x3, waiting for transfers between devices: 68.5 us -> 112 us  [full_columns(): own = lax.all_gather(own, 'seq', axis=0, tiled=True)]
    ppermute x0 -> x12, waiting for transfers between devices: none -> 21.6 us  [the longest x6 18.3 us: line_gather(): lax.ppermute(from_right[-1], 'seq', [(j, j - 1) for j in range(1, n - k +...]
    ppermute x0 -> x12, starting transfers between devices: none -> 18.4 us  [the longest x6 10.7 us: line_gather(): lax.ppermute(from_left[-1], 'seq', [(j, j + 1) for j in range(k - 1, n -...]
    all_gather x1 -> x0, waiting for transfers between devices: 10.7 us -> none  [per_device(): seen = lax.all_gather(packed, 'seq', axis=1, tiled=True)]
    another operation x1 -> x0, local copies, waits for them, and re-layouts: 3.5 us -> none  [per_device(): seen_keys = seen[0].reshape(-1, heads_here, HD)]
    select_n x0 -> x6, other arithmetic: none -> 3.28 us  [line_gather(): slots.append(jnp.where(here + m < n, from_right[m], from_left[n - m]))]
    slice x1 -> x0, local copies, waits for them, and re-layouts: 3.25 us -> none  [per_device(): seen_keys = seen[0].reshape(-1, heads_here, HD)]
  transfers between devices with their start and end apart: 9 -> 20, of which waited for: 6 -> 10; matrix products, arithmetic and copies ran while one was open for 9% -> 10% of each run, Pallas kernels for 0% -> 0%
where the time goes in v3:
time: 241 us; the launch traced here: 240 us
  waiting for transfers between devices  165 us (68%)
  starting transfers between devices  25.9 us (11%)
  matrix products  18.5 us (8%)
  between operations  13.5 us (6%)
  other arithmetic  10.8 us (4%)
  local copies, waits for them, and re-layouts  6.64 us (3%)
    all_gather x3, waiting for transfers between devices, full_columns(): own = lax.all_gather(own, 'seq', axis=0, tiled=True)  112 us
    ppermute x6, waiting for transfers between devices, line_gather(): lax.ppermute(from_right[-1], 'seq', [(j, j - 1) for j in range(1, n - k +...  18.3 us
    ppermute x2, waiting for transfers between devices, swap_gather(): other = lax.ppermute(piece, axis, [(0, 1), (1, 0)])  17.6 us
    dot_general x3, matrix products, per_device(): jnp.dot(block, piece, preferred_element_type=jnp.float32)  13.7 us
    ppermute x3, waiting for transfers between devices, full_columns(): other = lax.ppermute(own, 'groups', [(0, 1), (1, 0)])  12.9 us
    ppermute x6, starting transfers between devices, line_gather(): lax.ppermute(from_left[-1], 'seq', [(j, j + 1) for j in range(k - 1, n -...  10.7 us
    ppermute x6, starting transfers between devices, line_gather(): lax.ppermute(from_right[-1], 'seq', [(j, j - 1) for j in range(1, n - k +...  7.72 us
  transfers between devices with their start and end apart: 20, of which 10 were waited for; matrix products, arithmetic and copies ran while one was open for 10% of the time, Pallas kernels for 0%

profile of v3, /device:TPU:0, one launch (start us, length us, event | category | flops | bytes accessed | tf_op | source)
XLA Modules:
  0.0 240.0 jit_solution(11439956357201533546)
XLA Ops:
  8.7 1.9 constant_dynamic-slice_fusion
  11.5 3.0 %collective-permute-start = (bf16[192,2048]{1,0:T(8,128)(2,1)S(1)}, bf16[192,2048]{1,0:T(8,128)(2,1)}, u32[]{:S(2)}, u32[]{:S(2)}) collective-permute-start(bf16[192,2048]{1,0:T(8,128)(2,1)S(1)} %copy-done.4), channel_id=1, source_target_pairs={{0,2},{2,0},{1,3},{3,1},{4,6},{6,4},{5,7},{7,5},{8,10},{10,8},{9,1... | collective-permute-start | bytes 2359304 | tf_op jit(solution)/shard_map/ppermute | solution.py:34
  14.6 17.6 %collective-permute-done = bf16[192,2048]{1,0:T(8,128)(2,1)} collective-permute-done((bf16[192,2048]{1,0:T(8,128)(2,1)S(1)}, bf16[192,2048]{1,0:T(8,128)(2,1)}, u32[]{:S(2)}, u32[]{:S(2)}) %collective-permute-start) | collective-permute-done | bytes 786464 | tf_op jit(solution)/shard_map/ppermute | solution.py:34
  34.7 22.9 %all-gather.4.cloned.1.call-done = bf16[4096,256]{1,0:T(8,128)(2,1)} async-done(((bf16[1024,256]{1,0:T(8,128)(2,1)}), bf16[4096,256]{1,0:T(8,128)(2,1)}) %all-gather.4.cloned.1.call-update) | async-done | bytes 2097168 | tf_op jit(solution)/shard_map/all_gather | solution.py:45
  57.6 1.5 collective-permute-start.2
  59.1 44.8 %all-gather.8.cloned.1.call-done = bf16[4096,256]{1,0:T(8,128)(2,1)} async-done(((bf16[1024,256]{1,0:T(8,128)(2,1)}), bf16[4096,256]{1,0:T(8,128)(2,1)}) %all-gather.8.cloned.1.call-update) | async-done | bytes 2097168 | tf_op jit(solution)/shard_map/all_gather | solution.py:45
  103.9 1.5 collective-permute-start.10
  105.3 44.8 %all-gather.6.cloned.1.call-done = bf16[4096,256]{1,0:T(8,128)(2,1)} async-done(((bf16[1024,256]{1,0:T(8,128)(2,1)}), bf16[4096,256]{1,0:T(8,128)(2,1)}) %all-gather.6.cloned.1.call-update) | async-done | bytes 2097168 | tf_op jit(solution)/shard_map/all_gather | solution.py:45
  150.1 1.5 collective-permute-start.9
  151.6 2.3 broadcast_select_fusion.1
  154.0 4.6 %fusion.30 = bf16[384,512]{1,0:T(8,128)(2,1)S(1)} fusion(bf16[4096,256]{1,0:T(8,128)(2,1)} %collective-permute-done.2, bf16[4096,256]{1,0:T(8,128)(2,1)S(1)} %copy-done.11, bf16[384,2048]{1,0:T(8,128)(2,1)S(1)} %get-tuple-element.6, bf16[384,2048]{1,0:T(8,128)(2,1)S(1)} %get-tuple-element.5), kind=kOutput, calls=%fused_computation.31 | convolution fusion | flops 1625489408 | bytes 7733248 | tf_op jit(solution)/shard_map/dot_general | solution.py:59
  158.5 1.8 collective-permute-start.4
  161.7 3.4 %fusion.24 = bf16[384,512]{1,0:T(8,128)(2,1)S(1)} fusion(bf16[4096,256]{1,0:T(8,128)(2,1)} %collective-permute-done.10, bf16[4096,256]{1,0:T(8,128)(2,1)S(1)} %copy-done.10, bf16[384,2048]{1,0:T(8,128)(2,1)S(1)} %get-tuple-element.6, bf16[384,2048]{1,0:T(8,128)(2,1)S(1)} %get-tuple-element.5), kind=kOutput, calls=%fused_computation.29 | convolution fusion | flops 1625489408 | bytes 7733248 | tf_op jit(solution)/shard_map/dot_general | solution.py:59
  165.1 4.6 %collective-permute-start.12 = (bf16[384,512]{1,0:T(8,128)(2,1)S(1)}, bf16[384,512]{1,0:T(8,128)(2,1)S(1)}, u32[]{:S(2)}, u32[]{:S(2)}) collective-permute-start(bf16[384,512]{1,0:T(8,128)(2,1)S(1)} %fusion.24), channel_id=1, source_target_pairs={{0,4},{4,8},{8,12},{1,5},{5,9},{9,13},{2,6},{6,10},{10,14},{3,7},{... | collective-permute-start | bytes 1179656 | tf_op jit(solution)/shard_map/ppermute | solution.py:23
  173.8 3.4 %collective-permute-done.12 = bf16[384,512]{1,0:T(8,128)(2,1)S(1)} collective-permute-done((bf16[384,512]{1,0:T(8,128)(2,1)S(1)}, bf16[384,512]{1,0:T(8,128)(2,1)S(1)}, u32[]{:S(2)}, u32[]{:S(2)}) %collective-permute-start.12) | collective-permute-done | bytes 393248 | tf_op jit(solution)/shard_map/ppermute | solution.py:23
  178.6 5.1 %collective-permute-done.11 = bf16[384,512]{1,0:T(8,128)(2,1)S(1)} collective-permute-done((bf16[384,512]{1,0:T(8,128)(2,1)S(1)}, bf16[384,512]{1,0:T(8,128)(2,1)S(1)}, u32[]{:S(2)}, u32[]{:S(2)}) %collective-permute-start.11) | collective-permute-done | bytes 393248 | tf_op jit(solution)/shard_map/ppermute | solution.py:22
  184.9 12.9 %collective-permute-done.9 = bf16[4096,256]{1,0:T(8,128)(2,1)} collective-permute-done((bf16[4096,256]{1,0:T(8,128)(2,1)}, bf16[4096,256]{1,0:T(8,128)(2,1)}, u32[]{:S(2)}, u32[]{:S(2)}) %collective-permute-start.9) | collective-permute-done | bytes 2097184 | tf_op jit(solution)/shard_map/ppermute | solution.py:46
  197.8 5.7 %fusion.33 = bf16[48,4,8,128]{3,2,1,0:T(8,128)(2,1)} fusion(bf16[4096,256]{1,0:T(8,128)(2,1)} %collective-permute-done.9, bf16[4096,256]{1,0:T(8,128)(2,1)} %all-gather.6.cloned.1.call-done, bf16[384,2048]{1,0:T(8,128)(2,1)} %copy-done.3, bf16[384,2048]{1,0:T(8,128)(2,1)} %copy-done.2), kind=kOutput, calls=%fused_computation.32 | convolution fusion | flops 1625489408 | bytes 7733248 | tf_op jit(solution)/shard_map/dot_general | solution.py:59
  209.6 8.7 %collective-permute-done.8 = bf16[384,512]{1,0:T(8,128)(2,1)S(1)} collective-permute-done((bf16[384,512]{1,0:T(8,128)(2,1)S(1)}, bf16[384,512]{1,0:T(8,128)(2,1)S(1)}, u32[]{:S(2)}, u32[]{:S(2)}) %collective-permute-start.8) | collective-permute-done | bytes 393248 | tf_op jit(solution)/shard_map/ppermute | solution.py:22
  218.5 1.6 copy.10
  221.2 3.6 %collective-permute-done.16 = bf16[384,512]{1,0:T(8,128)(2,1)} collective-permute-done((bf16[384,512]{1,0:T(8,128)(2,1)}, bf16[384,512]{1,0:T(8,128)(2,1)}, u32[]{:S(2)}, u32[]{:S(2)}) %collective-permute-start.16) | collective-permute-done | bytes 393248 | tf_op jit(solution)/shard_map/ppermute | solution.py:22
  225.8 2.7 %multiply_reduce_fusion = (f32[4,384]{1,0:T(4,128)S(1)}, f32[4,384,1536]{2,1,0:T(8,128)S(1)}) fusion(bf16[48,4,8,128]{3,2,1,0:T(8,128)(2,1)} %fusion.33, bf16[384,512]{1,0:T(8,128)(2,1)S(1)} %broadcast_select_fusion.4, bf16[384,512]{1,0:T(8,128)(2,1)S(1)} %broadcast_select_fusion.6, bf16[384,512]{1,0:T(8,128)(2,1)S(1)} %broadcast_select_fusion.8, ...), kind=kOutput, calls=%fused_computation.1 | convolution fusion | flops 614988288 | bytes 11409408 | tf_op jit(solution)/shard_map/qhd,khd->hqk/dot_general | solution.py:77
  228.5 1.7 fusion
  230.2 2.1 fusion.39
  (65 shorter events, 22.9 us)
Async XLA Ops:
  6.5 51.1 %all-gather.4.cloned.1.call-start = ((), (), s32[]{:S(2)}) async-start(), calls=%async_computation | async-start | bytes 2621440 | tf_op jit(solution)/shard_map/all_gather | solution.py:45
  8.6 95.2 %all-gather.8.cloned.1.call-start = ((), (), s32[]{:S(2)}) async-start(), calls=%async_computation.2 | async-start | bytes 2621440 | tf_op jit(solution)/shard_map/all_gather | solution.py:45
  10.6 139.5 %all-gather.6.cloned.1.call-start = ((), (), s32[]{:S(2)}) async-start(), calls=%async_computation.1 | async-start | bytes 2621440 | tf_op jit(solution)/shard_map/all_gather | solution.py:45
  11.5 20.7 %collective-permute-start = (bf16[192,2048]{1,0:T(8,128)(2,1)S(1)}, bf16[192,2048]{1,0:T(8,128)(2,1)}, u32[]{:S(2)}, u32[]{:S(2)}) collective-permute-start(bf16[192,2048]{1,0:T(8,128)(2,1)S(1)} %copy-done.4), channel_id=1, source_target_pairs={{0,2},{2,0},{1,3},{3,1},{4,6},{6,4},{5,7},{7,5},{8,10},{10,8},{9,1... | collective-permute-start | bytes 2359304 | tf_op jit(solution)/shard_map/ppermute | solution.py:34
  34.7 116.9 %collective-permute-start.1 = (bf16[384,2048]{1,0:T(8,128)(2,1)}, bf16[384,2048]{1,0:T(8,128)(2,1)}, u32[]{:S(2)}, u32[]{:S(2)}) collective-permute-start(bf16[384,2048]{1,0:T(8,128)(2,1)} %pad_maximum_fusion.1), channel_id=1, source_target_pairs={{0,1},{1,0},{2,3},{3,2},{4,5},{5,4},{6,7},{7,6},{8,9},{9,8},{10,11... | collective-permute-start | bytes 4718600 | tf_op jit(solution)/shard_map/ppermute | solution.py:34
  57.6 96.3 %collective-permute-start.2 = (bf16[4096,256]{1,0:T(8,128)(2,1)}, bf16[4096,256]{1,0:T(8,128)(2,1)}, u32[]{:S(2)}, u32[]{:S(2)}) collective-permute-start(bf16[4096,256]{1,0:T(8,128)(2,1)} %all-gather.4.cloned.1.call-done), channel_id=1, source_target_pairs={{0,16},{16,0},{1,17},{17,1},{2,18},{18,2},{3,19},{19,3},{4,20},{20... | collective-permute-start | bytes 6291464 | tf_op jit(solution)/shard_map/ppermute | solution.py:46
  103.9 57.8 %collective-permute-start.10 = (bf16[4096,256]{1,0:T(8,128)(2,1)}, bf16[4096,256]{1,0:T(8,128)(2,1)}, u32[]{:S(2)}, u32[]{:S(2)}) collective-permute-start(bf16[4096,256]{1,0:T(8,128)(2,1)} %all-gather.8.cloned.1.call-done), channel_id=1, source_target_pairs={{0,16},{16,0},{1,17},{17,1},{2,18},{18,2},{3,19},{19,3},{4,20},{20... | collective-permute-start | bytes 6291464 | tf_op jit(solution)/shard_map/ppermute | solution.py:46
  150.1 47.7 %collective-permute-start.9 = (bf16[4096,256]{1,0:T(8,128)(2,1)}, bf16[4096,256]{1,0:T(8,128)(2,1)}, u32[]{:S(2)}, u32[]{:S(2)}) collective-permute-start(bf16[4096,256]{1,0:T(8,128)(2,1)} %all-gather.6.cloned.1.call-done), channel_id=1, source_target_pairs={{0,16},{16,0},{1,17},{17,1},{2,18},{18,2},{3,19},{19,3},{4,20},{20... | collective-permute-start | bytes 6291464 | tf_op jit(solution)/shard_map/ppermute | solution.py:46
  153.9 7.8 %copy-start.2 = (bf16[384,2048]{1,0:T(8,128)(2,1)}, bf16[384,2048]{1,0:T(8,128)(2,1)S(1)}, u32[]{:S(2)}) copy-start(bf16[384,2048]{1,0:T(8,128)(2,1)S(1)} %get-tuple-element.5) | copy-start | bytes 4718596
  158.5 12.5 %collective-permute-start.4 = (bf16[384,512]{1,0:T(8,128)(2,1)S(1)}, bf16[384,512]{1,0:T(8,128)(2,1)S(1)}, u32[]{:S(2)}, u32[]{:S(2)}) collective-permute-start(bf16[384,512]{1,0:T(8,128)(2,1)S(1)} %fusion.30), channel_id=1, source_target_pairs={{0,4},{4,8},{8,12},{1,5},{5,9},{9,13},{2,6},{6,10},{10,14},{3,7},{... | collective-permute-start | bytes 1179656 | tf_op jit(solution)/shard_map/ppermute | solution.py:23
  160.3 12.2 %collective-permute-start.3 = (bf16[384,512]{1,0:T(8,128)(2,1)S(1)}, bf16[384,512]{1,0:T(8,128)(2,1)S(1)}, u32[]{:S(2)}, u32[]{:S(2)}) collective-permute-start(bf16[384,512]{1,0:T(8,128)(2,1)S(1)} %fusion.30), channel_id=1, source_target_pairs={{4,0},{8,4},{12,8},{5,1},{9,5},{13,9},{6,2},{10,6},{14,10},{7,3},{... | collective-permute-start | bytes 1179656 | tf_op jit(solution)/shard_map/ppermute | solution.py:22
  165.1 12.0 %collective-permute-start.12 = (bf16[384,512]{1,0:T(8,128)(2,1)S(1)}, bf16[384,512]{1,0:T(8,128)(2,1)S(1)}, u32[]{:S(2)}, u32[]{:S(2)}) collective-permute-start(bf16[384,512]{1,0:T(8,128)(2,1)S(1)} %fusion.24), channel_id=1, source_target_pairs={{0,4},{4,8},{8,12},{1,5},{5,9},{9,13},{2,6},{6,10},{10,14},{3,7},{... | collective-permute-start | bytes 1179656 | tf_op jit(solution)/shard_map/ppermute | solution.py:23
  169.7 13.9 %collective-permute-start.11 = (bf16[384,512]{1,0:T(8,128)(2,1)S(1)}, bf16[384,512]{1,0:T(8,128)(2,1)S(1)}, u32[]{:S(2)}, u32[]{:S(2)}) collective-permute-start(bf16[384,512]{1,0:T(8,128)(2,1)S(1)} %fusion.24), channel_id=1, source_target_pairs={{4,0},{8,4},{12,8},{5,1},{9,5},{13,9},{6,2},{10,6},{14,10},{7,3},{... | collective-permute-start | bytes 1179656 | tf_op jit(solution)/shard_map/ppermute | solution.py:22
  171.0 32.5 %collective-permute-start.5 = (bf16[384,512]{1,0:T(8,128)(2,1)S(1)}, bf16[384,512]{1,0:T(8,128)(2,1)S(1)}, u32[]{:S(2)}, u32[]{:S(2)}) collective-permute-start(bf16[384,512]{1,0:T(8,128)(2,1)S(1)} %collective-permute-done.4), channel_id=1, source_target_pairs={{4,8},{8,12},{5,9},{9,13},{6,10},{10,14},{7,11},{11,15},{20,24},{2... | collective-permute-start | bytes 1179656 | tf_op jit(solution)/shard_map/ppermute | solution.py:23
  172.5 31.9 %collective-permute-start.7 = (bf16[384,512]{1,0:T(8,128)(2,1)S(1)}, bf16[384,512]{1,0:T(8,128)(2,1)S(1)}, u32[]{:S(2)}, u32[]{:S(2)}) collective-permute-start(bf16[384,512]{1,0:T(8,128)(2,1)S(1)} %collective-permute-done.3), channel_id=1, source_target_pairs={{4,0},{8,4},{5,1},{9,5},{6,2},{10,6},{7,3},{11,7},{20,16},{24,20},... | collective-permute-start | bytes 1179656 | tf_op jit(solution)/shard_map/ppermute | solution.py:22
  177.2 26.4 %copy-start.7 = (bf16[384,512]{1,0:T(8,128)(2,1)}, bf16[384,512]{1,0:T(8,128)(2,1)S(1)}, u32[]{:S(2)}) copy-start(bf16[384,512]{1,0:T(8,128)(2,1)S(1)} %collective-permute-done.12) | copy-start | bytes 1179652
  177.2 28.5 %collective-permute-start.13 = (bf16[384,512]{1,0:T(8,128)(2,1)S(1)}, bf16[384,512]{1,0:T(8,128)(2,1)}, u32[]{:S(2)}, u32[]{:S(2)}) collective-permute-start(bf16[384,512]{1,0:T(8,128)(2,1)S(1)} %collective-permute-done.12), channel_id=1, source_target_pairs={{4,8},{8,12},{5,9},{9,13},{6,10},{10,14},{7,11},{11,15},{20,24},{2... | collective-permute-start | bytes 1179656 | tf_op jit(solution)/shard_map/ppermute | solution.py:23
  183.6 19.9 %copy-start.8 = (bf16[384,512]{1,0:T(8,128)(2,1)}, bf16[384,512]{1,0:T(8,128)(2,1)S(1)}, u32[]{:S(2)}) copy-start(bf16[384,512]{1,0:T(8,128)(2,1)S(1)} %collective-permute-done.11) | copy-start | bytes 1179652
  183.6 23.5 %collective-permute-start.15 = (bf16[384,512]{1,0:T(8,128)(2,1)S(1)}, bf16[384,512]{1,0:T(8,128)(2,1)}, u32[]{:S(2)}, u32[]{:S(2)}) collective-permute-start(bf16[384,512]{1,0:T(8,128)(2,1)S(1)} %collective-permute-done.11), channel_id=1, source_target_pairs={{4,0},{8,4},{5,1},{9,5},{6,2},{10,6},{7,3},{11,7},{20,16},{24,20},... | collective-permute-start | bytes 1179656 | tf_op jit(solution)/shard_map/ppermute | solution.py:22
  203.5 14.8 %copy-start.6 = (bf16[384,512]{1,0:T(8,128)(2,1)S(1)}, bf16[384,512]{1,0:T(8,128)(2,1)}, u32[]{:S(2)}) copy-start(bf16[384,512]{1,0:T(8,128)(2,1)} %copy-done.5) | copy-start | bytes 1179652
  203.5 6.0 %collective-permute-start.6 = (bf16[384,512]{1,0:T(8,128)(2,1)S(1)}, bf16[384,512]{1,0:T(8,128)(2,1)S(1)}, u32[]{:S(2)}, u32[]{:S(2)}) collective-permute-start(bf16[384,512]{1,0:T(8,128)(2,1)S(1)} %collective-permute-done.5), channel_id=1, source_target_pairs={{8,12},{9,13},{10,14},{11,15},{24,28},{25,29},{26,30},{27,31}} | collective-permute-start | bytes 1179656 | tf_op jit(solution)/shard_map/ppermute | solution.py:23
  204.4 13.9 %collective-permute-start.8 = (bf16[384,512]{1,0:T(8,128)(2,1)S(1)}, bf16[384,512]{1,0:T(8,128)(2,1)S(1)}, u32[]{:S(2)}, u32[]{:S(2)}) collective-permute-start(bf16[384,512]{1,0:T(8,128)(2,1)S(1)} %collective-permute-done.7), channel_id=1, source_target_pairs={{4,0},{5,1},{6,2},{7,3},{20,16},{21,17},{22,18},{23,19}} | collective-permute-start | bytes 1179656 | tf_op jit(solution)/shard_map/ppermute | solution.py:22
  205.7 14.4 %collective-permute-start.14 = (bf16[384,512]{1,0:T(8,128)(2,1)}, bf16[384,512]{1,0:T(8,128)(2,1)}, u32[]{:S(2)}, u32[]{:S(2)}) collective-permute-start(bf16[384,512]{1,0:T(8,128)(2,1)} %collective-permute-done.13), channel_id=1, source_target_pairs={{8,12},{9,13},{10,14},{11,15},{24,28},{25,29},{26,30},{27,31}} | collective-permute-start | bytes 1179656 | tf_op jit(solution)/shard_map/ppermute | solution.py:23
  207.1 17.7 %collective-permute-start.16 = (bf16[384,512]{1,0:T(8,128)(2,1)}, bf16[384,512]{1,0:T(8,128)(2,1)}, u32[]{:S(2)}, u32[]{:S(2)}) collective-permute-start(bf16[384,512]{1,0:T(8,128)(2,1)} %collective-permute-done.15), channel_id=1, source_target_pairs={{4,0},{5,1},{6,2},{7,3},{20,16},{21,17},{22,18},{23,19}} | collective-permute-start | bytes 1179656 | tf_op jit(solution)/shard_map/ppermute | solution.py:22
  (8 other events, 36.4 us)
Sparse Core Ops, SparseCore 0:
  8.9 48.6 all-gather.3
  59.2 44.6 all-gather.7
  105.4 44.6 all-gather.5

commit v4 on v3

--- a/solution.py
+++ b/solution.py
@@ -37,14 +37,19 @@
     return jnp.concatenate([low, high], axis=dim)
 
 
-def full_columns(weight, shared):
+def full_columns(weight, shared, after=None):
     if not shared:
         return lax.all_gather(weight, "seq", axis=0, tiled=True)
-    half = weight.shape[1] // 2
-    own = lax.dynamic_slice_in_dim(weight, lax.axis_index("groups") * half, half, axis=1)
+    rows, half = weight.shape[0], weight.shape[1] // 2
+    group = lax.axis_index("groups")
+    own = lax.dynamic_slice_in_dim(weight, group * half, half, axis=1)
+    kept = lax.dynamic_slice_in_dim(weight, (1 - group) * half, half, axis=1)
     own = lax.all_gather(own, "seq", axis=0, tiled=True)
-    other = lax.ppermute(own, "groups", [(0, 1), (1, 0)])
-    return jnp.concatenate([own, other], axis=1)
+    own = jnp.roll(own, -lax.axis_index("seq") * rows, axis=0)
+    if after is not None:
+        own = lax.optimization_barrier((own, after))[0]
+    other = lax.ppermute(own[rows:], "groups", [(0, 1), (1, 0)])
+    return jnp.concatenate([own, jnp.concatenate([kept, other], axis=0)], axis=1)
 
 
 def per_device(acts, w_query, w_key, w_value):
@@ -54,17 +59,22 @@
     width = w_query.shape[1]
     heads_here = width // HD
     shared = lax.axis_size("groups") == 2 and width % (2 * HD) == 0
-    pieces = tuple(full_columns(w, shared) for w in (w_key, w_value, w_query))
-    key_sum, value_sum, query_sum = tuple(
-        (jnp.dot(block, piece, preferred_element_type=jnp.float32) for piece in pieces)
-    )
-    query = query_sum.astype(jnp.bfloat16).reshape(tokens_here, heads_here, HD)
+    if shared:
+        block = jnp.roll(block, -lax.axis_index("seq") * w_query.shape[0], axis=1)
+
+    def project(weight, after=None):
+        piece = full_columns(weight, shared, after)
+        return jnp.dot(block, piece, preferred_element_type=jnp.float32).astype(jnp.bfloat16)
+
+    key = project(w_key)
+    value = project(w_value)
+    query = project(w_query, key).reshape(tokens_here, heads_here, HD)
     if lax.axis_size("seq") == SPAN:
         seen = jnp.stack(
-            [line_gather(key_sum.astype(jnp.bfloat16)), line_gather(value_sum.astype(jnp.bfloat16))]
+            [line_gather(key), line_gather(value)]
         )
     else:
-        packed = jnp.stack([key_sum.astype(jnp.bfloat16), value_sum.astype(jnp.bfloat16)])
+        packed = jnp.stack([key, value])
         blocks_seen = [packed]
         current = packed
         for step in range(1, SPAN):

time: 241 us -> 230 us (0.954); the launches traced: 240 us -> 226 us
  waiting for transfers between devices: 165 us -> 129 us
  other arithmetic: 10.8 us -> 23.6 us
  starting transfers between devices: 25.9 us -> 30.9 us
  local copies, waits for them, and re-layouts: 6.64 us -> 11.4 us
    all_gather x3, waiting for transfers between devices: 112 us -> 64.7 us  [full_columns(): own = lax.all_gather(own, 'seq', axis=0, tiled=True)]
    ppermute x3, waiting for transfers between devices: 12.9 us -> 26 us  [full_columns(): other = lax.ppermute(own[rows:], 'groups', [(0, 1), (1, 0)])]
    concatenate x0 -> x4, other arithmetic: none -> 11.9 us  [the longest x3 9.01 us: full_columns(): own = jnp.roll(own, -lax.axis_index('seq') * rows, axis=0)]
    ppermute x6, starting transfers between devices: 10.7 us -> 15.5 us  [line_gather(): lax.ppermute(from_left[-1], 'seq', [(j, j + 1) for j in range(k - 1, n -...]
    select_n x2 -> x1, other arithmetic: 3.54 us -> 0.11 us  [swap_gather(): low = jnp.where(first, piece, other)]
    ppermute x6, waiting for transfers between devices: 3.37 us -> 0.02 us  [line_gather(): lax.ppermute(from_left[-1], 'seq', [(j, j + 1) for j in range(k - 1, n -...]
    ppermute x6, waiting for transfers between devices: 18.3 us -> 21 us  [line_gather(): lax.ppermute(from_right[-1], 'seq', [(j, j - 1) for j in range(1, n - k +...]
    slice x0 -> x3, local copies, waits for them, and re-layouts: none -> 2.67 us  [full_columns(): other = lax.ppermute(own[rows:], 'groups', [(0, 1), (1, 0)])]
  transfers between devices with their start and end apart: 20 -> 20, of which waited for: 10 -> 9; matrix products, arithmetic and copies ran while one was open for 10% -> 17% of each run, Pallas kernels for 0% -> 0%
where the time goes in v4:
time: 230 us; the launch traced here: 226 us
  waiting for transfers between devices  129 us (56%)
  starting transfers between devices  30.9 us (13%)
  other arithmetic  23.6 us (10%)
  matrix products  17.3 us (8%)
  between operations  13.5 us (6%)
  local copies, waits for them, and re-layouts  11.4 us (5%)
    all_gather x3, waiting for transfers between devices, full_columns(): own = lax.all_gather(own, 'seq', axis=0, tiled=True)  64.7 us
    ppermute x3, waiting for transfers between devices, full_columns(): other = lax.ppermute(own[rows:], 'groups', [(0, 1), (1, 0)])  26 us
    ppermute x6, waiting for transfers between devices, line_gather(): lax.ppermute(from_right[-1], 'seq', [(j, j - 1) for j in range(1, n - k +...  21 us
    ppermute x2, waiting for transfers between devices, swap_gather(): other = lax.ppermute(piece, axis, [(0, 1), (1, 0)])  17.5 us
    ppermute x6, starting transfers between devices, line_gather(): lax.ppermute(from_left[-1], 'seq', [(j, j + 1) for j in range(k - 1, n -...  15.5 us
    dot_general x3, matrix products, project(): jnp.dot(block, piece, preferred_element_type=jnp.float32)  13.5 us
    concatenate x3, other arithmetic, full_columns(): own = jnp.roll(own, -lax.axis_index('seq') * rows, axis=0)  9.01 us
    ppermute x6, starting transfers between devices, line_gather(): lax.ppermute(from_right[-1], 'seq', [(j, j - 1) for j in range(1, n - k +...  7.71 us
  transfers between devices with their start and end apart: 20, of which 9 were waited for; matrix products, arithmetic and copies ran while one was open for 17% of the time, Pallas kernels for 0%

profile of v4, /device:TPU:0, one launch (start us, length us, event | category | flops | bytes accessed | tf_op | source)
XLA Modules:
  0.0 226.1 jit_solution(2768710618162935756)
XLA Ops:
  6.5 2.4 %constant_dynamic-slice_fusion.4 = (bf16[1024,256]{1,0:T(8,128)(2,1)}, bf16[1024,256]{1,0:T(8,128)(2,1)}) fusion(bf16[1024,512]{1,0:T(8,128)(2,1)} %param.9, s32[]{:T(128)S(6)} %select_n.105, s32[]{:T(128)S(6)} %select_n.104), kind=kLoop, calls=%fused_computation.73 | loop fusion | bytes 2097160 | tf_op jit(solution)/shard_map/dynamic_slice | solution.py:46
  10.1 3.0 %collective-permute-start = (bf16[192,2048]{1,0:T(8,128)(2,1)S(1)}, bf16[192,2048]{1,0:T(8,128)(2,1)S(1)}, u32[]{:S(2)}, u32[]{:S(2)}) collective-permute-start(bf16[192,2048]{1,0:T(8,128)(2,1)S(1)} %copy-done.6), channel_id=1, source_target_pairs={{0,2},{2,0},{1,3},{3,1},{4,6},{6,4},{5,7},{7,5},{8,10},{10,8},{9,1... | collective-permute-start | bytes 2359304 | tf_op jit(solution)/shard_map/ppermute | solution.py:34
  13.1 17.5 %collective-permute-done = bf16[192,2048]{1,0:T(8,128)(2,1)S(1)} collective-permute-done((bf16[192,2048]{1,0:T(8,128)(2,1)S(1)}, bf16[192,2048]{1,0:T(8,128)(2,1)S(1)}, u32[]{:S(2)}, u32[]{:S(2)}) %collective-permute-start) | collective-permute-done | bytes 786464 | tf_op jit(solution)/shard_map/ppermute | solution.py:34
  32.2 25.5 %all-gather.4.cloned.1.call-done = bf16[4096,256]{1,0:T(8,128)(2,1)} async-done(((bf16[1024,256]{1,0:T(8,128)(2,1)}), bf16[4096,256]{1,0:T(8,128)(2,1)}) %all-gather.4.cloned.1.call-update) | async-done | bytes 2097168 | tf_op jit(solution)/shard_map/all_gather | solution.py:47
  57.7 3.0 %fusion.29 = bf16[4096,256]{1,0:T(8,128)(2,1)S(1)} fusion(s32[]{:T(128)S(6)} %select_n.103, bf16[4096,256]{1,0:T(8,128)(2,1)} %all-gather.4.cloned.1.call-done), kind=kLoop, calls=%fused_computation.40 | loop fusion | flops 4194304 | bytes 4194308 | tf_op jit(solution)/shard_map/jit(_roll_dynamic)/concatenate | solution.py:48
  64.8 39.2 %all-gather.8.cloned.1.call-done = bf16[4096,256]{1,0:T(8,128)(2,1)} async-done(((bf16[1024,256]{1,0:T(8,128)(2,1)}), bf16[4096,256]{1,0:T(8,128)(2,1)}) %all-gather.8.cloned.1.call-update) | async-done | bytes 2097168 | tf_op jit(solution)/shard_map/all_gather | solution.py:47
  104.0 3.0 %fusion.27 = bf16[4096,256]{1,0:T(8,128)(2,1)S(1)} fusion(s32[]{:T(128)S(6)} %select_n.103, bf16[4096,256]{1,0:T(8,128)(2,1)} %all-gather.8.cloned.1.call-done), kind=kLoop, calls=%fused_computation.38 | loop fusion | flops 4194304 | bytes 4194308 | tf_op jit(solution)/shard_map/jit(_roll_dynamic)/concatenate | solution.py:48
  108.6 2.2 broadcast_select_fusion
  110.9 2.9 %fusion.26 = bf16[384,4096]{1,0:T(8,128)(2,1)S(1)} fusion(s32[]{:T(128)S(6)} %select_n.103, bf16[384,2048]{1,0:T(8,128)(2,1)S(1)} %get-tuple-element.9, bf16[384,2048]{1,0:T(8,128)(2,1)S(1)} %get-tuple-element.8), kind=kLoop, calls=%fused_computation.37 | loop fusion | flops 12582912 | bytes 6291460 | tf_op jit(solution)/shard_map/jit(_roll_dynamic)/concatenate | solution.py:63
  113.9 4.3 %fusion.42 = bf16[384,512]{1,0:T(8,128)(2,1)S(1)} fusion(bf16[384,4096]{1,0:T(8,128)(2,1)S(1)} %fusion.26, bf16[3072,256]{1,0:T(8,128)(2,1)} %collective-permute-done.2, bf16[1024,256]{1,0:T(8,128)(2,1)S(1)} %copy-done.9, bf16[4096,256]{1,0:T(8,128)(2,1)S(1)} %copy-done.1), kind=kOutput, calls=%fused_computation.52 | convolution fusion | flops 1623392256 | bytes 7733248 | tf_op jit(solution)/shard_map/dot_general | solution.py:67
  119.5 5.3 %collective-permute-start.4 = (bf16[384,512]{1,0:T(8,128)(2,1)S(1)}, bf16[384,512]{1,0:T(8,128)(2,1)}, u32[]{:S(2)}, u32[]{:S(2)}) collective-permute-start(bf16[384,512]{1,0:T(8,128)(2,1)S(1)} %fusion.42), channel_id=1, source_target_pairs={{0,4},{4,8},{8,12},{1,5},{5,9},{9,13},{2,6},{6,10},{10,14},{3,7},{... | collective-permute-start | bytes 1179656 | tf_op jit(solution)/shard_map/ppermute | solution.py:23
  124.8 18.5 %collective-permute-done.9 = bf16[3072,256]{1,0:T(8,128)(2,1)S(1)} collective-permute-done((bf16[3072,256]{1,0:T(8,128)(2,1)S(1)}, bf16[3072,256]{1,0:T(8,128)(2,1)S(1)}, u32[]{:S(2)}, u32[]{:S(2)}) %collective-permute-start.9) | collective-permute-done | bytes 1572896 | tf_op jit(solution)/shard_map/ppermute | solution.py:51
  143.3 5.0 %fusion.39 = bf16[384,512]{1,0:T(8,128)(2,1)S(1)} fusion(bf16[384,4096]{1,0:T(8,128)(2,1)S(1)} %fusion.26, bf16[3072,256]{1,0:T(8,128)(2,1)S(1)} %collective-permute-done.9, bf16[1024,256]{1,0:T(8,128)(2,1)S(1)} %copy-done.8, bf16[4096,256]{1,0:T(8,128)(2,1)S(1)} %fusion.27), kind=kOutput, calls=%fused_computation.51 | convolution fusion | flops 1623392256 | bytes 7733248 | tf_op jit(solution)/shard_map/dot_general | solution.py:67
  149.6 5.3 %collective-permute-start.12 = (bf16[384,512]{1,0:T(8,128)(2,1)S(1)}, bf16[384,512]{1,0:T(8,128)(2,1)}, u32[]{:S(2)}, u32[]{:S(2)}) collective-permute-start(bf16[384,512]{1,0:T(8,128)(2,1)S(1)} %fusion.39), channel_id=1, source_target_pairs={{0,4},{4,8},{8,12},{1,5},{5,9},{9,13},{2,6},{6,10},{10,14},{3,7},{... | collective-permute-start | bytes 1179656 | tf_op jit(solution)/shard_map/ppermute | solution.py:23
  157.7 7.9 %collective-permute-done.11 = bf16[384,512]{1,0:T(8,128)(2,1)S(1)} collective-permute-done((bf16[384,512]{1,0:T(8,128)(2,1)S(1)}, bf16[384,512]{1,0:T(8,128)(2,1)S(1)}, u32[]{:S(2)}, u32[]{:S(2)}) %collective-permute-start.11) | collective-permute-done | bytes 393248 | tf_op jit(solution)/shard_map/ppermute | solution.py:22
  168.3 3.0 %fusion.28 = bf16[4096,256]{1,0:T(8,128)(2,1)S(1)} fusion(s32[]{:T(128)S(6)} %select_n.103, bf16[4096,256]{1,0:T(8,128)(2,1)} %all-gather.6.cloned.1.call-done), kind=kLoop, calls=%fused_computation.39 | loop fusion | flops 4194304 | bytes 4194308 | tf_op jit(solution)/shard_map/jit(_roll_dynamic)/concatenate | solution.py:48
  177.1 5.4 %collective-permute-done.15 = bf16[384,512]{1,0:T(8,128)(2,1)} collective-permute-done((bf16[384,512]{1,0:T(8,128)(2,1)S(1)}, bf16[384,512]{1,0:T(8,128)(2,1)}, u32[]{:S(2)}, u32[]{:S(2)}) %collective-permute-start.15) | collective-permute-done | bytes 393248 | tf_op jit(solution)/shard_map/ppermute | solution.py:22
  186.3 5.7 %collective-permute-done.8 = bf16[384,512]{1,0:T(8,128)(2,1)S(1)} collective-permute-done((bf16[384,512]{1,0:T(8,128)(2,1)}, bf16[384,512]{1,0:T(8,128)(2,1)S(1)}, u32[]{:S(2)}, u32[]{:S(2)}) %collective-permute-start.8) | collective-permute-done | bytes 393248 | tf_op jit(solution)/shard_map/ppermute | solution.py:22
  194.4 2.7 %copy.10 = bf16[1536,512]{0,1:T(8,128)(2,1)} copy(bf16[1536,512]{1,0:T(8,128)(2,1)} %pad_maximum_fusion.1) | data formatting | bytes 3145728 | tf_op jit(solution)/shard_map/reshape;squeeze;stack | solution.py:85
  197.1 2.0 collective-permute-done.16
  201.2 7.5 %collective-permute-done.10 = bf16[3072,256]{1,0:T(8,128)(2,1)} collective-permute-done((bf16[3072,256]{1,0:T(8,128)(2,1)}, bf16[3072,256]{1,0:T(8,128)(2,1)}, u32[]{:S(2)}, u32[]{:S(2)}) %collective-permute-start.10) | collective-permute-done | bytes 1572896 | tf_op jit(solution)/shard_map/ppermute | solution.py:51
  208.7 4.1 %fusion.45 = bf16[48,4,8,128]{3,2,1,0:T(8,128)(2,1)S(1)} fusion(bf16[384,4096]{1,0:T(8,128)(2,1)} %copy-done.2, bf16[3072,256]{1,0:T(8,128)(2,1)} %collective-permute-done.10, bf16[1024,256]{1,0:T(8,128)(2,1)S(1)} %copy-done.7, bf16[4096,256]{1,0:T(8,128)(2,1)S(1)} %fusion.28), kind=kOutput, calls=%fused_computation.53 | convolution fusion | flops 1623392256 | bytes 7733248 | tf_op jit(solution)/shard_map/dot_general | solution.py:67
  212.9 1.7 multiply_reduce_fusion
  216.3 2.1 fusion.51
  (70 shorter events, 33.2 us)
Async XLA Ops:
  6.5 51.2 %all-gather.4.cloned.1.call-start = ((), (), s32[]{:S(2)}) async-start(), calls=%async_computation | async-start | bytes 2621440 | tf_op jit(solution)/shard_map/all_gather | solution.py:47
  8.9 95.0 %all-gather.8.cloned.1.call-start = ((), (), s32[]{:S(2)}) async-start(), calls=%async_computation.2 | async-start | bytes 2621440 | tf_op jit(solution)/shard_map/all_gather | solution.py:47
  10.0 158.2 %all-gather.6.cloned.1.call-start = ((), (), s32[]{:S(2)}) async-start(), calls=%async_computation.1 | async-start | bytes 2621440 | tf_op jit(solution)/shard_map/all_gather | solution.py:47
  10.1 20.5 %collective-permute-start = (bf16[192,2048]{1,0:T(8,128)(2,1)S(1)}, bf16[192,2048]{1,0:T(8,128)(2,1)S(1)}, u32[]{:S(2)}, u32[]{:S(2)}) collective-permute-start(bf16[192,2048]{1,0:T(8,128)(2,1)S(1)} %copy-done.6), channel_id=1, source_target_pairs={{0,2},{2,0},{1,3},{3,1},{4,6},{6,4},{5,7},{7,5},{8,10},{10,8},{9,1... | collective-permute-start | bytes 2359304 | tf_op jit(solution)/shard_map/ppermute | solution.py:34
  13.1 17.9 %copy-start.5 = (bf16[1024,512]{1,0:T(8,128)(2,1)S(1)}, bf16[1024,512]{1,0:T(8,128)(2,1)}, u32[]{:S(2)}) copy-start(bf16[1024,512]{1,0:T(8,128)(2,1)} %param.7) | copy-start | bytes 3145732
  30.9 77.7 %collective-permute-start.1 = (bf16[384,2048]{1,0:T(8,128)(2,1)S(1)}, bf16[384,2048]{1,0:T(8,128)(2,1)}, u32[]{:S(2)}, u32[]{:S(2)}) collective-permute-start(bf16[384,2048]{1,0:T(8,128)(2,1)S(1)} %pad_maximum_fusion), channel_id=1, source_target_pairs={{0,1},{1,0},{2,3},{3,2},{4,5},{5,4},{6,7},{7,6},{8,9},{9,8},{10,11... | collective-permute-start | bytes 4718600 | tf_op jit(solution)/shard_map/ppermute | solution.py:34
  63.3 50.5 %collective-permute-start.2 = (bf16[3072,256]{1,0:T(8,128)(2,1)}, bf16[3072,256]{1,0:T(8,128)(2,1)}, u32[]{:S(2)}, u32[]{:S(2)}) collective-permute-start(bf16[3072,256]{1,0:T(8,128)(2,1)} %slice.12), channel_id=1, source_target_pairs={{0,16},{16,0},{1,17},{17,1},{2,18},{18,2},{3,19},{19,3},{4,20},{20... | collective-permute-start | bytes 4718600 | tf_op jit(solution)/shard_map/ppermute | solution.py:51
  107.1 36.2 %collective-permute-start.9 = (bf16[3072,256]{1,0:T(8,128)(2,1)S(1)}, bf16[3072,256]{1,0:T(8,128)(2,1)S(1)}, u32[]{:S(2)}, u32[]{:S(2)}) collective-permute-start(bf16[3072,256]{1,0:T(8,128)(2,1)S(1)} %slice.13), channel_id=1, source_target_pairs={{0,16},{16,0},{1,17},{17,1},{2,18},{18,2},{3,19},{19,3},{4,20},{20... | collective-permute-start | bytes 4718600 | tf_op jit(solution)/shard_map/ppermute | solution.py:51
  113.8 29.5 %copy-start.2 = (bf16[384,4096]{1,0:T(8,128)(2,1)}, bf16[384,4096]{1,0:T(8,128)(2,1)S(1)}, u32[]{:S(2)}) copy-start(bf16[384,4096]{1,0:T(8,128)(2,1)S(1)} %fusion.26) | copy-start | bytes 9437188
  113.9 29.4 %copy-start.8 = (bf16[1024,256]{1,0:T(8,128)(2,1)S(1)}, bf16[1024,256]{1,0:T(8,128)(2,1)}, u32[]{:S(2)}) copy-start(bf16[1024,256]{1,0:T(8,128)(2,1)} %get-tuple-element.14) | copy-start | bytes 1572868
  118.2 36.7 %collective-permute-start.3 = (bf16[384,512]{1,0:T(8,128)(2,1)S(1)}, bf16[384,512]{1,0:T(8,128)(2,1)}, u32[]{:S(2)}, u32[]{:S(2)}) collective-permute-start(bf16[384,512]{1,0:T(8,128)(2,1)S(1)} %fusion.42), channel_id=1, source_target_pairs={{4,0},{8,4},{12,8},{5,1},{9,5},{13,9},{6,2},{10,6},{14,10},{7,3},{... | collective-permute-start | bytes 1179656 | tf_op jit(solution)/shard_map/ppermute | solution.py:22
  119.5 36.7 %collective-permute-start.4 = (bf16[384,512]{1,0:T(8,128)(2,1)S(1)}, bf16[384,512]{1,0:T(8,128)(2,1)}, u32[]{:S(2)}, u32[]{:S(2)}) collective-permute-start(bf16[384,512]{1,0:T(8,128)(2,1)S(1)} %fusion.42), channel_id=1, source_target_pairs={{0,4},{4,8},{8,12},{1,5},{5,9},{9,13},{2,6},{6,10},{10,14},{3,7},{... | collective-permute-start | bytes 1179656 | tf_op jit(solution)/shard_map/ppermute | solution.py:23
  148.3 17.2 %collective-permute-start.11 = (bf16[384,512]{1,0:T(8,128)(2,1)S(1)}, bf16[384,512]{1,0:T(8,128)(2,1)S(1)}, u32[]{:S(2)}, u32[]{:S(2)}) collective-permute-start(bf16[384,512]{1,0:T(8,128)(2,1)S(1)} %fusion.39), channel_id=1, source_target_pairs={{4,0},{8,4},{12,8},{5,1},{9,5},{13,9},{6,2},{10,6},{14,10},{7,3},{... | collective-permute-start | bytes 1179656 | tf_op jit(solution)/shard_map/ppermute | solution.py:22
  149.6 17.2 %collective-permute-start.12 = (bf16[384,512]{1,0:T(8,128)(2,1)S(1)}, bf16[384,512]{1,0:T(8,128)(2,1)}, u32[]{:S(2)}, u32[]{:S(2)}) collective-permute-start(bf16[384,512]{1,0:T(8,128)(2,1)S(1)} %fusion.39), channel_id=1, source_target_pairs={{0,4},{4,8},{8,12},{1,5},{5,9},{9,13},{2,6},{6,10},{10,14},{3,7},{... | collective-permute-start | bytes 1179656 | tf_op jit(solution)/shard_map/ppermute | solution.py:23
  154.9 19.2 %collective-permute-start.7 = (bf16[384,512]{1,0:T(8,128)(2,1)}, bf16[384,512]{1,0:T(8,128)(2,1)}, u32[]{:S(2)}, u32[]{:S(2)}) collective-permute-start(bf16[384,512]{1,0:T(8,128)(2,1)} %collective-permute-done.3), channel_id=1, source_target_pairs={{4,0},{8,4},{5,1},{9,5},{6,2},{10,6},{7,3},{11,7},{20,16},{24,20},... | collective-permute-start | bytes 1179656 | tf_op jit(solution)/shard_map/ppermute | solution.py:22
  156.2 19.1 %collective-permute-start.5 = (bf16[384,512]{1,0:T(8,128)(2,1)}, bf16[384,512]{1,0:T(8,128)(2,1)}, u32[]{:S(2)}, u32[]{:S(2)}) collective-permute-start(bf16[384,512]{1,0:T(8,128)(2,1)} %collective-permute-done.4), channel_id=1, source_target_pairs={{4,8},{8,12},{5,9},{9,13},{6,10},{10,14},{7,11},{11,15},{20,24},{2... | collective-permute-start | bytes 1179656 | tf_op jit(solution)/shard_map/ppermute | solution.py:23
  165.6 17.0 %collective-permute-start.15 = (bf16[384,512]{1,0:T(8,128)(2,1)S(1)}, bf16[384,512]{1,0:T(8,128)(2,1)}, u32[]{:S(2)}, u32[]{:S(2)}) collective-permute-start(bf16[384,512]{1,0:T(8,128)(2,1)S(1)} %collective-permute-done.11), channel_id=1, source_target_pairs={{4,0},{8,4},{5,1},{9,5},{6,2},{10,6},{7,3},{11,7},{20,16},{24,20},... | collective-permute-start | bytes 1179656 | tf_op jit(solution)/shard_map/ppermute | solution.py:22
  166.9 16.9 %collective-permute-start.13 = (bf16[384,512]{1,0:T(8,128)(2,1)}, bf16[384,512]{1,0:T(8,128)(2,1)}, u32[]{:S(2)}, u32[]{:S(2)}) collective-permute-start(bf16[384,512]{1,0:T(8,128)(2,1)} %collective-permute-done.12), channel_id=1, source_target_pairs={{4,8},{8,12},{5,9},{9,13},{6,10},{10,14},{7,11},{11,15},{20,24},{2... | collective-permute-start | bytes 1179656 | tf_op jit(solution)/shard_map/ppermute | solution.py:23
  172.6 36.1 %collective-permute-start.10 = (bf16[3072,256]{1,0:T(8,128)(2,1)}, bf16[3072,256]{1,0:T(8,128)(2,1)}, u32[]{:S(2)}, u32[]{:S(2)}) collective-permute-start(bf16[3072,256]{1,0:T(8,128)(2,1)} %slice.11), channel_id=1, source_target_pairs={{0,16},{16,0},{1,17},{17,1},{2,18},{18,2},{3,19},{19,3},{4,20},{20... | collective-permute-start | bytes 4718600 | tf_op jit(solution)/shard_map/ppermute | solution.py:51
  174.1 17.9 %collective-permute-start.8 = (bf16[384,512]{1,0:T(8,128)(2,1)}, bf16[384,512]{1,0:T(8,128)(2,1)S(1)}, u32[]{:S(2)}, u32[]{:S(2)}) collective-permute-start(bf16[384,512]{1,0:T(8,128)(2,1)} %collective-permute-done.7), channel_id=1, source_target_pairs={{4,0},{5,1},{6,2},{7,3},{20,16},{21,17},{22,18},{23,19}} | collective-permute-start | bytes 1179656 | tf_op jit(solution)/shard_map/ppermute | solution.py:22
  175.4 16.6 %collective-permute-start.6 = (bf16[384,512]{1,0:T(8,128)(2,1)}, bf16[384,512]{1,0:T(8,128)(2,1)S(1)}, u32[]{:S(2)}, u32[]{:S(2)}) collective-permute-start(bf16[384,512]{1,0:T(8,128)(2,1)} %collective-permute-done.5), channel_id=1, source_target_pairs={{8,12},{9,13},{10,14},{11,15},{24,28},{25,29},{26,30},{27,31}} | collective-permute-start | bytes 1179656 | tf_op jit(solution)/shard_map/ppermute | solution.py:23
  182.5 16.5 %collective-permute-start.16 = (bf16[384,512]{1,0:T(8,128)(2,1)}, bf16[384,512]{1,0:T(8,128)(2,1)}, u32[]{:S(2)}, u32[]{:S(2)}) collective-permute-start(bf16[384,512]{1,0:T(8,128)(2,1)} %collective-permute-done.15), channel_id=1, source_target_pairs={{4,0},{5,1},{6,2},{7,3},{20,16},{21,17},{22,18},{23,19}} | collective-permute-start | bytes 1179656 | tf_op jit(solution)/shard_map/ppermute | solution.py:22
  183.8 16.3 %collective-permute-start.14 = (bf16[384,512]{1,0:T(8,128)(2,1)}, bf16[384,512]{1,0:T(8,128)(2,1)}, u32[]{:S(2)}, u32[]{:S(2)}) collective-permute-start(bf16[384,512]{1,0:T(8,128)(2,1)} %collective-permute-done.13), channel_id=1, source_target_pairs={{8,12},{9,13},{10,14},{11,15},{24,28},{25,29},{26,30},{27,31}} | collective-permute-start | bytes 1179656 | tf_op jit(solution)/shard_map/ppermute | solution.py:23
  194.4 14.3 %copy-start.7 = (bf16[1024,256]{1,0:T(8,128)(2,1)S(1)}, bf16[1024,256]{1,0:T(8,128)(2,1)}, u32[]{:S(2)}) copy-start(bf16[1024,256]{1,0:T(8,128)(2,1)} %get-tuple-element.12) | copy-start | bytes 1572868
  (7 other events, 22.0 us)
Sparse Core Ops, SparseCore 0:
  9.0 48.6 all-gather.3
  59.3 44.6 all-gather.7
  105.5 55.8 all-gather.5

commit v5 on v4

--- a/solution.py
+++ b/solution.py
@@ -37,19 +37,25 @@
     return jnp.concatenate([low, high], axis=dim)
 
 
-def full_columns(weight, shared, after=None):
+def column_chunks(weight, shared, after=None):
     if not shared:
-        return lax.all_gather(weight, "seq", axis=0, tiled=True)
+        return [lax.all_gather(weight, "seq", axis=0, tiled=True)]
     rows, half = weight.shape[0], weight.shape[1] // 2
     group = lax.axis_index("groups")
-    own = lax.dynamic_slice_in_dim(weight, group * half, half, axis=1)
-    kept = lax.dynamic_slice_in_dim(weight, (1 - group) * half, half, axis=1)
-    own = lax.all_gather(own, "seq", axis=0, tiled=True)
-    own = jnp.roll(own, -lax.axis_index("seq") * rows, axis=0)
-    if after is not None:
-        own = lax.optimization_barrier((own, after))[0]
-    other = lax.ppermute(own[rows:], "groups", [(0, 1), (1, 0)])
-    return jnp.concatenate([own, jnp.concatenate([kept, other], axis=0)], axis=1)
+    count = 2 if half % (2 * HD) == 0 else 1
+    width = half // count
+    owns, others = [], []
+    for k in range(count):
+        own = lax.dynamic_slice_in_dim(weight, group * half + k * width, width, axis=1)
+        kept = lax.dynamic_slice_in_dim(weight, (1 - group) * half + k * width, width, axis=1)
+        own = lax.all_gather(own, "seq", axis=0, tiled=True)
+        own = jnp.roll(own, -lax.axis_index("seq") * rows, axis=0)
+        if after is not None:
+            own = lax.optimization_barrier((own, after))[0]
+        other = lax.ppermute(own[rows:], "groups", [(0, 1), (1, 0)])
+        owns.append(own)
+        others.append(jnp.concatenate([kept, other], axis=0))
+    return owns + others
 
 
 def per_device(acts, w_query, w_key, w_value):
@@ -63,8 +69,13 @@
         block = jnp.roll(block, -lax.axis_index("seq") * w_query.shape[0], axis=1)
 
     def project(weight, after=None):
-        piece = full_columns(weight, shared, after)
-        return jnp.dot(block, piece, preferred_element_type=jnp.float32).astype(jnp.bfloat16)
+        return jnp.concatenate(
+            [
+                jnp.dot(block, piece, preferred_element_type=jnp.float32).astype(jnp.bfloat16)
+                for piece in column_chunks(weight, shared, after)
+            ],
+            axis=1,
+        )
 
     key = project(w_key)
     value = project(w_value)

time: 230 us -> 260 us (1.13); the launches traced: 226 us -> 259 us
  waiting for transfers between devices: 129 us -> 152 us
  other arithmetic: 23.6 us -> 29.6 us
    all_gather x3 -> x6, waiting for transfers between devices: 64.7 us -> 109 us  [column_chunks(): own = lax.all_gather(own, 'seq', axis=0, tiled=True)]
    ppermute x6, waiting for transfers between devices: 21 us -> 1.5 us  [line_gather(): lax.ppermute(from_right[-1], 'seq', [(j, j - 1) for j in range(1, n - k +...]
    concatenate x1 -> x2, other arithmetic: 1.32 us -> 5.21 us  [line_gather(): return jnp.concatenate(slots, axis=0)]
    ppermute x3 -> x6, starting transfers between devices: 4.48 us -> 8.12 us  [column_chunks(): other = lax.ppermute(own[rows:], 'groups', [(0, 1), (1, 0)])]
    ppermute x3 -> x6, waiting for transfers between devices: 26 us -> 23 us  [column_chunks(): other = lax.ppermute(own[rows:], 'groups', [(0, 1), (1, 0)])]
    concatenate x3 -> x8, other arithmetic: 9.01 us -> 11.8 us  [the longest x5 10.2 us: column_chunks(): own = jnp.roll(own, -lax.axis_index('seq') * rows, axis=0)]
    another operation x1 -> x0, local copies, waits for them, and re-layouts: 2.69 us -> none  [per_device(): seen_values = seen[1].reshape(-1, heads_here, HD)]
    dot_general x3 -> x12, matrix products: 13.5 us -> 15.8 us  [project(): jnp.dot(block, piece, preferred_element_type=jnp.float32)]
  transfers between devices with their start and end apart: 20 -> 26, of which waited for: 9 -> 9; matrix products, arithmetic and copies ran while one was open for 17% -> 18% of each run, Pallas kernels for 0% -> 0%
where the time goes in v5:
time: 260 us; the launch traced here: 259 us
  waiting for transfers between devices  152 us (58%)
  starting transfers between devices  32.8 us (13%)
  other arithmetic  29.6 us (11%)
  matrix products  19.4 us (7%)
  between operations  14.2 us (5%)
  local copies, waits for them, and re-layouts  10.8 us (4%)
    all_gather x6, waiting for transfers between devices, column_chunks(): own = lax.all_gather(own, 'seq', axis=0, tiled=True)  109 us
    ppermute x6, waiting for transfers between devices, column_chunks(): other = lax.ppermute(own[rows:], 'groups', [(0, 1), (1, 0)])  23 us
    ppermute x2, waiting for transfers between devices, swap_gather(): other = lax.ppermute(piece, axis, [(0, 1), (1, 0)])  17.6 us
    dot_general x12, matrix products, project(): jnp.dot(block, piece, preferred_element_type=jnp.float32)  15.8 us
    ppermute x6, starting transfers between devices, line_gather(): lax.ppermute(from_left[-1], 'seq', [(j, j + 1) for j in range(k - 1, n -...  13.5 us
    concatenate x5, other arithmetic, column_chunks(): own = jnp.roll(own, -lax.axis_index('seq') * rows, axis=0)  10.2 us
    ppermute x6, starting transfers between devices, column_chunks(): other = lax.ppermute(own[rows:], 'groups', [(0, 1), (1, 0)])  8.12 us
    ppermute x6, starting transfers between devices, line_gather(): lax.ppermute(from_right[-1], 'seq', [(j, j - 1) for j in range(1, n - k +...  7.84 us
  transfers between devices with their start and end apart: 26, of which 9 were waited for; matrix products, arithmetic and copies ran while one was open for 18% of the time, Pallas kernels for 0%

profile of v5, /device:TPU:0, one launch (start us, length us, event | category | flops | bytes accessed | tf_op | source)
XLA Modules:
  0.0 259.2 jit_solution(12496185557095535558)
XLA Ops:
  6.5 2.3 constant_dynamic-slice_fusion.9
  12.6 3.0 %collective-permute-start = (bf16[192,2048]{1,0:T(8,128)(2,1)S(1)}, bf16[192,2048]{1,0:T(8,128)(2,1)}, u32[]{:S(2)}, u32[]{:S(2)}) collective-permute-start(bf16[192,2048]{1,0:T(8,128)(2,1)S(1)} %copy-done.8), channel_id=1, source_target_pairs={{0,2},{2,0},{1,3},{3,1},{4,6},{6,4},{5,7},{7,5},{8,10},{10,8},{9,1... | collective-permute-start | bytes 2359304 | tf_op jit(solution)/shard_map/ppermute | solution.py:34
  15.6 17.6 %collective-permute-done = bf16[192,2048]{1,0:T(8,128)(2,1)} collective-permute-done((bf16[192,2048]{1,0:T(8,128)(2,1)S(1)}, bf16[192,2048]{1,0:T(8,128)(2,1)}, u32[]{:S(2)}, u32[]{:S(2)}) %collective-permute-start) | collective-permute-done | bytes 786464 | tf_op jit(solution)/shard_map/ppermute | solution.py:34
  34.7 4.9 %all-gather.9.cloned.1.call-done = bf16[4096,128]{1,0:T(8,128)(2,1)} async-done(((bf16[1024,128]{1,0:T(8,128)(2,1)}), bf16[4096,128]{1,0:T(8,128)(2,1)}) %all-gather.9.cloned.1.call-update) | async-done | bytes 1048592 | tf_op jit(solution)/shard_map/all_gather | solution.py:51
  39.6 1.9 fusion.16
  45.0 23.6 %all-gather.7.cloned.1.call-done = bf16[4096,128]{1,0:T(8,128)(2,1)} async-done(((bf16[1024,128]{1,0:T(8,128)(2,1)}), bf16[4096,128]{1,0:T(8,128)(2,1)}) %all-gather.7.cloned.1.call-update) | async-done | bytes 1048592 | tf_op jit(solution)/shard_map/all_gather | solution.py:51
  68.6 1.9 fusion.17
  74.0 23.7 %all-gather.15.cloned.1.call-done = bf16[4096,128]{1,0:T(8,128)(2,1)} async-done(((bf16[1024,128]{1,0:T(8,128)(2,1)}), bf16[4096,128]{1,0:T(8,128)(2,1)}) %all-gather.15.cloned.1.call-update) | async-done | bytes 1048592 | tf_op jit(solution)/shard_map/all_gather | solution.py:51
  97.7 1.9 fusion.13
  103.0 23.5 %all-gather.13.cloned.1.call-done = bf16[4096,128]{1,0:T(8,128)(2,1)} async-done(((bf16[1024,128]{1,0:T(8,128)(2,1)}), bf16[4096,128]{1,0:T(8,128)(2,1)}) %all-gather.13.cloned.1.call-update) | async-done | bytes 1048592 | tf_op jit(solution)/shard_map/all_gather | solution.py:51
  130.1 2.2 broadcast_select_fusion
  132.3 2.9 %fusion.8 = bf16[384,4096]{1,0:T(8,128)(2,1)S(1)} fusion(s32[]{:T(128)S(6)} %select_n.113, bf16[384,2048]{1,0:T(8,128)(2,1)S(1)} %get-tuple-element.11, bf16[384,2048]{1,0:T(8,128)(2,1)S(1)} %get-tuple-element.10), kind=kLoop, calls=%fused_computation.13 | loop fusion | flops 12582912 | bytes 6291460 | tf_op jit(solution)/shard_map/jit(_roll_dynamic)/concatenate | solution.py:69
  136.3 2.2 convolution_convert_fusion.8
  139.6 2.2 convolution_convert_fusion.9
  143.9 5.3 %collective-permute-start.5 = (bf16[384,512]{0,1:T(8,128)(2,1)}, bf16[384,512]{0,1:T(8,128)(2,1)}, u32[]{:S(2)}, u32[]{:S(2)}) collective-permute-start(bf16[384,512]{0,1:T(8,128)(2,1)} %pad_maximum_fusion.3), channel_id=1, source_target_pairs={{0,4},{4,8},{8,12},{1,5},{5,9},{9,13},{2,6},{6,10},{10,14},{3,7},{... | collective-permute-start | bytes 1179656 | tf_op jit(solution)/shard_map/ppermute | solution.py:23
  149.2 2.1 convolution_convert_fusion.4
  156.6 5.3 %collective-permute-start.15 = (bf16[384,512]{0,1:T(8,128)(2,1)}, bf16[384,512]{0,1:T(8,128)(2,1)}, u32[]{:S(2)}, u32[]{:S(2)}) collective-permute-start(bf16[384,512]{0,1:T(8,128)(2,1)} %pad_maximum_fusion.4), channel_id=1, source_target_pairs={{0,4},{4,8},{8,12},{1,5},{5,9},{9,13},{2,6},{6,10},{10,14},{3,7},{... | collective-permute-start | bytes 1179656 | tf_op jit(solution)/shard_map/ppermute | solution.py:23
  164.7 33.4 %all-gather.11.cloned.1.call-done = bf16[4096,128]{1,0:T(8,128)(2,1)} async-done(((bf16[1024,128]{1,0:T(8,128)(2,1)}), bf16[4096,128]{1,0:T(8,128)(2,1)}) %all-gather.11.cloned.1.call-update) | async-done | bytes 1048592 | tf_op jit(solution)/shard_map/all_gather | solution.py:51
  198.1 2.6 %fusion.12 = (bf16[4096,128]{1,0:T(8,128)(2,1)S(1)}, bf16[4096,128]{1,0:T(8,128)(2,1)S(1)}) fusion(s32[]{:T(128)S(6)} %select_n.113, bf16[4096,128]{1,0:T(8,128)(2,1)} %all-gather.17.cloned.1.call-done, bf16[4096,128]{1,0:T(8,128)(2,1)} %all-gather.11.cloned.1.call-done), kind=kLoop, calls=%fused_computation.44 | loop fusion | flops 4194304 | bytes 4194308 | tf_op jit(solution)/shard_map/jit(_roll_dynamic)/concatenate | solution.py:52
  210.3 10.9 %collective-permute-done.13 = bf16[3072,128]{1,0:T(8,128)(2,1)S(1)} collective-permute-done((bf16[3072,128]{1,0:T(8,128)(2,1)S(1)}, bf16[3072,128]{1,0:T(8,128)(2,1)S(1)}, u32[]{:S(2)}, u32[]{:S(2)}) %collective-permute-start.13) | collective-permute-done | bytes 786464 | tf_op jit(solution)/shard_map/ppermute | solution.py:55
  225.2 12.0 %collective-permute-done.12 = bf16[3072,128]{1,0:T(8,128)(2,1)S(1)} collective-permute-done((bf16[3072,128]{1,0:T(8,128)(2,1)S(1)}, bf16[3072,128]{1,0:T(8,128)(2,1)S(1)}, u32[]{:S(2)}, u32[]{:S(2)}) %collective-permute-start.12) | collective-permute-done | bytes 786464 | tf_op jit(solution)/shard_map/ppermute | solution.py:55
  239.6 2.6 %pad_maximum_fusion.2 = bf16[1536,512]{0,1:T(8,128)(2,1)S(1)} fusion(bf16[384,512]{0,1:T(8,128)(2,1)S(1)} %broadcast_select_fusion.4, bf16[384,512]{0,1:T(8,128)(2,1)S(1)} %broadcast_select_fusion.6, bf16[384,512]{0,1:T(8,128)(2,1)S(1)} %broadcast_select_fusion.8, bf16[384,128]{0,1:T(8,128)(2,1)S(1)} %copy-done.14, bf16[384,128]{0,1:T(8,128)(2,1)S(1)} %copy-done.16, ...), kind=kLoop, calls=%fused_computation.28 | loop fusion | flops 11010048 | bytes 3145728 | tf_op jit(solution)/shard_map/concatenate | solution.py:27
  246.6 2.6 %pad_maximum_fusion.1 = bf16[1536,512]{0,1:T(8,128)(2,1)S(1)} fusion(bf16[384,512]{0,1:T(8,128)(2,1)S(1)} %broadcast_select_fusion.5, bf16[384,512]{0,1:T(8,128)(2,1)S(1)} %broadcast_select_fusion.7, bf16[384,512]{0,1:T(8,128)(2,1)S(1)} %broadcast_select_fusion.9, bf16[384,128]{0,1:T(8,128)(2,1)S(1)} %copy-done.10, bf16[384,128]{0,1:T(8,128)(2,1)S(1)} %copy-done.12, ...), kind=kLoop, calls=%fused_computation.27 | loop fusion | flops 11010048 | bytes 3145728 | tf_op jit(solution)/shard_map/concatenate | solution.py:27
  249.2 2.1 fusion.39
  (124 shorter events, 52.2 us)
Async XLA Ops:
  6.5 33.1 %all-gather.9.cloned.1.call-start = ((), (), s32[]{:S(2)}) async-start(), calls=%async_computation.1 | async-start | bytes 1310720 | tf_op jit(solution)/shard_map/all_gather | solution.py:51
  8.8 59.8 %all-gather.7.cloned.1.call-start = ((), (), s32[]{:S(2)}) async-start(), calls=%async_computation | async-start | bytes 1310720 | tf_op jit(solution)/shard_map/all_gather | solution.py:51
  9.6 88.1 %all-gather.15.cloned.1.call-start = ((), (), s32[]{:S(2)}) async-start(), calls=%async_computation.4 | async-start | bytes 1310720 | tf_op jit(solution)/shard_map/all_gather | solution.py:51
  10.7 115.8 %all-gather.13.cloned.1.call-start = ((), (), s32[]{:S(2)}) async-start(), calls=%async_computation.3 | async-start | bytes 1310720 | tf_op jit(solution)/shard_map/all_gather | solution.py:51
  11.3 153.4 %all-gather.17.cloned.1.call-start = ((), (), s32[]{:S(2)}) async-start(), calls=%async_computation.5 | async-start | bytes 1310720 | tf_op jit(solution)/shard_map/all_gather | solution.py:51
  12.5 185.6 %all-gather.11.cloned.1.call-start = ((), (), s32[]{:S(2)}) async-start(), calls=%async_computation.2 | async-start | bytes 1310720 | tf_op jit(solution)/shard_map/all_gather | solution.py:51
  12.6 20.7 %collective-permute-start = (bf16[192,2048]{1,0:T(8,128)(2,1)S(1)}, bf16[192,2048]{1,0:T(8,128)(2,1)}, u32[]{:S(2)}, u32[]{:S(2)}) collective-permute-start(bf16[192,2048]{1,0:T(8,128)(2,1)S(1)} %copy-done.8), channel_id=1, source_target_pairs={{0,2},{2,0},{1,3},{3,1},{4,6},{6,4},{5,7},{7,5},{8,10},{10,8},{9,1... | collective-permute-start | bytes 2359304 | tf_op jit(solution)/shard_map/ppermute | solution.py:34
  34.6 95.4 %collective-permute-start.1 = (bf16[384,2048]{1,0:T(8,128)(2,1)S(1)}, bf16[384,2048]{1,0:T(8,128)(2,1)}, u32[]{:S(2)}, u32[]{:S(2)}) collective-permute-start(bf16[384,2048]{1,0:T(8,128)(2,1)S(1)} %pad_maximum_fusion), channel_id=1, source_target_pairs={{0,1},{1,0},{2,3},{3,2},{4,5},{5,4},{6,7},{7,6},{8,9},{9,8},{10,11... | collective-permute-start | bytes 4718600 | tf_op jit(solution)/shard_map/ppermute | solution.py:34
  43.5 92.8 %collective-permute-start.3 = (bf16[3072,128]{1,0:T(8,128)(2,1)}, bf16[3072,128]{1,0:T(8,128)(2,1)}, u32[]{:S(2)}, u32[]{:S(2)}) collective-permute-start(bf16[3072,128]{1,0:T(8,128)(2,1)} %slice.25), channel_id=1, source_target_pairs={{0,16},{16,0},{1,17},{17,1},{2,18},{18,2},{3,19},{19,3},{4,20},{20... | collective-permute-start | bytes 2359304 | tf_op jit(solution)/shard_map/ppermute | solution.py:55
  72.5 67.1 %collective-permute-start.2 = (bf16[3072,128]{1,0:T(8,128)(2,1)}, bf16[3072,128]{1,0:T(8,128)(2,1)}, u32[]{:S(2)}, u32[]{:S(2)}) collective-permute-start(bf16[3072,128]{1,0:T(8,128)(2,1)} %slice.24), channel_id=1, source_target_pairs={{0,16},{16,0},{1,17},{17,1},{2,18},{18,2},{3,19},{19,3},{4,20},{20... | collective-permute-start | bytes 2359304 | tf_op jit(solution)/shard_map/ppermute | solution.py:55
  101.6 47.7 %collective-permute-start.11 = (bf16[3072,128]{1,0:T(8,128)(2,1)}, bf16[3072,128]{1,0:T(8,128)(2,1)}, u32[]{:S(2)}, u32[]{:S(2)}) collective-permute-start(bf16[3072,128]{1,0:T(8,128)(2,1)} %slice.27), channel_id=1, source_target_pairs={{0,16},{16,0},{1,17},{17,1},{2,18},{18,2},{3,19},{19,3},{4,20},{20... | collective-permute-start | bytes 2359304 | tf_op jit(solution)/shard_map/ppermute | solution.py:55
  128.5 25.0 %collective-permute-start.10 = (bf16[3072,128]{1,0:T(8,128)(2,1)S(1)}, bf16[3072,128]{1,0:T(8,128)(2,1)S(1)}, u32[]{:S(2)}, u32[]{:S(2)}) collective-permute-start(bf16[3072,128]{1,0:T(8,128)(2,1)S(1)} %slice.26), channel_id=1, source_target_pairs={{0,16},{16,0},{1,17},{17,1},{2,18},{18,2},{3,19},{19,3},{4,20},{20... | collective-permute-start | bytes 2359304 | tf_op jit(solution)/shard_map/ppermute | solution.py:55
  142.6 20.8 %collective-permute-start.4 = (bf16[384,512]{0,1:T(8,128)(2,1)}, bf16[384,512]{0,1:T(8,128)(2,1)}, u32[]{:S(2)}, u32[]{:S(2)}) collective-permute-start(bf16[384,512]{0,1:T(8,128)(2,1)} %pad_maximum_fusion.3), channel_id=1, source_target_pairs={{4,0},{8,4},{12,8},{5,1},{9,5},{13,9},{6,2},{10,6},{14,10},{7,3},{... | collective-permute-start | bytes 1179656 | tf_op jit(solution)/shard_map/ppermute | solution.py:22
  143.9 58.4 %collective-permute-start.5 = (bf16[384,512]{0,1:T(8,128)(2,1)}, bf16[384,512]{0,1:T(8,128)(2,1)}, u32[]{:S(2)}, u32[]{:S(2)}) collective-permute-start(bf16[384,512]{0,1:T(8,128)(2,1)} %pad_maximum_fusion.3), channel_id=1, source_target_pairs={{0,4},{4,8},{8,12},{1,5},{5,9},{9,13},{2,6},{6,10},{10,14},{3,7},{... | collective-permute-start | bytes 1179656 | tf_op jit(solution)/shard_map/ppermute | solution.py:23
  155.3 48.8 %collective-permute-start.14 = (bf16[384,512]{0,1:T(8,128)(2,1)}, bf16[384,512]{0,1:T(8,128)(2,1)}, u32[]{:S(2)}, u32[]{:S(2)}) collective-permute-start(bf16[384,512]{0,1:T(8,128)(2,1)} %pad_maximum_fusion.4), channel_id=1, source_target_pairs={{4,0},{8,4},{12,8},{5,1},{9,5},{13,9},{6,2},{10,6},{14,10},{7,3},{... | collective-permute-start | bytes 1179656 | tf_op jit(solution)/shard_map/ppermute | solution.py:22
  156.6 48.2 %collective-permute-start.15 = (bf16[384,512]{0,1:T(8,128)(2,1)}, bf16[384,512]{0,1:T(8,128)(2,1)}, u32[]{:S(2)}, u32[]{:S(2)}) collective-permute-start(bf16[384,512]{0,1:T(8,128)(2,1)} %pad_maximum_fusion.4), channel_id=1, source_target_pairs={{0,4},{4,8},{8,12},{1,5},{5,9},{9,13},{2,6},{6,10},{10,14},{3,7},{... | collective-permute-start | bytes 1179656 | tf_op jit(solution)/shard_map/ppermute | solution.py:23
  163.4 42.7 %collective-permute-start.8 = (bf16[384,512]{0,1:T(8,128)(2,1)}, bf16[384,512]{0,1:T(8,128)(2,1)}, u32[]{:S(2)}, u32[]{:S(2)}) collective-permute-start(bf16[384,512]{0,1:T(8,128)(2,1)} %collective-permute-done.4), channel_id=1, source_target_pairs={{4,0},{8,4},{5,1},{9,5},{6,2},{10,6},{7,3},{11,7},{20,16},{24,20},... | collective-permute-start | bytes 1179656 | tf_op jit(solution)/shard_map/ppermute | solution.py:22
  200.8 20.5 %collective-permute-start.13 = (bf16[3072,128]{1,0:T(8,128)(2,1)S(1)}, bf16[3072,128]{1,0:T(8,128)(2,1)S(1)}, u32[]{:S(2)}, u32[]{:S(2)}) collective-permute-start(bf16[3072,128]{1,0:T(8,128)(2,1)S(1)} %slice.23), channel_id=1, source_target_pairs={{0,16},{16,0},{1,17},{17,1},{2,18},{18,2},{3,19},{19,3},{4,20},{20... | collective-permute-start | bytes 2359304 | tf_op jit(solution)/shard_map/ppermute | solution.py:55
  204.2 33.1 %collective-permute-start.12 = (bf16[3072,128]{1,0:T(8,128)(2,1)S(1)}, bf16[3072,128]{1,0:T(8,128)(2,1)S(1)}, u32[]{:S(2)}, u32[]{:S(2)}) collective-permute-start(bf16[3072,128]{1,0:T(8,128)(2,1)S(1)} %slice.22), channel_id=1, source_target_pairs={{0,16},{16,0},{1,17},{17,1},{2,18},{18,2},{3,19},{19,3},{4,20},{20... | collective-permute-start | bytes 2359304 | tf_op jit(solution)/shard_map/ppermute | solution.py:55
  204.8 17.2 %collective-permute-start.18 = (bf16[384,512]{0,1:T(8,128)(2,1)}, bf16[384,512]{0,1:T(8,128)(2,1)S(1)}, u32[]{:S(2)}, u32[]{:S(2)}) collective-permute-start(bf16[384,512]{0,1:T(8,128)(2,1)} %collective-permute-done.14), channel_id=1, source_target_pairs={{4,0},{8,4},{5,1},{9,5},{6,2},{10,6},{7,3},{11,7},{20,16},{24,20},... | collective-permute-start | bytes 1179656 | tf_op jit(solution)/shard_map/ppermute | solution.py:22
  206.1 17.2 %collective-permute-start.16 = (bf16[384,512]{0,1:T(8,128)(2,1)}, bf16[384,512]{0,1:T(8,128)(2,1)S(1)}, u32[]{:S(2)}, u32[]{:S(2)}) collective-permute-start(bf16[384,512]{0,1:T(8,128)(2,1)} %collective-permute-done.15), channel_id=1, source_target_pairs={{4,8},{8,12},{5,9},{9,13},{6,10},{10,14},{7,11},{11,15},{20,24},{2... | collective-permute-start | bytes 1179656 | tf_op jit(solution)/shard_map/ppermute | solution.py:23
  207.8 37.6 %collective-permute-start.9 = (bf16[384,512]{0,1:T(8,128)(2,1)}, bf16[384,512]{0,1:T(8,128)(2,1)S(1)}, u32[]{:S(2)}, u32[]{:S(2)}) collective-permute-start(bf16[384,512]{0,1:T(8,128)(2,1)} %collective-permute-done.8), channel_id=1, source_target_pairs={{4,0},{5,1},{6,2},{7,3},{20,16},{21,17},{22,18},{23,19}} | collective-permute-start | bytes 1179656 | tf_op jit(solution)/shard_map/ppermute | solution.py:22
  221.3 24.2 %collective-permute-start.7 = (bf16[384,512]{0,1:T(8,128)(2,1)S(1)}, bf16[384,512]{0,1:T(8,128)(2,1)S(1)}, u32[]{:S(2)}, u32[]{:S(2)}) collective-permute-start(bf16[384,512]{0,1:T(8,128)(2,1)S(1)} %collective-permute-done.6), channel_id=1, source_target_pairs={{8,12},{9,13},{10,14},{11,15},{24,28},{25,29},{26,30},{27,31}} | collective-permute-start | bytes 1179656 | tf_op jit(solution)/shard_map/ppermute | solution.py:23
  222.0 16.4 %collective-permute-start.19 = (bf16[384,512]{0,1:T(8,128)(2,1)S(1)}, bf16[384,512]{0,1:T(8,128)(2,1)S(1)}, u32[]{:S(2)}, u32[]{:S(2)}) collective-permute-start(bf16[384,512]{0,1:T(8,128)(2,1)S(1)} %collective-permute-done.18), channel_id=1, source_target_pairs={{4,0},{5,1},{6,2},{7,3},{20,16},{21,17},{22,18},{23,19}} | collective-permute-start | bytes 1179656 | tf_op jit(solution)/shard_map/ppermute | solution.py:22
  (24 other events, 137.5 us)
Sparse Core Ops, SparseCore 0:
  8.9 30.6 all-gather.8
  41.2 27.4 all-gather.6
  70.2 27.4 all-gather.14
  99.1 27.4 all-gather.12
  128.0 30.5 all-gather.16
  160.0 38.1 all-gather.10

commit v6 on v4

--- a/solution.py
+++ b/solution.py
@@ -98,6 +98,83 @@
     return attended
 
 
+def to_workers(piece):
+    near = lax.ppermute(piece, "seq", [(0, 1), (3, 2)])
+    across = lax.ppermute(piece, "seq", [(1, 2), (2, 1)])
+    far = lax.ppermute(near, "seq", [(1, 2), (2, 1)])
+    return [piece, near, across, far]
+
+
+def worker_columns(weight, after=None):
+    rows, half = weight.shape[0], weight.shape[1] // 2
+    group = lax.axis_index("groups")
+    own = lax.dynamic_slice_in_dim(weight, group * half, half, axis=1)
+    kept = lax.dynamic_slice_in_dim(weight, (1 - group) * half, half, axis=1)
+    foreign = jnp.concatenate(to_workers(own)[1:], axis=0)
+    if after is not None:
+        foreign = lax.optimization_barrier((foreign, after))[0]
+    other = lax.ppermute(foreign, "groups", [(0, 1), (1, 0)])
+    return jnp.concatenate(
+        [jnp.concatenate([own, foreign], axis=0), jnp.concatenate([kept, other], axis=0)], axis=1
+    )
+
+
+def paired_per_device(acts, w_query, w_key, w_value):
+    here = lax.axis_index("seq")
+    worker = (here == 1) | (here == 2)
+    near = jnp.where(here == 1, 0, 3)
+    order = [here, near, 3 - here, 3 - near]
+    both = jnp.stack([acts, lax.ppermute(acts, "seq", [(0, 1), (3, 2)])])
+    both = swap_gather(both, "row", 1)
+    both = swap_gather(both, "col", 2)
+    tokens = both.reshape(-1, both.shape[2])
+    rows = w_query.shape[0]
+    tokens = jnp.concatenate(
+        [lax.dynamic_slice_in_dim(tokens, index * rows, rows, axis=1) for index in order], axis=1
+    )
+    tokens_here = tokens.shape[0]
+    width = w_query.shape[1]
+    heads_here = width // HD
+
+    def project(weight, after=None):
+        piece = worker_columns(weight, after)
+        return jnp.dot(tokens, piece, preferred_element_type=jnp.float32).astype(jnp.bfloat16)
+
+    key = project(w_key)
+    value = project(w_value)
+    query = project(w_query, key).reshape(tokens_here, heads_here, HD)
+    packed = jnp.stack([key, value])
+    seen = jnp.concatenate([packed, lax.ppermute(packed, "seq", [(1, 2), (2, 1)])], axis=1)
+    seen_keys = seen[0].reshape(-1, heads_here, HD)
+    seen_values = seen[1].reshape(-1, heads_here, HD)
+    scale = 1.0 / jnp.sqrt(jnp.float32(HD))
+    scores = jnp.einsum("qhd,khd->hqk", query, seen_keys, preferred_element_type=jnp.float32) * scale
+    largest = scores.max(axis=-1, keepdims=True)
+    expos = jnp.exp(scores - largest)
+    running_total = jnp.sum(expos, axis=-1)
+    summed = jnp.einsum(
+        "hqk,khd->qhd", expos.astype(jnp.bfloat16), seen_values, preferred_element_type=jnp.float32
+    )
+    attended = summed / jnp.transpose(running_total)[:, :, None]
+    attended = attended.astype(jnp.bfloat16).reshape(tokens_here, width)
+    attended = jnp.roll(attended, lax.axis_index("groups") * (width // 2), axis=1)
+    block = tokens_here // 2
+    back = lax.ppermute(attended[block:], "seq", [(1, 0), (2, 3)])
+    return jnp.where(worker, attended[:block], back)
+
+
+def chosen(acts, w_query, w_key, w_value):
+    width = w_query.shape[1]
+    if (
+        lax.axis_size("seq") == 4
+        and SPAN == 4
+        and lax.axis_size("groups") == 2
+        and width % (2 * HD) == 0
+    ):
+        return paired_per_device(acts, w_query, w_key, w_value)
+    return per_device(acts, w_query, w_key, w_value)
+
+
 def solution(mesh):
     in_specs = (
         P(("groups", "seq", "row"), "col"),
@@ -107,5 +184,5 @@
     )
     out_specs = P(("groups", "seq"), ("row", "col"))
     return jax.shard_map(
-        per_device, mesh=mesh, in_specs=in_specs, out_specs=out_specs, check_vma=False
+        chosen, mesh=mesh, in_specs=in_specs, out_specs=out_specs, check_vma=False
     )

time: 230 us -> 320 us (1.39)
  waiting for transfers between devices: 129 us -> 206 us
  matrix products: 17.3 us -> 34.7 us
  between operations: 13.5 us -> 0.26 us
  other arithmetic: 23.6 us -> 32.3 us
  starting transfers between devices: 30.9 us -> 34.9 us
    ppermute x15, waiting for transfers between devices: 47 us -> 172 us  [the longest x3 81 us: worker_columns(): other = lax.ppermute(foreign, 'groups', [(0, 1), (1, 0)])]
    all_gather x3 -> x0, waiting for transfers between devices: 64.7 us -> none  [full_columns(): own = lax.all_gather(own, 'seq', axis=0, tiled=True)]
    dot_general x5, matrix products: 17.3 us -> 34.7 us  [the longest x3 18.3 us: project(): jnp.dot(tokens, piece, preferred_element_type=jnp.float32)]
    ppermute x2, waiting for transfers between devices: 17.5 us -> 33.9 us  [swap_gather(): other = lax.ppermute(piece, axis, [(0, 1), (1, 0)])]
    reduce_sum x1, other arithmetic: 1.68 us -> 9.69 us  [paired_per_device(): running_total = jnp.sum(expos, axis=-1)]
    select_n x7 -> x1, other arithmetic: 7.54 us -> 0.79 us  [paired_per_device(): return jnp.where(worker, attended[:block], back)]
    select_n x1 -> x2, other arithmetic: 0.11 us -> 6.28 us  [swap_gather(): low = jnp.where(first, piece, other)]
    ppermute x15, starting transfers between devices: 27.7 us -> 33.4 us  [the longest x3 14.4 us: to_workers(): near = lax.ppermute(piece, 'seq', [(0, 1), (3, 2)])]
  transfers between devices with their start and end apart: 20 -> 17, of which waited for: 9 -> 8; matrix products, arithmetic and copies ran while one was open for 17% -> 12% of each run, Pallas kernels for 0% -> 0%
where the time goes in v6:
time: 320 us; the launch traced here: 319 us
  waiting for transfers between devices  206 us (64%)
  starting transfers between devices  34.9 us (11%)
  matrix products  34.7 us (11%)
  other arithmetic  32.3 us (10%)
  local copies, waits for them, and re-layouts  11 us (3%)
    ppermute x3, waiting for transfers between devices, worker_columns(): other = lax.ppermute(foreign, 'groups', [(0, 1), (1, 0)])  81 us
    ppermute x1, waiting for transfers between devices, paired_per_device(): back = lax.ppermute(attended[block:], 'seq', [(1, 0), (2, 3)])  59.9 us
    ppermute x2, waiting for transfers between devices, swap_gather(): other = lax.ppermute(piece, axis, [(0, 1), (1, 0)])  33.9 us
    dot_general x3, matrix products, project(): jnp.dot(tokens, piece, preferred_element_type=jnp.float32)  18.3 us
    ppermute x1, waiting for transfers between devices, paired_per_device(): both = jnp.stack([acts, lax.ppermute(acts, 'seq', [(0, 1), (3, 2)])])  17 us
    ppermute x3, starting transfers between devices, to_workers(): near = lax.ppermute(piece, 'seq', [(0, 1), (3, 2)])  14.4 us
    ppermute x3, waiting for transfers between devices, to_workers(): near = lax.ppermute(piece, 'seq', [(0, 1), (3, 2)])  13.9 us
    reduce_sum x1, other arithmetic, paired_per_device(): running_total = jnp.sum(expos, axis=-1)  9.69 us
  transfers between devices with their start and end apart: 17, of which 8 were waited for; matrix products, arithmetic and copies ran while one was open for 12% of the time, Pallas kernels for 0%

profile of v6, /device:TPU:0, one launch (start us, length us, event | category | flops | bytes accessed | tf_op | source)
XLA Modules:
  0.0 318.9 jit_solution(16765527453105301127)
XLA Ops:
  0.0 5.0 %collective-permute-start = (bf16[192,2048]{1,0:T(8,128)(2,1)}, bf16[192,2048]{1,0:T(8,128)(2,1)S(1)}, u32[]{:S(2)}, u32[]{:S(2)}) collective-permute-start(bf16[192,2048]{1,0:T(8,128)(2,1)} %param.4), channel_id=1, source_target_pairs={{0,4},{12,8},{1,5},{13,9},{2,6},{14,10},{3,7},{15,11},{16,20},{28,... | collective-permute-start | bytes 2359304 | tf_op jit(solution)/shard_map/ppermute | solution.py:127
  5.0 17.0 %collective-permute-done = bf16[192,2048]{1,0:T(8,128)(2,1)S(1)} collective-permute-done((bf16[192,2048]{1,0:T(8,128)(2,1)}, bf16[192,2048]{1,0:T(8,128)(2,1)S(1)}, u32[]{:S(2)}, u32[]{:S(2)}) %collective-permute-start) | collective-permute-done | bytes 786464 | tf_op jit(solution)/shard_map/ppermute | solution.py:127
  25.8 33.9 %collective-permute-done.1 = bf16[2,192,2048]{2,1,0:T(8,128)(2,1)} collective-permute-done((bf16[2,192,2048]{2,1,0:T(8,128)(2,1)S(1)}, bf16[2,192,2048]{2,1,0:T(8,128)(2,1)}, u32[]{:S(2)}, u32[]{:S(2)}) %collective-permute-start.1) | collective-permute-done | bytes 1572896 | tf_op jit(solution)/shard_map/ppermute | solution.py:34
  63.6 2.3 constant_dynamic-slice_fusion.4
  65.9 5.1 %collective-permute-start.3 = (bf16[1024,256]{1,0:T(8,128)(2,1)}, bf16[1024,256]{1,0:T(8,128)(2,1)}, u32[]{:S(2)}, u32[]{:S(2)}) collective-permute-start(bf16[1024,256]{1,0:T(8,128)(2,1)} %get-tuple-element.20), channel_id=1, source_target_pairs={{0,4},{12,8},{1,5},{13,9},{2,6},{14,10},{3,7},{15,11},{16,20},{28,... | collective-permute-start | bytes 1572872 | tf_op jit(solution)/shard_map/ppermute | solution.py:102
  76.7 5.9 %collective-permute-done.3 = bf16[1024,256]{1,0:T(8,128)(2,1)} collective-permute-done((bf16[1024,256]{1,0:T(8,128)(2,1)}, bf16[1024,256]{1,0:T(8,128)(2,1)}, u32[]{:S(2)}, u32[]{:S(2)}) %collective-permute-start.3) | collective-permute-done | bytes 524320 | tf_op jit(solution)/shard_map/ppermute | solution.py:102
  85.6 8.0 %collective-permute-done.7 = bf16[1024,256]{1,0:T(8,128)(2,1)} collective-permute-done((bf16[1024,256]{1,0:T(8,128)(2,1)}, bf16[1024,256]{1,0:T(8,128)(2,1)}, u32[]{:S(2)}, u32[]{:S(2)}) %collective-permute-start.7) | collective-permute-done | bytes 524320 | tf_op jit(solution)/shard_map/ppermute | solution.py:102
  95.0 2.3 constant_dynamic-slice_fusion
  97.3 7.2 %collective-permute-start.12 = (bf16[1024,256]{1,0:T(8,128)(2,1)}, bf16[1024,256]{1,0:T(8,128)(2,1)}, u32[]{:S(2)}, u32[]{:S(2)}) collective-permute-start(bf16[1024,256]{1,0:T(8,128)(2,1)} %get-tuple-element.18), channel_id=1, source_target_pairs={{0,4},{12,8},{1,5},{13,9},{2,6},{14,10},{3,7},{15,11},{16,20},{28,... | collective-permute-start | bytes 1572872 | tf_op jit(solution)/shard_map/ppermute | solution.py:102
  104.5 2.6 pad_maximum_fusion.5
  108.7 2.7 pad_maximum_fusion.6
  111.9 4.2 %broadcast_select_fusion.1 = (bf16[2,384,2048]{2,1,0:T(8,128)(2,1)S(1)}, bf16[2,384,2048]{2,1,0:T(8,128)(2,1)}) fusion(bf16[2,384,2048]{2,1,0:T(8,128)(2,1)} %collective-permute-done.2, pred[]{:T(512)S(6)} %eq.18, bf16[2,192,2048]{2,1,0:T(8,128)(2,1)S(1)} %get-tuple-element.16, bf16[2,192,2048]{2,1,0:T(8,128)(2,1)S(1)} %get-tuple-element.15), kind=kLoop, calls=%fused_computation.44 | loop fusion | flops 9437184 | bytes 12582913 | tf_op jit(solution)/shard_map/jit(_where)/select_n | solution.py:35
  116.1 2.7 pad_maximum_fusion
  119.6 25.2 %collective-permute-done.6 = bf16[3072,256]{1,0:T(8,128)(2,1)} collective-permute-done((bf16[3072,256]{1,0:T(8,128)(2,1)}, bf16[3072,256]{1,0:T(8,128)(2,1)}, u32[]{:S(2)}, u32[]{:S(2)}) %collective-permute-start.6) | collective-permute-done | bytes 1572896 | tf_op jit(solution)/shard_map/ppermute | solution.py:116
  144.8 5.5 %fusion.46 = bf16[768,512]{1,0:T(8,128)(2,1)S(1)} fusion(bf16[3072,256]{1,0:T(8,128)(2,1)} %collective-permute-done.6, bf16[1024,256]{1,0:T(8,128)(2,1)S(1)} %copy-done.7, bf16[1024,256]{1,0:T(8,128)(2,1)} %collective-permute-done.5, bf16[1024,256]{1,0:T(8,128)(2,1)} %collective-permute-done.4, bf16[1024,256]{1,0:T(8,128)(2,1)} %collective-permute-done.3, ...), kind=kOutput, calls=%fused_computation.59 | convolution fusion | flops 3271950336 | bytes 11272192 | tf_op jit(solution)/shard_map/dot_general | solution.py:141
  150.3 26.3 %collective-permute-done.10 = bf16[3072,256]{1,0:T(8,128)(2,1)} collective-permute-done((bf16[3072,256]{1,0:T(8,128)(2,1)}, bf16[3072,256]{1,0:T(8,128)(2,1)}, u32[]{:S(2)}, u32[]{:S(2)}) %collective-permute-start.10) | collective-permute-done | bytes 1572896 | tf_op jit(solution)/shard_map/ppermute | solution.py:116
  176.7 5.4 %fusion.52 = bf16[1,768,512]{2,1,0:T(8,128)(2,1)S(1)} fusion(bf16[3072,256]{1,0:T(8,128)(2,1)} %collective-permute-done.10, bf16[1024,256]{1,0:T(8,128)(2,1)S(1)} %copy-done.6, bf16[1024,256]{1,0:T(8,128)(2,1)} %collective-permute-done.9, bf16[1024,256]{1,0:T(8,128)(2,1)} %collective-permute-done.8, bf16[1024,256]{1,0:T(8,128)(2,1)} %collective-permute-done.7, ...), kind=kOutput, calls=%fused_computation.61 | convolution fusion | flops 3271950336 | bytes 11272192 | tf_op jit(solution)/shard_map/dot_general | solution.py:141
  185.7 2.3 pad_maximum_fusion.8
  193.3 29.5 %collective-permute-done.15 = bf16[3072,256]{1,0:T(8,128)(2,1)} collective-permute-done((bf16[3072,256]{1,0:T(8,128)(2,1)}, bf16[3072,256]{1,0:T(8,128)(2,1)}, u32[]{:S(2)}, u32[]{:S(2)}) %collective-permute-start.15) | collective-permute-done | bytes 1572896 | tf_op jit(solution)/shard_map/ppermute | solution.py:116
  222.8 7.4 %fusion.49 = bf16[768,512]{0,1:T(8,128)(2,1)S(1)} fusion(bf16[3072,256]{1,0:T(8,128)(2,1)} %collective-permute-done.15, bf16[1024,256]{1,0:T(8,128)(2,1)} %get-tuple-element.17, bf16[3072,256]{1,0:T(8,128)(2,1)} %pad_maximum_fusion.8, bf16[1024,256]{1,0:T(8,128)(2,1)} %get-tuple-element.18, bf16[768,1024]{1,0:T(8,128)(2,1)} %copy-done.3, ...), kind=kOutput, calls=%fused_computation.60 | convolution fusion | flops 3263561728 | bytes 11272192 | tf_op jit(solution)/shard_map/dot_general | solution.py:141
  230.2 7.9 %multiply_reduce_fusion = (f32[4,768]{1,0:T(4,128)S(1)}, f32[4,768,1536]{2,1,0:T(8,128)}) fusion(bf16[768,4,128]{0,2,1:T(8,128)(2,1)S(1)} %bitcast.24, bf16[1536,4,128]{2,1,0:T(4,128)(2,1)S(1)} %reshape_squeeze.7), kind=kOutput, calls=%fused_computation.1 | convolution fusion | flops 1217393664 | bytes 21245952 | tf_op jit(solution)/shard_map/qhd,khd->hqk/dot_general | solution.py:151
  238.2 9.7 %fusion = f32[4,768]{1,0:T(4,128)S(1)} fusion(f32[4,768,1536]{2,1,0:T(8,128)} %get-tuple-element.24, f32[4,768]{1,0:T(4,128)S(1)} %get-tuple-element.23), kind=kLoop, calls=%fused_computation.2 | loop fusion | flops 14152704 | bytes 18898944 | tf_op jit(solution)/shard_map/reduce_sum | solution.py:154
  247.9 8.4 %fusion.38 = bf16[768,4,128]{0,2,1:T(8,128)(2,1)S(1)} fusion(bf16[1536,4,128]{0,2,1:T(8,128)(2,1)S(1)} %bitcast.23, f32[4,768,1536]{2,1,0:T(8,128)} %get-tuple-element.24, f32[4,768]{1,0:T(4,128)S(1)} %get-tuple-element.23, f32[768,4]{0,1:T(4,128)S(1)} %bitcast.26), kind=kOutput, calls=%fused_computation.53 | convolution fusion | flops 1222901760 | bytes 21258240 | tf_op jit(solution)/shard_map/hqk,khd->qhd/dot_general | solution.py:155
  258.2 59.9 %collective-permute-done.16 = bf16[384,512]{1,0:T(8,128)(2,1)S(1)} collective-permute-done((bf16[384,512]{1,0:T(8,128)(2,1)S(1)}, bf16[384,512]{1,0:T(8,128)(2,1)S(1)}, u32[]{:S(2)}, u32[]{:S(2)}) %collective-permute-start.16) | collective-permute-done | bytes 393248 | tf_op jit(solution)/shard_map/ppermute | solution.py:162
  (53 shorter events, 32.2 us)
Async XLA Ops:
  0.0 22.0 %collective-permute-start = (bf16[192,2048]{1,0:T(8,128)(2,1)}, bf16[192,2048]{1,0:T(8,128)(2,1)S(1)}, u32[]{:S(2)}, u32[]{:S(2)}) collective-permute-start(bf16[192,2048]{1,0:T(8,128)(2,1)} %param.4), channel_id=1, source_target_pairs={{0,4},{12,8},{1,5},{13,9},{2,6},{14,10},{3,7},{15,11},{16,20},{28,... | collective-permute-start | bytes 2359304 | tf_op jit(solution)/shard_map/ppermute | solution.py:127
  24.2 35.4 %collective-permute-start.1 = (bf16[2,192,2048]{2,1,0:T(8,128)(2,1)S(1)}, bf16[2,192,2048]{2,1,0:T(8,128)(2,1)}, u32[]{:S(2)}, u32[]{:S(2)}) collective-permute-start(bf16[2,192,2048]{2,1,0:T(8,128)(2,1)S(1)} %pad_maximum_fusion.4), channel_id=1, source_target_pairs={{0,2},{2,0},{1,3},{3,1},{4,6},{6,4},{5,7},{7,5},{8,10},{10,8},{9,1... | collective-permute-start | bytes 4718600 | tf_op jit(solution)/shard_map/ppermute | solution.py:34
  63.6 48.3 %collective-permute-start.2 = (bf16[2,384,2048]{2,1,0:T(8,128)(2,1)}, bf16[2,384,2048]{2,1,0:T(8,128)(2,1)}, u32[]{:S(2)}, u32[]{:S(2)}) collective-permute-start(bf16[2,384,2048]{2,1,0:T(8,128)(2,1)} %pad_maximum_fusion.2), channel_id=1, source_target_pairs={{0,1},{1,0},{2,3},{3,2},{4,5},{5,4},{6,7},{7,6},{8,9},{9,8},{10,11... | collective-permute-start | bytes 9437192 | tf_op jit(solution)/shard_map/ppermute | solution.py:34
  65.9 16.8 %collective-permute-start.3 = (bf16[1024,256]{1,0:T(8,128)(2,1)}, bf16[1024,256]{1,0:T(8,128)(2,1)}, u32[]{:S(2)}, u32[]{:S(2)}) collective-permute-start(bf16[1024,256]{1,0:T(8,128)(2,1)} %get-tuple-element.20), channel_id=1, source_target_pairs={{0,4},{12,8},{1,5},{13,9},{2,6},{14,10},{3,7},{15,11},{16,20},{28,... | collective-permute-start | bytes 1572872 | tf_op jit(solution)/shard_map/ppermute | solution.py:102
  73.2 20.3 %collective-permute-start.7 = (bf16[1024,256]{1,0:T(8,128)(2,1)}, bf16[1024,256]{1,0:T(8,128)(2,1)}, u32[]{:S(2)}, u32[]{:S(2)}) collective-permute-start(bf16[1024,256]{1,0:T(8,128)(2,1)} %get-tuple-element.22), channel_id=1, source_target_pairs={{0,4},{12,8},{1,5},{13,9},{2,6},{14,10},{3,7},{15,11},{16,20},{28,... | collective-permute-start | bytes 1572872 | tf_op jit(solution)/shard_map/ppermute | solution.py:102
  75.3 22.0 %collective-permute-start.4 = (bf16[1024,256]{1,0:T(8,128)(2,1)}, bf16[1024,256]{1,0:T(8,128)(2,1)}, u32[]{:S(2)}, u32[]{:S(2)}) collective-permute-start(bf16[1024,256]{1,0:T(8,128)(2,1)} %get-tuple-element.20), channel_id=1, source_target_pairs={{4,8},{8,4},{5,9},{9,5},{6,10},{10,6},{7,11},{11,7},{20,24},{24,20... | collective-permute-start | bytes 1572872 | tf_op jit(solution)/shard_map/ppermute | solution.py:103
  82.7 21.8 %collective-permute-start.5 = (bf16[1024,256]{1,0:T(8,128)(2,1)}, bf16[1024,256]{1,0:T(8,128)(2,1)}, u32[]{:S(2)}, u32[]{:S(2)}) collective-permute-start(bf16[1024,256]{1,0:T(8,128)(2,1)} %collective-permute-done.3), channel_id=1, source_target_pairs={{4,8},{8,4},{5,9},{9,5},{6,10},{10,6},{7,11},{11,7},{20,24},{24,20... | collective-permute-start | bytes 1572872 | tf_op jit(solution)/shard_map/ppermute | solution.py:104
  84.1 24.5 %collective-permute-start.8 = (bf16[1024,256]{1,0:T(8,128)(2,1)}, bf16[1024,256]{1,0:T(8,128)(2,1)}, u32[]{:S(2)}, u32[]{:S(2)}) collective-permute-start(bf16[1024,256]{1,0:T(8,128)(2,1)} %get-tuple-element.22), channel_id=1, source_target_pairs={{4,8},{8,4},{5,9},{9,5},{6,10},{10,6},{7,11},{11,7},{20,24},{24,20... | collective-permute-start | bytes 1572872 | tf_op jit(solution)/shard_map/ppermute | solution.py:103
  93.5 15.1 %collective-permute-start.9 = (bf16[1024,256]{1,0:T(8,128)(2,1)}, bf16[1024,256]{1,0:T(8,128)(2,1)}, u32[]{:S(2)}, u32[]{:S(2)}) collective-permute-start(bf16[1024,256]{1,0:T(8,128)(2,1)} %collective-permute-done.7), channel_id=1, source_target_pairs={{4,8},{8,4},{5,9},{9,5},{6,10},{10,6},{7,11},{11,7},{20,24},{24,20... | collective-permute-start | bytes 1572872 | tf_op jit(solution)/shard_map/ppermute | solution.py:104
  97.3 87.5 %collective-permute-start.12 = (bf16[1024,256]{1,0:T(8,128)(2,1)}, bf16[1024,256]{1,0:T(8,128)(2,1)}, u32[]{:S(2)}, u32[]{:S(2)}) collective-permute-start(bf16[1024,256]{1,0:T(8,128)(2,1)} %get-tuple-element.18), channel_id=1, source_target_pairs={{0,4},{12,8},{1,5},{13,9},{2,6},{14,10},{3,7},{15,11},{16,20},{28,... | collective-permute-start | bytes 1572872 | tf_op jit(solution)/shard_map/ppermute | solution.py:102
  107.1 37.6 %collective-permute-start.6 = (bf16[3072,256]{1,0:T(8,128)(2,1)}, bf16[3072,256]{1,0:T(8,128)(2,1)}, u32[]{:S(2)}, u32[]{:S(2)}) collective-permute-start(bf16[3072,256]{1,0:T(8,128)(2,1)} %pad_maximum_fusion.5), channel_id=1, source_target_pairs={{0,16},{16,0},{1,17},{17,1},{2,18},{18,2},{3,19},{19,3},{4,20},{20... | collective-permute-start | bytes 4718600 | tf_op jit(solution)/shard_map/ppermute | solution.py:116
  111.4 65.2 %collective-permute-start.10 = (bf16[3072,256]{1,0:T(8,128)(2,1)}, bf16[3072,256]{1,0:T(8,128)(2,1)}, u32[]{:S(2)}, u32[]{:S(2)}) collective-permute-start(bf16[3072,256]{1,0:T(8,128)(2,1)} %pad_maximum_fusion.6), channel_id=1, source_target_pairs={{0,16},{16,0},{1,17},{17,1},{2,18},{18,2},{3,19},{19,3},{4,20},{20... | collective-permute-start | bytes 4718600 | tf_op jit(solution)/shard_map/ppermute | solution.py:116
  118.8 26.0 %copy-start.7 = (bf16[1024,256]{1,0:T(8,128)(2,1)S(1)}, bf16[1024,256]{1,0:T(8,128)(2,1)}, u32[]{:S(2)}) copy-start(bf16[1024,256]{1,0:T(8,128)(2,1)} %get-tuple-element.19) | copy-start | bytes 1572868
  119.6 57.0 %copy-start.2 = (bf16[768,1024]{1,0:T(8,128)(2,1)}, bf16[768,1024]{1,0:T(8,128)(2,1)S(1)}, u32[]{:S(2)}) copy-start(bf16[768,1024]{1,0:T(8,128)(2,1)S(1)} %get-tuple-element.7) | copy-start | bytes 4718596
  119.6 57.0 %copy-start.3 = (bf16[768,1024]{1,0:T(8,128)(2,1)}, bf16[768,1024]{1,0:T(8,128)(2,1)S(1)}, u32[]{:S(2)}) copy-start(bf16[768,1024]{1,0:T(8,128)(2,1)S(1)} %get-tuple-element.8) | copy-start | bytes 4718596
  119.6 57.0 %copy-start.4 = (bf16[768,1024]{1,0:T(8,128)(2,1)}, bf16[768,1024]{1,0:T(8,128)(2,1)S(1)}, u32[]{:S(2)}) copy-start(bf16[768,1024]{1,0:T(8,128)(2,1)S(1)} %get-tuple-element.9) | copy-start | bytes 4718596
  119.6 57.0 %copy-start.5 = (bf16[768,1024]{1,0:T(8,128)(2,1)}, bf16[768,1024]{1,0:T(8,128)(2,1)S(1)}, u32[]{:S(2)}) copy-start(bf16[768,1024]{1,0:T(8,128)(2,1)S(1)} %get-tuple-element.10) | copy-start | bytes 4718596
  144.8 31.9 %copy-start.6 = (bf16[1024,256]{1,0:T(8,128)(2,1)S(1)}, bf16[1024,256]{1,0:T(8,128)(2,1)}, u32[]{:S(2)}) copy-start(bf16[1024,256]{1,0:T(8,128)(2,1)} %get-tuple-element.21) | copy-start | bytes 1572868
  182.3 7.2 %collective-permute-start.11 = (bf16[2,768,512]{2,1,0:T(8,128)(2,1)S(1)}, bf16[2,768,512]{2,1,0:T(8,128)(2,1)}, u32[]{:S(2)}, u32[]{:S(2)}) collective-permute-start(bf16[2,768,512]{2,1,0:T(8,128)(2,1)S(1)} %pad_maximum_fusion.7), channel_id=1, source_target_pairs={{4,8},{8,4},{5,9},{9,5},{6,10},{10,6},{7,11},{11,7},{20,24},{24,20... | collective-permute-start | bytes 4718600 | tf_op jit(solution)/shard_map/ppermute | solution.py:147
  184.1 1.6 collective-permute-start.13
  184.8 0.9 collective-permute-start.14
  188.0 34.9 %collective-permute-start.15 = (bf16[3072,256]{1,0:T(8,128)(2,1)}, bf16[3072,256]{1,0:T(8,128)(2,1)}, u32[]{:S(2)}, u32[]{:S(2)}) collective-permute-start(bf16[3072,256]{1,0:T(8,128)(2,1)} %pad_maximum_fusion.8), channel_id=1, source_target_pairs={{0,16},{16,0},{1,17},{17,1},{2,18},{18,2},{3,19},{19,3},{4,20},{20... | collective-permute-start | bytes 4718600 | tf_op jit(solution)/shard_map/ppermute | solution.py:116
  238.2 9.7 %copy-start.1 = (bf16[1,1536,512]{1,2,0:T(8,128)(2,1)S(1)}, bf16[1,1536,512]{1,2,0:T(8,128)(2,1)}, u32[]{:S(2)}) copy-start(bf16[1,1536,512]{1,2,0:T(8,128)(2,1)} %copy.11) | copy-start | bytes 4718596
  256.9 61.2 %collective-permute-start.16 = (bf16[384,512]{1,0:T(8,128)(2,1)S(1)}, bf16[384,512]{1,0:T(8,128)(2,1)S(1)}, u32[]{:S(2)}, u32[]{:S(2)}) collective-permute-start(bf16[384,512]{1,0:T(8,128)(2,1)S(1)} %slice.19), channel_id=1, source_target_pairs={{4,0},{8,12},{5,1},{9,13},{6,2},{10,14},{7,3},{11,15},{20,16},{24,... | collective-permute-start | bytes 1179656 | tf_op jit(solution)/shard_map/ppermute | solution.py:162
  (1 other events, 0.9 us)

commit v7 on v4

--- a/solution.py
+++ b/solution.py
@@ -44,11 +44,17 @@
     group = lax.axis_index("groups")
     own = lax.dynamic_slice_in_dim(weight, group * half, half, axis=1)
     kept = lax.dynamic_slice_in_dim(weight, (1 - group) * half, half, axis=1)
-    own = lax.all_gather(own, "seq", axis=0, tiled=True)
-    own = jnp.roll(own, -lax.axis_index("seq") * rows, axis=0)
-    if after is not None:
-        own = lax.optimization_barrier((own, after))[0]
-    other = lax.ppermute(own[rows:], "groups", [(0, 1), (1, 0)])
+    if after is None:
+        own = lax.all_gather(own, "seq", axis=0, tiled=True)
+        own = jnp.roll(own, -lax.axis_index("seq") * rows, axis=0)
+        other = lax.ppermute(own[rows:], "groups", [(0, 1), (1, 0)])
+    else:
+        own = line_gather(own) if lax.axis_size("seq") == SPAN else jnp.roll(
+            lax.all_gather(own, "seq", axis=0, tiled=True), -lax.axis_index("seq") * rows, axis=0
+        )
+        foreign = lax.optimization_barrier((own[rows:], after))[0]
+        both = lax.all_gather(foreign, "groups", axis=0, tiled=False)
+        other = both[1 - group]
     return jnp.concatenate([own, jnp.concatenate([kept, other], axis=0)], axis=1)
 
 

time: 230 us -> 275 us (1.20)
  starting transfers between devices: 30.9 us -> 69.7 us
  waiting for transfers between devices: 129 us -> 140 us
    ppermute x6 -> x9, waiting for transfers between devices: 21 us -> 102 us  [line_gather(): lax.ppermute(from_right[-1], 'seq', [(j, j - 1) for j in range(1, n - k +...]
    all_gather x3 -> x2, waiting for transfers between devices: 64.7 us -> 1.64 us  [full_columns(): own = lax.all_gather(own, 'seq', axis=0, tiled=True)]
    ppermute x6 -> x9, starting transfers between devices: 15.5 us -> 51.8 us  [line_gather(): lax.ppermute(from_left[-1], 'seq', [(j, j + 1) for j in range(k - 1, n -...]
    ppermute x2, waiting for transfers between devices: 17.5 us -> 0.01 us  [swap_gather(): other = lax.ppermute(piece, axis, [(0, 1), (1, 0)])]
    ppermute x3 -> x2, waiting for transfers between devices: 26 us -> 36.7 us  [full_columns(): other = lax.ppermute(own[rows:], 'groups', [(0, 1), (1, 0)])]
    ppermute x6 -> x9, starting transfers between devices: 7.71 us -> 11.6 us  [line_gather(): lax.ppermute(from_right[-1], 'seq', [(j, j - 1) for j in range(1, n - k +...]
    concatenate x3 -> x2, other arithmetic: 9.01 us -> 6.01 us  [full_columns(): own = jnp.roll(own, -lax.axis_index('seq') * rows, axis=0)]
  transfers between devices with their start and end apart: 20 -> 25, of which waited for: 9 -> 11; matrix products, arithmetic and copies ran while one was open for 17% -> 12% of each run, Pallas kernels for 0% -> 0%
where the time goes in v7:
time: 275 us; the launch traced here: 274 us
  waiting for transfers between devices  140 us (51%)
  starting transfers between devices  69.7 us (25%)
  other arithmetic  21.5 us (8%)
  matrix products  14.9 us (5%)
  between operations  13.7 us (5%)
  local copies, waits for them, and re-layouts  13.6 us (5%)
    ppermute x9, waiting for transfers between devices, line_gather(): lax.ppermute(from_right[-1], 'seq', [(j, j - 1) for j in range(1, n - k +...  102 us
    ppermute x9, starting transfers between devices, line_gather(): lax.ppermute(from_left[-1], 'seq', [(j, j + 1) for j in range(k - 1, n -...  51.8 us
    ppermute x2, waiting for transfers between devices, full_columns(): other = lax.ppermute(own[rows:], 'groups', [(0, 1), (1, 0)])  36.7 us
    ppermute x9, starting transfers between devices, line_gather(): lax.ppermute(from_right[-1], 'seq', [(j, j - 1) for j in range(1, n - k +...  11.6 us
    dot_general x3, matrix products, project(): jnp.dot(block, piece, preferred_element_type=jnp.float32)  11 us
    concatenate x2, other arithmetic, full_columns(): own = jnp.roll(own, -lax.axis_index('seq') * rows, axis=0)  6.01 us
  transfers between devices with their start and end apart: 25, of which 11 were waited for; matrix products, arithmetic and copies ran while one was open for 12% of the time, Pallas kernels for 0%

profile of v7, /device:TPU:0, one launch (start us, length us, event | category | flops | bytes accessed | tf_op | source)
XLA Modules:
  0.0 273.8 jit_solution(13690422452646455830)
XLA Ops:
  6.5 2.4 constant_dynamic-slice_fusion
  9.1 3.0 %collective-permute-start = (bf16[192,2048]{1,0:T(8,128)(2,1)}, bf16[192,2048]{1,0:T(8,128)(2,1)}, u32[]{:S(2)}, u32[]{:S(2)}) collective-permute-start(bf16[192,2048]{1,0:T(8,128)(2,1)} %param.6), channel_id=1, source_target_pairs={{0,2},{2,0},{1,3},{3,1},{4,6},{6,4},{5,7},{7,5},{8,10},{10,8},{9,1... | collective-permute-start | bytes 2359304 | tf_op jit(solution)/shard_map/ppermute | solution.py:34
  15.4 5.4 %collective-permute-start.10 = (bf16[1024,256]{1,0:T(8,128)(2,1)S(1)}, bf16[1024,256]{1,0:T(8,128)(2,1)}, u32[]{:S(2)}, u32[]{:S(2)}) collective-permute-start(bf16[1024,256]{1,0:T(8,128)(2,1)S(1)} %get-tuple-element.13), channel_id=1, source_target_pairs={{0,4},{4,8},{8,12},{1,5},{5,9},{9,13},{2,6},{6,10},{10,14},{3,7},{... | collective-permute-start | bytes 1572872 | tf_op jit(solution)/shard_map/ppermute | solution.py:23
  20.8 25.4 %collective-permute-done.9 = bf16[1024,256]{1,0:T(8,128)(2,1)S(1)} collective-permute-done((bf16[1024,256]{1,0:T(8,128)(2,1)S(1)}, bf16[1024,256]{1,0:T(8,128)(2,1)S(1)}, u32[]{:S(2)}, u32[]{:S(2)}) %collective-permute-start.9) | collective-permute-done | bytes 524320 | tf_op jit(solution)/shard_map/ppermute | solution.py:22
  49.4 24.9 %collective-permute-done.13 = bf16[1024,256]{1,0:T(8,128)(2,1)S(1)} collective-permute-done((bf16[1024,256]{1,0:T(8,128)(2,1)S(1)}, bf16[1024,256]{1,0:T(8,128)(2,1)S(1)}, u32[]{:S(2)}, u32[]{:S(2)}) %collective-permute-start.13) | collective-permute-done | bytes 524320 | tf_op jit(solution)/shard_map/ppermute | solution.py:22
  76.7 34.3 %collective-permute-done.14 = bf16[1024,256]{1,0:T(8,128)(2,1)S(1)} collective-permute-done((bf16[1024,256]{1,0:T(8,128)(2,1)S(1)}, bf16[1024,256]{1,0:T(8,128)(2,1)S(1)}, u32[]{:S(2)}, u32[]{:S(2)}) %collective-permute-start.14) | collective-permute-done | bytes 524320 | tf_op jit(solution)/shard_map/ppermute | solution.py:22
  113.9 3.0 %fusion.33 = bf16[4096,256]{1,0:T(8,128)(2,1)S(1)} fusion(s32[]{:T(128)S(6)} %select_n.126, bf16[4096,256]{1,0:T(8,128)(2,1)} %all-gather.7.cloned.1.call-done), kind=kLoop, calls=%fused_computation.42 | loop fusion | flops 4194304 | bytes 4194308 | tf_op jit(solution)/shard_map/jit(_roll_dynamic)/concatenate | solution.py:49
  122.6 3.0 %fusion.34 = bf16[4096,256]{1,0:T(8,128)(2,1)S(1)} fusion(s32[]{:T(128)S(6)} %select_n.126, bf16[4096,256]{1,0:T(8,128)(2,1)} %all-gather.5.cloned.1.call-done), kind=kLoop, calls=%fused_computation.43 | loop fusion | flops 4194304 | bytes 4194308 | tf_op jit(solution)/shard_map/jit(_roll_dynamic)/concatenate | solution.py:49
  128.6 2.2 broadcast_select_fusion
  130.8 2.9 %fusion.32 = bf16[384,4096]{1,0:T(8,128)(2,1)S(1)} fusion(s32[]{:T(128)S(6)} %select_n.126, bf16[384,2048]{1,0:T(8,128)(2,1)S(1)} %get-tuple-element.9, bf16[384,2048]{1,0:T(8,128)(2,1)S(1)} %get-tuple-element.8), kind=kLoop, calls=%fused_computation.41 | loop fusion | flops 12582912 | bytes 6291460 | tf_op jit(solution)/shard_map/jit(_roll_dynamic)/concatenate | solution.py:69
  133.8 16.5 %collective-permute-done.15 = bf16[3072,256]{1,0:T(8,128)(2,1)} collective-permute-done((bf16[3072,256]{1,0:T(8,128)(2,1)}, bf16[3072,256]{1,0:T(8,128)(2,1)}, u32[]{:S(2)}, u32[]{:S(2)}) %collective-permute-start.15) | collective-permute-done | bytes 1572896 | tf_op jit(solution)/shard_map/ppermute | solution.py:50
  150.3 3.3 %fusion.41 = bf16[384,512]{1,0:T(8,128)(2,1)S(1)} fusion(bf16[384,4096]{1,0:T(8,128)(2,1)S(1)} %fusion.32, bf16[3072,256]{1,0:T(8,128)(2,1)} %collective-permute-done.15, bf16[1024,256]{1,0:T(8,128)(2,1)S(1)} %copy-done.22, bf16[4096,256]{1,0:T(8,128)(2,1)S(1)} %copy-done.3), kind=kOutput, calls=%fused_computation.55 | convolution fusion | flops 1623392256 | bytes 7733248 | tf_op jit(solution)/shard_map/dot_general | solution.py:73
  153.7 20.2 %collective-permute-done.2 = bf16[3072,256]{1,0:T(8,128)(2,1)} collective-permute-done((bf16[3072,256]{1,0:T(8,128)(2,1)}, bf16[3072,256]{1,0:T(8,128)(2,1)}, u32[]{:S(2)}, u32[]{:S(2)}) %collective-permute-start.2) | collective-permute-done | bytes 1572896 | tf_op jit(solution)/shard_map/ppermute | solution.py:50
  173.9 4.7 %fusion.44 = bf16[384,512]{1,0:T(8,128)(2,1)S(1)} fusion(bf16[384,4096]{1,0:T(8,128)(2,1)} %copy-done.4, bf16[3072,256]{1,0:T(8,128)(2,1)} %collective-permute-done.2, bf16[1024,256]{1,0:T(8,128)(2,1)S(1)} %copy-done.23, bf16[4096,256]{1,0:T(8,128)(2,1)S(1)} %copy-done.1), kind=kOutput, calls=%fused_computation.56 | convolution fusion | flops 1623392256 | bytes 7733248 | tf_op jit(solution)/shard_map/dot_general | solution.py:73
  179.9 4.6 %collective-permute-start.4 = (bf16[384,512]{1,0:T(8,128)(2,1)S(1)}, bf16[384,512]{1,0:T(8,128)(2,1)S(1)}, u32[]{:S(2)}, u32[]{:S(2)}) collective-permute-start(bf16[384,512]{1,0:T(8,128)(2,1)S(1)} %fusion.44), channel_id=1, source_target_pairs={{0,4},{4,8},{8,12},{1,5},{5,9},{9,13},{2,6},{6,10},{10,14},{3,7},{... | collective-permute-start | bytes 1179656 | tf_op jit(solution)/shard_map/ppermute | solution.py:23
  185.8 36.3 %collective-permute-start.17 = (bf16[384,512]{1,0:T(8,128)(2,1)S(1)}, bf16[384,512]{1,0:T(8,128)(2,1)S(1)}, u32[]{:S(2)}, u32[]{:S(2)}) collective-permute-start(bf16[384,512]{1,0:T(8,128)(2,1)S(1)} %fusion.41), channel_id=1, source_target_pairs={{0,4},{4,8},{8,12},{1,5},{5,9},{9,13},{2,6},{6,10},{10,14},{3,7},{... | collective-permute-start | bytes 1179656 | tf_op jit(solution)/shard_map/ppermute | solution.py:23
  224.1 6.0 %collective-permute-done.16 = bf16[384,512]{1,0:T(8,128)(2,1)S(1)} collective-permute-done((bf16[384,512]{1,0:T(8,128)(2,1)S(1)}, bf16[384,512]{1,0:T(8,128)(2,1)S(1)}, u32[]{:S(2)}, u32[]{:S(2)}) %collective-permute-start.16) | collective-permute-done | bytes 393248 | tf_op jit(solution)/shard_map/ppermute | solution.py:22
  236.4 4.6 %collective-permute-done.20 = bf16[384,512]{1,0:T(8,128)(2,1)} collective-permute-done((bf16[384,512]{1,0:T(8,128)(2,1)S(1)}, bf16[384,512]{1,0:T(8,128)(2,1)}, u32[]{:S(2)}, u32[]{:S(2)}) %collective-permute-start.20) | collective-permute-done | bytes 393248 | tf_op jit(solution)/shard_map/ppermute | solution.py:22
  244.9 2.8 %collective-permute-done.8 = bf16[384,512]{1,0:T(8,128)(2,1)S(1)} collective-permute-done((bf16[384,512]{1,0:T(8,128)(2,1)S(1)}, bf16[384,512]{1,0:T(8,128)(2,1)S(1)}, u32[]{:S(2)}, u32[]{:S(2)}) %collective-permute-start.8) | collective-permute-done | bytes 393248 | tf_op jit(solution)/shard_map/ppermute | solution.py:22
  249.6 2.5 collective-permute-done.21
  252.0 1.8 broadcast_select_fusion.7
  253.8 1.8 broadcast_select_fusion.11
  257.6 2.9 %fusion.50 = bf16[48,4,8,128]{3,2,1,0:T(8,128)(2,1)S(1)} fusion(bf16[384,4096]{1,0:T(8,128)(2,1)S(1)} %copy-done.5, bf16[3072,256]{1,0:T(8,128)(2,1)S(1)} %dynamic-slice_bitcast_fusion, bf16[1024,256]{1,0:T(8,128)(2,1)S(1)} %copy-done.20, bf16[1024,256]{1,0:T(8,128)(2,1)S(1)} %copy-done.9, bf16[1024,256]{1,0:T(8,128)(2,1)S(1)} %copy-done.7, ...), kind=kOutput, calls=%fused_computation.58 | convolution fusion | flops 1635975168 | bytes 7733248 | tf_op jit(solution)/shard_map/dot_general | solution.py:73
  264.0 2.1 fusion.56
  (117 shorter events, 43.4 us)
Async XLA Ops:
  6.5 107.3 %all-gather.7.cloned.1.call-start = ((), (), s32[]{:S(2)}) async-start(), calls=%async_computation.1 | async-start | bytes 2621440 | tf_op jit(solution)/shard_map/all_gather | solution.py:48
  9.0 113.6 %all-gather.5.cloned.1.call-start = ((), (), s32[]{:S(2)}) async-start(), calls=%async_computation | async-start | bytes 2621440 | tf_op jit(solution)/shard_map/all_gather | solution.py:48
  9.1 39.1 %collective-permute-start = (bf16[192,2048]{1,0:T(8,128)(2,1)}, bf16[192,2048]{1,0:T(8,128)(2,1)}, u32[]{:S(2)}, u32[]{:S(2)}) collective-permute-start(bf16[192,2048]{1,0:T(8,128)(2,1)} %param.6), channel_id=1, source_target_pairs={{0,2},{2,0},{1,3},{3,1},{4,6},{6,4},{5,7},{7,5},{8,10},{10,8},{9,1... | collective-permute-start | bytes 2359304 | tf_op jit(solution)/shard_map/ppermute | solution.py:34
  13.2 242.4 %all-gather.9.cloned.1.call-start = ((), (), s32[]{:S(2)}) async-start(), calls=%async_computation.2 | async-start | bytes 4718592 | tf_op jit(solution)/shard_map/all_gather | solution.py:56
  14.1 32.0 %collective-permute-start.9 = (bf16[1024,256]{1,0:T(8,128)(2,1)S(1)}, bf16[1024,256]{1,0:T(8,128)(2,1)S(1)}, u32[]{:S(2)}, u32[]{:S(2)}) collective-permute-start(bf16[1024,256]{1,0:T(8,128)(2,1)S(1)} %get-tuple-element.13), channel_id=1, source_target_pairs={{4,0},{8,4},{12,8},{5,1},{9,5},{13,9},{6,2},{10,6},{14,10},{7,3},{... | collective-permute-start | bytes 1572872 | tf_op jit(solution)/shard_map/ppermute | solution.py:22
  15.4 32.0 %collective-permute-start.10 = (bf16[1024,256]{1,0:T(8,128)(2,1)S(1)}, bf16[1024,256]{1,0:T(8,128)(2,1)}, u32[]{:S(2)}, u32[]{:S(2)}) collective-permute-start(bf16[1024,256]{1,0:T(8,128)(2,1)S(1)} %get-tuple-element.13), channel_id=1, source_target_pairs={{0,4},{4,8},{8,12},{1,5},{5,9},{9,13},{2,6},{6,10},{10,14},{3,7},{... | collective-permute-start | bytes 1572872 | tf_op jit(solution)/shard_map/ppermute | solution.py:23
  46.2 28.2 %collective-permute-start.13 = (bf16[1024,256]{1,0:T(8,128)(2,1)S(1)}, bf16[1024,256]{1,0:T(8,128)(2,1)S(1)}, u32[]{:S(2)}, u32[]{:S(2)}) collective-permute-start(bf16[1024,256]{1,0:T(8,128)(2,1)S(1)} %collective-permute-done.9), channel_id=1, source_target_pairs={{4,0},{8,4},{5,1},{9,5},{6,2},{10,6},{7,3},{11,7},{20,16},{24,20},... | collective-permute-start | bytes 1572872 | tf_op jit(solution)/shard_map/ppermute | solution.py:22
  47.5 28.4 %collective-permute-start.11 = (bf16[1024,256]{1,0:T(8,128)(2,1)}, bf16[1024,256]{1,0:T(8,128)(2,1)S(1)}, u32[]{:S(2)}, u32[]{:S(2)}) collective-permute-start(bf16[1024,256]{1,0:T(8,128)(2,1)} %collective-permute-done.10), channel_id=1, source_target_pairs={{4,8},{8,12},{5,9},{9,13},{6,10},{10,14},{7,11},{11,15},{20,24},{2... | collective-permute-start | bytes 1572872 | tf_op jit(solution)/shard_map/ppermute | solution.py:23
  74.3 36.6 %collective-permute-start.14 = (bf16[1024,256]{1,0:T(8,128)(2,1)S(1)}, bf16[1024,256]{1,0:T(8,128)(2,1)S(1)}, u32[]{:S(2)}, u32[]{:S(2)}) collective-permute-start(bf16[1024,256]{1,0:T(8,128)(2,1)S(1)} %collective-permute-done.13), channel_id=1, source_target_pairs={{4,0},{5,1},{6,2},{7,3},{20,16},{21,17},{22,18},{23,19}} | collective-permute-start | bytes 1572872 | tf_op jit(solution)/shard_map/ppermute | solution.py:22
  75.8 52.8 %collective-permute-start.1 = (bf16[384,2048]{1,0:T(8,128)(2,1)S(1)}, bf16[384,2048]{1,0:T(8,128)(2,1)}, u32[]{:S(2)}, u32[]{:S(2)}) collective-permute-start(bf16[384,2048]{1,0:T(8,128)(2,1)S(1)} %pad_maximum_fusion), channel_id=1, source_target_pairs={{0,1},{1,0},{2,3},{3,2},{4,5},{5,4},{6,7},{7,6},{8,9},{9,8},{10,11... | collective-permute-start | bytes 4718600 | tf_op jit(solution)/shard_map/ppermute | solution.py:34
  75.9 35.1 %collective-permute-start.12 = (bf16[1024,256]{1,0:T(8,128)(2,1)S(1)}, bf16[1024,256]{1,0:T(8,128)(2,1)S(1)}, u32[]{:S(2)}, u32[]{:S(2)}) collective-permute-start(bf16[1024,256]{1,0:T(8,128)(2,1)S(1)} %collective-permute-done.11), channel_id=1, source_target_pairs={{8,12},{9,13},{10,14},{11,15},{24,28},{25,29},{26,30},{27,31}} | collective-permute-start | bytes 1572872 | tf_op jit(solution)/shard_map/ppermute | solution.py:23
  119.4 30.9 %collective-permute-start.15 = (bf16[3072,256]{1,0:T(8,128)(2,1)}, bf16[3072,256]{1,0:T(8,128)(2,1)}, u32[]{:S(2)}, u32[]{:S(2)}) collective-permute-start(bf16[3072,256]{1,0:T(8,128)(2,1)} %slice.11), channel_id=1, source_target_pairs={{0,16},{16,0},{1,17},{17,1},{2,18},{18,2},{3,19},{19,3},{4,20},{20... | collective-permute-start | bytes 4718600 | tf_op jit(solution)/shard_map/ppermute | solution.py:50
  127.0 46.9 %collective-permute-start.2 = (bf16[3072,256]{1,0:T(8,128)(2,1)}, bf16[3072,256]{1,0:T(8,128)(2,1)}, u32[]{:S(2)}, u32[]{:S(2)}) collective-permute-start(bf16[3072,256]{1,0:T(8,128)(2,1)} %slice.10), channel_id=1, source_target_pairs={{0,16},{16,0},{1,17},{17,1},{2,18},{18,2},{3,19},{19,3},{4,20},{20... | collective-permute-start | bytes 4718600 | tf_op jit(solution)/shard_map/ppermute | solution.py:50
  178.6 43.5 %collective-permute-start.3 = (bf16[384,512]{1,0:T(8,128)(2,1)S(1)}, bf16[384,512]{1,0:T(8,128)(2,1)S(1)}, u32[]{:S(2)}, u32[]{:S(2)}) collective-permute-start(bf16[384,512]{1,0:T(8,128)(2,1)S(1)} %fusion.44), channel_id=1, source_target_pairs={{4,0},{8,4},{12,8},{5,1},{9,5},{13,9},{6,2},{10,6},{14,10},{7,3},{... | collective-permute-start | bytes 1179656 | tf_op jit(solution)/shard_map/ppermute | solution.py:22
  179.9 43.5 %collective-permute-start.4 = (bf16[384,512]{1,0:T(8,128)(2,1)S(1)}, bf16[384,512]{1,0:T(8,128)(2,1)S(1)}, u32[]{:S(2)}, u32[]{:S(2)}) collective-permute-start(bf16[384,512]{1,0:T(8,128)(2,1)S(1)} %fusion.44), channel_id=1, source_target_pairs={{0,4},{4,8},{8,12},{1,5},{5,9},{9,13},{2,6},{6,10},{10,14},{3,7},{... | collective-permute-start | bytes 1179656 | tf_op jit(solution)/shard_map/ppermute | solution.py:23
  184.5 45.7 %collective-permute-start.16 = (bf16[384,512]{1,0:T(8,128)(2,1)S(1)}, bf16[384,512]{1,0:T(8,128)(2,1)S(1)}, u32[]{:S(2)}, u32[]{:S(2)}) collective-permute-start(bf16[384,512]{1,0:T(8,128)(2,1)S(1)} %fusion.41), channel_id=1, source_target_pairs={{4,0},{8,4},{12,8},{5,1},{9,5},{13,9},{6,2},{10,6},{14,10},{7,3},{... | collective-permute-start | bytes 1179656 | tf_op jit(solution)/shard_map/ppermute | solution.py:22
  185.8 45.7 %collective-permute-start.17 = (bf16[384,512]{1,0:T(8,128)(2,1)S(1)}, bf16[384,512]{1,0:T(8,128)(2,1)S(1)}, u32[]{:S(2)}, u32[]{:S(2)}) collective-permute-start(bf16[384,512]{1,0:T(8,128)(2,1)S(1)} %fusion.41), channel_id=1, source_target_pairs={{0,4},{4,8},{8,12},{1,5},{5,9},{9,13},{2,6},{6,10},{10,14},{3,7},{... | collective-permute-start | bytes 1179656 | tf_op jit(solution)/shard_map/ppermute | solution.py:23
  222.1 12.3 %collective-permute-start.7 = (bf16[384,512]{1,0:T(8,128)(2,1)S(1)}, bf16[384,512]{1,0:T(8,128)(2,1)S(1)}, u32[]{:S(2)}, u32[]{:S(2)}) collective-permute-start(bf16[384,512]{1,0:T(8,128)(2,1)S(1)} %collective-permute-done.3), channel_id=1, source_target_pairs={{4,0},{8,4},{5,1},{9,5},{6,2},{10,6},{7,3},{11,7},{20,16},{24,20},... | collective-permute-start | bytes 1179656 | tf_op jit(solution)/shard_map/ppermute | solution.py:22
  223.5 12.3 %collective-permute-start.5 = (bf16[384,512]{1,0:T(8,128)(2,1)S(1)}, bf16[384,512]{1,0:T(8,128)(2,1)S(1)}, u32[]{:S(2)}, u32[]{:S(2)}) collective-permute-start(bf16[384,512]{1,0:T(8,128)(2,1)S(1)} %collective-permute-done.4), channel_id=1, source_target_pairs={{4,8},{8,12},{5,9},{9,13},{6,10},{10,14},{7,11},{11,15},{20,24},{2... | collective-permute-start | bytes 1179656 | tf_op jit(solution)/shard_map/ppermute | solution.py:23
  230.2 10.9 %collective-permute-start.20 = (bf16[384,512]{1,0:T(8,128)(2,1)S(1)}, bf16[384,512]{1,0:T(8,128)(2,1)}, u32[]{:S(2)}, u32[]{:S(2)}) collective-permute-start(bf16[384,512]{1,0:T(8,128)(2,1)S(1)} %collective-permute-done.16), channel_id=1, source_target_pairs={{4,0},{8,4},{5,1},{9,5},{6,2},{10,6},{7,3},{11,7},{20,16},{24,20},... | collective-permute-start | bytes 1179656 | tf_op jit(solution)/shard_map/ppermute | solution.py:22
  234.4 13.3 %collective-permute-start.8 = (bf16[384,512]{1,0:T(8,128)(2,1)S(1)}, bf16[384,512]{1,0:T(8,128)(2,1)S(1)}, u32[]{:S(2)}, u32[]{:S(2)}) collective-permute-start(bf16[384,512]{1,0:T(8,128)(2,1)S(1)} %collective-permute-done.7), channel_id=1, source_target_pairs={{4,0},{5,1},{6,2},{7,3},{20,16},{21,17},{22,18},{23,19}} | collective-permute-start | bytes 1179656 | tf_op jit(solution)/shard_map/ppermute | solution.py:22
  235.7 12.0 %collective-permute-start.6 = (bf16[384,512]{1,0:T(8,128)(2,1)S(1)}, bf16[384,512]{1,0:T(8,128)(2,1)S(1)}, u32[]{:S(2)}, u32[]{:S(2)}) collective-permute-start(bf16[384,512]{1,0:T(8,128)(2,1)S(1)} %collective-permute-done.5), channel_id=1, source_target_pairs={{8,12},{9,13},{10,14},{11,15},{24,28},{25,29},{26,30},{27,31}} | collective-permute-start | bytes 1179656 | tf_op jit(solution)/shard_map/ppermute | solution.py:23
  241.1 10.9 %collective-permute-start.21 = (bf16[384,512]{1,0:T(8,128)(2,1)}, bf16[384,512]{1,0:T(8,128)(2,1)}, u32[]{:S(2)}, u32[]{:S(2)}) collective-permute-start(bf16[384,512]{1,0:T(8,128)(2,1)} %collective-permute-done.20), channel_id=1, source_target_pairs={{4,0},{5,1},{6,2},{7,3},{20,16},{21,17},{22,18},{23,19}} | collective-permute-start | bytes 1179656 | tf_op jit(solution)/shard_map/ppermute | solution.py:22
  242.4 11.4 %collective-permute-start.19 = (bf16[384,512]{1,0:T(8,128)(2,1)}, bf16[384,512]{1,0:T(8,128)(2,1)}, u32[]{:S(2)}, u32[]{:S(2)}) collective-permute-start(bf16[384,512]{1,0:T(8,128)(2,1)} %collective-permute-done.18), channel_id=1, source_target_pairs={{8,12},{9,13},{10,14},{11,15},{24,28},{25,29},{26,30},{27,31}} | collective-permute-start | bytes 1179656 | tf_op jit(solution)/shard_map/ppermute | solution.py:23
  (29 other events, 393.9 us)
Sparse Core Ops, SparseCore 0:
  9.1 63.5 all-gather.6
  74.3 48.2 all-gather.4
  153.8 59.3 all-gather.8

commit v8 on v4

--- a/solution.py
+++ b/solution.py
@@ -39,7 +39,7 @@
 
 def full_columns(weight, shared, after=None):
     if not shared:
-        return lax.all_gather(weight, "seq", axis=0, tiled=True)
+        return [lax.all_gather(weight, "seq", axis=0, tiled=True)]
     rows, half = weight.shape[0], weight.shape[1] // 2
     group = lax.axis_index("groups")
     own = lax.dynamic_slice_in_dim(weight, group * half, half, axis=1)
@@ -49,7 +49,7 @@
     if after is not None:
         own = lax.optimization_barrier((own, after))[0]
     other = lax.ppermute(own[rows:], "groups", [(0, 1), (1, 0)])
-    return jnp.concatenate([own, jnp.concatenate([kept, other], axis=0)], axis=1)
+    return [own, jnp.concatenate([kept, other], axis=0)]
 
 
 def per_device(acts, w_query, w_key, w_value):
@@ -63,16 +63,16 @@
         block = jnp.roll(block, -lax.axis_index("seq") * w_query.shape[0], axis=1)
 
     def project(weight, after=None):
-        piece = full_columns(weight, shared, after)
-        return jnp.dot(block, piece, preferred_element_type=jnp.float32).astype(jnp.bfloat16)
+        return [
+            jnp.dot(block, piece, preferred_element_type=jnp.float32).astype(jnp.bfloat16)
+            for piece in full_columns(weight, shared, after)
+        ]
 
-    key = project(w_key)
-    value = project(w_value)
-    query = project(w_query, key).reshape(tokens_here, heads_here, HD)
+    key = jnp.concatenate(project(w_key), axis=1)
+    value = jnp.concatenate(project(w_value), axis=1)
+    queries = project(w_query, key)
     if lax.axis_size("seq") == SPAN:
-        seen = jnp.stack(
-            [line_gather(key), line_gather(value)]
-        )
+        seen = jnp.stack([line_gather(key), line_gather(value)])
     else:
         packed = jnp.stack([key, value])
         blocks_seen = [packed]
@@ -84,15 +84,24 @@
     seen_keys = seen[0].reshape(-1, heads_here, HD)
     seen_values = seen[1].reshape(-1, heads_here, HD)
     scale = 1.0 / jnp.sqrt(jnp.float32(HD))
-    scores = jnp.einsum("qhd,khd->hqk", query, seen_keys, preferred_element_type=jnp.float32) * scale
-    largest = scores.max(axis=-1, keepdims=True)
-    expos = jnp.exp(scores - largest)
-    running_total = jnp.sum(expos, axis=-1)
-    summed = jnp.einsum(
-        "hqk,khd->qhd", expos.astype(jnp.bfloat16), seen_values, preferred_element_type=jnp.float32
-    )
-    attended = summed / jnp.transpose(running_total)[:, :, None]
-    attended = attended.astype(jnp.bfloat16).reshape(tokens_here, width)
+    outputs = []
+    first = 0
+    for query in queries:
+        count = query.shape[1] // HD
+        query = query.reshape(tokens_here, count, HD)
+        part_keys = seen_keys[:, first : first + count]
+        part_values = seen_values[:, first : first + count]
+        first += count
+        scores = jnp.einsum("qhd,khd->hqk", query, part_keys, preferred_element_type=jnp.float32) * scale
+        largest = scores.max(axis=-1, keepdims=True)
+        expos = jnp.exp(scores - largest)
+        running_total = jnp.sum(expos, axis=-1)
+        summed = jnp.einsum(
+            "hqk,khd->qhd", expos.astype(jnp.bfloat16), part_values, preferred_element_type=jnp.float32
+        )
+        attended = summed / jnp.transpose(running_total)[:, :, None]
+        outputs.append(attended.astype(jnp.bfloat16).reshape(tokens_here, count * HD))
+    attended = jnp.concatenate(outputs, axis=1)
     if shared:
         attended = jnp.roll(attended, lax.axis_index("groups") * (width // 2), axis=1)
     return attended

time: 230 us -> 227 us (0.987)
  local copies, waits for them, and re-layouts: 11.4 us -> 7.56 us
    ppermute x6, waiting for transfers between devices: 21 us -> 28.1 us  [line_gather(): lax.ppermute(from_right[-1], 'seq', [(j, j - 1) for j in range(1, n - k +...]
    all_gather x3, waiting for transfers between devices: 64.7 us -> 60.7 us  [full_columns(): own = lax.all_gather(own, 'seq', axis=0, tiled=True)]
    ppermute x3, waiting for transfers between devices: 26 us -> 22.4 us  [full_columns(): other = lax.ppermute(own[rows:], 'groups', [(0, 1), (1, 0)])]
    another operation x1 -> x0, local copies, waits for them, and re-layouts: 2.69 us -> none  [per_device(): seen_values = seen[1].reshape(-1, heads_here, HD)]
    dot_general x3 -> x6, matrix products: 13.5 us -> 11.7 us  [project(): jnp.dot(block, piece, preferred_element_type=jnp.float32)]
  transfers between devices with their start and end apart: 20 -> 20, of which waited for: 9 -> 10; matrix products, arithmetic and copies ran while one was open for 17% -> 17% of each run, Pallas kernels for 0% -> 0%
where the time goes in v8:
time: 227 us; the launch traced here: 223 us
  waiting for transfers between devices  130 us (57%)
  starting transfers between devices  30.9 us (14%)
  other arithmetic  25.4 us (11%)
  matrix products  15.7 us (7%)
  between operations  13.5 us (6%)
  local copies, waits for them, and re-layouts  7.56 us (3%)
    all_gather x3, waiting for transfers between devices, full_columns(): own = lax.all_gather(own, 'seq', axis=0, tiled=True)  60.7 us
    ppermute x6, waiting for transfers between devices, line_gather(): lax.ppermute(from_right[-1], 'seq', [(j, j - 1) for j in range(1, n - k +...  28.1 us
    ppermute x3, waiting for transfers between devices, full_columns(): other = lax.ppermute(own[rows:], 'groups', [(0, 1), (1, 0)])  22.4 us
    ppermute x2, waiting for transfers between devices, swap_gather(): other = lax.ppermute(piece, axis, [(0, 1), (1, 0)])  18.9 us
    ppermute x6, starting transfers between devices, line_gather(): lax.ppermute(from_left[-1], 'seq', [(j, j + 1) for j in range(k - 1, n -...  15.1 us
    dot_general x6, matrix products, project(): jnp.dot(block, piece, preferred_element_type=jnp.float32)  11.7 us
    concatenate x3, other arithmetic, full_columns(): own = jnp.roll(own, -lax.axis_index('seq') * rows, axis=0)  9.16 us
    ppermute x6, starting transfers between devices, line_gather(): lax.ppermute(from_right[-1], 'seq', [(j, j - 1) for j in range(1, n - k +...  8.09 us
  transfers between devices with their start and end apart: 20, of which 10 were waited for; matrix products, arithmetic and copies ran while one was open for 17% of the time, Pallas kernels for 0%

profile of v8, /device:TPU:0, one launch (start us, length us, event | category | flops | bytes accessed | tf_op | source)
XLA Modules:
  0.0 223.3 jit_solution(17060767257320522964)
XLA Ops:
  6.5 2.4 %constant_dynamic-slice_fusion.4 = (bf16[1024,256]{1,0:T(8,128)(2,1)}, bf16[1024,256]{1,0:T(8,128)(2,1)}) fusion(bf16[1024,512]{1,0:T(8,128)(2,1)} %param.9, s32[]{:T(128)S(6)} %select_n.105, s32[]{:T(128)S(6)} %select_n.104), kind=kLoop, calls=%fused_computation.84 | loop fusion | bytes 2097160 | tf_op jit(solution)/shard_map/dynamic_slice | solution.py:46
  9.0 3.0 %collective-permute-start = (bf16[192,2048]{1,0:T(8,128)(2,1)}, bf16[192,2048]{1,0:T(8,128)(2,1)S(1)}, u32[]{:S(2)}, u32[]{:S(2)}) collective-permute-start(bf16[192,2048]{1,0:T(8,128)(2,1)} %param.6), channel_id=1, source_target_pairs={{0,2},{2,0},{1,3},{3,1},{4,6},{6,4},{5,7},{7,5},{8,10},{10,8},{9,1... | collective-permute-start | bytes 2359304 | tf_op jit(solution)/shard_map/ppermute | solution.py:34
  13.2 16.6 %collective-permute-done = bf16[192,2048]{1,0:T(8,128)(2,1)S(1)} collective-permute-done((bf16[192,2048]{1,0:T(8,128)(2,1)}, bf16[192,2048]{1,0:T(8,128)(2,1)S(1)}, u32[]{:S(2)}, u32[]{:S(2)}) %collective-permute-start) | collective-permute-done | bytes 786464 | tf_op jit(solution)/shard_map/ppermute | solution.py:34
  31.3 2.3 %collective-permute-done.1 = bf16[384,2048]{1,0:T(8,128)(2,1)} collective-permute-done((bf16[384,2048]{1,0:T(8,128)(2,1)S(1)}, bf16[384,2048]{1,0:T(8,128)(2,1)}, u32[]{:S(2)}, u32[]{:S(2)}) %collective-permute-start.1) | collective-permute-done | bytes 1572896 | tf_op jit(solution)/shard_map/ppermute | solution.py:34
  33.6 4.0 %broadcast_select_fusion = (bf16[384,2048]{1,0:T(8,128)(2,1)}, bf16[384,2048]{1,0:T(8,128)(2,1)}) fusion(bf16[384,2048]{1,0:T(8,128)(2,1)} %collective-permute-done.1, pred[]{:T(512)S(6)} %eq.12, bf16[192,2048]{1,0:T(8,128)(2,1)S(1)} %get-tuple-element.11, bf16[192,2048]{1,0:T(8,128)(2,1)S(1)} %get-tuple-element.10), kind=kLoop, calls=%fused_computation.45 | loop fusion | flops 4718592 | bytes 6291457 | tf_op jit(solution)/shard_map/jit(_where)/select_n | solution.py:36
  37.6 20.1 %all-gather.4.cloned.1.call-done = bf16[4096,256]{1,0:T(8,128)(2,1)} async-done(((bf16[1024,256]{1,0:T(8,128)(2,1)}), bf16[4096,256]{1,0:T(8,128)(2,1)}) %all-gather.4.cloned.1.call-update) | async-done | bytes 2097168 | tf_op jit(solution)/shard_map/all_gather | solution.py:47
  57.7 3.0 %fusion.17 = bf16[4096,256]{1,0:T(8,128)(2,1)S(1)} fusion(s32[]{:T(128)S(6)} %select_n.103, bf16[4096,256]{1,0:T(8,128)(2,1)} %all-gather.4.cloned.1.call-done), kind=kLoop, calls=%fused_computation.29 | loop fusion | flops 4194304 | bytes 4194308 | tf_op jit(solution)/shard_map/jit(_roll_dynamic)/concatenate | solution.py:48
  63.4 40.5 %all-gather.8.cloned.1.call-done = bf16[4096,256]{1,0:T(8,128)(2,1)} async-done(((bf16[1024,256]{1,0:T(8,128)(2,1)}), bf16[4096,256]{1,0:T(8,128)(2,1)}) %all-gather.8.cloned.1.call-update) | async-done | bytes 2097168 | tf_op jit(solution)/shard_map/all_gather | solution.py:47
  104.0 3.2 %fusion.15 = bf16[4096,256]{1,0:T(8,128)(2,1)S(1)} fusion(s32[]{:T(128)S(6)} %select_n.103, bf16[4096,256]{1,0:T(8,128)(2,1)} %all-gather.8.cloned.1.call-done), kind=kLoop, calls=%fused_computation.27 | loop fusion | flops 4194304 | bytes 4194308 | tf_op jit(solution)/shard_map/jit(_roll_dynamic)/concatenate | solution.py:48
  107.2 1.5 collective-permute-start.9
  108.8 2.9 %fusion.6 = bf16[384,4096]{1,0:T(8,128)(2,1)S(1)} fusion(s32[]{:T(128)S(6)} %select_n.103, bf16[384,2048]{1,0:T(8,128)(2,1)S(1)} %copy-done.1, bf16[384,2048]{1,0:T(8,128)(2,1)S(1)} %copy-done), kind=kLoop, calls=%fused_computation.20 | loop fusion | flops 12582912 | bytes 6291460 | tf_op jit(solution)/shard_map/jit(_roll_dynamic)/concatenate | solution.py:63
  114.3 2.8 %fusion.42 = bf16[384,256]{0,1:T(8,128)(2,1)S(1)} fusion(bf16[384,4096]{1,0:T(8,128)(2,1)S(1)} %fusion.6, bf16[3072,256]{1,0:T(8,128)(2,1)} %collective-permute-done.2, bf16[1024,256]{1,0:T(8,128)(2,1)S(1)} %copy-done.11), kind=kOutput, calls=%fused_computation.51 | convolution fusion | flops 809598976 | bytes 5439488 | tf_op jit(solution)/shard_map/dot_general | solution.py:67
  119.2 5.3 %collective-permute-start.4 = (bf16[384,512]{0,1:T(8,128)(2,1)}, bf16[384,512]{0,1:T(8,128)(2,1)}, u32[]{:S(2)}, u32[]{:S(2)}) collective-permute-start(bf16[384,512]{0,1:T(8,128)(2,1)} %pad_maximum_fusion.3), channel_id=1, source_target_pairs={{0,4},{4,8},{8,12},{1,5},{5,9},{9,13},{2,6},{6,10},{10,14},{3,7},{... | collective-permute-start | bytes 1179656 | tf_op jit(solution)/shard_map/ppermute | solution.py:23
  124.5 18.9 %collective-permute-done.9 = bf16[3072,256]{1,0:T(8,128)(2,1)S(1)} collective-permute-done((bf16[3072,256]{1,0:T(8,128)(2,1)S(1)}, bf16[3072,256]{1,0:T(8,128)(2,1)S(1)}, u32[]{:S(2)}, u32[]{:S(2)}) %collective-permute-start.9) | collective-permute-done | bytes 1572896 | tf_op jit(solution)/shard_map/ppermute | solution.py:51
  146.9 5.5 %collective-permute-start.11 = (bf16[384,512]{0,1:T(8,128)(2,1)}, bf16[384,512]{0,1:T(8,128)(2,1)}, u32[]{:S(2)}, u32[]{:S(2)}) collective-permute-start(bf16[384,512]{0,1:T(8,128)(2,1)} %pad_maximum_fusion.4), channel_id=1, source_target_pairs={{0,4},{4,8},{8,12},{1,5},{5,9},{9,13},{2,6},{6,10},{10,14},{3,7},{... | collective-permute-start | bytes 1179656 | tf_op jit(solution)/shard_map/ppermute | solution.py:23
  152.4 1.5 collective-permute-start.7
  154.0 1.5 collective-permute-start.5
  155.5 10.2 %collective-permute-done.10 = bf16[384,512]{0,1:T(8,128)(2,1)} collective-permute-done((bf16[384,512]{0,1:T(8,128)(2,1)}, bf16[384,512]{0,1:T(8,128)(2,1)}, u32[]{:S(2)}, u32[]{:S(2)}) %collective-permute-start.10) | collective-permute-done | bytes 393248 | tf_op jit(solution)/shard_map/ppermute | solution.py:22
  168.4 3.0 %fusion.16 = bf16[4096,256]{1,0:T(8,128)(2,1)S(1)} fusion(s32[]{:T(128)S(6)} %select_n.103, bf16[4096,256]{1,0:T(8,128)(2,1)} %all-gather.6.cloned.1.call-done), kind=kLoop, calls=%fused_computation.28 | loop fusion | flops 4194304 | bytes 4194308 | tf_op jit(solution)/shard_map/jit(_roll_dynamic)/concatenate | solution.py:48
  177.7 4.5 %collective-permute-done.14 = bf16[384,512]{0,1:T(8,128)(2,1)} collective-permute-done((bf16[384,512]{0,1:T(8,128)(2,1)}, bf16[384,512]{0,1:T(8,128)(2,1)}, u32[]{:S(2)}, u32[]{:S(2)}) %collective-permute-start.14) | collective-permute-done | bytes 393248 | tf_op jit(solution)/shard_map/ppermute | solution.py:22
  186.3 7.3 %collective-permute-done.8 = bf16[384,512]{0,1:T(8,128)(2,1)S(1)} collective-permute-done((bf16[384,512]{0,1:T(8,128)(2,1)}, bf16[384,512]{0,1:T(8,128)(2,1)S(1)}, u32[]{:S(2)}, u32[]{:S(2)}) %collective-permute-start.8) | collective-permute-done | bytes 393248 | tf_op jit(solution)/shard_map/ppermute | solution.py:22
  193.7 6.1 %collective-permute-done.15 = bf16[384,512]{0,1:T(8,128)(2,1)S(1)} collective-permute-done((bf16[384,512]{0,1:T(8,128)(2,1)}, bf16[384,512]{0,1:T(8,128)(2,1)S(1)}, u32[]{:S(2)}, u32[]{:S(2)}) %collective-permute-start.15) | collective-permute-done | bytes 393248 | tf_op jit(solution)/shard_map/ppermute | solution.py:22
  205.4 3.5 %collective-permute-done.16 = bf16[3072,256]{1,0:T(8,128)(2,1)} collective-permute-done((bf16[3072,256]{1,0:T(8,128)(2,1)}, bf16[3072,256]{1,0:T(8,128)(2,1)}, u32[]{:S(2)}, u32[]{:S(2)}) %collective-permute-start.16) | collective-permute-done | bytes 1572896 | tf_op jit(solution)/shard_map/ppermute | solution.py:51
  208.9 3.8 %fusion.36 = bf16[384,256]{0,1:T(8,128)(2,1)S(1)} fusion(bf16[384,4096]{1,0:T(8,128)(2,1)} %copy-done.2, bf16[3072,256]{1,0:T(8,128)(2,1)} %collective-permute-done.16, bf16[1024,256]{1,0:T(8,128)(2,1)} %get-tuple-element.12), kind=kOutput, calls=%fused_computation.49 | convolution fusion | flops 809598976 | bytes 5439488 | tf_op jit(solution)/shard_map/dot_general | solution.py:67
  (83 shorter events, 36.4 us)
Async XLA Ops:
  6.5 51.2 %all-gather.4.cloned.1.call-start = ((), (), s32[]{:S(2)}) async-start(), calls=%async_computation | async-start | bytes 2621440 | tf_op jit(solution)/shard_map/all_gather | solution.py:47
  8.9 95.0 %all-gather.8.cloned.1.call-start = ((), (), s32[]{:S(2)}) async-start(), calls=%async_computation.2 | async-start | bytes 2621440 | tf_op jit(solution)/shard_map/all_gather | solution.py:47
  9.0 20.8 %collective-permute-start = (bf16[192,2048]{1,0:T(8,128)(2,1)}, bf16[192,2048]{1,0:T(8,128)(2,1)S(1)}, u32[]{:S(2)}, u32[]{:S(2)}) collective-permute-start(bf16[192,2048]{1,0:T(8,128)(2,1)} %param.6), channel_id=1, source_target_pairs={{0,2},{2,0},{1,3},{3,1},{4,6},{6,4},{5,7},{7,5},{8,10},{10,8},{9,1... | collective-permute-start | bytes 2359304 | tf_op jit(solution)/shard_map/ppermute | solution.py:34
  13.1 155.3 %all-gather.6.cloned.1.call-start = ((), (), s32[]{:S(2)}) async-start(), calls=%async_computation.1 | async-start | bytes 2621440 | tf_op jit(solution)/shard_map/all_gather | solution.py:47
  30.0 3.6 %collective-permute-start.1 = (bf16[384,2048]{1,0:T(8,128)(2,1)S(1)}, bf16[384,2048]{1,0:T(8,128)(2,1)}, u32[]{:S(2)}, u32[]{:S(2)}) collective-permute-start(bf16[384,2048]{1,0:T(8,128)(2,1)S(1)} %pad_maximum_fusion), channel_id=1, source_target_pairs={{0,1},{1,0},{2,3},{3,2},{4,5},{5,4},{6,7},{7,6},{8,9},{9,8},{10,11... | collective-permute-start | bytes 4718600 | tf_op jit(solution)/shard_map/ppermute | solution.py:34
  62.0 52.3 %collective-permute-start.2 = (bf16[3072,256]{1,0:T(8,128)(2,1)}, bf16[3072,256]{1,0:T(8,128)(2,1)}, u32[]{:S(2)}, u32[]{:S(2)}) collective-permute-start(bf16[3072,256]{1,0:T(8,128)(2,1)} %slice.28), channel_id=1, source_target_pairs={{0,16},{16,0},{1,17},{17,1},{2,18},{18,2},{3,19},{19,3},{4,20},{20... | collective-permute-start | bytes 4718600 | tf_op jit(solution)/shard_map/ppermute | solution.py:51
  107.2 36.2 %collective-permute-start.9 = (bf16[3072,256]{1,0:T(8,128)(2,1)S(1)}, bf16[3072,256]{1,0:T(8,128)(2,1)S(1)}, u32[]{:S(2)}, u32[]{:S(2)}) collective-permute-start(bf16[3072,256]{1,0:T(8,128)(2,1)S(1)} %slice.29), channel_id=1, source_target_pairs={{0,16},{16,0},{1,17},{17,1},{2,18},{18,2},{3,19},{19,3},{4,20},{20... | collective-permute-start | bytes 4718600 | tf_op jit(solution)/shard_map/ppermute | solution.py:51
  111.7 31.8 %copy-start.2 = (bf16[384,4096]{1,0:T(8,128)(2,1)}, bf16[384,4096]{1,0:T(8,128)(2,1)S(1)}, u32[]{:S(2)}) copy-start(bf16[384,4096]{1,0:T(8,128)(2,1)S(1)} %fusion.6) | copy-start | bytes 9437188
  114.3 29.1 %copy-start.12 = (bf16[1024,256]{1,0:T(8,128)(2,1)S(1)}, bf16[1024,256]{1,0:T(8,128)(2,1)}, u32[]{:S(2)}) copy-start(bf16[1024,256]{1,0:T(8,128)(2,1)} %get-tuple-element.14) | copy-start | bytes 1572868
  117.1 27.6 %copy-start.6 = (bf16[384,256]{0,1:T(8,128)(2,1)}, bf16[384,256]{0,1:T(8,128)(2,1)S(1)}, u32[]{:S(2)}) copy-start(bf16[384,256]{0,1:T(8,128)(2,1)S(1)} %fusion.42) | copy-start | bytes 589828
  117.9 34.5 %collective-permute-start.3 = (bf16[384,512]{0,1:T(8,128)(2,1)}, bf16[384,512]{0,1:T(8,128)(2,1)}, u32[]{:S(2)}, u32[]{:S(2)}) collective-permute-start(bf16[384,512]{0,1:T(8,128)(2,1)} %pad_maximum_fusion.3), channel_id=1, source_target_pairs={{4,0},{8,4},{12,8},{5,1},{9,5},{13,9},{6,2},{10,6},{14,10},{7,3},{... | collective-permute-start | bytes 1179656 | tf_op jit(solution)/shard_map/ppermute | solution.py:22
  119.2 34.8 %collective-permute-start.4 = (bf16[384,512]{0,1:T(8,128)(2,1)}, bf16[384,512]{0,1:T(8,128)(2,1)}, u32[]{:S(2)}, u32[]{:S(2)}) collective-permute-start(bf16[384,512]{0,1:T(8,128)(2,1)} %pad_maximum_fusion.3), channel_id=1, source_target_pairs={{0,4},{4,8},{8,12},{1,5},{5,9},{9,13},{2,6},{6,10},{10,14},{3,7},{... | collective-permute-start | bytes 1179656 | tf_op jit(solution)/shard_map/ppermute | solution.py:23
  145.6 20.1 %collective-permute-start.10 = (bf16[384,512]{0,1:T(8,128)(2,1)}, bf16[384,512]{0,1:T(8,128)(2,1)}, u32[]{:S(2)}, u32[]{:S(2)}) collective-permute-start(bf16[384,512]{0,1:T(8,128)(2,1)} %pad_maximum_fusion.4), channel_id=1, source_target_pairs={{4,0},{8,4},{12,8},{5,1},{9,5},{13,9},{6,2},{10,6},{14,10},{7,3},{... | collective-permute-start | bytes 1179656 | tf_op jit(solution)/shard_map/ppermute | solution.py:22
  146.9 20.1 %collective-permute-start.11 = (bf16[384,512]{0,1:T(8,128)(2,1)}, bf16[384,512]{0,1:T(8,128)(2,1)}, u32[]{:S(2)}, u32[]{:S(2)}) collective-permute-start(bf16[384,512]{0,1:T(8,128)(2,1)} %pad_maximum_fusion.4), channel_id=1, source_target_pairs={{0,4},{4,8},{8,12},{1,5},{5,9},{9,13},{2,6},{6,10},{10,14},{3,7},{... | collective-permute-start | bytes 1179656 | tf_op jit(solution)/shard_map/ppermute | solution.py:23
  152.4 23.1 %collective-permute-start.7 = (bf16[384,512]{0,1:T(8,128)(2,1)}, bf16[384,512]{0,1:T(8,128)(2,1)}, u32[]{:S(2)}, u32[]{:S(2)}) collective-permute-start(bf16[384,512]{0,1:T(8,128)(2,1)} %collective-permute-done.3), channel_id=1, source_target_pairs={{4,0},{8,4},{5,1},{9,5},{6,2},{10,6},{7,3},{11,7},{20,16},{24,20},... | collective-permute-start | bytes 1179656 | tf_op jit(solution)/shard_map/ppermute | solution.py:22
  154.0 23.0 %collective-permute-start.5 = (bf16[384,512]{0,1:T(8,128)(2,1)}, bf16[384,512]{0,1:T(8,128)(2,1)}, u32[]{:S(2)}, u32[]{:S(2)}) collective-permute-start(bf16[384,512]{0,1:T(8,128)(2,1)} %collective-permute-done.4), channel_id=1, source_target_pairs={{4,8},{8,12},{5,9},{9,13},{6,10},{10,14},{7,11},{11,15},{20,24},{2... | collective-permute-start | bytes 1179656 | tf_op jit(solution)/shard_map/ppermute | solution.py:23
  165.7 16.6 %collective-permute-start.14 = (bf16[384,512]{0,1:T(8,128)(2,1)}, bf16[384,512]{0,1:T(8,128)(2,1)}, u32[]{:S(2)}, u32[]{:S(2)}) collective-permute-start(bf16[384,512]{0,1:T(8,128)(2,1)} %collective-permute-done.10), channel_id=1, source_target_pairs={{4,0},{8,4},{5,1},{9,5},{6,2},{10,6},{7,3},{11,7},{20,16},{24,20},... | collective-permute-start | bytes 1179656 | tf_op jit(solution)/shard_map/ppermute | solution.py:22
  167.0 16.5 %collective-permute-start.12 = (bf16[384,512]{0,1:T(8,128)(2,1)}, bf16[384,512]{0,1:T(8,128)(2,1)}, u32[]{:S(2)}, u32[]{:S(2)}) collective-permute-start(bf16[384,512]{0,1:T(8,128)(2,1)} %collective-permute-done.11), channel_id=1, source_target_pairs={{4,8},{8,12},{5,9},{9,13},{6,10},{10,14},{7,11},{11,15},{20,24},{2... | collective-permute-start | bytes 1179656 | tf_op jit(solution)/shard_map/ppermute | solution.py:23
  172.8 36.1 %collective-permute-start.16 = (bf16[3072,256]{1,0:T(8,128)(2,1)}, bf16[3072,256]{1,0:T(8,128)(2,1)}, u32[]{:S(2)}, u32[]{:S(2)}) collective-permute-start(bf16[3072,256]{1,0:T(8,128)(2,1)} %slice.26), channel_id=1, source_target_pairs={{0,16},{16,0},{1,17},{17,1},{2,18},{18,2},{3,19},{19,3},{4,20},{20... | collective-permute-start | bytes 4718600 | tf_op jit(solution)/shard_map/ppermute | solution.py:51
  175.5 25.4 %copy-start.7 = (bf16[384,256]{0,1:T(8,128)(2,1)S(1)}, bf16[384,256]{0,1:T(8,128)(2,1)}, u32[]{:S(2)}) copy-start(bf16[384,256]{0,1:T(8,128)(2,1)} %copy-done.6) | copy-start | bytes 589828
  175.5 18.1 %collective-permute-start.8 = (bf16[384,512]{0,1:T(8,128)(2,1)}, bf16[384,512]{0,1:T(8,128)(2,1)S(1)}, u32[]{:S(2)}, u32[]{:S(2)}) collective-permute-start(bf16[384,512]{0,1:T(8,128)(2,1)} %collective-permute-done.7), channel_id=1, source_target_pairs={{4,0},{5,1},{6,2},{7,3},{20,16},{21,17},{22,18},{23,19}} | collective-permute-start | bytes 1179656 | tf_op jit(solution)/shard_map/ppermute | solution.py:22
  177.0 22.9 %collective-permute-start.6 = (bf16[384,512]{0,1:T(8,128)(2,1)}, bf16[384,512]{0,1:T(8,128)(2,1)S(1)}, u32[]{:S(2)}, u32[]{:S(2)}) collective-permute-start(bf16[384,512]{0,1:T(8,128)(2,1)} %collective-permute-done.5), channel_id=1, source_target_pairs={{8,12},{9,13},{10,14},{11,15},{24,28},{25,29},{26,30},{27,31}} | collective-permute-start | bytes 1179656 | tf_op jit(solution)/shard_map/ppermute | solution.py:23
  182.2 17.6 %collective-permute-start.15 = (bf16[384,512]{0,1:T(8,128)(2,1)}, bf16[384,512]{0,1:T(8,128)(2,1)S(1)}, u32[]{:S(2)}, u32[]{:S(2)}) collective-permute-start(bf16[384,512]{0,1:T(8,128)(2,1)} %collective-permute-done.14), channel_id=1, source_target_pairs={{4,0},{5,1},{6,2},{7,3},{20,16},{21,17},{22,18},{23,19}} | collective-permute-start | bytes 1179656 | tf_op jit(solution)/shard_map/ppermute | solution.py:22
  183.5 17.6 %collective-permute-start.13 = (bf16[384,512]{0,1:T(8,128)(2,1)}, bf16[384,512]{0,1:T(8,128)(2,1)S(1)}, u32[]{:S(2)}, u32[]{:S(2)}) collective-permute-start(bf16[384,512]{0,1:T(8,128)(2,1)} %collective-permute-done.12), channel_id=1, source_target_pairs={{8,12},{9,13},{10,14},{11,15},{24,28},{25,29},{26,30},{27,31}} | collective-permute-start | bytes 1179656 | tf_op jit(solution)/shard_map/ppermute | solution.py:23
  (9 other events, 87.7 us)
Sparse Core Ops, SparseCore 0:
  9.0 48.6 all-gather.3
  59.3 44.6 all-gather.7
  105.6 56.1 all-gather.5

commit v9 on v8

--- a/solution.py
+++ b/solution.py
@@ -44,8 +44,11 @@
     group = lax.axis_index("groups")
     own = lax.dynamic_slice_in_dim(weight, group * half, half, axis=1)
     kept = lax.dynamic_slice_in_dim(weight, (1 - group) * half, half, axis=1)
-    own = lax.all_gather(own, "seq", axis=0, tiled=True)
-    own = jnp.roll(own, -lax.axis_index("seq") * rows, axis=0)
+    if lax.axis_size("seq") == SPAN:
+        own = line_gather(own)
+    else:
+        own = lax.all_gather(own, "seq", axis=0, tiled=True)
+        own = jnp.roll(own, -lax.axis_index("seq") * rows, axis=0)
     if after is not None:
         own = lax.optimization_barrier((own, after))[0]
     other = lax.ppermute(own[rows:], "groups", [(0, 1), (1, 0)])

time: 227 us -> 240 us (1.057)
  starting transfers between devices: 30.9 us -> 57.3 us
  waiting for transfers between devices: 130 us -> 147 us
  other arithmetic: 25.4 us -> 10.6 us
  between operations: 13.5 us -> 0.68 us
    ppermute x6 -> x15, waiting for transfers between devices: 28.1 us -> 95.9 us  [line_gather(): lax.ppermute(from_right[-1], 'seq', [(j, j - 1) for j in range(1, n - k +...]
    all_gather x3 -> x0, waiting for transfers between devices: 60.7 us -> none  [full_columns(): own = lax.all_gather(own, 'seq', axis=0, tiled=True)]
    ppermute x3, waiting for transfers between devices: 22.4 us -> 51.1 us  [full_columns(): other = lax.ppermute(own[rows:], 'groups', [(0, 1), (1, 0)])]
    ppermute x2, waiting for transfers between devices: 18.9 us -> 0.01 us  [swap_gather(): other = lax.ppermute(piece, axis, [(0, 1), (1, 0)])]
    ppermute x6 -> x15, starting transfers between devices: 15.1 us -> 31.3 us  [line_gather(): lax.ppermute(from_left[-1], 'seq', [(j, j + 1) for j in range(k - 1, n -...]
    ppermute x6 -> x15, starting transfers between devices: 8.09 us -> 19.3 us  [line_gather(): lax.ppermute(from_right[-1], 'seq', [(j, j - 1) for j in range(1, n - k +...]
    concatenate x3 -> x0, other arithmetic: 9.16 us -> none  [full_columns(): own = jnp.roll(own, -lax.axis_index('seq') * rows, axis=0)]
    select_n x1, other arithmetic: 3.97 us -> 0.95 us  [swap_gather(): high = jnp.where(first, other, piece)]
  transfers between devices with their start and end apart: 20 -> 35, of which waited for: 10 -> 16; matrix products, arithmetic and copies ran while one was open for 17% -> 10% of each run, Pallas kernels for 0% -> 0%
where the time goes in v9:
time: 240 us; the launch traced here: 237 us
  waiting for transfers between devices  147 us (61%)
  starting transfers between devices  57.3 us (24%)
  matrix products  15.6 us (6%)
  other arithmetic  10.6 us (4%)
  local copies, waits for them, and re-layouts  5.37 us (2%)
    ppermute x15, waiting for transfers between devices, line_gather(): lax.ppermute(from_right[-1], 'seq', [(j, j - 1) for j in range(1, n - k +...  95.9 us
    ppermute x3, waiting for transfers between devices, full_columns(): other = lax.ppermute(own[rows:], 'groups', [(0, 1), (1, 0)])  51.1 us
    ppermute x15, starting transfers between devices, line_gather(): lax.ppermute(from_left[-1], 'seq', [(j, j + 1) for j in range(k - 1, n -...  31.3 us
    ppermute x15, starting transfers between devices, line_gather(): lax.ppermute(from_right[-1], 'seq', [(j, j - 1) for j in range(1, n - k +...  19.3 us
    dot_general x6, matrix products, project(): jnp.dot(block, piece, preferred_element_type=jnp.float32)  11.6 us
  transfers between devices with their start and end apart: 35, of which 16 were waited for; matrix products, arithmetic and copies ran while one was open for 10% of the time, Pallas kernels for 0%

profile of v9, /device:TPU:0, one launch (start us, length us, event | category | flops | bytes accessed | tf_op | source)
XLA Modules:
  0.0 236.8 jit_solution(5042007773312885257)
XLA Ops:
  0.0 2.9 %collective-permute-start = (bf16[192,2048]{1,0:T(8,128)(2,1)}, bf16[192,2048]{1,0:T(8,128)(2,1)S(1)}, u32[]{:S(2)}, u32[]{:S(2)}) collective-permute-start(bf16[192,2048]{1,0:T(8,128)(2,1)} %param.4), channel_id=1, source_target_pairs={{0,2},{2,0},{1,3},{3,1},{4,6},{6,4},{5,7},{7,5},{8,10},{10,8},{9,1... | collective-permute-start | bytes 2359304 | tf_op jit(solution)/shard_map/ppermute | solution.py:34
  2.9 2.3 constant_dynamic-slice_fusion.4
  6.5 5.4 %collective-permute-start.3 = (bf16[1024,256]{1,0:T(8,128)(2,1)}, bf16[1024,256]{1,0:T(8,128)(2,1)}, u32[]{:S(2)}, u32[]{:S(2)}) collective-permute-start(bf16[1024,256]{1,0:T(8,128)(2,1)} %get-tuple-element.16), channel_id=1, source_target_pairs={{0,4},{4,8},{8,12},{1,5},{5,9},{9,13},{2,6},{6,10},{10,14},{3,7},{... | collective-permute-start | bytes 1572872 | tf_op jit(solution)/shard_map/ppermute | solution.py:23
  15.3 5.4 %collective-permute-start.16 = (bf16[1024,256]{1,0:T(8,128)(2,1)S(1)}, bf16[1024,256]{1,0:T(8,128)(2,1)}, u32[]{:S(2)}, u32[]{:S(2)}) collective-permute-start(bf16[1024,256]{1,0:T(8,128)(2,1)S(1)} %get-tuple-element.12), channel_id=1, source_target_pairs={{0,4},{4,8},{8,12},{1,5},{5,9},{9,13},{2,6},{6,10},{10,14},{3,7},{... | collective-permute-start | bytes 1572872 | tf_op jit(solution)/shard_map/ppermute | solution.py:23
  23.8 4.4 %collective-permute-start.22 = (bf16[1024,256]{1,0:T(8,128)(2,1)S(1)}, bf16[1024,256]{1,0:T(8,128)(2,1)S(1)}, u32[]{:S(2)}, u32[]{:S(2)}) collective-permute-start(bf16[1024,256]{1,0:T(8,128)(2,1)S(1)} %get-tuple-element.14), channel_id=1, source_target_pairs={{0,4},{4,8},{8,12},{1,5},{5,9},{9,13},{2,6},{6,10},{10,14},{3,7},{... | collective-permute-start | bytes 1572872 | tf_op jit(solution)/shard_map/ppermute | solution.py:23
  28.2 5.3 %collective-permute-done.15 = bf16[1024,256]{1,0:T(8,128)(2,1)} collective-permute-done((bf16[1024,256]{1,0:T(8,128)(2,1)S(1)}, bf16[1024,256]{1,0:T(8,128)(2,1)}, u32[]{:S(2)}, u32[]{:S(2)}) %collective-permute-start.15) | collective-permute-done | bytes 524320 | tf_op jit(solution)/shard_map/ppermute | solution.py:22
  37.0 7.7 %collective-permute-done.21 = bf16[1024,256]{1,0:T(8,128)(2,1)S(1)} collective-permute-done((bf16[1024,256]{1,0:T(8,128)(2,1)S(1)}, bf16[1024,256]{1,0:T(8,128)(2,1)S(1)}, u32[]{:S(2)}, u32[]{:S(2)}) %collective-permute-start.21) | collective-permute-done | bytes 524320 | tf_op jit(solution)/shard_map/ppermute | solution.py:22
  46.8 9.1 %collective-permute-done.6 = bf16[1024,256]{1,0:T(8,128)(2,1)S(1)} collective-permute-done((bf16[1024,256]{1,0:T(8,128)(2,1)}, bf16[1024,256]{1,0:T(8,128)(2,1)S(1)}, u32[]{:S(2)}, u32[]{:S(2)}) %collective-permute-start.6) | collective-permute-done | bytes 524320 | tf_op jit(solution)/shard_map/ppermute | solution.py:22
  56.8 10.4 %collective-permute-done.19 = bf16[1024,256]{1,0:T(8,128)(2,1)S(1)} collective-permute-done((bf16[1024,256]{1,0:T(8,128)(2,1)}, bf16[1024,256]{1,0:T(8,128)(2,1)S(1)}, u32[]{:S(2)}, u32[]{:S(2)}) %collective-permute-start.19) | collective-permute-done | bytes 524320 | tf_op jit(solution)/shard_map/ppermute | solution.py:22
  69.2 9.2 %collective-permute-done.25 = bf16[1024,256]{1,0:T(8,128)(2,1)S(1)} collective-permute-done((bf16[1024,256]{1,0:T(8,128)(2,1)S(1)}, bf16[1024,256]{1,0:T(8,128)(2,1)S(1)}, u32[]{:S(2)}, u32[]{:S(2)}) %collective-permute-start.25) | collective-permute-done | bytes 524320 | tf_op jit(solution)/shard_map/ppermute | solution.py:22
  80.4 9.2 %collective-permute-done.7 = bf16[1024,256]{1,0:T(8,128)(2,1)S(1)} collective-permute-done((bf16[1024,256]{1,0:T(8,128)(2,1)S(1)}, bf16[1024,256]{1,0:T(8,128)(2,1)S(1)}, u32[]{:S(2)}, u32[]{:S(2)}) %collective-permute-start.7) | collective-permute-done | bytes 524320 | tf_op jit(solution)/shard_map/ppermute | solution.py:22
  92.9 17.7 %collective-permute-done.26 = bf16[1024,256]{1,0:T(8,128)(2,1)S(1)} collective-permute-done((bf16[1024,256]{1,0:T(8,128)(2,1)S(1)}, bf16[1024,256]{1,0:T(8,128)(2,1)S(1)}, u32[]{:S(2)}, u32[]{:S(2)}) %collective-permute-start.26) | collective-permute-done | bytes 524320 | tf_op jit(solution)/shard_map/ppermute | solution.py:22
  113.9 2.9 %fusion.6 = bf16[384,4096]{1,0:T(8,128)(2,1)S(1)} fusion(s32[]{:T(128)S(6)} %select_n.140, bf16[384,2048]{1,0:T(8,128)(2,1)S(1)} %get-tuple-element.8, bf16[384,2048]{1,0:T(8,128)(2,1)S(1)} %get-tuple-element.7), kind=kLoop, calls=%fused_computation.14 | loop fusion | flops 12582912 | bytes 6291460 | tf_op jit(solution)/shard_map/jit(_roll_dynamic)/concatenate | solution.py:66
  116.9 2.7 %fusion.61 = bf16[384,256]{0,1:T(8,128)(2,1)S(1)} fusion(bf16[384,4096]{1,0:T(8,128)(2,1)S(1)} %fusion.6, bf16[1024,256]{1,0:T(8,128)(2,1)S(1)} %broadcast_select_fusion.6, bf16[1024,256]{1,0:T(8,128)(2,1)S(1)} %broadcast_select_fusion.9, bf16[1024,256]{1,0:T(8,128)(2,1)S(1)} %broadcast_select_fusion.12, bf16[1024,256]{1,0:T(8,128)(2,1)} %get-tuple-element.16), kind=kOutput, calls=%fused_computation.63 | convolution fusion | flops 813793280 | bytes 5439488 | tf_op jit(solution)/shard_map/dot_general | solution.py:70
  120.9 27.1 %collective-permute-done.8 = bf16[3072,256]{1,0:T(8,128)(2,1)S(1)} collective-permute-done((bf16[3072,256]{1,0:T(8,128)(2,1)S(1)}, bf16[3072,256]{1,0:T(8,128)(2,1)S(1)}, u32[]{:S(2)}, u32[]{:S(2)}) %collective-permute-start.8) | collective-permute-done | bytes 1572896 | tf_op jit(solution)/shard_map/ppermute | solution.py:54
  150.6 4.6 %collective-permute-start.10 = (bf16[384,512]{0,1:T(8,128)(2,1)S(1)}, bf16[384,512]{0,1:T(8,128)(2,1)S(1)}, u32[]{:S(2)}, u32[]{:S(2)}) collective-permute-start(bf16[384,512]{0,1:T(8,128)(2,1)S(1)} %pad_maximum_fusion.6), channel_id=1, source_target_pairs={{0,4},{4,8},{8,12},{1,5},{5,9},{9,13},{2,6},{6,10},{10,14},{3,7},{... | collective-permute-start | bytes 1179656 | tf_op jit(solution)/shard_map/ppermute | solution.py:23
  155.2 24.1 %collective-permute-done.27 = bf16[3072,256]{1,0:T(8,128)(2,1)S(1)} collective-permute-done((bf16[3072,256]{1,0:T(8,128)(2,1)S(1)}, bf16[3072,256]{1,0:T(8,128)(2,1)S(1)}, u32[]{:S(2)}, u32[]{:S(2)}) %collective-permute-start.27) | collective-permute-done | bytes 1572896 | tf_op jit(solution)/shard_map/ppermute | solution.py:54
  181.9 4.6 %collective-permute-start.29 = (bf16[384,512]{0,1:T(8,128)(2,1)S(1)}, bf16[384,512]{0,1:T(8,128)(2,1)S(1)}, u32[]{:S(2)}, u32[]{:S(2)}) collective-permute-start(bf16[384,512]{0,1:T(8,128)(2,1)S(1)} %pad_maximum_fusion.7), channel_id=1, source_target_pairs={{0,4},{4,8},{8,12},{1,5},{5,9},{9,13},{2,6},{6,10},{10,14},{3,7},{... | collective-permute-start | bytes 1179656 | tf_op jit(solution)/shard_map/ppermute | solution.py:23
  189.7 3.4 %collective-permute-done.28 = bf16[384,512]{0,1:T(8,128)(2,1)S(1)} collective-permute-done((bf16[384,512]{0,1:T(8,128)(2,1)S(1)}, bf16[384,512]{0,1:T(8,128)(2,1)S(1)}, u32[]{:S(2)}, u32[]{:S(2)}) %collective-permute-start.28) | collective-permute-done | bytes 393248 | tf_op jit(solution)/shard_map/ppermute | solution.py:22
  198.4 3.3 %collective-permute-done.13 = bf16[384,512]{0,1:T(8,128)(2,1)S(1)} collective-permute-done((bf16[384,512]{0,1:T(8,128)(2,1)S(1)}, bf16[384,512]{0,1:T(8,128)(2,1)S(1)}, u32[]{:S(2)}, u32[]{:S(2)}) %collective-permute-start.13) | collective-permute-done | bytes 393248 | tf_op jit(solution)/shard_map/ppermute | solution.py:22
  203.7 6.4 %collective-permute-done.32 = bf16[384,512]{0,1:T(8,128)(2,1)S(1)} collective-permute-done((bf16[384,512]{0,1:T(8,128)(2,1)S(1)}, bf16[384,512]{0,1:T(8,128)(2,1)S(1)}, u32[]{:S(2)}, u32[]{:S(2)}) %collective-permute-start.32) | collective-permute-done | bytes 393248 | tf_op jit(solution)/shard_map/ppermute | solution.py:22
  212.2 6.3 %collective-permute-done.14 = bf16[384,512]{0,1:T(8,128)(2,1)S(1)} collective-permute-done((bf16[384,512]{0,1:T(8,128)(2,1)S(1)}, bf16[384,512]{0,1:T(8,128)(2,1)S(1)}, u32[]{:S(2)}, u32[]{:S(2)}) %collective-permute-start.14) | collective-permute-done | bytes 393248 | tf_op jit(solution)/shard_map/ppermute | solution.py:22
  218.7 6.3 %collective-permute-done.33 = bf16[384,512]{0,1:T(8,128)(2,1)S(1)} collective-permute-done((bf16[384,512]{0,1:T(8,128)(2,1)S(1)}, bf16[384,512]{0,1:T(8,128)(2,1)S(1)}, u32[]{:S(2)}, u32[]{:S(2)}) %collective-permute-start.33) | collective-permute-done | bytes 393248 | tf_op jit(solution)/shard_map/ppermute | solution.py:22
  228.5 3.8 %fusion.49 = bf16[384,256]{0,1:T(8,128)(2,1)S(1)} fusion(bf16[384,4096]{1,0:T(8,128)(2,1)} %copy-done, bf16[3072,256]{1,0:T(8,128)(2,1)} %collective-permute-done.34, bf16[1024,256]{1,0:T(8,128)(2,1)} %get-tuple-element.11), kind=kOutput, calls=%fused_computation.59 | convolution fusion | flops 809598976 | bytes 5439488 | tf_op jit(solution)/shard_map/dot_general | solution.py:70
  (103 shorter events, 51.8 us)
Async XLA Ops:
  0.0 34.8 %collective-permute-start = (bf16[192,2048]{1,0:T(8,128)(2,1)}, bf16[192,2048]{1,0:T(8,128)(2,1)S(1)}, u32[]{:S(2)}, u32[]{:S(2)}) collective-permute-start(bf16[192,2048]{1,0:T(8,128)(2,1)} %param.4), channel_id=1, source_target_pairs={{0,2},{2,0},{1,3},{3,1},{4,6},{6,4},{5,7},{7,5},{8,10},{10,8},{9,1... | collective-permute-start | bytes 2359304 | tf_op jit(solution)/shard_map/ppermute | solution.py:34
  6.5 17.2 %collective-permute-start.3 = (bf16[1024,256]{1,0:T(8,128)(2,1)}, bf16[1024,256]{1,0:T(8,128)(2,1)}, u32[]{:S(2)}, u32[]{:S(2)}) collective-permute-start(bf16[1024,256]{1,0:T(8,128)(2,1)} %get-tuple-element.16), channel_id=1, source_target_pairs={{0,4},{4,8},{8,12},{1,5},{5,9},{9,13},{2,6},{6,10},{10,14},{3,7},{... | collective-permute-start | bytes 1572872 | tf_op jit(solution)/shard_map/ppermute | solution.py:23
  14.0 19.6 %collective-permute-start.15 = (bf16[1024,256]{1,0:T(8,128)(2,1)S(1)}, bf16[1024,256]{1,0:T(8,128)(2,1)}, u32[]{:S(2)}, u32[]{:S(2)}) collective-permute-start(bf16[1024,256]{1,0:T(8,128)(2,1)S(1)} %get-tuple-element.12), channel_id=1, source_target_pairs={{4,0},{8,4},{12,8},{5,1},{9,5},{13,9},{6,2},{10,6},{14,10},{7,3},{... | collective-permute-start | bytes 1572872 | tf_op jit(solution)/shard_map/ppermute | solution.py:22
  15.3 20.4 %collective-permute-start.16 = (bf16[1024,256]{1,0:T(8,128)(2,1)S(1)}, bf16[1024,256]{1,0:T(8,128)(2,1)}, u32[]{:S(2)}, u32[]{:S(2)}) collective-permute-start(bf16[1024,256]{1,0:T(8,128)(2,1)S(1)} %get-tuple-element.12), channel_id=1, source_target_pairs={{0,4},{4,8},{8,12},{1,5},{5,9},{9,13},{2,6},{6,10},{10,14},{3,7},{... | collective-permute-start | bytes 1572872 | tf_op jit(solution)/shard_map/ppermute | solution.py:23
  22.3 22.4 %collective-permute-start.21 = (bf16[1024,256]{1,0:T(8,128)(2,1)S(1)}, bf16[1024,256]{1,0:T(8,128)(2,1)S(1)}, u32[]{:S(2)}, u32[]{:S(2)}) collective-permute-start(bf16[1024,256]{1,0:T(8,128)(2,1)S(1)} %get-tuple-element.14), channel_id=1, source_target_pairs={{4,0},{8,4},{12,8},{5,1},{9,5},{13,9},{6,2},{10,6},{14,10},{7,3},{... | collective-permute-start | bytes 1572872 | tf_op jit(solution)/shard_map/ppermute | solution.py:22
  23.8 21.7 %collective-permute-start.22 = (bf16[1024,256]{1,0:T(8,128)(2,1)S(1)}, bf16[1024,256]{1,0:T(8,128)(2,1)S(1)}, u32[]{:S(2)}, u32[]{:S(2)}) collective-permute-start(bf16[1024,256]{1,0:T(8,128)(2,1)S(1)} %get-tuple-element.14), channel_id=1, source_target_pairs={{0,4},{4,8},{8,12},{1,5},{5,9},{9,13},{2,6},{6,10},{10,14},{3,7},{... | collective-permute-start | bytes 1572872 | tf_op jit(solution)/shard_map/ppermute | solution.py:23
  33.5 22.4 %collective-permute-start.6 = (bf16[1024,256]{1,0:T(8,128)(2,1)}, bf16[1024,256]{1,0:T(8,128)(2,1)S(1)}, u32[]{:S(2)}, u32[]{:S(2)}) collective-permute-start(bf16[1024,256]{1,0:T(8,128)(2,1)} %collective-permute-done.2), channel_id=1, source_target_pairs={{4,0},{8,4},{5,1},{9,5},{6,2},{10,6},{7,3},{11,7},{20,16},{24,20},... | collective-permute-start | bytes 1572872 | tf_op jit(solution)/shard_map/ppermute | solution.py:22
  34.8 21.8 %collective-permute-start.4 = (bf16[1024,256]{1,0:T(8,128)(2,1)}, bf16[1024,256]{1,0:T(8,128)(2,1)S(1)}, u32[]{:S(2)}, u32[]{:S(2)}) collective-permute-start(bf16[1024,256]{1,0:T(8,128)(2,1)} %collective-permute-done.3), channel_id=1, source_target_pairs={{4,8},{8,12},{5,9},{9,13},{6,10},{10,14},{7,11},{11,15},{20,24},{2... | collective-permute-start | bytes 1572872 | tf_op jit(solution)/shard_map/ppermute | solution.py:23
  35.7 31.5 %collective-permute-start.19 = (bf16[1024,256]{1,0:T(8,128)(2,1)}, bf16[1024,256]{1,0:T(8,128)(2,1)S(1)}, u32[]{:S(2)}, u32[]{:S(2)}) collective-permute-start(bf16[1024,256]{1,0:T(8,128)(2,1)} %collective-permute-done.15), channel_id=1, source_target_pairs={{4,0},{8,4},{5,1},{9,5},{6,2},{10,6},{7,3},{11,7},{20,16},{24,20},... | collective-permute-start | bytes 1572872 | tf_op jit(solution)/shard_map/ppermute | solution.py:22
  44.7 23.8 %collective-permute-start.17 = (bf16[1024,256]{1,0:T(8,128)(2,1)}, bf16[1024,256]{1,0:T(8,128)(2,1)S(1)}, u32[]{:S(2)}, u32[]{:S(2)}) collective-permute-start(bf16[1024,256]{1,0:T(8,128)(2,1)} %collective-permute-done.16), channel_id=1, source_target_pairs={{4,8},{8,12},{5,9},{9,13},{6,10},{10,14},{7,11},{11,15},{20,24},{2... | collective-permute-start | bytes 1572872 | tf_op jit(solution)/shard_map/ppermute | solution.py:23
  45.5 32.9 %collective-permute-start.25 = (bf16[1024,256]{1,0:T(8,128)(2,1)S(1)}, bf16[1024,256]{1,0:T(8,128)(2,1)S(1)}, u32[]{:S(2)}, u32[]{:S(2)}) collective-permute-start(bf16[1024,256]{1,0:T(8,128)(2,1)S(1)} %collective-permute-done.21), channel_id=1, source_target_pairs={{4,0},{8,4},{5,1},{9,5},{6,2},{10,6},{7,3},{11,7},{20,16},{24,20},... | collective-permute-start | bytes 1572872 | tf_op jit(solution)/shard_map/ppermute | solution.py:22
  55.9 23.8 %collective-permute-start.23 = (bf16[1024,256]{1,0:T(8,128)(2,1)S(1)}, bf16[1024,256]{1,0:T(8,128)(2,1)S(1)}, u32[]{:S(2)}, u32[]{:S(2)}) collective-permute-start(bf16[1024,256]{1,0:T(8,128)(2,1)S(1)} %collective-permute-done.22), channel_id=1, source_target_pairs={{4,8},{8,12},{5,9},{9,13},{6,10},{10,14},{7,11},{11,15},{20,24},{2... | collective-permute-start | bytes 1572872 | tf_op jit(solution)/shard_map/ppermute | solution.py:23
  56.6 56.4 %collective-permute-start.1 = (bf16[384,2048]{1,0:T(8,128)(2,1)S(1)}, bf16[384,2048]{1,0:T(8,128)(2,1)S(1)}, u32[]{:S(2)}, u32[]{:S(2)}) collective-permute-start(bf16[384,2048]{1,0:T(8,128)(2,1)S(1)} %pad_maximum_fusion.1), channel_id=1, source_target_pairs={{0,1},{1,0},{2,3},{3,2},{4,5},{5,4},{6,7},{7,6},{8,9},{9,8},{10,11... | collective-permute-start | bytes 4718600 | tf_op jit(solution)/shard_map/ppermute | solution.py:34
  67.1 22.5 %collective-permute-start.7 = (bf16[1024,256]{1,0:T(8,128)(2,1)S(1)}, bf16[1024,256]{1,0:T(8,128)(2,1)S(1)}, u32[]{:S(2)}, u32[]{:S(2)}) collective-permute-start(bf16[1024,256]{1,0:T(8,128)(2,1)S(1)} %collective-permute-done.6), channel_id=1, source_target_pairs={{4,0},{5,1},{6,2},{7,3},{20,16},{21,17},{22,18},{23,19}} | collective-permute-start | bytes 1572872 | tf_op jit(solution)/shard_map/ppermute | solution.py:22
  68.4 22.5 %collective-permute-start.5 = (bf16[1024,256]{1,0:T(8,128)(2,1)S(1)}, bf16[1024,256]{1,0:T(8,128)(2,1)S(1)}, u32[]{:S(2)}, u32[]{:S(2)}) collective-permute-start(bf16[1024,256]{1,0:T(8,128)(2,1)S(1)} %collective-permute-done.4), channel_id=1, source_target_pairs={{8,12},{9,13},{10,14},{11,15},{24,28},{25,29},{26,30},{27,31}} | collective-permute-start | bytes 1572872 | tf_op jit(solution)/shard_map/ppermute | solution.py:23
  78.4 103.5 %collective-permute-start.20 = (bf16[1024,256]{1,0:T(8,128)(2,1)S(1)}, bf16[1024,256]{1,0:T(8,128)(2,1)S(1)}, u32[]{:S(2)}, u32[]{:S(2)}) collective-permute-start(bf16[1024,256]{1,0:T(8,128)(2,1)S(1)} %collective-permute-done.19), channel_id=1, source_target_pairs={{4,0},{5,1},{6,2},{7,3},{20,16},{21,17},{22,18},{23,19}} | collective-permute-start | bytes 1572872 | tf_op jit(solution)/shard_map/ppermute | solution.py:22
  79.7 106.9 %collective-permute-start.18 = (bf16[1024,256]{1,0:T(8,128)(2,1)S(1)}, bf16[1024,256]{1,0:T(8,128)(2,1)S(1)}, u32[]{:S(2)}, u32[]{:S(2)}) collective-permute-start(bf16[1024,256]{1,0:T(8,128)(2,1)S(1)} %collective-permute-done.17), channel_id=1, source_target_pairs={{8,12},{9,13},{10,14},{11,15},{24,28},{25,29},{26,30},{27,31}} | collective-permute-start | bytes 1572872 | tf_op jit(solution)/shard_map/ppermute | solution.py:23
  89.6 21.0 %collective-permute-start.26 = (bf16[1024,256]{1,0:T(8,128)(2,1)S(1)}, bf16[1024,256]{1,0:T(8,128)(2,1)S(1)}, u32[]{:S(2)}, u32[]{:S(2)}) collective-permute-start(bf16[1024,256]{1,0:T(8,128)(2,1)S(1)} %collective-permute-done.25), channel_id=1, source_target_pairs={{4,0},{5,1},{6,2},{7,3},{20,16},{21,17},{22,18},{23,19}} | collective-permute-start | bytes 1572872 | tf_op jit(solution)/shard_map/ppermute | solution.py:22
  91.0 21.2 %collective-permute-start.24 = (bf16[1024,256]{1,0:T(8,128)(2,1)S(1)}, bf16[1024,256]{1,0:T(8,128)(2,1)S(1)}, u32[]{:S(2)}, u32[]{:S(2)}) collective-permute-start(bf16[1024,256]{1,0:T(8,128)(2,1)S(1)} %collective-permute-done.23), channel_id=1, source_target_pairs={{8,12},{9,13},{10,14},{11,15},{24,28},{25,29},{26,30},{27,31}} | collective-permute-start | bytes 1572872 | tf_op jit(solution)/shard_map/ppermute | solution.py:23
  110.6 37.3 %collective-permute-start.8 = (bf16[3072,256]{1,0:T(8,128)(2,1)S(1)}, bf16[3072,256]{1,0:T(8,128)(2,1)S(1)}, u32[]{:S(2)}, u32[]{:S(2)}) collective-permute-start(bf16[3072,256]{1,0:T(8,128)(2,1)S(1)} %pad_maximum_fusion.2), channel_id=1, source_target_pairs={{0,16},{16,0},{1,17},{17,1},{2,18},{18,2},{3,19},{19,3},{4,20},{20... | collective-permute-start | bytes 4718600 | tf_op jit(solution)/shard_map/ppermute | solution.py:54
  112.4 66.9 %collective-permute-start.27 = (bf16[3072,256]{1,0:T(8,128)(2,1)S(1)}, bf16[3072,256]{1,0:T(8,128)(2,1)S(1)}, u32[]{:S(2)}, u32[]{:S(2)}) collective-permute-start(bf16[3072,256]{1,0:T(8,128)(2,1)S(1)} %pad_maximum_fusion.4), channel_id=1, source_target_pairs={{0,16},{16,0},{1,17},{17,1},{2,18},{18,2},{3,19},{19,3},{4,20},{20... | collective-permute-start | bytes 4718600 | tf_op jit(solution)/shard_map/ppermute | solution.py:54
  149.3 38.4 %collective-permute-start.9 = (bf16[384,512]{0,1:T(8,128)(2,1)S(1)}, bf16[384,512]{0,1:T(8,128)(2,1)S(1)}, u32[]{:S(2)}, u32[]{:S(2)}) collective-permute-start(bf16[384,512]{0,1:T(8,128)(2,1)S(1)} %pad_maximum_fusion.6), channel_id=1, source_target_pairs={{4,0},{8,4},{12,8},{5,1},{9,5},{13,9},{6,2},{10,6},{14,10},{7,3},{... | collective-permute-start | bytes 1179656 | tf_op jit(solution)/shard_map/ppermute | solution.py:22
  150.6 38.4 %collective-permute-start.10 = (bf16[384,512]{0,1:T(8,128)(2,1)S(1)}, bf16[384,512]{0,1:T(8,128)(2,1)S(1)}, u32[]{:S(2)}, u32[]{:S(2)}) collective-permute-start(bf16[384,512]{0,1:T(8,128)(2,1)S(1)} %pad_maximum_fusion.6), channel_id=1, source_target_pairs={{0,4},{4,8},{8,12},{1,5},{5,9},{9,13},{2,6},{6,10},{10,14},{3,7},{... | collective-permute-start | bytes 1179656 | tf_op jit(solution)/shard_map/ppermute | solution.py:23
  195.5 32.9 %collective-permute-start.34 = (bf16[3072,256]{1,0:T(8,128)(2,1)S(1)}, bf16[3072,256]{1,0:T(8,128)(2,1)}, u32[]{:S(2)}, u32[]{:S(2)}) collective-permute-start(bf16[3072,256]{1,0:T(8,128)(2,1)S(1)} %slice.22), channel_id=1, source_target_pairs={{0,16},{16,0},{1,17},{17,1},{2,18},{18,2},{3,19},{19,3},{4,20},{20... | collective-permute-start | bytes 4718600 | tf_op jit(solution)/shard_map/ppermute | solution.py:54
  (17 other events, 330.3 us)

commit v10 on v8

--- a/solution.py
+++ b/solution.py
@@ -49,7 +49,7 @@
     if after is not None:
         own = lax.optimization_barrier((own, after))[0]
     other = lax.ppermute(own[rows:], "groups", [(0, 1), (1, 0)])
-    return [own, jnp.concatenate([kept, other], axis=0)]
+    return [own, (kept, other)]
 
 
 def per_device(acts, w_query, w_key, w_value):
@@ -62,11 +62,16 @@
     if shared:
         block = jnp.roll(block, -lax.axis_index("seq") * w_query.shape[0], axis=1)
 
+    def product(piece):
+        if isinstance(piece, tuple):
+            kept, other = piece
+            rows = kept.shape[0]
+            early = jnp.dot(block[:, :rows], kept, preferred_element_type=jnp.float32)
+            return early + jnp.dot(block[:, rows:], other, preferred_element_type=jnp.float32)
+        return jnp.dot(block, piece, preferred_element_type=jnp.float32)
+
     def project(weight, after=None):
-        return [
-            jnp.dot(block, piece, preferred_element_type=jnp.float32).astype(jnp.bfloat16)
-            for piece in full_columns(weight, shared, after)
-        ]
+        return [product(piece).astype(jnp.bfloat16) for piece in full_columns(weight, shared, after)]
 
     key = jnp.concatenate(project(w_key), axis=1)
     value = jnp.concatenate(project(w_value), axis=1)

time: 227 us -> 228 us (level)
    all_gather x3, waiting for transfers between devices: 60.7 us -> 58.3 us  [full_columns(): own = lax.all_gather(own, 'seq', axis=0, tiled=True)]
    dot_general x6 -> x9, matrix products: 11.7 us -> 13.1 us  [the longest x3 6.59 us: product(): jnp.dot(block[:, rows:], other, preferred_element_type=jnp.float32)]
  transfers between devices with their start and end apart: 20 -> 20, of which waited for: 10 -> 10; matrix products, arithmetic and copies ran while one was open for 17% -> 18% of each run, Pallas kernels for 0% -> 0%
where the time goes in v10:
time: 228 us; the launch traced here: 225 us
  waiting for transfers between devices  130 us (57%)
  starting transfers between devices  29.4 us (13%)
  other arithmetic  26 us (11%)
  matrix products  17.1 us (8%)
  between operations  13.6 us (6%)
  local copies, waits for them, and re-layouts  8.29 us (4%)
    all_gather x3, waiting for transfers between devices, full_columns(): own = lax.all_gather(own, 'seq', axis=0, tiled=True)  58.3 us
    ppermute x6, waiting for transfers between devices, line_gather(): lax.ppermute(from_right[-1], 'seq', [(j, j - 1) for j in range(1, n - k +...  30.1 us
    ppermute x3, waiting for transfers between devices, full_columns(): other = lax.ppermute(own[rows:], 'groups', [(0, 1), (1, 0)])  23.1 us
    ppermute x2, waiting for transfers between devices, swap_gather(): other = lax.ppermute(piece, axis, [(0, 1), (1, 0)])  18.7 us
    ppermute x6, starting transfers between devices, line_gather(): lax.ppermute(from_left[-1], 'seq', [(j, j + 1) for j in range(k - 1, n -...  14.1 us
    concatenate x3, other arithmetic, full_columns(): own = jnp.roll(own, -lax.axis_index('seq') * rows, axis=0)  9.31 us
    ppermute x6, starting transfers between devices, line_gather(): lax.ppermute(from_right[-1], 'seq', [(j, j - 1) for j in range(1, n - k +...  7.72 us
    dot_general x3, matrix products, product(): jnp.dot(block[:, rows:], other, preferred_element_type=jnp.float32)  6.59 us
  transfers between devices with their start and end apart: 20, of which 10 were waited for; matrix products, arithmetic and copies ran while one was open for 18% of the time, Pallas kernels for 0%

profile of v10, /device:TPU:0, one launch (start us, length us, event | category | flops | bytes accessed | tf_op | source)
XLA Modules:
  0.0 224.6 jit_solution(14703766533001946385)
XLA Ops:
  8.7 3.0 %collective-permute-start = (bf16[192,2048]{1,0:T(8,128)(2,1)}, bf16[192,2048]{1,0:T(8,128)(2,1)}, u32[]{:S(2)}, u32[]{:S(2)}) collective-permute-start(bf16[192,2048]{1,0:T(8,128)(2,1)} %param.6), channel_id=1, source_target_pairs={{0,2},{2,0},{1,3},{3,1},{4,6},{6,4},{5,7},{7,5},{8,10},{10,8},{9,1... | collective-permute-start | bytes 2359304 | tf_op jit(solution)/shard_map/ppermute | solution.py:34
  11.7 1.9 constant_dynamic-slice_fusion
  13.7 15.9 %collective-permute-done = bf16[192,2048]{1,0:T(8,128)(2,1)} collective-permute-done((bf16[192,2048]{1,0:T(8,128)(2,1)}, bf16[192,2048]{1,0:T(8,128)(2,1)}, u32[]{:S(2)}, u32[]{:S(2)}) %collective-permute-start) | collective-permute-done | bytes 786464 | tf_op jit(solution)/shard_map/ppermute | solution.py:34
  33.0 2.8 %collective-permute-done.1 = bf16[384,2048]{1,0:T(8,128)(2,1)} collective-permute-done((bf16[384,2048]{1,0:T(8,128)(2,1)}, bf16[384,2048]{1,0:T(8,128)(2,1)}, u32[]{:S(2)}, u32[]{:S(2)}) %collective-permute-start.1) | collective-permute-done | bytes 1572896 | tf_op jit(solution)/shard_map/ppermute | solution.py:34
  35.9 4.0 %broadcast_select_fusion = (bf16[384,2048]{1,0:T(8,128)(2,1)}, bf16[384,2048]{1,0:T(8,128)(2,1)}) fusion(bf16[384,2048]{1,0:T(8,128)(2,1)} %collective-permute-done.1, pred[]{:T(512)S(6)} %eq.12, bf16[192,2048]{1,0:T(8,128)(2,1)S(1)} %get-tuple-element.11, bf16[192,2048]{1,0:T(8,128)(2,1)S(1)} %get-tuple-element.10), kind=kLoop, calls=%fused_computation.39 | loop fusion | flops 4718592 | bytes 6291457 | tf_op jit(solution)/shard_map/jit(_where)/select_n | solution.py:36
  39.9 17.7 %all-gather.4.cloned.1.call-done = bf16[4096,256]{1,0:T(8,128)(2,1)} async-done(((bf16[1024,256]{1,0:T(8,128)(2,1)}), bf16[4096,256]{1,0:T(8,128)(2,1)}) %all-gather.4.cloned.1.call-update) | async-done | bytes 2097168 | tf_op jit(solution)/shard_map/all_gather | solution.py:47
  57.6 3.0 %fusion.17 = bf16[4096,256]{1,0:T(8,128)(2,1)S(1)} fusion(s32[]{:T(128)S(6)} %select_n.103, bf16[4096,256]{1,0:T(8,128)(2,1)} %all-gather.4.cloned.1.call-done), kind=kLoop, calls=%fused_computation.29 | loop fusion | flops 4194304 | bytes 4194308 | tf_op jit(solution)/shard_map/jit(_roll_dynamic)/concatenate | solution.py:48
  63.3 40.5 %all-gather.8.cloned.1.call-done = bf16[4096,256]{1,0:T(8,128)(2,1)} async-done(((bf16[1024,256]{1,0:T(8,128)(2,1)}), bf16[4096,256]{1,0:T(8,128)(2,1)}) %all-gather.8.cloned.1.call-update) | async-done | bytes 2097168 | tf_op jit(solution)/shard_map/all_gather | solution.py:47
  103.9 3.2 %fusion.15 = bf16[4096,256]{1,0:T(8,128)(2,1)S(1)} fusion(s32[]{:T(128)S(6)} %select_n.103, bf16[4096,256]{1,0:T(8,128)(2,1)} %all-gather.8.cloned.1.call-done), kind=kLoop, calls=%fused_computation.27 | loop fusion | flops 4194304 | bytes 4194308 | tf_op jit(solution)/shard_map/jit(_roll_dynamic)/concatenate | solution.py:48
  107.1 1.5 collective-permute-start.9
  108.7 2.9 %fusion.6 = bf16[384,4096]{1,0:T(8,128)(2,1)S(1)} fusion(s32[]{:T(128)S(6)} %select_n.103, bf16[384,2048]{1,0:T(8,128)(2,1)S(1)} %copy-done.4, bf16[384,2048]{1,0:T(8,128)(2,1)S(1)} %copy-done.3), kind=kLoop, calls=%fused_computation.20 | loop fusion | flops 12582912 | bytes 6291460 | tf_op jit(solution)/shard_map/jit(_roll_dynamic)/concatenate | solution.py:63
  114.2 2.4 %fusion.22 = f32[384,256]{0,1:T(8,128)S(1)} fusion(bf16[3072,256]{1,0:T(8,128)(2,1)} %collective-permute-done.2, bf16[384,4096]{1,0:T(8,128)(2,1)S(1)} %fusion.6), kind=kOutput, calls=%fused_computation.34 | convolution fusion | flops 603979776 | bytes 4325376 | tf_op jit(solution)/shard_map/dot_general | solution.py:70
  119.2 5.3 %collective-permute-start.4 = (bf16[384,512]{0,1:T(8,128)(2,1)}, bf16[384,512]{0,1:T(8,128)(2,1)}, u32[]{:S(2)}, u32[]{:S(2)}) collective-permute-start(bf16[384,512]{0,1:T(8,128)(2,1)} %pad_maximum_fusion.3), channel_id=1, source_target_pairs={{0,4},{4,8},{8,12},{1,5},{5,9},{9,13},{2,6},{6,10},{10,14},{3,7},{... | collective-permute-start | bytes 1179656 | tf_op jit(solution)/shard_map/ppermute | solution.py:23
  124.5 18.8 %collective-permute-done.9 = bf16[3072,256]{1,0:T(8,128)(2,1)S(1)} collective-permute-done((bf16[3072,256]{1,0:T(8,128)(2,1)S(1)}, bf16[3072,256]{1,0:T(8,128)(2,1)S(1)}, u32[]{:S(2)}, u32[]{:S(2)}) %collective-permute-start.9) | collective-permute-done | bytes 1572896 | tf_op jit(solution)/shard_map/ppermute | solution.py:51
  146.2 4.6 %collective-permute-start.11 = (bf16[384,512]{0,1:T(8,128)(2,1)S(1)}, bf16[384,512]{0,1:T(8,128)(2,1)S(1)}, u32[]{:S(2)}, u32[]{:S(2)}) collective-permute-start(bf16[384,512]{0,1:T(8,128)(2,1)S(1)} %pad_maximum_fusion.4), channel_id=1, source_target_pairs={{0,4},{4,8},{8,12},{1,5},{5,9},{9,13},{2,6},{6,10},{10,14},{3,7},{... | collective-permute-start | bytes 1179656 | tf_op jit(solution)/shard_map/ppermute | solution.py:23
  153.6 11.9 %collective-permute-done.10 = bf16[384,512]{0,1:T(8,128)(2,1)S(1)} collective-permute-done((bf16[384,512]{0,1:T(8,128)(2,1)S(1)}, bf16[384,512]{0,1:T(8,128)(2,1)S(1)}, u32[]{:S(2)}, u32[]{:S(2)}) %collective-permute-start.10) | collective-permute-done | bytes 393248 | tf_op jit(solution)/shard_map/ppermute | solution.py:22
  168.2 3.2 %fusion.16 = bf16[4096,256]{1,0:T(8,128)(2,1)S(1)} fusion(s32[]{:T(128)S(6)} %select_n.103, bf16[4096,256]{1,0:T(8,128)(2,1)} %all-gather.6.cloned.1.call-done), kind=kLoop, calls=%fused_computation.28 | loop fusion | flops 4194304 | bytes 4194308 | tf_op jit(solution)/shard_map/jit(_roll_dynamic)/concatenate | solution.py:48
  172.7 1.5 collective-permute-start.16
  177.5 4.6 %collective-permute-done.14 = bf16[384,512]{0,1:T(8,128)(2,1)} collective-permute-done((bf16[384,512]{0,1:T(8,128)(2,1)S(1)}, bf16[384,512]{0,1:T(8,128)(2,1)}, u32[]{:S(2)}, u32[]{:S(2)}) %collective-permute-start.14) | collective-permute-done | bytes 393248 | tf_op jit(solution)/shard_map/ppermute | solution.py:22
  186.2 6.9 %collective-permute-done.8 = bf16[384,512]{0,1:T(8,128)(2,1)S(1)} collective-permute-done((bf16[384,512]{0,1:T(8,128)(2,1)}, bf16[384,512]{0,1:T(8,128)(2,1)S(1)}, u32[]{:S(2)}, u32[]{:S(2)}) %collective-permute-start.8) | collective-permute-done | bytes 393248 | tf_op jit(solution)/shard_map/ppermute | solution.py:22
  193.2 6.6 %collective-permute-done.15 = bf16[384,512]{0,1:T(8,128)(2,1)S(1)} collective-permute-done((bf16[384,512]{0,1:T(8,128)(2,1)}, bf16[384,512]{0,1:T(8,128)(2,1)S(1)}, u32[]{:S(2)}, u32[]{:S(2)}) %collective-permute-start.15) | collective-permute-done | bytes 393248 | tf_op jit(solution)/shard_map/ppermute | solution.py:22
  204.4 4.3 %collective-permute-done.16 = bf16[3072,256]{1,0:T(8,128)(2,1)} collective-permute-done((bf16[3072,256]{1,0:T(8,128)(2,1)}, bf16[3072,256]{1,0:T(8,128)(2,1)}, u32[]{:S(2)}, u32[]{:S(2)}) %collective-permute-start.16) | collective-permute-done | bytes 1572896 | tf_op jit(solution)/shard_map/ppermute | solution.py:51
  208.7 3.1 %fusion.18 = f32[384,256]{0,1:T(8,128)S(1)} fusion(bf16[3072,256]{1,0:T(8,128)(2,1)} %collective-permute-done.16, bf16[384,4096]{1,0:T(8,128)(2,1)} %copy-done.1), kind=kOutput, calls=%fused_computation.30 | convolution fusion | flops 603979776 | bytes 4325376 | tf_op jit(solution)/shard_map/dot_general | solution.py:70
  211.9 1.6 fusion.61
  (86 shorter events, 39.7 us)
Async XLA Ops:
  6.5 23.0 %copy-start.10 = (bf16[192,2048]{1,0:T(8,128)(2,1)S(1)}, bf16[192,2048]{1,0:T(8,128)(2,1)}, u32[]{:S(2)}) copy-start(bf16[192,2048]{1,0:T(8,128)(2,1)} %param.6) | copy-start | bytes 2359300
  6.5 51.1 %all-gather.4.cloned.1.call-start = ((), (), s32[]{:S(2)}) async-start(), calls=%async_computation | async-start | bytes 2621440 | tf_op jit(solution)/shard_map/all_gather | solution.py:47
  8.6 95.2 %all-gather.8.cloned.1.call-start = ((), (), s32[]{:S(2)}) async-start(), calls=%async_computation.2 | async-start | bytes 2621440 | tf_op jit(solution)/shard_map/all_gather | solution.py:47
  8.7 20.9 %collective-permute-start = (bf16[192,2048]{1,0:T(8,128)(2,1)}, bf16[192,2048]{1,0:T(8,128)(2,1)}, u32[]{:S(2)}, u32[]{:S(2)}) collective-permute-start(bf16[192,2048]{1,0:T(8,128)(2,1)} %param.6), channel_id=1, source_target_pairs={{0,2},{2,0},{1,3},{3,1},{4,6},{6,4},{5,7},{7,5},{8,10},{10,8},{9,1... | collective-permute-start | bytes 2359304 | tf_op jit(solution)/shard_map/ppermute | solution.py:34
  13.6 154.6 %all-gather.6.cloned.1.call-start = ((), (), s32[]{:S(2)}) async-start(), calls=%async_computation.1 | async-start | bytes 2621440 | tf_op jit(solution)/shard_map/all_gather | solution.py:47
  13.6 18.5 %copy-start.8 = (bf16[1024,512]{1,0:T(8,128)(2,1)S(1)}, bf16[1024,512]{1,0:T(8,128)(2,1)}, u32[]{:S(2)}) copy-start(bf16[1024,512]{1,0:T(8,128)(2,1)} %param.7) | copy-start | bytes 3145732
  32.1 3.8 %collective-permute-start.1 = (bf16[384,2048]{1,0:T(8,128)(2,1)}, bf16[384,2048]{1,0:T(8,128)(2,1)}, u32[]{:S(2)}, u32[]{:S(2)}) collective-permute-start(bf16[384,2048]{1,0:T(8,128)(2,1)} %pad_maximum_fusion), channel_id=1, source_target_pairs={{0,1},{1,0},{2,3},{3,2},{4,5},{5,4},{6,7},{7,6},{8,9},{9,8},{10,11... | collective-permute-start | bytes 4718600 | tf_op jit(solution)/shard_map/ppermute | solution.py:34
  61.9 52.3 %collective-permute-start.2 = (bf16[3072,256]{1,0:T(8,128)(2,1)}, bf16[3072,256]{1,0:T(8,128)(2,1)}, u32[]{:S(2)}, u32[]{:S(2)}) collective-permute-start(bf16[3072,256]{1,0:T(8,128)(2,1)} %slice.42), channel_id=1, source_target_pairs={{0,16},{16,0},{1,17},{17,1},{2,18},{18,2},{3,19},{19,3},{4,20},{20... | collective-permute-start | bytes 4718600 | tf_op jit(solution)/shard_map/ppermute | solution.py:51
  107.1 36.2 %collective-permute-start.9 = (bf16[3072,256]{1,0:T(8,128)(2,1)S(1)}, bf16[3072,256]{1,0:T(8,128)(2,1)S(1)}, u32[]{:S(2)}, u32[]{:S(2)}) collective-permute-start(bf16[3072,256]{1,0:T(8,128)(2,1)S(1)} %slice.43), channel_id=1, source_target_pairs={{0,16},{16,0},{1,17},{17,1},{2,18},{18,2},{3,19},{19,3},{4,20},{20... | collective-permute-start | bytes 4718600 | tf_op jit(solution)/shard_map/ppermute | solution.py:51
  111.6 32.8 %copy-start.1 = (bf16[384,4096]{1,0:T(8,128)(2,1)}, bf16[384,4096]{1,0:T(8,128)(2,1)S(1)}, u32[]{:S(2)}) copy-start(bf16[384,4096]{1,0:T(8,128)(2,1)S(1)} %fusion.6) | copy-start | bytes 9437188
  117.1 27.2 %copy-start.7 = (bf16[1024,512]{1,0:T(8,128)(2,1)S(1)}, bf16[1024,512]{1,0:T(8,128)(2,1)}, u32[]{:S(2)}) copy-start(bf16[1024,512]{1,0:T(8,128)(2,1)} %param.8) | copy-start | bytes 3145732
  117.9 32.9 %collective-permute-start.3 = (bf16[384,512]{0,1:T(8,128)(2,1)}, bf16[384,512]{0,1:T(8,128)(2,1)}, u32[]{:S(2)}, u32[]{:S(2)}) collective-permute-start(bf16[384,512]{0,1:T(8,128)(2,1)} %pad_maximum_fusion.3), channel_id=1, source_target_pairs={{4,0},{8,4},{12,8},{5,1},{9,5},{13,9},{6,2},{10,6},{14,10},{7,3},{... | collective-permute-start | bytes 1179656 | tf_op jit(solution)/shard_map/ppermute | solution.py:22
  119.2 32.9 %collective-permute-start.4 = (bf16[384,512]{0,1:T(8,128)(2,1)}, bf16[384,512]{0,1:T(8,128)(2,1)}, u32[]{:S(2)}, u32[]{:S(2)}) collective-permute-start(bf16[384,512]{0,1:T(8,128)(2,1)} %pad_maximum_fusion.3), channel_id=1, source_target_pairs={{0,4},{4,8},{8,12},{1,5},{5,9},{9,13},{2,6},{6,10},{10,14},{3,7},{... | collective-permute-start | bytes 1179656 | tf_op jit(solution)/shard_map/ppermute | solution.py:23
  144.9 20.6 %collective-permute-start.10 = (bf16[384,512]{0,1:T(8,128)(2,1)S(1)}, bf16[384,512]{0,1:T(8,128)(2,1)S(1)}, u32[]{:S(2)}, u32[]{:S(2)}) collective-permute-start(bf16[384,512]{0,1:T(8,128)(2,1)S(1)} %pad_maximum_fusion.4), channel_id=1, source_target_pairs={{4,0},{8,4},{12,8},{5,1},{9,5},{13,9},{6,2},{10,6},{14,10},{7,3},{... | collective-permute-start | bytes 1179656 | tf_op jit(solution)/shard_map/ppermute | solution.py:22
  146.2 20.6 %collective-permute-start.11 = (bf16[384,512]{0,1:T(8,128)(2,1)S(1)}, bf16[384,512]{0,1:T(8,128)(2,1)S(1)}, u32[]{:S(2)}, u32[]{:S(2)}) collective-permute-start(bf16[384,512]{0,1:T(8,128)(2,1)S(1)} %pad_maximum_fusion.4), channel_id=1, source_target_pairs={{0,4},{4,8},{8,12},{1,5},{5,9},{9,13},{2,6},{6,10},{10,14},{3,7},{... | collective-permute-start | bytes 1179656 | tf_op jit(solution)/shard_map/ppermute | solution.py:23
  150.8 24.6 %collective-permute-start.7 = (bf16[384,512]{0,1:T(8,128)(2,1)}, bf16[384,512]{0,1:T(8,128)(2,1)}, u32[]{:S(2)}, u32[]{:S(2)}) collective-permute-start(bf16[384,512]{0,1:T(8,128)(2,1)} %collective-permute-done.3), channel_id=1, source_target_pairs={{4,0},{8,4},{5,1},{9,5},{6,2},{10,6},{7,3},{11,7},{20,16},{24,20},... | collective-permute-start | bytes 1179656 | tf_op jit(solution)/shard_map/ppermute | solution.py:22
  152.2 24.6 %collective-permute-start.5 = (bf16[384,512]{0,1:T(8,128)(2,1)}, bf16[384,512]{0,1:T(8,128)(2,1)}, u32[]{:S(2)}, u32[]{:S(2)}) collective-permute-start(bf16[384,512]{0,1:T(8,128)(2,1)} %collective-permute-done.4), channel_id=1, source_target_pairs={{4,8},{8,12},{5,9},{9,13},{6,10},{10,14},{7,11},{11,15},{20,24},{2... | collective-permute-start | bytes 1179656 | tf_op jit(solution)/shard_map/ppermute | solution.py:23
  165.5 16.6 %collective-permute-start.14 = (bf16[384,512]{0,1:T(8,128)(2,1)S(1)}, bf16[384,512]{0,1:T(8,128)(2,1)}, u32[]{:S(2)}, u32[]{:S(2)}) collective-permute-start(bf16[384,512]{0,1:T(8,128)(2,1)S(1)} %collective-permute-done.10), channel_id=1, source_target_pairs={{4,0},{8,4},{5,1},{9,5},{6,2},{10,6},{7,3},{11,7},{20,16},{24,20},... | collective-permute-start | bytes 1179656 | tf_op jit(solution)/shard_map/ppermute | solution.py:22
  166.8 16.6 %collective-permute-start.12 = (bf16[384,512]{0,1:T(8,128)(2,1)S(1)}, bf16[384,512]{0,1:T(8,128)(2,1)}, u32[]{:S(2)}, u32[]{:S(2)}) collective-permute-start(bf16[384,512]{0,1:T(8,128)(2,1)S(1)} %collective-permute-done.11), channel_id=1, source_target_pairs={{4,8},{8,12},{5,9},{9,13},{6,10},{10,14},{7,11},{11,15},{20,24},{2... | collective-permute-start | bytes 1179656 | tf_op jit(solution)/shard_map/ppermute | solution.py:23
  172.7 36.0 %collective-permute-start.16 = (bf16[3072,256]{1,0:T(8,128)(2,1)}, bf16[3072,256]{1,0:T(8,128)(2,1)}, u32[]{:S(2)}, u32[]{:S(2)}) collective-permute-start(bf16[3072,256]{1,0:T(8,128)(2,1)} %slice.38), channel_id=1, source_target_pairs={{0,16},{16,0},{1,17},{17,1},{2,18},{18,2},{3,19},{19,3},{4,20},{20... | collective-permute-start | bytes 4718600 | tf_op jit(solution)/shard_map/ppermute | solution.py:51
  175.5 17.7 %collective-permute-start.8 = (bf16[384,512]{0,1:T(8,128)(2,1)}, bf16[384,512]{0,1:T(8,128)(2,1)S(1)}, u32[]{:S(2)}, u32[]{:S(2)}) collective-permute-start(bf16[384,512]{0,1:T(8,128)(2,1)} %collective-permute-done.7), channel_id=1, source_target_pairs={{4,0},{5,1},{6,2},{7,3},{20,16},{21,17},{22,18},{23,19}} | collective-permute-start | bytes 1179656 | tf_op jit(solution)/shard_map/ppermute | solution.py:22
  176.8 23.1 %collective-permute-start.6 = (bf16[384,512]{0,1:T(8,128)(2,1)}, bf16[384,512]{0,1:T(8,128)(2,1)S(1)}, u32[]{:S(2)}, u32[]{:S(2)}) collective-permute-start(bf16[384,512]{0,1:T(8,128)(2,1)} %collective-permute-done.5), channel_id=1, source_target_pairs={{8,12},{9,13},{10,14},{11,15},{24,28},{25,29},{26,30},{27,31}} | collective-permute-start | bytes 1179656 | tf_op jit(solution)/shard_map/ppermute | solution.py:23
  182.1 17.7 %collective-permute-start.15 = (bf16[384,512]{0,1:T(8,128)(2,1)}, bf16[384,512]{0,1:T(8,128)(2,1)S(1)}, u32[]{:S(2)}, u32[]{:S(2)}) collective-permute-start(bf16[384,512]{0,1:T(8,128)(2,1)} %collective-permute-done.14), channel_id=1, source_target_pairs={{4,0},{5,1},{6,2},{7,3},{20,16},{21,17},{22,18},{23,19}} | collective-permute-start | bytes 1179656 | tf_op jit(solution)/shard_map/ppermute | solution.py:22
  183.4 17.7 %collective-permute-start.13 = (bf16[384,512]{0,1:T(8,128)(2,1)}, bf16[384,512]{0,1:T(8,128)(2,1)S(1)}, u32[]{:S(2)}, u32[]{:S(2)}) collective-permute-start(bf16[384,512]{0,1:T(8,128)(2,1)} %collective-permute-done.12), channel_id=1, source_target_pairs={{8,12},{9,13},{10,14},{11,15},{24,28},{25,29},{26,30},{27,31}} | collective-permute-start | bytes 1179656 | tf_op jit(solution)/shard_map/ppermute | solution.py:23
  (9 other events, 49.8 us)
Sparse Core Ops, SparseCore 0:
  8.9 48.6 all-gather.3
  59.2 44.6 all-gather.7
  105.4 56.4 all-gather.5

commit v11 on v8

--- a/solution.py
+++ b/solution.py
@@ -48,8 +48,10 @@
     own = jnp.roll(own, -lax.axis_index("seq") * rows, axis=0)
     if after is not None:
         own = lax.optimization_barrier((own, after))[0]
-    other = lax.ppermute(own[rows:], "groups", [(0, 1), (1, 0)])
-    return [own, jnp.concatenate([kept, other], axis=0)]
+    split = rows + (own.shape[0] - rows) // 2
+    first = lax.ppermute(own[rows:split], "groups", [(0, 1), (1, 0)])
+    second = lax.ppermute(own[split:], "groups", [(0, 1), (1, 0)])
+    return [own, jnp.concatenate([kept, first, second], axis=0)]
 
 
 def per_device(acts, w_query, w_key, w_value):

time: 227 us -> 261 us (1.15); the launches traced: 223 us -> 260 us
  waiting for transfers between devices: 130 us -> 168 us
  matrix products: 15.7 us -> 21.4 us
  other arithmetic: 25.4 us -> 20.5 us
  starting transfers between devices: 30.9 us -> 27.5 us
    all_gather x3, waiting for transfers between devices: 60.7 us -> 99.2 us  [full_columns(): own = lax.all_gather(own, 'seq', axis=0, tiled=True)]
    ppermute x6, waiting for transfers between devices: 28.1 us -> 15.3 us  [line_gather(): lax.ppermute(from_right[-1], 'seq', [(j, j - 1) for j in range(1, n - k +...]
    ppermute x3 -> x6, waiting for transfers between devices: 22.4 us -> 30.5 us  [the longest x3 29.8 us: full_columns(): first = lax.ppermute(own[rows:split], 'groups', [(0, 1), (1, 0)])]
    dot_general x6, matrix products: 11.7 us -> 16.7 us  [project(): jnp.dot(block, piece, preferred_element_type=jnp.float32)]
    ppermute x6, starting transfers between devices: 15.1 us -> 10.5 us  [line_gather(): lax.ppermute(from_left[-1], 'seq', [(j, j + 1) for j in range(k - 1, n -...]
    ppermute x6, waiting for transfers between devices: 0.02 us -> 2.73 us  [line_gather(): lax.ppermute(from_left[-1], 'seq', [(j, j + 1) for j in range(k - 1, n -...]
    concatenate x3 -> x2, other arithmetic: 9.16 us -> 6.88 us  [full_columns(): own = jnp.roll(own, -lax.axis_index('seq') * rows, axis=0)]
    ppermute x3 -> x6, starting transfers between devices: 4.49 us -> 6.08 us  [the longest x3 4.43 us: full_columns(): second = lax.ppermute(own[split:], 'groups', [(0, 1), (1, 0)])]
  transfers between devices with their start and end apart: 20 -> 23, of which waited for: 10 -> 12; matrix products, arithmetic and copies ran while one was open for 17% -> 16% of each run, Pallas kernels for 0% -> 0%
where the time goes in v11:
time: 261 us; the launch traced here: 260 us
  waiting for transfers between devices  168 us (64%)
  starting transfers between devices  27.5 us (11%)
  matrix products  21.4 us (8%)
  other arithmetic  20.5 us (8%)
  between operations  13.6 us (5%)
  local copies, waits for them, and re-layouts  9.45 us (4%)
    all_gather x3, waiting for transfers between devices, full_columns(): own = lax.all_gather(own, 'seq', axis=0, tiled=True)  99.2 us
    ppermute x3, waiting for transfers between devices, full_columns(): first = lax.ppermute(own[rows:split], 'groups', [(0, 1), (1, 0)])  29.8 us
    ppermute x2, waiting for transfers between devices, swap_gather(): other = lax.ppermute(piece, axis, [(0, 1), (1, 0)])  19.9 us
    dot_general x6, matrix products, project(): jnp.dot(block, piece, preferred_element_type=jnp.float32)  16.7 us
    ppermute x6, waiting for transfers between devices, line_gather(): lax.ppermute(from_right[-1], 'seq', [(j, j - 1) for j in range(1, n - k +...  15.3 us
    ppermute x6, starting transfers between devices, line_gather(): lax.ppermute(from_left[-1], 'seq', [(j, j + 1) for j in range(k - 1, n -...  10.5 us
    ppermute x6, starting transfers between devices, line_gather(): lax.ppermute(from_right[-1], 'seq', [(j, j - 1) for j in range(1, n - k +...  7.71 us
    concatenate x2, other arithmetic, full_columns(): own = jnp.roll(own, -lax.axis_index('seq') * rows, axis=0)  6.88 us
  transfers between devices with their start and end apart: 23, of which 12 were waited for; matrix products, arithmetic and copies ran while one was open for 16% of the time, Pallas kernels for 0%

profile of v11, /device:TPU:0, one launch (start us, length us, event | category | flops | bytes accessed | tf_op | source)
XLA Modules:
  0.0 260.2 jit_solution(10549199281910649526)
XLA Ops:
  6.5 2.4 constant_dynamic-slice_fusion.1
  10.1 3.0 %collective-permute-start = (bf16[192,2048]{1,0:T(8,128)(2,1)S(1)}, bf16[192,2048]{1,0:T(8,128)(2,1)S(1)}, u32[]{:S(2)}, u32[]{:S(2)}) collective-permute-start(bf16[192,2048]{1,0:T(8,128)(2,1)S(1)} %copy-done.8), channel_id=1, source_target_pairs={{0,2},{2,0},{1,3},{3,1},{4,6},{6,4},{5,7},{7,5},{8,10},{10,8},{9,1... | collective-permute-start | bytes 2359304 | tf_op jit(solution)/shard_map/ppermute | solution.py:34
  13.2 17.5 %collective-permute-done = bf16[192,2048]{1,0:T(8,128)(2,1)S(1)} collective-permute-done((bf16[192,2048]{1,0:T(8,128)(2,1)S(1)}, bf16[192,2048]{1,0:T(8,128)(2,1)S(1)}, u32[]{:S(2)}, u32[]{:S(2)}) %collective-permute-start) | collective-permute-done | bytes 786464 | tf_op jit(solution)/shard_map/ppermute | solution.py:34
  32.1 2.4 collective-permute-done.1
  34.6 2.2 broadcast_select_fusion
  36.8 4.1 %fusion.6 = bf16[384,4096]{1,0:T(8,128)(2,1)} fusion(s32[]{:T(128)S(6)} %select_n.103, bf16[384,2048]{1,0:T(8,128)(2,1)S(1)} %get-tuple-element.9, bf16[384,2048]{1,0:T(8,128)(2,1)S(1)} %get-tuple-element.8), kind=kLoop, calls=%fused_computation.20 | loop fusion | flops 12582912 | bytes 6291460 | tf_op jit(solution)/shard_map/jit(_roll_dynamic)/concatenate | solution.py:65
  40.9 16.8 %all-gather.8.cloned.1.call-done = bf16[4096,256]{1,0:T(8,128)(2,1)} async-done(((bf16[1024,256]{1,0:T(8,128)(2,1)}), bf16[4096,256]{1,0:T(8,128)(2,1)}) %all-gather.8.cloned.1.call-update) | async-done | bytes 2097168 | tf_op jit(solution)/shard_map/all_gather | solution.py:47
  57.7 46.3 %all-gather.4.cloned.1.call-done = bf16[4096,256]{1,0:T(8,128)(2,1)} async-done(((bf16[1024,256]{1,0:T(8,128)(2,1)}), bf16[4096,256]{1,0:T(8,128)(2,1)}) %all-gather.4.cloned.1.call-update) | async-done | bytes 2097168 | tf_op jit(solution)/shard_map/all_gather | solution.py:47
  104.0 3.7 %fusion.15 = (bf16[4096,256]{1,0:T(8,128)(2,1)S(1)}, bf16[4096,256]{1,0:T(8,128)(2,1)S(1)}) fusion(s32[]{:T(128)S(6)} %select_n.103, bf16[4096,256]{1,0:T(8,128)(2,1)} %all-gather.8.cloned.1.call-done, bf16[4096,256]{1,0:T(8,128)(2,1)} %all-gather.4.cloned.1.call-done), kind=kLoop, calls=%fused_computation.27 | loop fusion | flops 8388608 | bytes 8388612 | tf_op jit(solution)/shard_map/jit(_roll_dynamic)/concatenate | solution.py:48
  114.1 36.1 %all-gather.6.cloned.1.call-done = bf16[4096,256]{1,0:T(8,128)(2,1)} async-done(((bf16[1024,256]{1,0:T(8,128)(2,1)}), bf16[4096,256]{1,0:T(8,128)(2,1)}) %all-gather.6.cloned.1.call-update) | async-done | bytes 2097168 | tf_op jit(solution)/shard_map/all_gather | solution.py:47
  150.2 3.2 %fusion.16 = bf16[4096,256]{1,0:T(8,128)(2,1)S(1)} fusion(s32[]{:T(128)S(6)} %select_n.103, bf16[4096,256]{1,0:T(8,128)(2,1)} %all-gather.6.cloned.1.call-done), kind=kLoop, calls=%fused_computation.28 | loop fusion | flops 4194304 | bytes 4194308 | tf_op jit(solution)/shard_map/jit(_roll_dynamic)/concatenate | solution.py:48
  153.4 3.3 %convolution_convert_fusion.2 = bf16[384,256]{0,1:T(8,128)(2,1)S(1)} fusion(bf16[384,4096]{1,0:T(8,128)(2,1)} %fusion.6, bf16[4096,256]{1,0:T(8,128)(2,1)S(1)} %copy-done.3), kind=kOutput, calls=%fused_computation.60 | convolution fusion | flops 805404672 | bytes 5439488 | tf_op jit(solution)/shard_map/dot_general | solution.py:69
  158.2 2.7 %fusion.48 = bf16[384,256]{0,1:T(8,128)(2,1)S(1)} fusion(bf16[384,4096]{1,0:T(8,128)(2,1)S(1)} %copy-done.4, bf16[1536,256]{1,0:T(8,128)(2,1)} %collective-permute-done.3, bf16[1536,256]{1,0:T(8,128)(2,1)} %collective-permute-done.2, bf16[1024,256]{1,0:T(8,128)(2,1)S(1)} %copy-done.11), kind=kOutput, calls=%fused_computation.57 | convolution fusion | flops 811696128 | bytes 5439488 | tf_op jit(solution)/shard_map/dot_general | solution.py:69
  163.5 15.7 %collective-permute-done.10 = bf16[1536,256]{1,0:T(8,128)(2,1)} collective-permute-done((bf16[1536,256]{1,0:T(8,128)(2,1)S(1)}, bf16[1536,256]{1,0:T(8,128)(2,1)}, u32[]{:S(2)}, u32[]{:S(2)}) %collective-permute-start.10) | collective-permute-done | bytes 786464 | tf_op jit(solution)/shard_map/ppermute | solution.py:52
  179.2 2.7 %fusion.45 = bf16[384,256]{0,1:T(8,128)(2,1)S(1)} fusion(bf16[384,4096]{1,0:T(8,128)(2,1)S(1)} %copy-done.4, bf16[1536,256]{1,0:T(8,128)(2,1)} %collective-permute-done.11, bf16[1536,256]{1,0:T(8,128)(2,1)} %collective-permute-done.10, bf16[1024,256]{1,0:T(8,128)(2,1)S(1)} %copy-done.10), kind=kOutput, calls=%fused_computation.56 | convolution fusion | flops 811696128 | bytes 5439488 | tf_op jit(solution)/shard_map/dot_general | solution.py:69
  184.0 1.5 collective-permute-start.19
  186.1 2.5 collective-permute-start.5
  189.8 5.3 %collective-permute-start.13 = (bf16[384,512]{0,1:T(8,128)(2,1)}, bf16[384,512]{0,1:T(8,128)(2,1)}, u32[]{:S(2)}, u32[]{:S(2)}) collective-permute-start(bf16[384,512]{0,1:T(8,128)(2,1)} %pad_maximum_fusion.4), channel_id=1, source_target_pairs={{0,4},{4,8},{8,12},{1,5},{5,9},{9,13},{2,6},{6,10},{10,14},{3,7},{... | collective-permute-start | bytes 1179656 | tf_op jit(solution)/shard_map/ppermute | solution.py:23
  195.2 3.3 %convolution_convert_fusion = bf16[384,256]{0,1:T(8,128)(2,1)S(1)} fusion(bf16[384,4096]{1,0:T(8,128)(2,1)} %fusion.6, bf16[4096,256]{1,0:T(8,128)(2,1)S(1)} %fusion.16), kind=kOutput, calls=%fused_computation.58 | convolution fusion | flops 805404672 | bytes 5439488 | tf_op jit(solution)/shard_map/dot_general | solution.py:69
  200.6 2.7 %collective-permute-done.13 = bf16[384,512]{0,1:T(8,128)(2,1)} collective-permute-done((bf16[384,512]{0,1:T(8,128)(2,1)}, bf16[384,512]{0,1:T(8,128)(2,1)}, u32[]{:S(2)}, u32[]{:S(2)}) %collective-permute-start.13) | collective-permute-done | bytes 393248 | tf_op jit(solution)/shard_map/ppermute | solution.py:23
  205.5 14.1 %collective-permute-done.18 = bf16[1536,256]{1,0:T(8,128)(2,1)} collective-permute-done((bf16[1536,256]{1,0:T(8,128)(2,1)}, bf16[1536,256]{1,0:T(8,128)(2,1)}, u32[]{:S(2)}, u32[]{:S(2)}) %collective-permute-start.18) | collective-permute-done | bytes 786464 | tf_op jit(solution)/shard_map/ppermute | solution.py:52
  219.6 3.3 %fusion.42 = bf16[384,256]{0,1:T(8,128)(2,1)} fusion(bf16[384,4096]{1,0:T(8,128)(2,1)S(1)} %copy-done.5, bf16[1536,256]{1,0:T(8,128)(2,1)} %collective-permute-done.19, bf16[1536,256]{1,0:T(8,128)(2,1)} %collective-permute-done.18, bf16[1024,256]{1,0:T(8,128)(2,1)S(1)} %copy-done.9), kind=kOutput, calls=%fused_computation.55 | convolution fusion | flops 811696128 | bytes 5439488 | tf_op jit(solution)/shard_map/dot_general | solution.py:69
  227.1 15.3 %collective-permute-done.17 = bf16[384,512]{0,1:T(8,128)(2,1)S(1)} collective-permute-done((bf16[384,512]{0,1:T(8,128)(2,1)S(1)}, bf16[384,512]{0,1:T(8,128)(2,1)S(1)}, u32[]{:S(2)}, u32[]{:S(2)}) %collective-permute-start.17) | collective-permute-done | bytes 393248 | tf_op jit(solution)/shard_map/ppermute | solution.py:22
  246.7 1.8 fusion.60
  (88 shorter events, 34.7 us)
Async XLA Ops:
  6.5 51.2 %all-gather.8.cloned.1.call-start = ((), (), s32[]{:S(2)}) async-start(), calls=%async_computation.2 | async-start | bytes 2621440 | tf_op jit(solution)/shard_map/all_gather | solution.py:47
  8.9 95.0 %all-gather.4.cloned.1.call-start = ((), (), s32[]{:S(2)}) async-start(), calls=%async_computation | async-start | bytes 2621440 | tf_op jit(solution)/shard_map/all_gather | solution.py:47
  10.1 140.2 %all-gather.6.cloned.1.call-start = ((), (), s32[]{:S(2)}) async-start(), calls=%async_computation.1 | async-start | bytes 2621440 | tf_op jit(solution)/shard_map/all_gather | solution.py:47
  10.1 20.5 %collective-permute-start = (bf16[192,2048]{1,0:T(8,128)(2,1)S(1)}, bf16[192,2048]{1,0:T(8,128)(2,1)S(1)}, u32[]{:S(2)}, u32[]{:S(2)}) collective-permute-start(bf16[192,2048]{1,0:T(8,128)(2,1)S(1)} %copy-done.8), channel_id=1, source_target_pairs={{0,2},{2,0},{1,3},{3,1},{4,6},{6,4},{5,7},{7,5},{8,10},{10,8},{9,1... | collective-permute-start | bytes 2359304 | tf_op jit(solution)/shard_map/ppermute | solution.py:34
  31.0 3.6 %collective-permute-start.1 = (bf16[384,2048]{1,0:T(8,128)(2,1)S(1)}, bf16[384,2048]{1,0:T(8,128)(2,1)}, u32[]{:S(2)}, u32[]{:S(2)}) collective-permute-start(bf16[384,2048]{1,0:T(8,128)(2,1)S(1)} %pad_maximum_fusion), channel_id=1, source_target_pairs={{0,1},{1,0},{2,3},{3,2},{4,5},{5,4},{6,7},{7,6},{8,9},{9,8},{10,11... | collective-permute-start | bytes 4718600 | tf_op jit(solution)/shard_map/ppermute | solution.py:34
  109.1 49.1 %collective-permute-start.3 = (bf16[1536,256]{1,0:T(8,128)(2,1)}, bf16[1536,256]{1,0:T(8,128)(2,1)}, u32[]{:S(2)}, u32[]{:S(2)}) collective-permute-start(bf16[1536,256]{1,0:T(8,128)(2,1)} %get-tuple-element.15), channel_id=1, source_target_pairs={{0,16},{16,0},{1,17},{17,1},{2,18},{18,2},{3,19},{19,3},{4,20},{20... | collective-permute-start | bytes 2359304 | tf_op jit(solution)/shard_map/ppermute | solution.py:53
  110.5 47.7 %collective-permute-start.2 = (bf16[1536,256]{1,0:T(8,128)(2,1)}, bf16[1536,256]{1,0:T(8,128)(2,1)}, u32[]{:S(2)}, u32[]{:S(2)}) collective-permute-start(bf16[1536,256]{1,0:T(8,128)(2,1)} %get-tuple-element.14), channel_id=1, source_target_pairs={{0,16},{16,0},{1,17},{17,1},{2,18},{18,2},{3,19},{19,3},{4,20},{20... | collective-permute-start | bytes 2359304 | tf_op jit(solution)/shard_map/ppermute | solution.py:52
  112.1 51.4 %collective-permute-start.11 = (bf16[1536,256]{1,0:T(8,128)(2,1)}, bf16[1536,256]{1,0:T(8,128)(2,1)}, u32[]{:S(2)}, u32[]{:S(2)}) collective-permute-start(bf16[1536,256]{1,0:T(8,128)(2,1)} %get-tuple-element.13), channel_id=1, source_target_pairs={{0,16},{16,0},{1,17},{17,1},{2,18},{18,2},{3,19},{19,3},{4,20},{20... | collective-permute-start | bytes 2359304 | tf_op jit(solution)/shard_map/ppermute | solution.py:53
  113.6 65.7 %collective-permute-start.10 = (bf16[1536,256]{1,0:T(8,128)(2,1)S(1)}, bf16[1536,256]{1,0:T(8,128)(2,1)}, u32[]{:S(2)}, u32[]{:S(2)}) collective-permute-start(bf16[1536,256]{1,0:T(8,128)(2,1)S(1)} %get-tuple-element.12), channel_id=1, source_target_pairs={{0,16},{16,0},{1,17},{17,1},{2,18},{18,2},{3,19},{19,3},{4,20},{20... | collective-permute-start | bytes 2359304 | tf_op jit(solution)/shard_map/ppermute | solution.py:52
  161.7 28.1 %collective-permute-start.4 = (bf16[384,512]{0,1:T(8,128)(2,1)}, bf16[384,512]{0,1:T(8,128)(2,1)}, u32[]{:S(2)}, u32[]{:S(2)}) collective-permute-start(bf16[384,512]{0,1:T(8,128)(2,1)} %pad_maximum_fusion.3), channel_id=1, source_target_pairs={{4,0},{8,4},{12,8},{5,1},{9,5},{13,9},{6,2},{10,6},{14,10},{7,3},{... | collective-permute-start | bytes 1179656 | tf_op jit(solution)/shard_map/ppermute | solution.py:22
  184.0 20.8 %collective-permute-start.19 = (bf16[1536,256]{1,0:T(8,128)(2,1)}, bf16[1536,256]{1,0:T(8,128)(2,1)}, u32[]{:S(2)}, u32[]{:S(2)}) collective-permute-start(bf16[1536,256]{1,0:T(8,128)(2,1)} %get-tuple-element.11), channel_id=1, source_target_pairs={{0,16},{16,0},{1,17},{17,1},{2,18},{18,2},{3,19},{19,3},{4,20},{20... | collective-permute-start | bytes 2359304 | tf_op jit(solution)/shard_map/ppermute | solution.py:53
  185.5 34.1 %collective-permute-start.18 = (bf16[1536,256]{1,0:T(8,128)(2,1)}, bf16[1536,256]{1,0:T(8,128)(2,1)}, u32[]{:S(2)}, u32[]{:S(2)}) collective-permute-start(bf16[1536,256]{1,0:T(8,128)(2,1)} %get-tuple-element.10), channel_id=1, source_target_pairs={{0,16},{16,0},{1,17},{17,1},{2,18},{18,2},{3,19},{19,3},{4,20},{20... | collective-permute-start | bytes 2359304 | tf_op jit(solution)/shard_map/ppermute | solution.py:52
  186.1 12.4 %collective-permute-start.5 = (bf16[384,512]{0,1:T(8,128)(2,1)}, bf16[384,512]{0,1:T(8,128)(2,1)}, u32[]{:S(2)}, u32[]{:S(2)}) collective-permute-start(bf16[384,512]{0,1:T(8,128)(2,1)} %pad_maximum_fusion.3), channel_id=1, source_target_pairs={{0,4},{4,8},{8,12},{1,5},{5,9},{9,13},{2,6},{6,10},{10,14},{3,7},{... | collective-permute-start | bytes 1179656 | tf_op jit(solution)/shard_map/ppermute | solution.py:23
  188.5 11.4 %collective-permute-start.12 = (bf16[384,512]{0,1:T(8,128)(2,1)}, bf16[384,512]{0,1:T(8,128)(2,1)}, u32[]{:S(2)}, u32[]{:S(2)}) collective-permute-start(bf16[384,512]{0,1:T(8,128)(2,1)} %pad_maximum_fusion.4), channel_id=1, source_target_pairs={{4,0},{8,4},{12,8},{5,1},{9,5},{13,9},{6,2},{10,6},{14,10},{7,3},{... | collective-permute-start | bytes 1179656 | tf_op jit(solution)/shard_map/ppermute | solution.py:22
  189.8 13.5 %collective-permute-start.13 = (bf16[384,512]{0,1:T(8,128)(2,1)}, bf16[384,512]{0,1:T(8,128)(2,1)}, u32[]{:S(2)}, u32[]{:S(2)}) collective-permute-start(bf16[384,512]{0,1:T(8,128)(2,1)} %pad_maximum_fusion.4), channel_id=1, source_target_pairs={{0,4},{4,8},{8,12},{1,5},{5,9},{9,13},{2,6},{6,10},{10,14},{3,7},{... | collective-permute-start | bytes 1179656 | tf_op jit(solution)/shard_map/ppermute | solution.py:23
  195.2 24.5 %copy-start.9 = (bf16[1024,256]{1,0:T(8,128)(2,1)S(1)}, bf16[1024,256]{1,0:T(8,128)(2,1)}, u32[]{:S(2)}) copy-start(bf16[1024,256]{1,0:T(8,128)(2,1)} %get-tuple-element.18) | copy-start | bytes 1572868
  198.5 24.5 %collective-permute-start.8 = (bf16[384,512]{0,1:T(8,128)(2,1)}, bf16[384,512]{0,1:T(8,128)(2,1)S(1)}, u32[]{:S(2)}, u32[]{:S(2)}) collective-permute-start(bf16[384,512]{0,1:T(8,128)(2,1)} %collective-permute-done.4), channel_id=1, source_target_pairs={{4,0},{8,4},{5,1},{9,5},{6,2},{10,6},{7,3},{11,7},{20,16},{24,20},... | collective-permute-start | bytes 1179656 | tf_op jit(solution)/shard_map/ppermute | solution.py:22
  199.9 24.4 %collective-permute-start.6 = (bf16[384,512]{0,1:T(8,128)(2,1)}, bf16[384,512]{0,1:T(8,128)(2,1)S(1)}, u32[]{:S(2)}, u32[]{:S(2)}) collective-permute-start(bf16[384,512]{0,1:T(8,128)(2,1)} %collective-permute-done.5), channel_id=1, source_target_pairs={{4,8},{8,12},{5,9},{9,13},{6,10},{10,14},{7,11},{11,15},{20,24},{2... | collective-permute-start | bytes 1179656 | tf_op jit(solution)/shard_map/ppermute | solution.py:23
  203.3 21.7 %collective-permute-start.16 = (bf16[384,512]{0,1:T(8,128)(2,1)}, bf16[384,512]{0,1:T(8,128)(2,1)S(1)}, u32[]{:S(2)}, u32[]{:S(2)}) collective-permute-start(bf16[384,512]{0,1:T(8,128)(2,1)} %collective-permute-done.12), channel_id=1, source_target_pairs={{4,0},{8,4},{5,1},{9,5},{6,2},{10,6},{7,3},{11,7},{20,16},{24,20},... | collective-permute-start | bytes 1179656 | tf_op jit(solution)/shard_map/ppermute | solution.py:22
  204.8 21.5 %collective-permute-start.14 = (bf16[384,512]{0,1:T(8,128)(2,1)}, bf16[384,512]{0,1:T(8,128)(2,1)S(1)}, u32[]{:S(2)}, u32[]{:S(2)}) collective-permute-start(bf16[384,512]{0,1:T(8,128)(2,1)} %collective-permute-done.13), channel_id=1, source_target_pairs={{4,8},{8,12},{5,9},{9,13},{6,10},{10,14},{7,11},{11,15},{20,24},{2... | collective-permute-start | bytes 1179656 | tf_op jit(solution)/shard_map/ppermute | solution.py:23
  223.0 21.5 %collective-permute-start.9 = (bf16[384,512]{0,1:T(8,128)(2,1)S(1)}, bf16[384,512]{0,1:T(8,128)(2,1)S(1)}, u32[]{:S(2)}, u32[]{:S(2)}) collective-permute-start(bf16[384,512]{0,1:T(8,128)(2,1)S(1)} %collective-permute-done.8), channel_id=1, source_target_pairs={{4,0},{5,1},{6,2},{7,3},{20,16},{21,17},{22,18},{23,19}} | collective-permute-start | bytes 1179656 | tf_op jit(solution)/shard_map/ppermute | solution.py:22
  224.3 21.2 %collective-permute-start.7 = (bf16[384,512]{0,1:T(8,128)(2,1)S(1)}, bf16[384,512]{0,1:T(8,128)(2,1)S(1)}, u32[]{:S(2)}, u32[]{:S(2)}) collective-permute-start(bf16[384,512]{0,1:T(8,128)(2,1)S(1)} %collective-permute-done.6), channel_id=1, source_target_pairs={{8,12},{9,13},{10,14},{11,15},{24,28},{25,29},{26,30},{27,31}} | collective-permute-start | bytes 1179656 | tf_op jit(solution)/shard_map/ppermute | solution.py:23
  225.0 17.4 %collective-permute-start.17 = (bf16[384,512]{0,1:T(8,128)(2,1)S(1)}, bf16[384,512]{0,1:T(8,128)(2,1)S(1)}, u32[]{:S(2)}, u32[]{:S(2)}) collective-permute-start(bf16[384,512]{0,1:T(8,128)(2,1)S(1)} %collective-permute-done.16), channel_id=1, source_target_pairs={{4,0},{5,1},{6,2},{7,3},{20,16},{21,17},{22,18},{23,19}} | collective-permute-start | bytes 1179656 | tf_op jit(solution)/shard_map/ppermute | solution.py:22
  226.3 16.1 %collective-permute-start.15 = (bf16[384,512]{0,1:T(8,128)(2,1)S(1)}, bf16[384,512]{0,1:T(8,128)(2,1)S(1)}, u32[]{:S(2)}, u32[]{:S(2)}) collective-permute-start(bf16[384,512]{0,1:T(8,128)(2,1)S(1)} %collective-permute-done.14), channel_id=1, source_target_pairs={{8,12},{9,13},{10,14},{11,15},{24,28},{25,29},{26,30},{27,31}} | collective-permute-start | bytes 1179656 | tf_op jit(solution)/shard_map/ppermute | solution.py:23
  (12 other events, 92.3 us)
Sparse Core Ops, SparseCore 0:
  9.0 48.6 all-gather.7
  59.3 44.6 all-gather.3
  105.6 44.6 all-gather.5

commit v12 on v11

--- a/solution.py
+++ b/solution.py
@@ -45,9 +45,9 @@
     own = lax.dynamic_slice_in_dim(weight, group * half, half, axis=1)
     kept = lax.dynamic_slice_in_dim(weight, (1 - group) * half, half, axis=1)
     own = lax.all_gather(own, "seq", axis=0, tiled=True)
-    own = jnp.roll(own, -lax.axis_index("seq") * rows, axis=0)
     if after is not None:
         own = lax.optimization_barrier((own, after))[0]
+    own = jnp.roll(own, -lax.axis_index("seq") * rows, axis=0)
     split = rows + (own.shape[0] - rows) // 2
     first = lax.ppermute(own[rows:split], "groups", [(0, 1), (1, 0)])
     second = lax.ppermute(own[split:], "groups", [(0, 1), (1, 0)])

time: 261 us -> 268 us (1.027); the launches traced: 260 us -> 263 us
  waiting for transfers between devices: 168 us -> 187 us
  matrix products: 21.4 us -> 14.1 us
  local copies, waits for them, and re-layouts: 9.45 us -> 5.14 us
  other arithmetic: 20.5 us -> 16.8 us
    ppermute x3, waiting for transfers between devices: 0.73 us -> 40.5 us  [full_columns(): second = lax.ppermute(own[split:], 'groups', [(0, 1), (1, 0)])]
    all_gather x3, waiting for transfers between devices: 99.2 us -> 66.9 us  [full_columns(): own = lax.all_gather(own, 'seq', axis=0, tiled=True)]
    ppermute x3, waiting for transfers between devices: 29.8 us -> 44.4 us  [full_columns(): first = lax.ppermute(own[rows:split], 'groups', [(0, 1), (1, 0)])]
    dot_general x6, matrix products: 16.7 us -> 7.78 us  [project(): jnp.dot(block, piece, preferred_element_type=jnp.float32)]
    slice x3, local copies, waits for them, and re-layouts: 3.63 us -> 0.31 us  [full_columns(): first = lax.ppermute(own[rows:split], 'groups', [(0, 1), (1, 0)])]
    ppermute x6, waiting for transfers between devices: 2.73 us -> 0.02 us  [line_gather(): lax.ppermute(from_left[-1], 'seq', [(j, j + 1) for j in range(k - 1, n -...]
  transfers between devices with their start and end apart: 23 -> 23, of which waited for: 12 -> 13; matrix products, arithmetic and copies ran while one was open for 16% -> 10% of each run, Pallas kernels for 0% -> 0%
where the time goes in v12:
time: 268 us; the launch traced here: 263 us
  waiting for transfers between devices  187 us (70%)
  starting transfers between devices  26.5 us (10%)
  other arithmetic  16.8 us (6%)
  matrix products  14.1 us (5%)
  between operations  13.6 us (5%)
  local copies, waits for them, and re-layouts  5.14 us (2%)
    all_gather x3, waiting for transfers between devices, full_columns(): own = lax.all_gather(own, 'seq', axis=0, tiled=True)  66.9 us
    ppermute x3, waiting for transfers between devices, full_columns(): first = lax.ppermute(own[rows:split], 'groups', [(0, 1), (1, 0)])  44.4 us
    ppermute x3, waiting for transfers between devices, full_columns(): second = lax.ppermute(own[split:], 'groups', [(0, 1), (1, 0)])  40.5 us
    ppermute x2, waiting for transfers between devices, swap_gather(): other = lax.ppermute(piece, axis, [(0, 1), (1, 0)])  19.9 us
    ppermute x6, waiting for transfers between devices, line_gather(): lax.ppermute(from_right[-1], 'seq', [(j, j - 1) for j in range(1, n - k +...  14.9 us
    ppermute x6, starting transfers between devices, line_gather(): lax.ppermute(from_left[-1], 'seq', [(j, j + 1) for j in range(k - 1, n -...  9.14 us
    ppermute x6, starting transfers between devices, line_gather(): lax.ppermute(from_right[-1], 'seq', [(j, j - 1) for j in range(1, n - k +...  7.92 us
    dot_general x6, matrix products, project(): jnp.dot(block, piece, preferred_element_type=jnp.float32)  7.78 us
  transfers between devices with their start and end apart: 23, of which 13 were waited for; matrix products, arithmetic and copies ran while one was open for 10% of the time, Pallas kernels for 0%

profile of v12, /device:TPU:0, one launch (start us, length us, event | category | flops | bytes accessed | tf_op | source)
XLA Modules:
  0.0 262.8 jit_solution(5435996826248855192)
XLA Ops:
  6.5 2.4 constant_dynamic-slice_fusion.1
  10.2 3.0 %collective-permute-start = (bf16[192,2048]{1,0:T(8,128)(2,1)S(1)}, bf16[192,2048]{1,0:T(8,128)(2,1)S(1)}, u32[]{:S(2)}, u32[]{:S(2)}) collective-permute-start(bf16[192,2048]{1,0:T(8,128)(2,1)S(1)} %copy-done.6), channel_id=1, source_target_pairs={{0,2},{2,0},{1,3},{3,1},{4,6},{6,4},{5,7},{7,5},{8,10},{10,8},{9,1... | collective-permute-start | bytes 2359304 | tf_op jit(solution)/shard_map/ppermute | solution.py:34
  13.2 17.5 %collective-permute-done = bf16[192,2048]{1,0:T(8,128)(2,1)S(1)} collective-permute-done((bf16[192,2048]{1,0:T(8,128)(2,1)S(1)}, bf16[192,2048]{1,0:T(8,128)(2,1)S(1)}, u32[]{:S(2)}, u32[]{:S(2)}) %collective-permute-start) | collective-permute-done | bytes 786464 | tf_op jit(solution)/shard_map/ppermute | solution.py:34
  32.2 2.4 collective-permute-done.1
  34.6 3.4 %broadcast_select_fusion = (bf16[384,2048]{1,0:T(8,128)(2,1)S(1)}, bf16[384,2048]{1,0:T(8,128)(2,1)}) fusion(bf16[384,2048]{1,0:T(8,128)(2,1)} %collective-permute-done.1, pred[]{:T(512)S(6)} %eq.12, bf16[192,2048]{1,0:T(8,128)(2,1)S(1)} %get-tuple-element.17, bf16[192,2048]{1,0:T(8,128)(2,1)S(1)} %get-tuple-element.16), kind=kLoop, calls=%fused_computation.51 | loop fusion | flops 4718592 | bytes 6291457 | tf_op jit(solution)/shard_map/jit(_where)/select_n | solution.py:36
  38.0 19.8 %all-gather.8.cloned.1.call-done = bf16[4096,256]{1,0:T(8,128)(2,1)} async-done(((bf16[1024,256]{1,0:T(8,128)(2,1)}), bf16[4096,256]{1,0:T(8,128)(2,1)}) %all-gather.8.cloned.1.call-update) | async-done | bytes 2097168 | tf_op jit(solution)/shard_map/all_gather | solution.py:47
  57.8 3.0 %fusion.16 = bf16[4096,256]{1,0:T(8,128)(2,1)S(1)} fusion(s32[]{:T(128)S(6)} %select_n.103, bf16[4096,256]{1,0:T(8,128)(2,1)} %all-gather.8.cloned.1.call-done), kind=kLoop, calls=%fused_computation.28 | loop fusion | flops 4194304 | bytes 4194308 | tf_op jit(solution)/shard_map/jit(_roll_dynamic)/concatenate | solution.py:50
  60.9 1.5 collective-permute-start.11
  63.0 2.9 %fusion.6 = bf16[384,4096]{1,0:T(8,128)(2,1)S(1)} fusion(s32[]{:T(128)S(6)} %select_n.103, bf16[384,2048]{1,0:T(8,128)(2,1)S(1)} %copy-done.1, bf16[384,2048]{1,0:T(8,128)(2,1)S(1)} %get-tuple-element.8), kind=kLoop, calls=%fused_computation.20 | loop fusion | flops 12582912 | bytes 6291460 | tf_op jit(solution)/shard_map/jit(_roll_dynamic)/concatenate | solution.py:65
  67.2 14.2 %collective-permute-done.11 = bf16[1536,256]{1,0:T(8,128)(2,1)S(1)} collective-permute-done((bf16[1536,256]{1,0:T(8,128)(2,1)S(1)}, bf16[1536,256]{1,0:T(8,128)(2,1)S(1)}, u32[]{:S(2)}, u32[]{:S(2)}) %collective-permute-start.11) | collective-permute-done | bytes 786464 | tf_op jit(solution)/shard_map/ppermute | solution.py:53
  81.4 15.7 %collective-permute-done.10 = bf16[1536,256]{1,0:T(8,128)(2,1)S(1)} collective-permute-done((bf16[1536,256]{1,0:T(8,128)(2,1)S(1)}, bf16[1536,256]{1,0:T(8,128)(2,1)S(1)}, u32[]{:S(2)}, u32[]{:S(2)}) %collective-permute-start.10) | collective-permute-done | bytes 786464 | tf_op jit(solution)/shard_map/ppermute | solution.py:52
  99.7 4.6 %collective-permute-start.13 = (bf16[384,512]{0,1:T(8,128)(2,1)S(1)}, bf16[384,512]{0,1:T(8,128)(2,1)S(1)}, u32[]{:S(2)}, u32[]{:S(2)}) collective-permute-start(bf16[384,512]{0,1:T(8,128)(2,1)S(1)} %pad_maximum_fusion.4), channel_id=1, source_target_pairs={{0,4},{4,8},{8,12},{1,5},{5,9},{9,13},{2,6},{6,10},{10,14},{3,7},{... | collective-permute-start | bytes 1179656 | tf_op jit(solution)/shard_map/ppermute | solution.py:23
  105.2 46.2 %all-gather.4.cloned.1.call-done = bf16[4096,256]{1,0:T(8,128)(2,1)} async-done(((bf16[1024,256]{1,0:T(8,128)(2,1)}), bf16[4096,256]{1,0:T(8,128)(2,1)}) %all-gather.4.cloned.1.call-update) | async-done | bytes 2097168 | tf_op jit(solution)/shard_map/all_gather | solution.py:47
  151.4 3.7 %fusion.15 = (bf16[4096,256]{1,0:T(8,128)(2,1)S(1)}, bf16[4096,256]{1,0:T(8,128)(2,1)S(1)}) fusion(s32[]{:T(128)S(6)} %select_n.103, bf16[4096,256]{1,0:T(8,128)(2,1)} %all-gather.6.cloned.1.call-done, bf16[4096,256]{1,0:T(8,128)(2,1)} %all-gather.4.cloned.1.call-done), kind=kLoop, calls=%fused_computation.27 | loop fusion | flops 8388608 | bytes 8388612 | tf_op jit(solution)/shard_map/jit(_roll_dynamic)/concatenate | solution.py:50
  155.3 1.5 collective-permute-start.3
  158.8 1.5 collective-permute-start.19
  163.7 12.1 %collective-permute-done.3 = bf16[1536,256]{1,0:T(8,128)(2,1)S(1)} collective-permute-done((bf16[1536,256]{1,0:T(8,128)(2,1)S(1)}, bf16[1536,256]{1,0:T(8,128)(2,1)S(1)}, u32[]{:S(2)}, u32[]{:S(2)}) %collective-permute-start.3) | collective-permute-done | bytes 786464 | tf_op jit(solution)/shard_map/ppermute | solution.py:53
  176.5 16.2 %collective-permute-done.2 = bf16[1536,256]{1,0:T(8,128)(2,1)S(1)} collective-permute-done((bf16[1536,256]{1,0:T(8,128)(2,1)S(1)}, bf16[1536,256]{1,0:T(8,128)(2,1)S(1)}, u32[]{:S(2)}, u32[]{:S(2)}) %collective-permute-start.2) | collective-permute-done | bytes 786464 | tf_op jit(solution)/shard_map/ppermute | solution.py:52
  195.3 14.2 %collective-permute-done.19 = bf16[1536,256]{1,0:T(8,128)(2,1)S(1)} collective-permute-done((bf16[1536,256]{1,0:T(8,128)(2,1)S(1)}, bf16[1536,256]{1,0:T(8,128)(2,1)S(1)}, u32[]{:S(2)}, u32[]{:S(2)}) %collective-permute-start.19) | collective-permute-done | bytes 786464 | tf_op jit(solution)/shard_map/ppermute | solution.py:53
  209.5 1.8 collective-permute-start.5
  212.6 12.6 %collective-permute-done.18 = bf16[1536,256]{1,0:T(8,128)(2,1)S(1)} collective-permute-done((bf16[1536,256]{1,0:T(8,128)(2,1)S(1)}, bf16[1536,256]{1,0:T(8,128)(2,1)S(1)}, u32[]{:S(2)}, u32[]{:S(2)}) %collective-permute-start.18) | collective-permute-done | bytes 786464 | tf_op jit(solution)/shard_map/ppermute | solution.py:52
  232.3 6.9 %collective-permute-done.8 = bf16[384,512]{0,1:T(8,128)(2,1)S(1)} collective-permute-done((bf16[384,512]{0,1:T(8,128)(2,1)S(1)}, bf16[384,512]{0,1:T(8,128)(2,1)S(1)}, u32[]{:S(2)}, u32[]{:S(2)}) %collective-permute-start.8) | collective-permute-done | bytes 393248 | tf_op jit(solution)/shard_map/ppermute | solution.py:22
  242.1 8.0 %collective-permute-done.9 = bf16[384,512]{0,1:T(8,128)(2,1)S(1)} collective-permute-done((bf16[384,512]{0,1:T(8,128)(2,1)S(1)}, bf16[384,512]{0,1:T(8,128)(2,1)S(1)}, u32[]{:S(2)}, u32[]{:S(2)}) %collective-permute-start.9) | collective-permute-done | bytes 393248 | tf_op jit(solution)/shard_map/ppermute | solution.py:22
  251.6 3.4 %fusion.54 = bf16[384,2,128]{0,2,1:T(8,128)(2,1)S(1)} fusion(bf16[1536,4,128]{0,2,1:T(8,128)(2,1)S(1)} %bitcast.36, f32[2,384,1536]{2,1,0:T(8,128)} %copy-done, f32[2,384]{1,0:T(2,128)S(1)} %get-tuple-element.26, f32[384,2]{0,1:T(2,128)S(1)} %bitcast.42), kind=kOutput, calls=%fused_computation.62 | convolution fusion | flops 305725440 | bytes 6494208 | tf_op jit(solution)/shard_map/hqk,khd->qhd/dot_general | solution.py:101
  (82 shorter events, 30.6 us)
Async XLA Ops:
  6.5 51.2 %all-gather.8.cloned.1.call-start = ((), (), s32[]{:S(2)}) async-start(), calls=%async_computation.2 | async-start | bytes 2621440 | tf_op jit(solution)/shard_map/all_gather | solution.py:47
  9.0 96.2 %all-gather.6.cloned.1.call-start = ((), (), s32[]{:S(2)}) async-start(), calls=%async_computation.1 | async-start | bytes 2621440 | tf_op jit(solution)/shard_map/all_gather | solution.py:47
  10.1 141.3 %all-gather.4.cloned.1.call-start = ((), (), s32[]{:S(2)}) async-start(), calls=%async_computation | async-start | bytes 2621440 | tf_op jit(solution)/shard_map/all_gather | solution.py:47
  10.2 20.5 %collective-permute-start = (bf16[192,2048]{1,0:T(8,128)(2,1)S(1)}, bf16[192,2048]{1,0:T(8,128)(2,1)S(1)}, u32[]{:S(2)}, u32[]{:S(2)}) collective-permute-start(bf16[192,2048]{1,0:T(8,128)(2,1)S(1)} %copy-done.6), channel_id=1, source_target_pairs={{0,2},{2,0},{1,3},{3,1},{4,6},{6,4},{5,7},{7,5},{8,10},{10,8},{9,1... | collective-permute-start | bytes 2359304 | tf_op jit(solution)/shard_map/ppermute | solution.py:34
  31.0 3.6 %collective-permute-start.1 = (bf16[384,2048]{1,0:T(8,128)(2,1)S(1)}, bf16[384,2048]{1,0:T(8,128)(2,1)}, u32[]{:S(2)}, u32[]{:S(2)}) collective-permute-start(bf16[384,2048]{1,0:T(8,128)(2,1)S(1)} %pad_maximum_fusion), channel_id=1, source_target_pairs={{0,1},{1,0},{2,3},{3,2},{4,5},{5,4},{6,7},{7,6},{8,9},{9,8},{10,11... | collective-permute-start | bytes 4718600 | tf_op jit(solution)/shard_map/ppermute | solution.py:34
  60.9 20.5 %collective-permute-start.11 = (bf16[1536,256]{1,0:T(8,128)(2,1)S(1)}, bf16[1536,256]{1,0:T(8,128)(2,1)S(1)}, u32[]{:S(2)}, u32[]{:S(2)}) collective-permute-start(bf16[1536,256]{1,0:T(8,128)(2,1)S(1)} %get-tuple-element.13), channel_id=1, source_target_pairs={{0,16},{16,0},{1,17},{17,1},{2,18},{18,2},{3,19},{19,3},{4,20},{20... | collective-permute-start | bytes 2359304 | tf_op jit(solution)/shard_map/ppermute | solution.py:53
  62.4 34.7 %collective-permute-start.10 = (bf16[1536,256]{1,0:T(8,128)(2,1)S(1)}, bf16[1536,256]{1,0:T(8,128)(2,1)S(1)}, u32[]{:S(2)}, u32[]{:S(2)}) collective-permute-start(bf16[1536,256]{1,0:T(8,128)(2,1)S(1)} %get-tuple-element.12), channel_id=1, source_target_pairs={{0,16},{16,0},{1,17},{17,1},{2,18},{18,2},{3,19},{19,3},{4,20},{20... | collective-permute-start | bytes 2359304 | tf_op jit(solution)/shard_map/ppermute | solution.py:52
  98.4 61.9 %collective-permute-start.12 = (bf16[384,512]{0,1:T(8,128)(2,1)S(1)}, bf16[384,512]{0,1:T(8,128)(2,1)S(1)}, u32[]{:S(2)}, u32[]{:S(2)}) collective-permute-start(bf16[384,512]{0,1:T(8,128)(2,1)S(1)} %pad_maximum_fusion.4), channel_id=1, source_target_pairs={{4,0},{8,4},{12,8},{5,1},{9,5},{13,9},{6,2},{10,6},{14,10},{7,3},{... | collective-permute-start | bytes 1179656 | tf_op jit(solution)/shard_map/ppermute | solution.py:22
  99.7 62.5 %collective-permute-start.13 = (bf16[384,512]{0,1:T(8,128)(2,1)S(1)}, bf16[384,512]{0,1:T(8,128)(2,1)S(1)}, u32[]{:S(2)}, u32[]{:S(2)}) collective-permute-start(bf16[384,512]{0,1:T(8,128)(2,1)S(1)} %pad_maximum_fusion.4), channel_id=1, source_target_pairs={{0,4},{4,8},{8,12},{1,5},{5,9},{9,13},{2,6},{6,10},{10,14},{3,7},{... | collective-permute-start | bytes 1179656 | tf_op jit(solution)/shard_map/ppermute | solution.py:23
  155.3 20.5 %collective-permute-start.3 = (bf16[1536,256]{1,0:T(8,128)(2,1)S(1)}, bf16[1536,256]{1,0:T(8,128)(2,1)S(1)}, u32[]{:S(2)}, u32[]{:S(2)}) collective-permute-start(bf16[1536,256]{1,0:T(8,128)(2,1)S(1)} %get-tuple-element.15), channel_id=1, source_target_pairs={{0,16},{16,0},{1,17},{17,1},{2,18},{18,2},{3,19},{19,3},{4,20},{20... | collective-permute-start | bytes 2359304 | tf_op jit(solution)/shard_map/ppermute | solution.py:53
  156.8 35.8 %collective-permute-start.2 = (bf16[1536,256]{1,0:T(8,128)(2,1)S(1)}, bf16[1536,256]{1,0:T(8,128)(2,1)S(1)}, u32[]{:S(2)}, u32[]{:S(2)}) collective-permute-start(bf16[1536,256]{1,0:T(8,128)(2,1)S(1)} %get-tuple-element.14), channel_id=1, source_target_pairs={{0,16},{16,0},{1,17},{17,1},{2,18},{18,2},{3,19},{19,3},{4,20},{20... | collective-permute-start | bytes 2359304 | tf_op jit(solution)/shard_map/ppermute | solution.py:52
  158.8 50.7 %collective-permute-start.19 = (bf16[1536,256]{1,0:T(8,128)(2,1)S(1)}, bf16[1536,256]{1,0:T(8,128)(2,1)S(1)}, u32[]{:S(2)}, u32[]{:S(2)}) collective-permute-start(bf16[1536,256]{1,0:T(8,128)(2,1)S(1)} %get-tuple-element.11), channel_id=1, source_target_pairs={{0,16},{16,0},{1,17},{17,1},{2,18},{18,2},{3,19},{19,3},{4,20},{20... | collective-permute-start | bytes 2359304 | tf_op jit(solution)/shard_map/ppermute | solution.py:53
  160.3 64.8 %collective-permute-start.18 = (bf16[1536,256]{1,0:T(8,128)(2,1)S(1)}, bf16[1536,256]{1,0:T(8,128)(2,1)S(1)}, u32[]{:S(2)}, u32[]{:S(2)}) collective-permute-start(bf16[1536,256]{1,0:T(8,128)(2,1)S(1)} %get-tuple-element.10), channel_id=1, source_target_pairs={{0,16},{16,0},{1,17},{17,1},{2,18},{18,2},{3,19},{19,3},{4,20},{20... | collective-permute-start | bytes 2359304 | tf_op jit(solution)/shard_map/ppermute | solution.py:52
  162.2 49.1 %collective-permute-start.16 = (bf16[384,512]{0,1:T(8,128)(2,1)S(1)}, bf16[384,512]{0,1:T(8,128)(2,1)S(1)}, u32[]{:S(2)}, u32[]{:S(2)}) collective-permute-start(bf16[384,512]{0,1:T(8,128)(2,1)S(1)} %collective-permute-done.12), channel_id=1, source_target_pairs={{4,0},{8,4},{5,1},{9,5},{6,2},{10,6},{7,3},{11,7},{20,16},{24,20},... | collective-permute-start | bytes 1179656 | tf_op jit(solution)/shard_map/ppermute | solution.py:22
  175.8 50.7 %collective-permute-start.14 = (bf16[384,512]{0,1:T(8,128)(2,1)S(1)}, bf16[384,512]{0,1:T(8,128)(2,1)S(1)}, u32[]{:S(2)}, u32[]{:S(2)}) collective-permute-start(bf16[384,512]{0,1:T(8,128)(2,1)S(1)} %collective-permute-done.13), channel_id=1, source_target_pairs={{4,8},{8,12},{5,9},{9,13},{6,10},{10,14},{7,11},{11,15},{20,24},{2... | collective-permute-start | bytes 1179656 | tf_op jit(solution)/shard_map/ppermute | solution.py:23
  192.6 32.6 %copy-start.7 = (bf16[1024,256]{1,0:T(8,128)(2,1)S(1)}, bf16[1024,256]{1,0:T(8,128)(2,1)}, u32[]{:S(2)}) copy-start(bf16[1024,256]{1,0:T(8,128)(2,1)} %get-tuple-element.18) | copy-start | bytes 1572868
  194.0 33.3 %collective-permute-start.4 = (bf16[384,512]{0,1:T(8,128)(2,1)S(1)}, bf16[384,512]{0,1:T(8,128)(2,1)S(1)}, u32[]{:S(2)}, u32[]{:S(2)}) collective-permute-start(bf16[384,512]{0,1:T(8,128)(2,1)S(1)} %pad_maximum_fusion.3), channel_id=1, source_target_pairs={{4,0},{8,4},{12,8},{5,1},{9,5},{13,9},{6,2},{10,6},{14,10},{7,3},{... | collective-permute-start | bytes 1179656 | tf_op jit(solution)/shard_map/ppermute | solution.py:22
  209.5 19.1 %collective-permute-start.5 = (bf16[384,512]{0,1:T(8,128)(2,1)S(1)}, bf16[384,512]{0,1:T(8,128)(2,1)S(1)}, u32[]{:S(2)}, u32[]{:S(2)}) collective-permute-start(bf16[384,512]{0,1:T(8,128)(2,1)S(1)} %pad_maximum_fusion.3), channel_id=1, source_target_pairs={{0,4},{4,8},{8,12},{1,5},{5,9},{9,13},{2,6},{6,10},{10,14},{3,7},{... | collective-permute-start | bytes 1179656 | tf_op jit(solution)/shard_map/ppermute | solution.py:23
  211.3 17.9 %collective-permute-start.17 = (bf16[384,512]{0,1:T(8,128)(2,1)S(1)}, bf16[384,512]{0,1:T(8,128)(2,1)S(1)}, u32[]{:S(2)}, u32[]{:S(2)}) collective-permute-start(bf16[384,512]{0,1:T(8,128)(2,1)S(1)} %collective-permute-done.16), channel_id=1, source_target_pairs={{4,0},{5,1},{6,2},{7,3},{20,16},{21,17},{22,18},{23,19}} | collective-permute-start | bytes 1179656 | tf_op jit(solution)/shard_map/ppermute | solution.py:22
  226.5 2.8 %collective-permute-start.15 = (bf16[384,512]{0,1:T(8,128)(2,1)S(1)}, bf16[384,512]{0,1:T(8,128)(2,1)S(1)}, u32[]{:S(2)}, u32[]{:S(2)}) collective-permute-start(bf16[384,512]{0,1:T(8,128)(2,1)S(1)} %collective-permute-done.14), channel_id=1, source_target_pairs={{8,12},{9,13},{10,14},{11,15},{24,28},{25,29},{26,30},{27,31}} | collective-permute-start | bytes 1179656 | tf_op jit(solution)/shard_map/ppermute | solution.py:23
  227.3 11.9 %collective-permute-start.8 = (bf16[384,512]{0,1:T(8,128)(2,1)S(1)}, bf16[384,512]{0,1:T(8,128)(2,1)S(1)}, u32[]{:S(2)}, u32[]{:S(2)}) collective-permute-start(bf16[384,512]{0,1:T(8,128)(2,1)S(1)} %collective-permute-done.4), channel_id=1, source_target_pairs={{4,0},{8,4},{5,1},{9,5},{6,2},{10,6},{7,3},{11,7},{20,16},{24,20},... | collective-permute-start | bytes 1179656 | tf_op jit(solution)/shard_map/ppermute | solution.py:22
  228.6 12.8 %collective-permute-start.6 = (bf16[384,512]{0,1:T(8,128)(2,1)S(1)}, bf16[384,512]{0,1:T(8,128)(2,1)S(1)}, u32[]{:S(2)}, u32[]{:S(2)}) collective-permute-start(bf16[384,512]{0,1:T(8,128)(2,1)S(1)} %collective-permute-done.5), channel_id=1, source_target_pairs={{4,8},{8,12},{5,9},{9,13},{6,10},{10,14},{7,11},{11,15},{20,24},{2... | collective-permute-start | bytes 1179656 | tf_op jit(solution)/shard_map/ppermute | solution.py:23
  239.2 10.9 %collective-permute-start.9 = (bf16[384,512]{0,1:T(8,128)(2,1)S(1)}, bf16[384,512]{0,1:T(8,128)(2,1)S(1)}, u32[]{:S(2)}, u32[]{:S(2)}) collective-permute-start(bf16[384,512]{0,1:T(8,128)(2,1)S(1)} %collective-permute-done.8), channel_id=1, source_target_pairs={{4,0},{5,1},{6,2},{7,3},{20,16},{21,17},{22,18},{23,19}} | collective-permute-start | bytes 1179656 | tf_op jit(solution)/shard_map/ppermute | solution.py:22
  241.4 8.8 %collective-permute-start.7 = (bf16[384,512]{0,1:T(8,128)(2,1)S(1)}, bf16[384,512]{0,1:T(8,128)(2,1)S(1)}, u32[]{:S(2)}, u32[]{:S(2)}) collective-permute-start(bf16[384,512]{0,1:T(8,128)(2,1)S(1)} %collective-permute-done.6), channel_id=1, source_target_pairs={{8,12},{9,13},{10,14},{11,15},{24,28},{25,29},{26,30},{27,31}} | collective-permute-start | bytes 1179656 | tf_op jit(solution)/shard_map/ppermute | solution.py:23
  (9 other events, 156.0 us)
Sparse Core Ops, SparseCore 0:
  9.1 48.6 all-gather.7
  59.3 45.8 all-gather.5
  106.8 44.6 all-gather.3

commit v13 on v8

--- a/solution.py
+++ b/solution.py
@@ -52,6 +52,35 @@
     return [own, jnp.concatenate([kept, other], axis=0)]
 
 
+def chained_columns(weight):
+    n = lax.axis_size("seq")
+    here = lax.axis_index("seq")
+    half = weight.shape[1] // 2
+    group = lax.axis_index("groups")
+    own = lax.dynamic_slice_in_dim(weight, group * half, half, axis=1)
+    kept = lax.dynamic_slice_in_dim(weight, (1 - group) * half, half, axis=1)
+
+    def across(piece, places):
+        pairs = [(g * n + j, (1 - g) * n + j) for g in range(2) for j in places]
+        return lax.ppermute(piece, ("groups", "seq"), pairs)
+
+    right, left = [own], [own]
+    right_other, left_other = [kept], [kept]
+    for k in range(1, n):
+        right.append(lax.ppermute(right[-1], "seq", [(j, j - 1) for j in range(1, n - k + 1)]))
+        left.append(lax.ppermute(left[-1], "seq", [(j, j + 1) for j in range(k - 1, n - 1)]))
+        right_other.append(across(right[k], range(0, n - k)))
+        left_other.append(across(left[k], range(k, n)))
+
+    def slots(first, from_right, from_left):
+        chosen = [first]
+        for m in range(1, n):
+            chosen.append(jnp.where(here + m < n, from_right[m], from_left[n - m]))
+        return jnp.concatenate(chosen, axis=0)
+
+    return [slots(own, right, left), slots(kept, right_other, left_other)]
+
+
 def per_device(acts, w_query, w_key, w_value):
     block = swap_gather(acts, "row", 0)
     block = swap_gather(block, "col", 1)
@@ -68,7 +97,16 @@
             for piece in full_columns(weight, shared, after)
         ]
 
-    key = jnp.concatenate(project(w_key), axis=1)
+    if shared and lax.axis_size("seq") == SPAN:
+        key = jnp.concatenate(
+            [
+                jnp.dot(block, piece, preferred_element_type=jnp.float32).astype(jnp.bfloat16)
+                for piece in chained_columns(w_key)
+            ],
+            axis=1,
+        )
+    else:
+        key = jnp.concatenate(project(w_key), axis=1)
     value = jnp.concatenate(project(w_value), axis=1)
     queries = project(w_query, key)
     if lax.axis_size("seq") == SPAN:

time: 227 us -> 260 us (1.15)
  starting transfers between devices: 30.9 us -> 55 us
  waiting for transfers between devices: 130 us -> 146 us
  other arithmetic: 25.4 us -> 17 us
    ppermute x0 -> x12, waiting for transfers between devices: none -> 98.1 us  [the longest x3 70.2 us: chained_columns(): lax.ppermute(right[-1], 'seq', [(j, j - 1) for j in range(1, n - k + 1)])]
    all_gather x3 -> x2, waiting for transfers between devices: 60.7 us -> 0.02 us  [full_columns(): own = lax.all_gather(own, 'seq', axis=0, tiled=True)]
    ppermute x0 -> x12, starting transfers between devices: none -> 20.1 us  [the longest x6 11.3 us: across(): return lax.ppermute(piece, ('groups', 'seq'), pairs)]
    ppermute x2, waiting for transfers between devices: 18.9 us -> 0.01 us  [swap_gather(): other = lax.ppermute(piece, axis, [(0, 1), (1, 0)])]
    ppermute x3 -> x2, waiting for transfers between devices: 22.4 us -> 14.6 us  [full_columns(): other = lax.ppermute(own[rows:], 'groups', [(0, 1), (1, 0)])]
    dot_general x6 -> x4, matrix products: 11.7 us -> 6.59 us  [project(): jnp.dot(block, piece, preferred_element_type=jnp.float32)]
    ppermute x6, waiting for transfers between devices: 28.1 us -> 33.2 us  [line_gather(): lax.ppermute(from_right[-1], 'seq', [(j, j - 1) for j in range(1, n - k +...]
    dot_general x0 -> x2, matrix products: none -> 4.08 us  [per_device(): jnp.dot(block, piece, preferred_element_type=jnp.float32)]
  transfers between devices with their start and end apart: 20 -> 30, of which waited for: 10 -> 12; matrix products, arithmetic and copies ran while one was open for 17% -> 12% of each run, Pallas kernels for 0% -> 0%
where the time goes in v13:
time: 260 us; the launch traced here: 255 us
  waiting for transfers between devices  146 us (56%)
  starting transfers between devices  55 us (21%)
  other arithmetic  17 us (7%)
  matrix products  17 us (7%)
  between operations  14.1 us (5%)
  local copies, waits for them, and re-layouts  6.15 us (2%)
    ppermute x3, waiting for transfers between devices, chained_columns(): lax.ppermute(right[-1], 'seq', [(j, j - 1) for j in range(1, n - k + 1)])  70.2 us
    ppermute x6, waiting for transfers between devices, line_gather(): lax.ppermute(from_right[-1], 'seq', [(j, j - 1) for j in range(1, n - k +...  33.2 us
    ppermute x6, starting transfers between devices, line_gather(): lax.ppermute(from_left[-1], 'seq', [(j, j + 1) for j in range(k - 1, n -...  19 us
    ppermute x3, waiting for transfers between devices, chained_columns(): lax.ppermute(left[-1], 'seq', [(j, j + 1) for j in range(k - 1, n - 1)])  17.9 us
    ppermute x2, waiting for transfers between devices, full_columns(): other = lax.ppermute(own[rows:], 'groups', [(0, 1), (1, 0)])  14.6 us
    ppermute x6, starting transfers between devices, across(): return lax.ppermute(piece, ('groups', 'seq'), pairs)  11.3 us
    ppermute x6, waiting for transfers between devices, across(): return lax.ppermute(piece, ('groups', 'seq'), pairs)  9.92 us
    ppermute x6, starting transfers between devices, line_gather(): lax.ppermute(from_right[-1], 'seq', [(j, j - 1) for j in range(1, n - k +...  7.94 us
  transfers between devices with their start and end apart: 30, of which 12 were waited for; matrix products, arithmetic and copies ran while one was open for 12% of the time, Pallas kernels for 0%

profile of v13, /device:TPU:0, one launch (start us, length us, event | category | flops | bytes accessed | tf_op | source)
XLA Modules:
  0.0 255.2 jit_solution(17537096781986874376)
XLA Ops:
  9.1 3.0 %collective-permute-start = (bf16[192,2048]{1,0:T(8,128)(2,1)}, bf16[192,2048]{1,0:T(8,128)(2,1)}, u32[]{:S(2)}, u32[]{:S(2)}) collective-permute-start(bf16[192,2048]{1,0:T(8,128)(2,1)} %param.6), channel_id=1, source_target_pairs={{0,2},{2,0},{1,3},{3,1},{4,6},{6,4},{5,7},{7,5},{8,10},{10,8},{9,1... | collective-permute-start | bytes 2359304 | tf_op jit(solution)/shard_map/ppermute | solution.py:34
  13.2 3.5 %collective-permute-start.10 = (bf16[1024,256]{1,0:T(8,128)(2,1)}, bf16[1024,256]{1,0:T(8,128)(2,1)S(1)}, u32[]{:S(2)}, u32[]{:S(2)}) collective-permute-start(bf16[1024,256]{1,0:T(8,128)(2,1)} %get-tuple-element.15), channel_id=1, source_target_pairs={{0,4},{4,8},{8,12},{1,5},{5,9},{9,13},{2,6},{6,10},{10,14},{3,7},{... | collective-permute-start | bytes 1572872 | tf_op jit(solution)/shard_map/ppermute | solution.py:71
  18.9 17.9 %collective-permute-done.10 = bf16[1024,256]{1,0:T(8,128)(2,1)S(1)} collective-permute-done((bf16[1024,256]{1,0:T(8,128)(2,1)}, bf16[1024,256]{1,0:T(8,128)(2,1)S(1)}, u32[]{:S(2)}, u32[]{:S(2)}) %collective-permute-start.10) | collective-permute-done | bytes 524320 | tf_op jit(solution)/shard_map/ppermute | solution.py:71
  38.2 16.5 %collective-permute-done.9 = bf16[1024,256]{1,0:T(8,128)(2,1)S(1)} collective-permute-done((bf16[1024,256]{1,0:T(8,128)(2,1)}, bf16[1024,256]{1,0:T(8,128)(2,1)S(1)}, u32[]{:S(2)}, u32[]{:S(2)}) %collective-permute-start.9) | collective-permute-done | bytes 524320 | tf_op jit(solution)/shard_map/ppermute | solution.py:70
  57.3 19.5 %collective-permute-done.13 = bf16[1024,256]{1,0:T(8,128)(2,1)S(1)} collective-permute-done((bf16[1024,256]{1,0:T(8,128)(2,1)S(1)}, bf16[1024,256]{1,0:T(8,128)(2,1)S(1)}, u32[]{:S(2)}, u32[]{:S(2)}) %collective-permute-start.13) | collective-permute-done | bytes 524320 | tf_op jit(solution)/shard_map/ppermute | solution.py:70
  78.3 3.4 %collective-permute-start.17 = (bf16[1024,256]{1,0:T(8,128)(2,1)S(1)}, bf16[1024,256]{1,0:T(8,128)(2,1)S(1)}, u32[]{:S(2)}, u32[]{:S(2)}) collective-permute-start(bf16[1024,256]{1,0:T(8,128)(2,1)S(1)} %collective-permute-done.13), channel_id=1, source_target_pairs={{0,16},{4,20},{16,0},{20,4},{1,17},{5,21},{17,1},{21,5},{2,18},{6,... | collective-permute-start | bytes 1572872 | tf_op jit(solution)/shard_map/ppermute | solution.py:65
  82.5 34.2 %collective-permute-done.14 = bf16[1024,256]{1,0:T(8,128)(2,1)S(1)} collective-permute-done((bf16[1024,256]{1,0:T(8,128)(2,1)S(1)}, bf16[1024,256]{1,0:T(8,128)(2,1)S(1)}, u32[]{:S(2)}, u32[]{:S(2)}) %collective-permute-start.14) | collective-permute-done | bytes 524320 | tf_op jit(solution)/shard_map/ppermute | solution.py:70
  117.4 3.9 %collective-permute-start.19 = (bf16[1024,256]{1,0:T(8,128)(2,1)S(1)}, bf16[1024,256]{1,0:T(8,128)(2,1)S(1)}, u32[]{:S(2)}, u32[]{:S(2)}) collective-permute-start(bf16[1024,256]{1,0:T(8,128)(2,1)S(1)} %collective-permute-done.14), channel_id=1, source_target_pairs={{0,16},{16,0},{1,17},{17,1},{2,18},{18,2},{3,19},{19,3}} | collective-permute-start | bytes 1572872 | tf_op jit(solution)/shard_map/ppermute | solution.py:65
  124.2 4.4 %collective-permute-done.19 = bf16[1024,256]{1,0:T(8,128)(2,1)S(1)} collective-permute-done((bf16[1024,256]{1,0:T(8,128)(2,1)S(1)}, bf16[1024,256]{1,0:T(8,128)(2,1)S(1)}, u32[]{:S(2)}, u32[]{:S(2)}) %collective-permute-start.19) | collective-permute-done | bytes 524320 | tf_op jit(solution)/shard_map/ppermute | solution.py:65
  128.6 5.6 %collective-permute-done.15 = bf16[1024,256]{1,0:T(8,128)(2,1)S(1)} collective-permute-done((bf16[1024,256]{1,0:T(8,128)(2,1)S(1)}, bf16[1024,256]{1,0:T(8,128)(2,1)S(1)}, u32[]{:S(2)}, u32[]{:S(2)}) %collective-permute-start.15) | collective-permute-done | bytes 524320 | tf_op jit(solution)/shard_map/ppermute | solution.py:65
  135.0 2.9 %fusion.6 = bf16[384,4096]{1,0:T(8,128)(2,1)S(1)} fusion(s32[]{:T(128)S(6)} %select_n.135, bf16[384,2048]{1,0:T(8,128)(2,1)S(1)} %get-tuple-element.9, bf16[384,2048]{1,0:T(8,128)(2,1)S(1)} %get-tuple-element.8), kind=kLoop, calls=%fused_computation.18 | loop fusion | flops 12582912 | bytes 6291460 | tf_op jit(solution)/shard_map/jit(_roll_dynamic)/concatenate | solution.py:92
  137.9 2.8 %fusion.53 = bf16[384,256]{0,1:T(8,128)(2,1)S(1)} fusion(bf16[384,4096]{1,0:T(8,128)(2,1)S(1)} %fusion.6, bf16[1024,256]{1,0:T(8,128)(2,1)S(1)} %broadcast_select_fusion.5, bf16[1024,256]{1,0:T(8,128)(2,1)S(1)} %broadcast_select_fusion.7, bf16[1024,256]{1,0:T(8,128)(2,1)S(1)} %broadcast_select_fusion.9, bf16[1024,256]{1,0:T(8,128)(2,1)} %get-tuple-element.15), kind=kOutput, calls=%fused_computation.60 | convolution fusion | flops 813793280 | bytes 5439488 | tf_op jit(solution)/shard_map/dot_general | solution.py:103
  143.4 5.3 %collective-permute-start.22 = (bf16[384,512]{0,1:T(8,128)(2,1)S(1)}, bf16[384,512]{0,1:T(8,128)(2,1)}, u32[]{:S(2)}, u32[]{:S(2)}) collective-permute-start(bf16[384,512]{0,1:T(8,128)(2,1)S(1)} %pad_maximum_fusion.4), channel_id=1, source_target_pairs={{0,4},{4,8},{8,12},{1,5},{5,9},{9,13},{2,6},{6,10},{10,14},{3,7},{... | collective-permute-start | bytes 1179656 | tf_op jit(solution)/shard_map/ppermute | solution.py:23
  148.7 3.8 %collective-permute-done.21 = bf16[384,512]{0,1:T(8,128)(2,1)} collective-permute-done((bf16[384,512]{0,1:T(8,128)(2,1)S(1)}, bf16[384,512]{0,1:T(8,128)(2,1)}, u32[]{:S(2)}, u32[]{:S(2)}) %collective-permute-start.21) | collective-permute-done | bytes 393248 | tf_op jit(solution)/shard_map/ppermute | solution.py:22
  154.7 3.0 %fusion.16 = bf16[4096,256]{1,0:T(8,128)(2,1)S(1)} fusion(s32[]{:T(128)S(6)} %select_n.135, bf16[4096,256]{1,0:T(8,128)(2,1)} %all-gather.3.cloned.1.call-done), kind=kLoop, calls=%fused_computation.26 | loop fusion | flops 4194304 | bytes 4194308 | tf_op jit(solution)/shard_map/jit(_roll_dynamic)/concatenate | solution.py:48
  159.1 4.8 %collective-permute-start.2 = (bf16[3072,256]{1,0:T(8,128)(2,1)}, bf16[3072,256]{1,0:T(8,128)(2,1)}, u32[]{:S(2)}, u32[]{:S(2)}) collective-permute-start(bf16[3072,256]{1,0:T(8,128)(2,1)} %slice.24), channel_id=1, source_target_pairs={{0,16},{16,0},{1,17},{17,1},{2,18},{18,2},{3,19},{19,3},{4,20},{20... | collective-permute-start | bytes 4718600 | tf_op jit(solution)/shard_map/ppermute | solution.py:51
  163.9 3.2 %fusion.15 = bf16[4096,256]{1,0:T(8,128)(2,1)S(1)} fusion(s32[]{:T(128)S(6)} %select_n.135, bf16[4096,256]{1,0:T(8,128)(2,1)} %all-gather.5.cloned.1.call-done), kind=kLoop, calls=%fused_computation.25 | loop fusion | flops 4194304 | bytes 4194308 | tf_op jit(solution)/shard_map/jit(_roll_dynamic)/concatenate | solution.py:48
  173.0 6.4 %collective-permute-done.26 = bf16[384,512]{0,1:T(8,128)(2,1)S(1)} collective-permute-done((bf16[384,512]{0,1:T(8,128)(2,1)}, bf16[384,512]{0,1:T(8,128)(2,1)S(1)}, u32[]{:S(2)}, u32[]{:S(2)}) %collective-permute-start.26) | collective-permute-done | bytes 393248 | tf_op jit(solution)/shard_map/ppermute | solution.py:22
  180.8 14.6 %collective-permute-done.2 = bf16[3072,256]{1,0:T(8,128)(2,1)} collective-permute-done((bf16[3072,256]{1,0:T(8,128)(2,1)}, bf16[3072,256]{1,0:T(8,128)(2,1)}, u32[]{:S(2)}, u32[]{:S(2)}) %collective-permute-start.2) | collective-permute-done | bytes 1572896 | tf_op jit(solution)/shard_map/ppermute | solution.py:51
  195.3 2.7 %fusion.56 = bf16[384,256]{0,1:T(8,128)(2,1)S(1)} fusion(bf16[384,4096]{1,0:T(8,128)(2,1)S(1)} %copy-done.2, bf16[3072,256]{1,0:T(8,128)(2,1)} %collective-permute-done.2, bf16[1024,256]{1,0:T(8,128)(2,1)S(1)} %copy-done.6), kind=kOutput, calls=%fused_computation.61 | convolution fusion | flops 809598976 | bytes 5439488 | tf_op jit(solution)/shard_map/dot_general | solution.py:96
  200.3 10.7 %collective-permute-start.4 = (bf16[384,512]{0,1:T(8,128)(2,1)S(1)}, bf16[384,512]{0,1:T(8,128)(2,1)S(1)}, u32[]{:S(2)}, u32[]{:S(2)}) collective-permute-start(bf16[384,512]{0,1:T(8,128)(2,1)S(1)} %pad_maximum_fusion.3), channel_id=1, source_target_pairs={{0,4},{4,8},{8,12},{1,5},{5,9},{9,13},{2,6},{6,10},{10,14},{3,7},{... | collective-permute-start | bytes 1179656 | tf_op jit(solution)/shard_map/ppermute | solution.py:23
  218.1 5.4 %collective-permute-done.7 = bf16[384,512]{0,1:T(8,128)(2,1)S(1)} collective-permute-done((bf16[384,512]{0,1:T(8,128)(2,1)S(1)}, bf16[384,512]{0,1:T(8,128)(2,1)S(1)}, u32[]{:S(2)}, u32[]{:S(2)}) %collective-permute-start.7) | collective-permute-done | bytes 393248 | tf_op jit(solution)/shard_map/ppermute | solution.py:22
  226.7 15.5 %collective-permute-done.8 = bf16[384,512]{0,1:T(8,128)(2,1)S(1)} collective-permute-done((bf16[384,512]{0,1:T(8,128)(2,1)S(1)}, bf16[384,512]{0,1:T(8,128)(2,1)S(1)}, u32[]{:S(2)}, u32[]{:S(2)}) %collective-permute-start.8) | collective-permute-done | bytes 393248 | tf_op jit(solution)/shard_map/ppermute | solution.py:22
  243.7 3.4 %fusion.62 = bf16[384,2,128]{0,2,1:T(8,128)(2,1)S(1)} fusion(bf16[1536,4,128]{0,2,1:T(8,128)(2,1)S(1)} %bitcast.35, f32[2,384,1536]{2,1,0:T(8,128)} %copy-done, f32[2,384]{1,0:T(2,128)S(1)} %get-tuple-element.20, f32[384,2]{0,1:T(2,128)S(1)} %bitcast.41), kind=kOutput, calls=%fused_computation.65 | convolution fusion | flops 305725440 | bytes 6494208 | tf_op jit(solution)/shard_map/hqk,khd->qhd/dot_general | solution.py:137
  (96 shorter events, 44.7 us)
Async XLA Ops:
  6.5 148.2 %all-gather.3.cloned.1.call-start = ((), (), s32[]{:S(2)}) async-start(), calls=%async_computation | async-start | bytes 2621440 | tf_op jit(solution)/shard_map/all_gather | solution.py:47
  9.0 154.9 %all-gather.5.cloned.1.call-start = ((), (), s32[]{:S(2)}) async-start(), calls=%async_computation.1 | async-start | bytes 2621440 | tf_op jit(solution)/shard_map/all_gather | solution.py:47
  9.1 47.0 %collective-permute-start = (bf16[192,2048]{1,0:T(8,128)(2,1)}, bf16[192,2048]{1,0:T(8,128)(2,1)}, u32[]{:S(2)}, u32[]{:S(2)}) collective-permute-start(bf16[192,2048]{1,0:T(8,128)(2,1)} %param.6), channel_id=1, source_target_pairs={{0,2},{2,0},{1,3},{3,1},{4,6},{6,4},{5,7},{7,5},{8,10},{10,8},{9,1... | collective-permute-start | bytes 2359304 | tf_op jit(solution)/shard_map/ppermute | solution.py:34
  13.2 23.7 %collective-permute-start.10 = (bf16[1024,256]{1,0:T(8,128)(2,1)}, bf16[1024,256]{1,0:T(8,128)(2,1)S(1)}, u32[]{:S(2)}, u32[]{:S(2)}) collective-permute-start(bf16[1024,256]{1,0:T(8,128)(2,1)} %get-tuple-element.15), channel_id=1, source_target_pairs={{0,4},{4,8},{8,12},{1,5},{5,9},{9,13},{2,6},{6,10},{10,14},{3,7},{... | collective-permute-start | bytes 1572872 | tf_op jit(solution)/shard_map/ppermute | solution.py:71
  16.7 38.1 %collective-permute-start.9 = (bf16[1024,256]{1,0:T(8,128)(2,1)}, bf16[1024,256]{1,0:T(8,128)(2,1)S(1)}, u32[]{:S(2)}, u32[]{:S(2)}) collective-permute-start(bf16[1024,256]{1,0:T(8,128)(2,1)} %get-tuple-element.15), channel_id=1, source_target_pairs={{4,0},{8,4},{12,8},{5,1},{9,5},{13,9},{6,2},{10,6},{14,10},{7,3},{... | collective-permute-start | bytes 1572872 | tf_op jit(solution)/shard_map/ppermute | solution.py:70
  36.8 87.3 %collective-permute-start.20 = (bf16[1024,256]{1,0:T(8,128)(2,1)S(1)}, bf16[1024,256]{1,0:T(8,128)(2,1)S(1)}, u32[]{:S(2)}, u32[]{:S(2)}) collective-permute-start(bf16[1024,256]{1,0:T(8,128)(2,1)S(1)} %collective-permute-done.10), channel_id=1, source_target_pairs={{4,20},{8,24},{12,28},{20,4},{24,8},{28,12},{5,21},{9,25},{13,29},... | collective-permute-start | bytes 1572872 | tf_op jit(solution)/shard_map/ppermute | solution.py:65
  37.5 44.2 %collective-permute-start.11 = (bf16[1024,256]{1,0:T(8,128)(2,1)S(1)}, bf16[1024,256]{1,0:T(8,128)(2,1)S(1)}, u32[]{:S(2)}, u32[]{:S(2)}) collective-permute-start(bf16[1024,256]{1,0:T(8,128)(2,1)S(1)} %collective-permute-done.10), channel_id=1, source_target_pairs={{4,8},{8,12},{5,9},{9,13},{6,10},{10,14},{7,11},{11,15},{20,24},{2... | collective-permute-start | bytes 1572872 | tf_op jit(solution)/shard_map/ppermute | solution.py:71
  54.7 22.1 %collective-permute-start.13 = (bf16[1024,256]{1,0:T(8,128)(2,1)S(1)}, bf16[1024,256]{1,0:T(8,128)(2,1)S(1)}, u32[]{:S(2)}, u32[]{:S(2)}) collective-permute-start(bf16[1024,256]{1,0:T(8,128)(2,1)S(1)} %collective-permute-done.9), channel_id=1, source_target_pairs={{4,0},{8,4},{5,1},{9,5},{6,2},{10,6},{7,3},{11,7},{20,16},{24,20},... | collective-permute-start | bytes 1572872 | tf_op jit(solution)/shard_map/ppermute | solution.py:70
  76.8 39.8 %collective-permute-start.14 = (bf16[1024,256]{1,0:T(8,128)(2,1)S(1)}, bf16[1024,256]{1,0:T(8,128)(2,1)S(1)}, u32[]{:S(2)}, u32[]{:S(2)}) collective-permute-start(bf16[1024,256]{1,0:T(8,128)(2,1)S(1)} %collective-permute-done.13), channel_id=1, source_target_pairs={{4,0},{5,1},{6,2},{7,3},{20,16},{21,17},{22,18},{23,19}} | collective-permute-start | bytes 1572872 | tf_op jit(solution)/shard_map/ppermute | solution.py:70
  78.2 56.0 %collective-permute-start.1 = (bf16[384,2048]{1,0:T(8,128)(2,1)S(1)}, bf16[384,2048]{1,0:T(8,128)(2,1)S(1)}, u32[]{:S(2)}, u32[]{:S(2)}) collective-permute-start(bf16[384,2048]{1,0:T(8,128)(2,1)S(1)} %pad_maximum_fusion), channel_id=1, source_target_pairs={{0,1},{1,0},{2,3},{3,2},{4,5},{5,4},{6,7},{7,6},{8,9},{9,8},{10,11... | collective-permute-start | bytes 4718600 | tf_op jit(solution)/shard_map/ppermute | solution.py:34
  78.3 43.1 %collective-permute-start.17 = (bf16[1024,256]{1,0:T(8,128)(2,1)S(1)}, bf16[1024,256]{1,0:T(8,128)(2,1)S(1)}, u32[]{:S(2)}, u32[]{:S(2)}) collective-permute-start(bf16[1024,256]{1,0:T(8,128)(2,1)S(1)} %collective-permute-done.13), channel_id=1, source_target_pairs={{0,16},{4,20},{16,0},{20,4},{1,17},{5,21},{17,1},{21,5},{2,18},{6,... | collective-permute-start | bytes 1572872 | tf_op jit(solution)/shard_map/ppermute | solution.py:65
  81.8 35.7 %collective-permute-start.12 = (bf16[1024,256]{1,0:T(8,128)(2,1)S(1)}, bf16[1024,256]{1,0:T(8,128)(2,1)S(1)}, u32[]{:S(2)}, u32[]{:S(2)}) collective-permute-start(bf16[1024,256]{1,0:T(8,128)(2,1)S(1)} %collective-permute-done.11), channel_id=1, source_target_pairs={{8,12},{9,13},{10,14},{11,15},{24,28},{25,29},{26,30},{27,31}} | collective-permute-start | bytes 1572872 | tf_op jit(solution)/shard_map/ppermute | solution.py:71
  117.4 11.1 %collective-permute-start.19 = (bf16[1024,256]{1,0:T(8,128)(2,1)S(1)}, bf16[1024,256]{1,0:T(8,128)(2,1)S(1)}, u32[]{:S(2)}, u32[]{:S(2)}) collective-permute-start(bf16[1024,256]{1,0:T(8,128)(2,1)S(1)} %collective-permute-done.14), channel_id=1, source_target_pairs={{0,16},{16,0},{1,17},{17,1},{2,18},{18,2},{3,19},{19,3}} | collective-permute-start | bytes 1572872 | tf_op jit(solution)/shard_map/ppermute | solution.py:65
  121.4 12.7 %collective-permute-start.15 = (bf16[1024,256]{1,0:T(8,128)(2,1)S(1)}, bf16[1024,256]{1,0:T(8,128)(2,1)S(1)}, u32[]{:S(2)}, u32[]{:S(2)}) collective-permute-start(bf16[1024,256]{1,0:T(8,128)(2,1)S(1)} %collective-permute-done.9), channel_id=1, source_target_pairs={{0,16},{4,20},{8,24},{16,0},{20,4},{24,8},{1,17},{5,21},{9,25},{17... | collective-permute-start | bytes 1572872 | tf_op jit(solution)/shard_map/ppermute | solution.py:65
  123.4 10.8 %collective-permute-start.16 = (bf16[1024,256]{1,0:T(8,128)(2,1)S(1)}, bf16[1024,256]{1,0:T(8,128)(2,1)S(1)}, u32[]{:S(2)}, u32[]{:S(2)}) collective-permute-start(bf16[1024,256]{1,0:T(8,128)(2,1)S(1)} %collective-permute-done.12), channel_id=1, source_target_pairs={{12,28},{28,12},{13,29},{29,13},{14,30},{30,14},{15,31},{31,15}} | collective-permute-start | bytes 1572872 | tf_op jit(solution)/shard_map/ppermute | solution.py:65
  152.5 15.8 %collective-permute-start.25 = (bf16[384,512]{0,1:T(8,128)(2,1)}, bf16[384,512]{0,1:T(8,128)(2,1)}, u32[]{:S(2)}, u32[]{:S(2)}) collective-permute-start(bf16[384,512]{0,1:T(8,128)(2,1)} %collective-permute-done.21), channel_id=1, source_target_pairs={{4,0},{8,4},{5,1},{9,5},{6,2},{10,6},{7,3},{11,7},{20,16},{24,20},... | collective-permute-start | bytes 1179656 | tf_op jit(solution)/shard_map/ppermute | solution.py:22
  153.8 17.3 %collective-permute-start.23 = (bf16[384,512]{0,1:T(8,128)(2,1)}, bf16[384,512]{0,1:T(8,128)(2,1)S(1)}, u32[]{:S(2)}, u32[]{:S(2)}) collective-permute-start(bf16[384,512]{0,1:T(8,128)(2,1)} %collective-permute-done.22), channel_id=1, source_target_pairs={{4,8},{8,12},{5,9},{9,13},{6,10},{10,14},{7,11},{11,15},{20,24},{2... | collective-permute-start | bytes 1179656 | tf_op jit(solution)/shard_map/ppermute | solution.py:23
  159.1 36.3 %collective-permute-start.2 = (bf16[3072,256]{1,0:T(8,128)(2,1)}, bf16[3072,256]{1,0:T(8,128)(2,1)}, u32[]{:S(2)}, u32[]{:S(2)}) collective-permute-start(bf16[3072,256]{1,0:T(8,128)(2,1)} %slice.24), channel_id=1, source_target_pairs={{0,16},{16,0},{1,17},{17,1},{2,18},{18,2},{3,19},{19,3},{4,20},{20... | collective-permute-start | bytes 4718600 | tf_op jit(solution)/shard_map/ppermute | solution.py:51
  168.4 11.1 %collective-permute-start.26 = (bf16[384,512]{0,1:T(8,128)(2,1)}, bf16[384,512]{0,1:T(8,128)(2,1)S(1)}, u32[]{:S(2)}, u32[]{:S(2)}) collective-permute-start(bf16[384,512]{0,1:T(8,128)(2,1)} %collective-permute-done.25), channel_id=1, source_target_pairs={{4,0},{5,1},{6,2},{7,3},{20,16},{21,17},{22,18},{23,19}} | collective-permute-start | bytes 1179656 | tf_op jit(solution)/shard_map/ppermute | solution.py:22
  171.1 44.1 %collective-permute-start.27 = (bf16[3072,256]{1,0:T(8,128)(2,1)S(1)}, bf16[3072,256]{1,0:T(8,128)(2,1)S(1)}, u32[]{:S(2)}, u32[]{:S(2)}) collective-permute-start(bf16[3072,256]{1,0:T(8,128)(2,1)S(1)} %slice.22), channel_id=1, source_target_pairs={{0,16},{16,0},{1,17},{17,1},{2,18},{18,2},{3,19},{19,3},{4,20},{20... | collective-permute-start | bytes 4718600 | tf_op jit(solution)/shard_map/ppermute | solution.py:51
  198.1 15.8 %collective-permute-start.3 = (bf16[384,512]{0,1:T(8,128)(2,1)S(1)}, bf16[384,512]{0,1:T(8,128)(2,1)S(1)}, u32[]{:S(2)}, u32[]{:S(2)}) collective-permute-start(bf16[384,512]{0,1:T(8,128)(2,1)S(1)} %pad_maximum_fusion.3), channel_id=1, source_target_pairs={{4,0},{8,4},{12,8},{5,1},{9,5},{13,9},{6,2},{10,6},{14,10},{7,3},{... | collective-permute-start | bytes 1179656 | tf_op jit(solution)/shard_map/ppermute | solution.py:22
  200.3 16.2 %collective-permute-start.4 = (bf16[384,512]{0,1:T(8,128)(2,1)S(1)}, bf16[384,512]{0,1:T(8,128)(2,1)S(1)}, u32[]{:S(2)}, u32[]{:S(2)}) collective-permute-start(bf16[384,512]{0,1:T(8,128)(2,1)S(1)} %pad_maximum_fusion.3), channel_id=1, source_target_pairs={{0,4},{4,8},{8,12},{1,5},{5,9},{9,13},{2,6},{6,10},{10,14},{3,7},{... | collective-permute-start | bytes 1179656 | tf_op jit(solution)/shard_map/ppermute | solution.py:23
  223.5 18.7 %collective-permute-start.8 = (bf16[384,512]{0,1:T(8,128)(2,1)S(1)}, bf16[384,512]{0,1:T(8,128)(2,1)S(1)}, u32[]{:S(2)}, u32[]{:S(2)}) collective-permute-start(bf16[384,512]{0,1:T(8,128)(2,1)S(1)} %collective-permute-done.7), channel_id=1, source_target_pairs={{4,0},{5,1},{6,2},{7,3},{20,16},{21,17},{22,18},{23,19}} | collective-permute-start | bytes 1179656 | tf_op jit(solution)/shard_map/ppermute | solution.py:22
  226.0 16.3 %collective-permute-start.6 = (bf16[384,512]{0,1:T(8,128)(2,1)S(1)}, bf16[384,512]{0,1:T(8,128)(2,1)S(1)}, u32[]{:S(2)}, u32[]{:S(2)}) collective-permute-start(bf16[384,512]{0,1:T(8,128)(2,1)S(1)} %collective-permute-done.5), channel_id=1, source_target_pairs={{8,12},{9,13},{10,14},{11,15},{24,28},{25,29},{26,30},{27,31}} | collective-permute-start | bytes 1179656 | tf_op jit(solution)/shard_map/ppermute | solution.py:23
  (14 other events, 176.3 us)
Sparse Core Ops, SparseCore 0:
  9.1 63.1 all-gather.2
  73.9 50.8 all-gather.4

commit v14 on v10

--- a/solution.py
+++ b/solution.py
@@ -2,6 +2,7 @@
 import jax.numpy as jnp
 from jax import lax
 from jax.sharding import PartitionSpec as P
+from jax.experimental import pallas as pl
 
 HD = 128
 SPAN = 4
@@ -52,6 +53,35 @@
     return [own, (kept, other)]
 
 
+def late_kernel(block_ref, kept_ref, other_ref, keys_ref, values_ref, out_ref):
+    rows = kept_ref.shape[0]
+    query = jnp.dot(block_ref[:, :rows], kept_ref[...], preferred_element_type=jnp.float32)
+    query = query + jnp.dot(block_ref[:, rows:], other_ref[...], preferred_element_type=jnp.float32)
+    query = query.astype(jnp.bfloat16)
+    scale = 1.0 / jnp.sqrt(jnp.float32(HD))
+    for head in range(out_ref.shape[1] // HD):
+        cols = slice(head * HD, (head + 1) * HD)
+        scores = lax.dot_general(
+            query[:, cols],
+            keys_ref[:, cols],
+            (((1,), (1,)), ((), ())),
+            preferred_element_type=jnp.float32,
+        ) * scale
+        largest = scores.max(axis=-1, keepdims=True)
+        expos = jnp.exp(scores - largest)
+        total = expos.sum(axis=-1, keepdims=True)
+        summed = jnp.dot(expos.astype(jnp.bfloat16), values_ref[:, cols], preferred_element_type=jnp.float32)
+        out_ref[:, cols] = (summed / total).astype(jnp.bfloat16)
+
+
+def late_half(block, kept, other, keys, values, interpret=False):
+    return pl.pallas_call(
+        late_kernel,
+        out_shape=jax.ShapeDtypeStruct((block.shape[0], kept.shape[1]), jnp.bfloat16),
+        interpret=interpret,
+    )(block, kept, other, keys, values)
+
+
 def per_device(acts, w_query, w_key, w_value):
     block = swap_gather(acts, "row", 0)
     block = swap_gather(block, "col", 1)
@@ -64,18 +94,12 @@
 
     def product(piece):
         if isinstance(piece, tuple):
-            kept, other = piece
-            rows = kept.shape[0]
-            early = jnp.dot(block[:, :rows], kept, preferred_element_type=jnp.float32)
-            return early + jnp.dot(block[:, rows:], other, preferred_element_type=jnp.float32)
-        return jnp.dot(block, piece, preferred_element_type=jnp.float32)
+            piece = jnp.concatenate(piece, axis=0)
+        return jnp.dot(block, piece, preferred_element_type=jnp.float32).astype(jnp.bfloat16)
 
-    def project(weight, after=None):
-        return [product(piece).astype(jnp.bfloat16) for piece in full_columns(weight, shared, after)]
-
-    key = jnp.concatenate(project(w_key), axis=1)
-    value = jnp.concatenate(project(w_value), axis=1)
-    queries = project(w_query, key)
+    key = jnp.concatenate([product(piece) for piece in full_columns(w_key, shared)], axis=1)
+    value = jnp.concatenate([product(piece) for piece in full_columns(w_value, shared)], axis=1)
+    queries = full_columns(w_query, shared, key)
     if lax.axis_size("seq") == SPAN:
         seen = jnp.stack([line_gather(key), line_gather(value)])
     else:
@@ -91,7 +115,14 @@
     scale = 1.0 / jnp.sqrt(jnp.float32(HD))
     outputs = []
     first = 0
-    for query in queries:
+    for piece in queries:
+        if isinstance(piece, tuple):
+            count = piece[0].shape[1] // HD
+            columns = slice(first * HD, (first + count) * HD)
+            first += count
+            outputs.append(late_half(block, piece[0], piece[1], seen[0][:, columns], seen[1][:, columns]))
+            continue
+        query = product(piece)
         count = query.shape[1] // HD
         query = query.reshape(tokens_here, count, HD)
         part_keys = seen_keys[:, first : first + count]

time: 228 us -> 228 us (level)
  Pallas kernels: 0 us -> 8.17 us
  matrix products: 17.1 us -> 9.38 us
  local copies, waits for them, and re-layouts: 8.29 us -> 14.1 us
  starting transfers between devices: 29.4 us -> 24.6 us
    ppermute x6, waiting for transfers between devices: 30.1 us -> 16.2 us  [line_gather(): lax.ppermute(from_right[-1], 'seq', [(j, j - 1) for j in range(1, n - k +...]
    ppermute x6, waiting for transfers between devices: 0.02 us -> 11.6 us  [line_gather(): lax.ppermute(from_left[-1], 'seq', [(j, j + 1) for j in range(k - 1, n -...]
    pallas_call x0 -> x1, Pallas kernels: none -> 8.17 us  [late_half(): pl.pallas_call(late_kernel, out_shape=jax.ShapeDtypeStruct((block.shape[0...]
    dot_general x9 -> x5, matrix products: 13.1 us -> 7.36 us  [product(): jnp.dot(block, piece, preferred_element_type=jnp.float32)]
    ppermute x6, starting transfers between devices: 14.1 us -> 9.12 us  [line_gather(): lax.ppermute(from_left[-1], 'seq', [(j, j + 1) for j in range(k - 1, n -...]
    select_n x6, other arithmetic: 3.34 us -> 5.85 us  [line_gather(): slots.append(jnp.where(here + m < n, from_right[m], from_left[n - m]))]
    slice x0 -> x3, local copies, waits for them, and re-layouts: none -> 2.5 us  [the longest x1 0.99 us: per_device(): seen[0][:, columns]]
  transfers between devices with their start and end apart: 20 -> 20, of which waited for: 10 -> 11; matrix products, arithmetic and copies ran while one was open for 18% -> 20% of each run, Pallas kernels for 0% -> 0%
where the time goes in v14:
time: 228 us; the launch traced here: 226 us
  waiting for transfers between devices  128 us (56%)
  other arithmetic  27.9 us (12%)
  starting transfers between devices  24.6 us (11%)
  local copies, waits for them, and re-layouts  14.1 us (6%)
  between operations  13.6 us (6%)
  matrix products  9.38 us (4%)
  Pallas kernels  8.17 us (4%)
    all_gather x3, waiting for transfers between devices, full_columns(): own = lax.all_gather(own, 'seq', axis=0, tiled=True)  59.4 us
    ppermute x3, waiting for transfers between devices, full_columns(): other = lax.ppermute(own[rows:], 'groups', [(0, 1), (1, 0)])  22.3 us
    ppermute x2, waiting for transfers between devices, swap_gather(): other = lax.ppermute(piece, axis, [(0, 1), (1, 0)])  19 us
    ppermute x6, waiting for transfers between devices, line_gather(): lax.ppermute(from_right[-1], 'seq', [(j, j - 1) for j in range(1, n - k +...  16.2 us
    ppermute x6, waiting for transfers between devices, line_gather(): lax.ppermute(from_left[-1], 'seq', [(j, j + 1) for j in range(k - 1, n -...  11.6 us
    ppermute x6, starting transfers between devices, line_gather(): lax.ppermute(from_left[-1], 'seq', [(j, j + 1) for j in range(k - 1, n -...  9.12 us
    concatenate x3, other arithmetic, full_columns(): own = jnp.roll(own, -lax.axis_index('seq') * rows, axis=0)  9.02 us
    pallas_call x1, Pallas kernels, late_half(): pl.pallas_call(late_kernel, out_shape=jax.ShapeDtypeStruct((block.shape[0...  8.17 us
  transfers between devices with their start and end apart: 20, of which 11 were waited for; matrix products, arithmetic and copies ran while one was open for 20% of the time, Pallas kernels for 0%

profile of v14, /device:TPU:0, one launch (start us, length us, event | category | flops | bytes accessed | tf_op | source)
XLA Modules:
  0.0 226.2 jit_solution(17587198207464870635)
XLA Ops:
  6.5 2.4 %constant_dynamic-slice_fusion.1 = (bf16[1024,256]{1,0:T(8,128)(2,1)}, bf16[1024,256]{1,0:T(8,128)(2,1)}) fusion(bf16[1024,512]{1,0:T(8,128)(2,1)} %param.8, s32[]{:T(128)S(6)} %select_n.105, s32[]{:T(128)S(6)} %select_n.104), kind=kLoop, calls=%fused_computation.64 | loop fusion | bytes 2097160 | tf_op jit(solution)/shard_map/dynamic_slice | solution.py:47
  9.1 3.0 %collective-permute-start = (bf16[192,2048]{1,0:T(8,128)(2,1)}, bf16[192,2048]{1,0:T(8,128)(2,1)S(1)}, u32[]{:S(2)}, u32[]{:S(2)}) collective-permute-start(bf16[192,2048]{1,0:T(8,128)(2,1)} %param.6), channel_id=1, source_target_pairs={{0,2},{2,0},{1,3},{3,1},{4,6},{6,4},{5,7},{7,5},{8,10},{10,8},{9,1... | collective-permute-start | bytes 2359304 | tf_op jit(solution)/shard_map/ppermute | solution.py:35
  13.2 16.6 %collective-permute-done = bf16[192,2048]{1,0:T(8,128)(2,1)S(1)} collective-permute-done((bf16[192,2048]{1,0:T(8,128)(2,1)}, bf16[192,2048]{1,0:T(8,128)(2,1)S(1)}, u32[]{:S(2)}, u32[]{:S(2)}) %collective-permute-start) | collective-permute-done | bytes 786464 | tf_op jit(solution)/shard_map/ppermute | solution.py:35
  31.3 2.4 %collective-permute-done.1 = bf16[384,2048]{1,0:T(8,128)(2,1)} collective-permute-done((bf16[384,2048]{1,0:T(8,128)(2,1)S(1)}, bf16[384,2048]{1,0:T(8,128)(2,1)}, u32[]{:S(2)}, u32[]{:S(2)}) %collective-permute-start.1) | collective-permute-done | bytes 1572896 | tf_op jit(solution)/shard_map/ppermute | solution.py:35
  33.7 3.9 %broadcast_select_fusion = (bf16[384,2048]{1,0:T(8,128)(2,1)}, bf16[384,2048]{1,0:T(8,128)(2,1)}) fusion(bf16[384,2048]{1,0:T(8,128)(2,1)} %collective-permute-done.1, pred[]{:T(512)S(6)} %eq.12, bf16[192,2048]{1,0:T(8,128)(2,1)S(1)} %get-tuple-element.11, bf16[192,2048]{1,0:T(8,128)(2,1)S(1)} %get-tuple-element.10), kind=kLoop, calls=%fused_computation.34 | loop fusion | flops 4718592 | bytes 6291457 | tf_op jit(solution)/shard_map/jit(_where)/select_n | solution.py:37
  37.6 20.2 %all-gather.8.cloned.1.call-done = bf16[4096,256]{1,0:T(8,128)(2,1)} async-done(((bf16[1024,256]{1,0:T(8,128)(2,1)}), bf16[4096,256]{1,0:T(8,128)(2,1)}) %all-gather.8.cloned.1.call-update) | async-done | bytes 2097168 | tf_op jit(solution)/shard_map/all_gather | solution.py:48
  57.8 3.0 %fusion.9 = bf16[4096,256]{1,0:T(8,128)(2,1)S(1)} fusion(s32[]{:T(128)S(6)} %select_n.103, bf16[4096,256]{1,0:T(8,128)(2,1)} %all-gather.8.cloned.1.call-done), kind=kLoop, calls=%fused_computation.20 | loop fusion | flops 4194304 | bytes 4194308 | tf_op jit(solution)/shard_map/jit(_roll_dynamic)/concatenate | solution.py:49
  64.9 39.2 %all-gather.4.cloned.1.call-done = bf16[4096,256]{1,0:T(8,128)(2,1)} async-done(((bf16[1024,256]{1,0:T(8,128)(2,1)}), bf16[4096,256]{1,0:T(8,128)(2,1)}) %all-gather.4.cloned.1.call-update) | async-done | bytes 2097168 | tf_op jit(solution)/shard_map/all_gather | solution.py:48
  104.1 3.0 %fusion.11 = bf16[4096,256]{1,0:T(8,128)(2,1)S(1)} fusion(s32[]{:T(128)S(6)} %select_n.103, bf16[4096,256]{1,0:T(8,128)(2,1)} %all-gather.4.cloned.1.call-done), kind=kLoop, calls=%fused_computation.22 | loop fusion | flops 4194304 | bytes 4194308 | tf_op jit(solution)/shard_map/jit(_roll_dynamic)/concatenate | solution.py:49
  108.7 3.7 %fusion.4.block_ref = bf16[384,4096]{1,0:T(8,128)(2,1)S(1)} fusion(s32[]{:T(128)S(6)} %select_n.103, bf16[384,2048]{1,0:T(8,128)(2,1)} %get-tuple-element.9, bf16[384,2048]{1,0:T(8,128)(2,1)} %get-tuple-element.8), kind=kLoop, calls=%fused_computation.16 | loop fusion | flops 12582912 | bytes 6291460 | tf_op jit(solution)/shard_map/jit(_roll_dynamic)/concatenate | solution.py:93
  114.7 2.5 %fusion.23 = bf16[384,256]{1,0:T(8,128)(2,1)S(1)} fusion(bf16[384,4096]{1,0:T(8,128)(2,1)S(1)} %fusion.4.block_ref, bf16[3072,256]{1,0:T(8,128)(2,1)} %collective-permute-done.9, bf16[1024,256]{1,0:T(8,128)(2,1)S(1)} %copy-done.13), kind=kOutput, calls=%fused_computation.37 | convolution fusion | flops 809598976 | bytes 5439488 | tf_op jit(solution)/shard_map/dot_general | solution.py:98
  117.2 2.6 %collective-permute-start.11 = (bf16[384,512]{1,0:T(8,128)(2,1)S(1)}, bf16[384,512]{1,0:T(8,128)(2,1)}, u32[]{:S(2)}, u32[]{:S(2)}) collective-permute-start(bf16[384,512]{1,0:T(8,128)(2,1)S(1)} %pad_maximum_fusion.4), channel_id=1, source_target_pairs={{0,4},{4,8},{8,12},{1,5},{5,9},{9,13},{2,6},{6,10},{10,14},{3,7},{... | collective-permute-start | bytes 1179656 | tf_op jit(solution)/shard_map/ppermute | solution.py:24
  121.1 22.3 %collective-permute-done.2 = bf16[3072,256]{1,0:T(8,128)(2,1)S(1)} collective-permute-done((bf16[3072,256]{1,0:T(8,128)(2,1)S(1)}, bf16[3072,256]{1,0:T(8,128)(2,1)S(1)}, u32[]{:S(2)}, u32[]{:S(2)}) %collective-permute-start.2) | collective-permute-done | bytes 1572896 | tf_op jit(solution)/shard_map/ppermute | solution.py:52
  145.2 2.2 collective-permute-start.4
  151.9 11.6 %collective-permute-done.4 = bf16[384,512]{1,0:T(8,128)(2,1)} collective-permute-done((bf16[384,512]{1,0:T(8,128)(2,1)}, bf16[384,512]{1,0:T(8,128)(2,1)}, u32[]{:S(2)}, u32[]{:S(2)}) %collective-permute-start.4) | collective-permute-done | bytes 393248 | tf_op jit(solution)/shard_map/ppermute | solution.py:24
  167.4 3.0 %fusion.10 = bf16[4096,256]{1,0:T(8,128)(2,1)S(1)} fusion(s32[]{:T(128)S(6)} %select_n.103, bf16[4096,256]{1,0:T(8,128)(2,1)} %all-gather.6.cloned.1.call-done), kind=kLoop, calls=%fused_computation.21 | loop fusion | flops 4194304 | bytes 4194308 | tf_op jit(solution)/shard_map/jit(_roll_dynamic)/concatenate | solution.py:49
  173.2 2.0 convolution_convert_fusion
  178.0 4.3 %collective-permute-done.7 = bf16[384,512]{1,0:T(8,128)(2,1)} collective-permute-done((bf16[384,512]{1,0:T(8,128)(2,1)}, bf16[384,512]{1,0:T(8,128)(2,1)}, u32[]{:S(2)}, u32[]{:S(2)}) %collective-permute-start.7) | collective-permute-done | bytes 393248 | tf_op jit(solution)/shard_map/ppermute | solution.py:23
  186.8 1.9 broadcast_select_fusion.9
  188.6 4.0 %collective-permute-done.15 = bf16[384,512]{1,0:T(8,128)(2,1)S(1)} collective-permute-done((bf16[384,512]{1,0:T(8,128)(2,1)}, bf16[384,512]{1,0:T(8,128)(2,1)S(1)}, u32[]{:S(2)}, u32[]{:S(2)}) %collective-permute-start.15) | collective-permute-done | bytes 393248 | tf_op jit(solution)/shard_map/ppermute | solution.py:23
  192.9 6.4 %collective-permute-done.8 = bf16[384,512]{1,0:T(8,128)(2,1)S(1)} collective-permute-done((bf16[384,512]{1,0:T(8,128)(2,1)}, bf16[384,512]{1,0:T(8,128)(2,1)S(1)}, u32[]{:S(2)}, u32[]{:S(2)}) %collective-permute-start.8) | collective-permute-done | bytes 393248 | tf_op jit(solution)/shard_map/ppermute | solution.py:23
  203.7 1.6 copy.18
  209.5 8.2 %shard_map.46 = bf16[384,256]{1,0:T(8,128)(2,1)} custom-call(bf16[384,4096]{1,0:T(8,128)(2,1)} %copy-done, bf16[1024,256]{1,0:T(8,128)(2,1)} %get-tuple-element.12.kept_ref, bf16[3072,256]{1,0:T(8,128)(2,1)} %collective-permute-done.16.other_ref, bf16[1536,256]{1,0:T(8,128)(2,1)} %slice.31.keys_ref, bf16[1536,256]{1,0:T(8,128)(2,1)} %slice.32.values_ref), custom_call_target="tpu_custom_call" | custom-call | tf_op jit(solution)/shard_map/pallas_call | solution.py:78
  217.7 1.9 fusion.39
  (90 shorter events, 40.8 us)
Async XLA Ops:
  6.5 51.3 %all-gather.8.cloned.1.call-start = ((), (), s32[]{:S(2)}) async-start(), calls=%async_computation.2 | async-start | bytes 2621440 | tf_op jit(solution)/shard_map/all_gather | solution.py:48
  9.0 95.0 %all-gather.4.cloned.1.call-start = ((), (), s32[]{:S(2)}) async-start(), calls=%async_computation | async-start | bytes 2621440 | tf_op jit(solution)/shard_map/all_gather | solution.py:48
  9.1 20.8 %collective-permute-start = (bf16[192,2048]{1,0:T(8,128)(2,1)}, bf16[192,2048]{1,0:T(8,128)(2,1)S(1)}, u32[]{:S(2)}, u32[]{:S(2)}) collective-permute-start(bf16[192,2048]{1,0:T(8,128)(2,1)} %param.6), channel_id=1, source_target_pairs={{0,2},{2,0},{1,3},{3,1},{4,6},{6,4},{5,7},{7,5},{8,10},{10,8},{9,1... | collective-permute-start | bytes 2359304 | tf_op jit(solution)/shard_map/ppermute | solution.py:35
  13.2 154.2 %all-gather.6.cloned.1.call-start = ((), (), s32[]{:S(2)}) async-start(), calls=%async_computation.1 | async-start | bytes 2621440 | tf_op jit(solution)/shard_map/all_gather | solution.py:48
  30.1 3.6 %collective-permute-start.1 = (bf16[384,2048]{1,0:T(8,128)(2,1)S(1)}, bf16[384,2048]{1,0:T(8,128)(2,1)}, u32[]{:S(2)}, u32[]{:S(2)}) collective-permute-start(bf16[384,2048]{1,0:T(8,128)(2,1)S(1)} %pad_maximum_fusion), channel_id=1, source_target_pairs={{0,1},{1,0},{2,3},{3,2},{4,5},{5,4},{6,7},{7,6},{8,9},{9,8},{10,11... | collective-permute-start | bytes 4718600 | tf_op jit(solution)/shard_map/ppermute | solution.py:35
  63.4 51.0 %collective-permute-start.9 = (bf16[3072,256]{1,0:T(8,128)(2,1)}, bf16[3072,256]{1,0:T(8,128)(2,1)}, u32[]{:S(2)}, u32[]{:S(2)}) collective-permute-start(bf16[3072,256]{1,0:T(8,128)(2,1)} %slice.29), channel_id=1, source_target_pairs={{0,16},{16,0},{1,17},{17,1},{2,18},{18,2},{3,19},{19,3},{4,20},{20... | collective-permute-start | bytes 4718600 | tf_op jit(solution)/shard_map/ppermute | solution.py:52
  107.2 36.2 %collective-permute-start.2 = (bf16[3072,256]{1,0:T(8,128)(2,1)S(1)}, bf16[3072,256]{1,0:T(8,128)(2,1)S(1)}, u32[]{:S(2)}, u32[]{:S(2)}) collective-permute-start(bf16[3072,256]{1,0:T(8,128)(2,1)S(1)} %slice.28), channel_id=1, source_target_pairs={{0,16},{16,0},{1,17},{17,1},{2,18},{18,2},{3,19},{19,3},{4,20},{20... | collective-permute-start | bytes 4718600 | tf_op jit(solution)/shard_map/ppermute | solution.py:52
  112.4 60.8 %copy-start = (bf16[384,4096]{1,0:T(8,128)(2,1)}, bf16[384,4096]{1,0:T(8,128)(2,1)S(1)}, u32[]{:S(2)}) copy-start(bf16[384,4096]{1,0:T(8,128)(2,1)S(1)} %fusion.4.block_ref) | copy-start | bytes 9437188
  114.4 29.9 %copy-start.6 = (bf16[384,256]{1,0:T(8,128)(2,1)}, bf16[384,256]{1,0:T(8,128)(2,1)S(1)}, u32[]{:S(2)}) copy-start(bf16[384,256]{1,0:T(8,128)(2,1)S(1)} %convolution_convert_fusion.2) | copy-start | bytes 589828
  114.7 28.6 %copy-start.14 = (bf16[1024,256]{1,0:T(8,128)(2,1)S(1)}, bf16[1024,256]{1,0:T(8,128)(2,1)}, u32[]{:S(2)}) copy-start(bf16[1024,256]{1,0:T(8,128)(2,1)} %get-tuple-element.16) | copy-start | bytes 1572868
  117.2 27.2 %copy-start.9 = (bf16[384,256]{1,0:T(8,128)(2,1)}, bf16[384,256]{1,0:T(8,128)(2,1)S(1)}, u32[]{:S(2)}) copy-start(bf16[384,256]{1,0:T(8,128)(2,1)S(1)} %fusion.23) | copy-start | bytes 589828
  117.2 31.5 %collective-permute-start.11 = (bf16[384,512]{1,0:T(8,128)(2,1)S(1)}, bf16[384,512]{1,0:T(8,128)(2,1)}, u32[]{:S(2)}, u32[]{:S(2)}) collective-permute-start(bf16[384,512]{1,0:T(8,128)(2,1)S(1)} %pad_maximum_fusion.4), channel_id=1, source_target_pairs={{0,4},{4,8},{8,12},{1,5},{5,9},{9,13},{2,6},{6,10},{10,14},{3,7},{... | collective-permute-start | bytes 1179656 | tf_op jit(solution)/shard_map/ppermute | solution.py:24
  119.8 30.8 %collective-permute-start.10 = (bf16[384,512]{1,0:T(8,128)(2,1)S(1)}, bf16[384,512]{1,0:T(8,128)(2,1)}, u32[]{:S(2)}, u32[]{:S(2)}) collective-permute-start(bf16[384,512]{1,0:T(8,128)(2,1)S(1)} %pad_maximum_fusion.4), channel_id=1, source_target_pairs={{4,0},{8,4},{12,8},{5,1},{9,5},{13,9},{6,2},{10,6},{14,10},{7,3},{... | collective-permute-start | bytes 1179656 | tf_op jit(solution)/shard_map/ppermute | solution.py:23
  145.2 18.3 %collective-permute-start.4 = (bf16[384,512]{1,0:T(8,128)(2,1)}, bf16[384,512]{1,0:T(8,128)(2,1)}, u32[]{:S(2)}, u32[]{:S(2)}) collective-permute-start(bf16[384,512]{1,0:T(8,128)(2,1)} %pad_maximum_fusion.3), channel_id=1, source_target_pairs={{0,4},{4,8},{8,12},{1,5},{5,9},{9,13},{2,6},{6,10},{10,14},{3,7},{... | collective-permute-start | bytes 1179656 | tf_op jit(solution)/shard_map/ppermute | solution.py:24
  147.4 18.5 %collective-permute-start.3 = (bf16[384,512]{1,0:T(8,128)(2,1)}, bf16[384,512]{1,0:T(8,128)(2,1)}, u32[]{:S(2)}, u32[]{:S(2)}) collective-permute-start(bf16[384,512]{1,0:T(8,128)(2,1)} %pad_maximum_fusion.3), channel_id=1, source_target_pairs={{4,0},{8,4},{12,8},{5,1},{9,5},{13,9},{6,2},{10,6},{14,10},{7,3},{... | collective-permute-start | bytes 1179656 | tf_op jit(solution)/shard_map/ppermute | solution.py:23
  148.7 26.4 %collective-permute-start.12 = (bf16[384,512]{1,0:T(8,128)(2,1)}, bf16[384,512]{1,0:T(8,128)(2,1)}, u32[]{:S(2)}, u32[]{:S(2)}) collective-permute-start(bf16[384,512]{1,0:T(8,128)(2,1)} %collective-permute-done.11), channel_id=1, source_target_pairs={{4,8},{8,12},{5,9},{9,13},{6,10},{10,14},{7,11},{11,15},{20,24},{2... | collective-permute-start | bytes 1179656 | tf_op jit(solution)/shard_map/ppermute | solution.py:24
  150.6 25.4 %collective-permute-start.14 = (bf16[384,512]{1,0:T(8,128)(2,1)}, bf16[384,512]{1,0:T(8,128)(2,1)}, u32[]{:S(2)}, u32[]{:S(2)}) collective-permute-start(bf16[384,512]{1,0:T(8,128)(2,1)} %collective-permute-done.10), channel_id=1, source_target_pairs={{4,0},{8,4},{5,1},{9,5},{6,2},{10,6},{7,3},{11,7},{20,16},{24,20},... | collective-permute-start | bytes 1179656 | tf_op jit(solution)/shard_map/ppermute | solution.py:23
  163.4 13.8 %collective-permute-start.5 = (bf16[384,512]{1,0:T(8,128)(2,1)}, bf16[384,512]{1,0:T(8,128)(2,1)}, u32[]{:S(2)}, u32[]{:S(2)}) collective-permute-start(bf16[384,512]{1,0:T(8,128)(2,1)} %collective-permute-done.4), channel_id=1, source_target_pairs={{4,8},{8,12},{5,9},{9,13},{6,10},{10,14},{7,11},{11,15},{20,24},{2... | collective-permute-start | bytes 1179656 | tf_op jit(solution)/shard_map/ppermute | solution.py:24
  165.9 16.4 %collective-permute-start.7 = (bf16[384,512]{1,0:T(8,128)(2,1)}, bf16[384,512]{1,0:T(8,128)(2,1)}, u32[]{:S(2)}, u32[]{:S(2)}) collective-permute-start(bf16[384,512]{1,0:T(8,128)(2,1)} %collective-permute-done.3), channel_id=1, source_target_pairs={{4,0},{8,4},{5,1},{9,5},{6,2},{10,6},{7,3},{11,7},{20,16},{24,20},... | collective-permute-start | bytes 1179656 | tf_op jit(solution)/shard_map/ppermute | solution.py:23
  171.7 37.8 %collective-permute-start.16 = (bf16[3072,256]{1,0:T(8,128)(2,1)}, bf16[3072,256]{1,0:T(8,128)(2,1)}, u32[]{:S(2)}, u32[]{:S(2)}) collective-permute-start(bf16[3072,256]{1,0:T(8,128)(2,1)} %slice.25), channel_id=1, source_target_pairs={{0,16},{16,0},{1,17},{17,1},{2,18},{18,2},{3,19},{19,3},{4,20},{20... | collective-permute-start | bytes 4718600 | tf_op jit(solution)/shard_map/ppermute | solution.py:52
  175.2 10.5 %collective-permute-start.13 = (bf16[384,512]{1,0:T(8,128)(2,1)}, bf16[384,512]{1,0:T(8,128)(2,1)S(1)}, u32[]{:S(2)}, u32[]{:S(2)}) collective-permute-start(bf16[384,512]{1,0:T(8,128)(2,1)} %collective-permute-done.12), channel_id=1, source_target_pairs={{8,12},{9,13},{10,14},{11,15},{24,28},{25,29},{26,30},{27,31}} | collective-permute-start | bytes 1179656 | tf_op jit(solution)/shard_map/ppermute | solution.py:24
  176.0 16.7 %collective-permute-start.15 = (bf16[384,512]{1,0:T(8,128)(2,1)}, bf16[384,512]{1,0:T(8,128)(2,1)S(1)}, u32[]{:S(2)}, u32[]{:S(2)}) collective-permute-start(bf16[384,512]{1,0:T(8,128)(2,1)} %collective-permute-done.14), channel_id=1, source_target_pairs={{4,0},{5,1},{6,2},{7,3},{20,16},{21,17},{22,18},{23,19}} | collective-permute-start | bytes 1179656 | tf_op jit(solution)/shard_map/ppermute | solution.py:23
  177.3 9.5 %collective-permute-start.6 = (bf16[384,512]{1,0:T(8,128)(2,1)}, bf16[384,512]{1,0:T(8,128)(2,1)S(1)}, u32[]{:S(2)}, u32[]{:S(2)}) collective-permute-start(bf16[384,512]{1,0:T(8,128)(2,1)} %collective-permute-done.5), channel_id=1, source_target_pairs={{8,12},{9,13},{10,14},{11,15},{24,28},{25,29},{26,30},{27,31}} | collective-permute-start | bytes 1179656 | tf_op jit(solution)/shard_map/ppermute | solution.py:24
  182.3 16.9 %collective-permute-start.8 = (bf16[384,512]{1,0:T(8,128)(2,1)}, bf16[384,512]{1,0:T(8,128)(2,1)S(1)}, u32[]{:S(2)}, u32[]{:S(2)}) collective-permute-start(bf16[384,512]{1,0:T(8,128)(2,1)} %collective-permute-done.7), channel_id=1, source_target_pairs={{4,0},{5,1},{6,2},{7,3},{20,16},{21,17},{22,18},{23,19}} | collective-permute-start | bytes 1179656 | tf_op jit(solution)/shard_map/ppermute | solution.py:23
  (12 other events, 96.4 us)
Sparse Core Ops, SparseCore 0:
  9.1 48.6 all-gather.7
  59.4 44.6 all-gather.3
  105.6 57.4 all-gather.5

commit v15 on v14

--- a/solution.py
+++ b/solution.py
@@ -53,20 +53,13 @@
     return [own, (kept, other)]
 
 
-def late_kernel(block_ref, kept_ref, other_ref, keys_ref, values_ref, out_ref):
-    rows = kept_ref.shape[0]
-    query = jnp.dot(block_ref[:, :rows], kept_ref[...], preferred_element_type=jnp.float32)
-    query = query + jnp.dot(block_ref[:, rows:], other_ref[...], preferred_element_type=jnp.float32)
+def late_kernel(early_ref, block_ref, other_ref, keys_ref, values_ref, out_ref):
+    query = early_ref[...] + jnp.dot(block_ref[...], other_ref[...], preferred_element_type=jnp.float32)
     query = query.astype(jnp.bfloat16)
     scale = 1.0 / jnp.sqrt(jnp.float32(HD))
     for head in range(out_ref.shape[1] // HD):
         cols = slice(head * HD, (head + 1) * HD)
-        scores = lax.dot_general(
-            query[:, cols],
-            keys_ref[:, cols],
-            (((1,), (1,)), ((), ())),
-            preferred_element_type=jnp.float32,
-        ) * scale
+        scores = jnp.dot(query[:, cols], keys_ref[cols, :], preferred_element_type=jnp.float32) * scale
         largest = scores.max(axis=-1, keepdims=True)
         expos = jnp.exp(scores - largest)
         total = expos.sum(axis=-1, keepdims=True)
@@ -74,12 +67,12 @@
         out_ref[:, cols] = (summed / total).astype(jnp.bfloat16)
 
 
-def late_half(block, kept, other, keys, values, interpret=False):
+def late_half(early, block, other, keys_t, values, interpret=False):
     return pl.pallas_call(
         late_kernel,
-        out_shape=jax.ShapeDtypeStruct((block.shape[0], kept.shape[1]), jnp.bfloat16),
+        out_shape=jax.ShapeDtypeStruct(early.shape, jnp.bfloat16),
         interpret=interpret,
-    )(block, kept, other, keys, values)
+    )(early, block, other, keys_t, values)
 
 
 def per_device(acts, w_query, w_key, w_value):
@@ -120,7 +113,11 @@
             count = piece[0].shape[1] // HD
             columns = slice(first * HD, (first + count) * HD)
             first += count
-            outputs.append(late_half(block, piece[0], piece[1], seen[0][:, columns], seen[1][:, columns]))
+            rows = piece[0].shape[0]
+            early = jnp.dot(block[:, :rows], piece[0], preferred_element_type=jnp.float32)
+            outputs.append(
+                late_half(early, block[:, rows:], piece[1], seen[0][:, columns].T, seen[1][:, columns])
+            )
             continue
         query = product(piece)
         count = query.shape[1] // HD

time: 228 us -> 228 us (level)
  matrix products: 9.38 us -> 12.9 us
  local copies, waits for them, and re-layouts: 14.1 us -> 16.9 us
    ppermute x6, waiting for transfers between devices: 11.6 us -> 6.99 us  [line_gather(): lax.ppermute(from_left[-1], 'seq', [(j, j + 1) for j in range(k - 1, n -...]
    ppermute x6, waiting for transfers between devices: 16.2 us -> 18.7 us  [line_gather(): lax.ppermute(from_right[-1], 'seq', [(j, j - 1) for j in range(1, n - k +...]
    dynamic_slice x3 -> x2, local copies, waits for them, and re-layouts: 4.58 us -> 3.47 us  [full_columns(): kept = lax.dynamic_slice_in_dim(weight, (1 - group) * half, half, axis=1)]
  transfers between devices with their start and end apart: 20 -> 20, of which waited for: 11 -> 9; matrix products, arithmetic and copies ran while one was open for 20% -> 22% of each run, Pallas kernels for 0% -> 0%
where the time goes in v15:
time: 228 us; the launch traced here: 227 us
  waiting for transfers between devices  127 us (56%)
  other arithmetic  26 us (11%)
  starting transfers between devices  23.7 us (10%)
  local copies, waits for them, and re-layouts  16.9 us (7%)
  between operations  13.5 us (6%)
  matrix products  12.9 us (6%)
  Pallas kernels  7.38 us (3%)
    all_gather x3, waiting for transfers between devices, full_columns(): own = lax.all_gather(own, 'seq', axis=0, tiled=True)  58.1 us
    ppermute x3, waiting for transfers between devices, full_columns(): other = lax.ppermute(own[rows:], 'groups', [(0, 1), (1, 0)])  23.8 us
    ppermute x2, waiting for transfers between devices, swap_gather(): other = lax.ppermute(piece, axis, [(0, 1), (1, 0)])  19.5 us
    ppermute x6, waiting for transfers between devices, line_gather(): lax.ppermute(from_right[-1], 'seq', [(j, j - 1) for j in range(1, n - k +...  18.7 us
    concatenate x3, other arithmetic, full_columns(): own = jnp.roll(own, -lax.axis_index('seq') * rows, axis=0)  9.17 us
    dot_general x5, matrix products, product(): jnp.dot(block, piece, preferred_element_type=jnp.float32)  8.59 us
    ppermute x6, starting transfers between devices, line_gather(): lax.ppermute(from_left[-1], 'seq', [(j, j + 1) for j in range(k - 1, n -...  8.29 us
    ppermute x6, starting transfers between devices, line_gather(): lax.ppermute(from_right[-1], 'seq', [(j, j - 1) for j in range(1, n - k +...  7.88 us
  transfers between devices with their start and end apart: 20, of which 9 were waited for; matrix products, arithmetic and copies ran while one was open for 22% of the time, Pallas kernels for 0%

profile of v15, /device:TPU:0, one launch (start us, length us, event | category | flops | bytes accessed | tf_op | source)
XLA Modules:
  0.0 227.5 jit_solution(9574988128789795764)
XLA Ops:
  6.6 2.4 %constant_dynamic-slice_fusion = (bf16[1024,256]{1,0:T(8,128)(2,1)}, bf16[1024,256]{1,0:T(8,128)(2,1)}) fusion(bf16[1024,512]{1,0:T(8,128)(2,1)} %param.8, s32[]{:T(128)S(6)} %select_n.105, s32[]{:T(128)S(6)} %select_n.104), kind=kLoop, calls=%fused_computation.68 | loop fusion | bytes 2097160 | tf_op jit(solution)/shard_map/dynamic_slice | solution.py:47
  9.1 3.0 %collective-permute-start = (bf16[192,2048]{1,0:T(8,128)(2,1)}, bf16[192,2048]{1,0:T(8,128)(2,1)}, u32[]{:S(2)}, u32[]{:S(2)}) collective-permute-start(bf16[192,2048]{1,0:T(8,128)(2,1)} %param.6), channel_id=1, source_target_pairs={{0,2},{2,0},{1,3},{3,1},{4,6},{6,4},{5,7},{7,5},{8,10},{10,8},{9,1... | collective-permute-start | bytes 2359304 | tf_op jit(solution)/shard_map/ppermute | solution.py:35
  13.2 16.7 %collective-permute-done = bf16[192,2048]{1,0:T(8,128)(2,1)} collective-permute-done((bf16[192,2048]{1,0:T(8,128)(2,1)}, bf16[192,2048]{1,0:T(8,128)(2,1)}, u32[]{:S(2)}, u32[]{:S(2)}) %collective-permute-start) | collective-permute-done | bytes 786464 | tf_op jit(solution)/shard_map/ppermute | solution.py:35
  33.5 2.8 %collective-permute-done.1 = bf16[384,2048]{1,0:T(8,128)(2,1)} collective-permute-done((bf16[384,2048]{1,0:T(8,128)(2,1)}, bf16[384,2048]{1,0:T(8,128)(2,1)}, u32[]{:S(2)}, u32[]{:S(2)}) %collective-permute-start.1) | collective-permute-done | bytes 1572896 | tf_op jit(solution)/shard_map/ppermute | solution.py:35
  36.3 4.0 %broadcast_select_fusion = (bf16[384,2048]{1,0:T(8,128)(2,1)}, bf16[384,2048]{1,0:T(8,128)(2,1)}) fusion(bf16[384,2048]{1,0:T(8,128)(2,1)} %collective-permute-done.1, pred[]{:T(512)S(6)} %eq.12, bf16[192,2048]{1,0:T(8,128)(2,1)S(1)} %get-tuple-element.11, bf16[192,2048]{1,0:T(8,128)(2,1)S(1)} %get-tuple-element.10), kind=kLoop, calls=%fused_computation.34 | loop fusion | flops 4718592 | bytes 6291457 | tf_op jit(solution)/shard_map/jit(_where)/select_n | solution.py:37
  40.2 17.5 %all-gather.8.cloned.1.call-done = bf16[4096,256]{1,0:T(8,128)(2,1)} async-done(((bf16[1024,256]{1,0:T(8,128)(2,1)}), bf16[4096,256]{1,0:T(8,128)(2,1)}) %all-gather.8.cloned.1.call-update) | async-done | bytes 2097168 | tf_op jit(solution)/shard_map/all_gather | solution.py:48
  57.8 3.0 %fusion.9 = bf16[4096,256]{1,0:T(8,128)(2,1)S(1)} fusion(s32[]{:T(128)S(6)} %select_n.103, bf16[4096,256]{1,0:T(8,128)(2,1)} %all-gather.8.cloned.1.call-done), kind=kLoop, calls=%fused_computation.20 | loop fusion | flops 4194304 | bytes 4194308 | tf_op jit(solution)/shard_map/jit(_roll_dynamic)/concatenate | solution.py:49
  63.6 40.5 %all-gather.4.cloned.1.call-done = bf16[4096,256]{1,0:T(8,128)(2,1)} async-done(((bf16[1024,256]{1,0:T(8,128)(2,1)}), bf16[4096,256]{1,0:T(8,128)(2,1)}) %all-gather.4.cloned.1.call-update) | async-done | bytes 2097168 | tf_op jit(solution)/shard_map/all_gather | solution.py:48
  104.1 3.2 %fusion.11 = bf16[4096,256]{1,0:T(8,128)(2,1)S(1)} fusion(s32[]{:T(128)S(6)} %select_n.103, bf16[4096,256]{1,0:T(8,128)(2,1)} %all-gather.4.cloned.1.call-done), kind=kLoop, calls=%fused_computation.22 | loop fusion | flops 4194304 | bytes 4194308 | tf_op jit(solution)/shard_map/jit(_roll_dynamic)/concatenate | solution.py:49
  108.9 2.9 %fusion.4 = bf16[384,4096]{1,0:T(8,128)(2,1)S(1)} fusion(s32[]{:T(128)S(6)} %select_n.103, bf16[384,2048]{1,0:T(8,128)(2,1)S(1)} %copy-done.4, bf16[384,2048]{1,0:T(8,128)(2,1)S(1)} %copy-done.3), kind=kLoop, calls=%fused_computation.16 | loop fusion | flops 12582912 | bytes 6291460 | tf_op jit(solution)/shard_map/jit(_roll_dynamic)/concatenate | solution.py:86
  114.0 2.5 %fusion.23 = bf16[384,256]{1,0:T(8,128)(2,1)S(1)} fusion(bf16[384,4096]{1,0:T(8,128)(2,1)S(1)} %fusion.4, bf16[3072,256]{1,0:T(8,128)(2,1)} %collective-permute-done.9, bf16[1024,256]{1,0:T(8,128)(2,1)S(1)} %copy-done.8), kind=kOutput, calls=%fused_computation.37 | convolution fusion | flops 809598976 | bytes 5439488 | tf_op jit(solution)/shard_map/dot_general | solution.py:91
  116.5 1.9 collective-permute-start.11
  119.7 23.8 %collective-permute-done.2 = bf16[3072,256]{1,0:T(8,128)(2,1)S(1)} collective-permute-done((bf16[3072,256]{1,0:T(8,128)(2,1)S(1)}, bf16[3072,256]{1,0:T(8,128)(2,1)S(1)}, u32[]{:S(2)}, u32[]{:S(2)}) %collective-permute-start.2) | collective-permute-done | bytes 1572896 | tf_op jit(solution)/shard_map/ppermute | solution.py:52
  144.5 2.2 collective-permute-start.4
  148.1 3.2 %slice.40.block_ref = bf16[384,3072]{1,0:T(8,128)(2,1)} slice(bf16[384,4096]{1,0:T(8,128)(2,1)} %copy-done.2), slice={[0:384], [1024:4096]} | slice | bytes 4718592 | tf_op jit(solution)/shard_map/slice | solution.py:119
  151.3 2.3 fusion.35.early_ref
  156.3 7.0 %collective-permute-done.4 = bf16[384,512]{1,0:T(8,128)(2,1)} collective-permute-done((bf16[384,512]{1,0:T(8,128)(2,1)S(1)}, bf16[384,512]{1,0:T(8,128)(2,1)}, u32[]{:S(2)}, u32[]{:S(2)}) %collective-permute-start.4) | collective-permute-done | bytes 393248 | tf_op jit(solution)/shard_map/ppermute | solution.py:24
  164.0 2.0 collective-permute-done.3
  167.4 3.0 %fusion.10 = bf16[4096,256]{1,0:T(8,128)(2,1)S(1)} fusion(s32[]{:T(128)S(6)} %select_n.103, bf16[4096,256]{1,0:T(8,128)(2,1)} %all-gather.6.cloned.1.call-done), kind=kLoop, calls=%fused_computation.21 | loop fusion | flops 4194304 | bytes 4194308 | tf_op jit(solution)/shard_map/jit(_roll_dynamic)/concatenate | solution.py:49
  173.2 3.2 %convolution_convert_fusion = bf16[384,256]{0,1:T(8,128)(2,1)S(1)} fusion(bf16[384,4096]{1,0:T(8,128)(2,1)} %copy-done.2, bf16[4096,256]{1,0:T(8,128)(2,1)S(1)} %fusion.10), kind=kOutput, calls=%fused_computation.39 | convolution fusion | flops 805404672 | bytes 5439488 | tf_op jit(solution)/shard_map/dot_general | solution.py:91
  179.8 2.4 %collective-permute-done.7 = bf16[384,512]{1,0:T(8,128)(2,1)S(1)} collective-permute-done((bf16[384,512]{1,0:T(8,128)(2,1)}, bf16[384,512]{1,0:T(8,128)(2,1)S(1)}, u32[]{:S(2)}, u32[]{:S(2)}) %collective-permute-start.7) | collective-permute-done | bytes 393248 | tf_op jit(solution)/shard_map/ppermute | solution.py:23
  185.6 14.4 %collective-permute-done.8 = bf16[384,512]{1,0:T(8,128)(2,1)S(1)} collective-permute-done((bf16[384,512]{1,0:T(8,128)(2,1)S(1)}, bf16[384,512]{1,0:T(8,128)(2,1)S(1)}, u32[]{:S(2)}, u32[]{:S(2)}) %collective-permute-start.8) | collective-permute-done | bytes 393248 | tf_op jit(solution)/shard_map/ppermute | solution.py:23
  211.6 7.4 %shard_map.46 = bf16[384,256]{1,0:T(8,128)(2,1)} custom-call(f32[384,256]{1,0:T(8,128)} %fusion.35.early_ref, bf16[384,3072]{1,0:T(8,128)(2,1)} %slice.40.block_ref, bf16[3072,256]{1,0:T(8,128)(2,1)} %collective-permute-done.16.other_ref, bf16[256,1536]{1,0:T(8,128)(2,1)} %copy.13.keys_ref, bf16[1536,256]{1,0:T(8,128)(2,1)} %slice.42.values_ref), custom_call_target="tpu_custom_call" | custom-call | tf_op jit(solution)/shard_map/pallas_call | solution.py:71
  219.0 1.9 fusion.42
  (86 shorter events, 40.9 us)
Async XLA Ops:
  6.5 26.0 %copy-start = (bf16[1024,512]{1,0:T(8,128)(2,1)S(1)}, bf16[1024,512]{1,0:T(8,128)(2,1)}, u32[]{:S(2)}) copy-start(bf16[1024,512]{1,0:T(8,128)(2,1)} %param.7) | copy-start | bytes 3145732
  6.5 23.4 %copy-start.7 = (bf16[192,2048]{1,0:T(8,128)(2,1)S(1)}, bf16[192,2048]{1,0:T(8,128)(2,1)}, u32[]{:S(2)}) copy-start(bf16[192,2048]{1,0:T(8,128)(2,1)} %param.6) | copy-start | bytes 2359300
  6.5 51.3 %all-gather.8.cloned.1.call-start = ((), (), s32[]{:S(2)}) async-start(), calls=%async_computation.2 | async-start | bytes 2621440 | tf_op jit(solution)/shard_map/all_gather | solution.py:48
  9.0 95.0 %all-gather.4.cloned.1.call-start = ((), (), s32[]{:S(2)}) async-start(), calls=%async_computation | async-start | bytes 2621440 | tf_op jit(solution)/shard_map/all_gather | solution.py:48
  9.1 20.9 %collective-permute-start = (bf16[192,2048]{1,0:T(8,128)(2,1)}, bf16[192,2048]{1,0:T(8,128)(2,1)}, u32[]{:S(2)}, u32[]{:S(2)}) collective-permute-start(bf16[192,2048]{1,0:T(8,128)(2,1)} %param.6), channel_id=1, source_target_pairs={{0,2},{2,0},{1,3},{3,1},{4,6},{6,4},{5,7},{7,5},{8,10},{10,8},{9,1... | collective-permute-start | bytes 2359304 | tf_op jit(solution)/shard_map/ppermute | solution.py:35
  13.1 154.3 %all-gather.6.cloned.1.call-start = ((), (), s32[]{:S(2)}) async-start(), calls=%async_computation.1 | async-start | bytes 2621440 | tf_op jit(solution)/shard_map/all_gather | solution.py:48
  32.5 3.8 %collective-permute-start.1 = (bf16[384,2048]{1,0:T(8,128)(2,1)}, bf16[384,2048]{1,0:T(8,128)(2,1)}, u32[]{:S(2)}, u32[]{:S(2)}) collective-permute-start(bf16[384,2048]{1,0:T(8,128)(2,1)} %pad_maximum_fusion), channel_id=1, source_target_pairs={{0,1},{1,0},{2,3},{3,2},{4,5},{5,4},{6,7},{7,6},{8,9},{9,8},{10,11... | collective-permute-start | bytes 4718600 | tf_op jit(solution)/shard_map/ppermute | solution.py:35
  62.1 51.7 %collective-permute-start.9 = (bf16[3072,256]{1,0:T(8,128)(2,1)}, bf16[3072,256]{1,0:T(8,128)(2,1)}, u32[]{:S(2)}, u32[]{:S(2)}) collective-permute-start(bf16[3072,256]{1,0:T(8,128)(2,1)} %slice.37), channel_id=1, source_target_pairs={{0,16},{16,0},{1,17},{17,1},{2,18},{18,2},{3,19},{19,3},{4,20},{20... | collective-permute-start | bytes 4718600 | tf_op jit(solution)/shard_map/ppermute | solution.py:52
  107.3 36.2 %collective-permute-start.2 = (bf16[3072,256]{1,0:T(8,128)(2,1)S(1)}, bf16[3072,256]{1,0:T(8,128)(2,1)S(1)}, u32[]{:S(2)}, u32[]{:S(2)}) collective-permute-start(bf16[3072,256]{1,0:T(8,128)(2,1)S(1)} %slice.36), channel_id=1, source_target_pairs={{0,16},{16,0},{1,17},{17,1},{2,18},{18,2},{3,19},{19,3},{4,20},{20... | collective-permute-start | bytes 4718600 | tf_op jit(solution)/shard_map/ppermute | solution.py:52
  111.8 31.8 %copy-start.2 = (bf16[384,4096]{1,0:T(8,128)(2,1)}, bf16[384,4096]{1,0:T(8,128)(2,1)S(1)}, u32[]{:S(2)}) copy-start(bf16[384,4096]{1,0:T(8,128)(2,1)S(1)} %fusion.4) | copy-start | bytes 9437188
  114.0 29.5 %copy-start.9 = (bf16[1024,256]{1,0:T(8,128)(2,1)S(1)}, bf16[1024,256]{1,0:T(8,128)(2,1)}, u32[]{:S(2)}) copy-start(bf16[1024,256]{1,0:T(8,128)(2,1)} %get-tuple-element.14) | copy-start | bytes 1572868
  116.5 37.0 %collective-permute-start.11 = (bf16[384,512]{1,0:T(8,128)(2,1)S(1)}, bf16[384,512]{1,0:T(8,128)(2,1)S(1)}, u32[]{:S(2)}, u32[]{:S(2)}) collective-permute-start(bf16[384,512]{1,0:T(8,128)(2,1)S(1)} %pad_maximum_fusion.4), channel_id=1, source_target_pairs={{0,4},{4,8},{8,12},{1,5},{5,9},{9,13},{2,6},{6,10},{10,14},{3,7},{... | collective-permute-start | bytes 1179656 | tf_op jit(solution)/shard_map/ppermute | solution.py:24
  118.4 36.6 %collective-permute-start.10 = (bf16[384,512]{1,0:T(8,128)(2,1)S(1)}, bf16[384,512]{1,0:T(8,128)(2,1)S(1)}, u32[]{:S(2)}, u32[]{:S(2)}) collective-permute-start(bf16[384,512]{1,0:T(8,128)(2,1)S(1)} %pad_maximum_fusion.4), channel_id=1, source_target_pairs={{4,0},{8,4},{12,8},{5,1},{9,5},{13,9},{6,2},{10,6},{14,10},{7,3},{... | collective-permute-start | bytes 1179656 | tf_op jit(solution)/shard_map/ppermute | solution.py:23
  144.5 18.7 %collective-permute-start.4 = (bf16[384,512]{1,0:T(8,128)(2,1)S(1)}, bf16[384,512]{1,0:T(8,128)(2,1)}, u32[]{:S(2)}, u32[]{:S(2)}) collective-permute-start(bf16[384,512]{1,0:T(8,128)(2,1)S(1)} %pad_maximum_fusion.3), channel_id=1, source_target_pairs={{0,4},{4,8},{8,12},{1,5},{5,9},{9,13},{2,6},{6,10},{10,14},{3,7},{... | collective-permute-start | bytes 1179656 | tf_op jit(solution)/shard_map/ppermute | solution.py:24
  146.8 19.1 %collective-permute-start.3 = (bf16[384,512]{1,0:T(8,128)(2,1)S(1)}, bf16[384,512]{1,0:T(8,128)(2,1)}, u32[]{:S(2)}, u32[]{:S(2)}) collective-permute-start(bf16[384,512]{1,0:T(8,128)(2,1)S(1)} %pad_maximum_fusion.3), channel_id=1, source_target_pairs={{4,0},{8,4},{12,8},{5,1},{9,5},{13,9},{6,2},{10,6},{14,10},{7,3},{... | collective-permute-start | bytes 1179656 | tf_op jit(solution)/shard_map/ppermute | solution.py:23
  153.6 22.8 %collective-permute-start.12 = (bf16[384,512]{1,0:T(8,128)(2,1)S(1)}, bf16[384,512]{1,0:T(8,128)(2,1)}, u32[]{:S(2)}, u32[]{:S(2)}) collective-permute-start(bf16[384,512]{1,0:T(8,128)(2,1)S(1)} %collective-permute-done.11), channel_id=1, source_target_pairs={{4,8},{8,12},{5,9},{9,13},{6,10},{10,14},{7,11},{11,15},{20,24},{2... | collective-permute-start | bytes 1179656 | tf_op jit(solution)/shard_map/ppermute | solution.py:24
  155.0 22.8 %collective-permute-start.14 = (bf16[384,512]{1,0:T(8,128)(2,1)S(1)}, bf16[384,512]{1,0:T(8,128)(2,1)}, u32[]{:S(2)}, u32[]{:S(2)}) collective-permute-start(bf16[384,512]{1,0:T(8,128)(2,1)S(1)} %collective-permute-done.10), channel_id=1, source_target_pairs={{4,0},{8,4},{5,1},{9,5},{6,2},{10,6},{7,3},{11,7},{20,16},{24,20},... | collective-permute-start | bytes 1179656 | tf_op jit(solution)/shard_map/ppermute | solution.py:23
  163.3 15.8 %collective-permute-start.5 = (bf16[384,512]{1,0:T(8,128)(2,1)}, bf16[384,512]{1,0:T(8,128)(2,1)S(1)}, u32[]{:S(2)}, u32[]{:S(2)}) collective-permute-start(bf16[384,512]{1,0:T(8,128)(2,1)} %collective-permute-done.4), channel_id=1, source_target_pairs={{4,8},{8,12},{5,9},{9,13},{6,10},{10,14},{7,11},{11,15},{20,24},{2... | collective-permute-start | bytes 1179656 | tf_op jit(solution)/shard_map/ppermute | solution.py:24
  165.9 16.3 %collective-permute-start.7 = (bf16[384,512]{1,0:T(8,128)(2,1)}, bf16[384,512]{1,0:T(8,128)(2,1)S(1)}, u32[]{:S(2)}, u32[]{:S(2)}) collective-permute-start(bf16[384,512]{1,0:T(8,128)(2,1)} %collective-permute-done.3), channel_id=1, source_target_pairs={{4,0},{8,4},{5,1},{9,5},{6,2},{10,6},{7,3},{11,7},{20,16},{24,20},... | collective-permute-start | bytes 1179656 | tf_op jit(solution)/shard_map/ppermute | solution.py:23
  171.8 39.9 %collective-permute-start.16 = (bf16[3072,256]{1,0:T(8,128)(2,1)}, bf16[3072,256]{1,0:T(8,128)(2,1)}, u32[]{:S(2)}, u32[]{:S(2)}) collective-permute-start(bf16[3072,256]{1,0:T(8,128)(2,1)} %slice.33), channel_id=1, source_target_pairs={{0,16},{16,0},{1,17},{17,1},{2,18},{18,2},{3,19},{19,3},{4,20},{20... | collective-permute-start | bytes 4718600 | tf_op jit(solution)/shard_map/ppermute | solution.py:52
  176.4 26.3 %collective-permute-start.13 = (bf16[384,512]{1,0:T(8,128)(2,1)}, bf16[384,512]{1,0:T(8,128)(2,1)}, u32[]{:S(2)}, u32[]{:S(2)}) collective-permute-start(bf16[384,512]{1,0:T(8,128)(2,1)} %collective-permute-done.12), channel_id=1, source_target_pairs={{8,12},{9,13},{10,14},{11,15},{24,28},{25,29},{26,30},{27,31}} | collective-permute-start | bytes 1179656 | tf_op jit(solution)/shard_map/ppermute | solution.py:24
  177.8 25.9 %collective-permute-start.15 = (bf16[384,512]{1,0:T(8,128)(2,1)}, bf16[384,512]{1,0:T(8,128)(2,1)}, u32[]{:S(2)}, u32[]{:S(2)}) collective-permute-start(bf16[384,512]{1,0:T(8,128)(2,1)} %collective-permute-done.14), channel_id=1, source_target_pairs={{4,0},{5,1},{6,2},{7,3},{20,16},{21,17},{22,18},{23,19}} | collective-permute-start | bytes 1179656 | tf_op jit(solution)/shard_map/ppermute | solution.py:23
  179.1 5.5 %collective-permute-start.6 = (bf16[384,512]{1,0:T(8,128)(2,1)S(1)}, bf16[384,512]{1,0:T(8,128)(2,1)S(1)}, u32[]{:S(2)}, u32[]{:S(2)}) collective-permute-start(bf16[384,512]{1,0:T(8,128)(2,1)S(1)} %collective-permute-done.5), channel_id=1, source_target_pairs={{8,12},{9,13},{10,14},{11,15},{24,28},{25,29},{26,30},{27,31}} | collective-permute-start | bytes 1179656 | tf_op jit(solution)/shard_map/ppermute | solution.py:24
  182.2 17.8 %collective-permute-start.8 = (bf16[384,512]{1,0:T(8,128)(2,1)S(1)}, bf16[384,512]{1,0:T(8,128)(2,1)S(1)}, u32[]{:S(2)}, u32[]{:S(2)}) collective-permute-start(bf16[384,512]{1,0:T(8,128)(2,1)S(1)} %collective-permute-done.7), channel_id=1, source_target_pairs={{4,0},{5,1},{6,2},{7,3},{20,16},{21,17},{22,18},{23,19}} | collective-permute-start | bytes 1179656 | tf_op jit(solution)/shard_map/ppermute | solution.py:23
  (9 other events, 63.5 us)
Sparse Core Ops, SparseCore 0:
  9.1 48.6 all-gather.7
  59.4 44.6 all-gather.3
  105.6 57.7 all-gather.5

commit v16 on v8

--- a/solution.py
+++ b/solution.py
@@ -47,7 +47,9 @@
     own = lax.all_gather(own, "seq", axis=0, tiled=True)
     own = jnp.roll(own, -lax.axis_index("seq") * rows, axis=0)
     if after is not None:
-        own = lax.optimization_barrier((own, after))[0]
+        own, after = lax.optimization_barrier((own, after))
+        other = lax.ppermute(own[rows:], "groups", [(0, 1), (1, 0)])
+        return [own, jnp.concatenate([kept, other], axis=0)], after
     other = lax.ppermute(own[rows:], "groups", [(0, 1), (1, 0)])
     return [own, jnp.concatenate([kept, other], axis=0)]
 
@@ -62,15 +64,19 @@
     if shared:
         block = jnp.roll(block, -lax.axis_index("seq") * w_query.shape[0], axis=1)
 
-    def project(weight, after=None):
+    def project(pieces):
         return [
             jnp.dot(block, piece, preferred_element_type=jnp.float32).astype(jnp.bfloat16)
-            for piece in full_columns(weight, shared, after)
+            for piece in pieces
         ]
 
-    key = jnp.concatenate(project(w_key), axis=1)
-    value = jnp.concatenate(project(w_value), axis=1)
-    queries = project(w_query, key)
+    key = jnp.concatenate(project(full_columns(w_key, shared)), axis=1)
+    value = jnp.concatenate(project(full_columns(w_value, shared)), axis=1)
+    if shared:
+        query_pieces, key = full_columns(w_query, shared, key)
+    else:
+        query_pieces = full_columns(w_query, shared)
+    queries = project(query_pieces)
     if lax.axis_size("seq") == SPAN:
         seen = jnp.stack([line_gather(key), line_gather(value)])
     else:

time: 227 us -> 234 us (1.031)
  waiting for transfers between devices: 130 us -> 140 us
  other arithmetic: 25.4 us -> 22.4 us
    all_gather x3, waiting for transfers between devices: 60.7 us -> 94.4 us  [full_columns(): own = lax.all_gather(own, 'seq', axis=0, tiled=True)]
    ppermute x3, waiting for transfers between devices: 22.4 us -> 0.87 us  [full_columns(): other = lax.ppermute(own[rows:], 'groups', [(0, 1), (1, 0)])]
    ppermute x6, waiting for transfers between devices: 28.1 us -> 24.2 us  [line_gather(): lax.ppermute(from_right[-1], 'seq', [(j, j - 1) for j in range(1, n - k +...]
  transfers between devices with their start and end apart: 20 -> 20, of which waited for: 10 -> 11; matrix products, arithmetic and copies ran while one was open for 17% -> 17% of each run, Pallas kernels for 0% -> 0%
where the time goes in v16:
time: 234 us; the launch traced here: 232 us
  waiting for transfers between devices  140 us (60%)
  starting transfers between devices  29.6 us (13%)
  other arithmetic  22.4 us (10%)
  matrix products  17.9 us (8%)
  between operations  13.5 us (6%)
  local copies, waits for them, and re-layouts  8.67 us (4%)
    all_gather x3, waiting for transfers between devices, full_columns(): own = lax.all_gather(own, 'seq', axis=0, tiled=True)  94.4 us
    ppermute x6, waiting for transfers between devices, line_gather(): lax.ppermute(from_right[-1], 'seq', [(j, j - 1) for j in range(1, n - k +...  24.2 us
    ppermute x2, waiting for transfers between devices, swap_gather(): other = lax.ppermute(piece, axis, [(0, 1), (1, 0)])  19.9 us
    ppermute x6, starting transfers between devices, line_gather(): lax.ppermute(from_left[-1], 'seq', [(j, j + 1) for j in range(k - 1, n -...  14.1 us
    dot_general x6, matrix products, project(): jnp.dot(block, piece, preferred_element_type=jnp.float32)  13.8 us
    concatenate x3, other arithmetic, full_columns(): own = jnp.roll(own, -lax.axis_index('seq') * rows, axis=0)  9.31 us
    ppermute x6, starting transfers between devices, line_gather(): lax.ppermute(from_right[-1], 'seq', [(j, j - 1) for j in range(1, n - k +...  7.89 us
  transfers between devices with their start and end apart: 20, of which 11 were waited for; matrix products, arithmetic and copies ran while one was open for 17% of the time, Pallas kernels for 0%

profile of v16, /device:TPU:0, one launch (start us, length us, event | category | flops | bytes accessed | tf_op | source)
XLA Modules:
  0.0 231.6 jit_solution(2103305290947346183)
XLA Ops:
  6.5 2.4 %constant_dynamic-slice_fusion.4 = (bf16[1024,256]{1,0:T(8,128)(2,1)}, bf16[1024,256]{1,0:T(8,128)(2,1)}) fusion(bf16[1024,512]{1,0:T(8,128)(2,1)} %param.9, s32[]{:T(128)S(6)} %select_n.105, s32[]{:T(128)S(6)} %select_n.104), kind=kLoop, calls=%fused_computation.84 | loop fusion | bytes 2097160 | tf_op jit(solution)/shard_map/dynamic_slice | solution.py:46
  10.1 3.0 %collective-permute-start = (bf16[192,2048]{1,0:T(8,128)(2,1)S(1)}, bf16[192,2048]{1,0:T(8,128)(2,1)S(1)}, u32[]{:S(2)}, u32[]{:S(2)}) collective-permute-start(bf16[192,2048]{1,0:T(8,128)(2,1)S(1)} %copy-done.9), channel_id=1, source_target_pairs={{0,2},{2,0},{1,3},{3,1},{4,6},{6,4},{5,7},{7,5},{8,10},{10,8},{9,1... | collective-permute-start | bytes 2359304 | tf_op jit(solution)/shard_map/ppermute | solution.py:34
  13.1 17.5 %collective-permute-done = bf16[192,2048]{1,0:T(8,128)(2,1)S(1)} collective-permute-done((bf16[192,2048]{1,0:T(8,128)(2,1)S(1)}, bf16[192,2048]{1,0:T(8,128)(2,1)S(1)}, u32[]{:S(2)}, u32[]{:S(2)}) %collective-permute-start) | collective-permute-done | bytes 786464 | tf_op jit(solution)/shard_map/ppermute | solution.py:34
  32.2 2.4 %collective-permute-done.1 = bf16[384,2048]{1,0:T(8,128)(2,1)} collective-permute-done((bf16[384,2048]{1,0:T(8,128)(2,1)S(1)}, bf16[384,2048]{1,0:T(8,128)(2,1)}, u32[]{:S(2)}, u32[]{:S(2)}) %collective-permute-start.1) | collective-permute-done | bytes 1572896 | tf_op jit(solution)/shard_map/ppermute | solution.py:34
  34.6 2.2 broadcast_select_fusion
  36.8 4.1 %fusion.6 = bf16[384,4096]{1,0:T(8,128)(2,1)} fusion(s32[]{:T(128)S(6)} %select_n.103, bf16[384,2048]{1,0:T(8,128)(2,1)S(1)} %get-tuple-element.11, bf16[384,2048]{1,0:T(8,128)(2,1)S(1)} %get-tuple-element.10), kind=kLoop, calls=%fused_computation.20 | loop fusion | flops 12582912 | bytes 6291460 | tf_op jit(solution)/shard_map/jit(_roll_dynamic)/concatenate | solution.py:65
  40.9 16.9 %all-gather.4.cloned.1.call-done = bf16[4096,256]{1,0:T(8,128)(2,1)} async-done(((bf16[1024,256]{1,0:T(8,128)(2,1)}), bf16[4096,256]{1,0:T(8,128)(2,1)}) %all-gather.4.cloned.1.call-update) | async-done | bytes 2097168 | tf_op jit(solution)/shard_map/all_gather | solution.py:47
  57.7 3.0 %fusion.17 = bf16[4096,256]{1,0:T(8,128)(2,1)S(1)} fusion(s32[]{:T(128)S(6)} %select_n.103, bf16[4096,256]{1,0:T(8,128)(2,1)} %all-gather.4.cloned.1.call-done), kind=kLoop, calls=%fused_computation.29 | loop fusion | flops 4194304 | bytes 4194308 | tf_op jit(solution)/shard_map/jit(_roll_dynamic)/concatenate | solution.py:48
  63.5 40.5 %all-gather.8.cloned.1.call-done = bf16[4096,256]{1,0:T(8,128)(2,1)} async-done(((bf16[1024,256]{1,0:T(8,128)(2,1)}), bf16[4096,256]{1,0:T(8,128)(2,1)}) %all-gather.8.cloned.1.call-update) | async-done | bytes 2097168 | tf_op jit(solution)/shard_map/all_gather | solution.py:47
  104.0 3.2 %fusion.15 = bf16[4096,256]{1,0:T(8,128)(2,1)S(1)} fusion(s32[]{:T(128)S(6)} %select_n.103, bf16[4096,256]{1,0:T(8,128)(2,1)} %all-gather.8.cloned.1.call-done), kind=kLoop, calls=%fused_computation.27 | loop fusion | flops 4194304 | bytes 4194308 | tf_op jit(solution)/shard_map/jit(_roll_dynamic)/concatenate | solution.py:48
  111.2 2.0 convolution_convert_fusion.1
  113.2 37.1 %all-gather.6.cloned.1.call-done = bf16[4096,256]{1,0:T(8,128)(2,1)} async-done(((bf16[1024,256]{1,0:T(8,128)(2,1)}), bf16[4096,256]{1,0:T(8,128)(2,1)}) %all-gather.6.cloned.1.call-update) | async-done | bytes 2097168 | tf_op jit(solution)/shard_map/all_gather | solution.py:47
  150.2 3.2 %fusion.16 = bf16[4096,256]{1,0:T(8,128)(2,1)S(1)} fusion(s32[]{:T(128)S(6)} %select_n.103, bf16[4096,256]{1,0:T(8,128)(2,1)} %all-gather.6.cloned.1.call-done), kind=kLoop, calls=%fused_computation.28 | loop fusion | flops 4194304 | bytes 4194308 | tf_op jit(solution)/shard_map/jit(_roll_dynamic)/concatenate | solution.py:48
  153.4 2.8 %fusion.42 = bf16[384,256]{0,1:T(8,128)(2,1)S(1)} fusion(bf16[384,4096]{1,0:T(8,128)(2,1)S(1)} %copy-done.1, bf16[3072,256]{1,0:T(8,128)(2,1)} %collective-permute-done.2, bf16[1024,256]{1,0:T(8,128)(2,1)S(1)} %copy-done.11), kind=kOutput, calls=%fused_computation.51 | convolution fusion | flops 809598976 | bytes 5439488 | tf_op jit(solution)/shard_map/dot_general | solution.py:69
  157.8 5.3 %collective-permute-start.4 = (bf16[384,512]{0,1:T(8,128)(2,1)S(1)}, bf16[384,512]{0,1:T(8,128)(2,1)}, u32[]{:S(2)}, u32[]{:S(2)}) collective-permute-start(bf16[384,512]{0,1:T(8,128)(2,1)S(1)} %pad_maximum_fusion.3), channel_id=1, source_target_pairs={{0,4},{4,8},{8,12},{1,5},{5,9},{9,13},{2,6},{6,10},{10,14},{3,7},{... | collective-permute-start | bytes 1179656 | tf_op jit(solution)/shard_map/ppermute | solution.py:23
  163.1 2.7 %fusion.39 = bf16[384,256]{0,1:T(8,128)(2,1)S(1)} fusion(bf16[384,4096]{1,0:T(8,128)(2,1)S(1)} %copy-done.1, bf16[3072,256]{1,0:T(8,128)(2,1)} %collective-permute-done.9, bf16[1024,256]{1,0:T(8,128)(2,1)S(1)} %copy-done.10), kind=kOutput, calls=%fused_computation.50 | convolution fusion | flops 809598976 | bytes 5439488 | tf_op jit(solution)/shard_map/dot_general | solution.py:69
  167.2 5.3 %collective-permute-start.11 = (bf16[384,512]{0,1:T(8,128)(2,1)S(1)}, bf16[384,512]{0,1:T(8,128)(2,1)}, u32[]{:S(2)}, u32[]{:S(2)}) collective-permute-start(bf16[384,512]{0,1:T(8,128)(2,1)S(1)} %pad_maximum_fusion.4), channel_id=1, source_target_pairs={{0,4},{4,8},{8,12},{1,5},{5,9},{9,13},{2,6},{6,10},{10,14},{3,7},{... | collective-permute-start | bytes 1179656 | tf_op jit(solution)/shard_map/ppermute | solution.py:23
  174.5 5.5 %collective-permute-done.10 = bf16[384,512]{0,1:T(8,128)(2,1)} collective-permute-done((bf16[384,512]{0,1:T(8,128)(2,1)S(1)}, bf16[384,512]{0,1:T(8,128)(2,1)}, u32[]{:S(2)}, u32[]{:S(2)}) %collective-permute-start.10) | collective-permute-done | bytes 393248 | tf_op jit(solution)/shard_map/ppermute | solution.py:22
  181.2 1.5 collective-permute-start.12
  186.8 1.5 collective-permute-done.7
  190.4 6.4 %collective-permute-done.14 = bf16[384,512]{0,1:T(8,128)(2,1)} collective-permute-done((bf16[384,512]{0,1:T(8,128)(2,1)}, bf16[384,512]{0,1:T(8,128)(2,1)}, u32[]{:S(2)}, u32[]{:S(2)}) %collective-permute-start.14) | collective-permute-done | bytes 393248 | tf_op jit(solution)/shard_map/ppermute | solution.py:22
  200.9 4.2 %collective-permute-done.8 = bf16[384,512]{0,1:T(8,128)(2,1)S(1)} collective-permute-done((bf16[384,512]{0,1:T(8,128)(2,1)}, bf16[384,512]{0,1:T(8,128)(2,1)S(1)}, u32[]{:S(2)}, u32[]{:S(2)}) %collective-permute-start.8) | collective-permute-done | bytes 393248 | tf_op jit(solution)/shard_map/ppermute | solution.py:22
  205.2 6.6 %collective-permute-done.15 = bf16[384,512]{0,1:T(8,128)(2,1)S(1)} collective-permute-done((bf16[384,512]{0,1:T(8,128)(2,1)}, bf16[384,512]{0,1:T(8,128)(2,1)S(1)}, u32[]{:S(2)}, u32[]{:S(2)}) %collective-permute-start.15) | collective-permute-done | bytes 393248 | tf_op jit(solution)/shard_map/ppermute | solution.py:22
  217.2 3.8 %fusion.36 = bf16[384,256]{0,1:T(8,128)(2,1)S(1)} fusion(bf16[384,4096]{1,0:T(8,128)(2,1)} %fusion.6, bf16[3072,256]{1,0:T(8,128)(2,1)} %collective-permute-done.16, bf16[1024,256]{1,0:T(8,128)(2,1)} %get-tuple-element.14), kind=kOutput, calls=%fused_computation.49 | convolution fusion | flops 809598976 | bytes 5439488 | tf_op jit(solution)/shard_map/dot_general | solution.py:69
  (83 shorter events, 35.2 us)
Async XLA Ops:
  6.5 51.2 %all-gather.4.cloned.1.call-start = ((), (), s32[]{:S(2)}) async-start(), calls=%async_computation | async-start | bytes 2621440 | tf_op jit(solution)/shard_map/all_gather | solution.py:47
  8.9 95.0 %all-gather.8.cloned.1.call-start = ((), (), s32[]{:S(2)}) async-start(), calls=%async_computation.2 | async-start | bytes 2621440 | tf_op jit(solution)/shard_map/all_gather | solution.py:47
  10.1 140.2 %all-gather.6.cloned.1.call-start = ((), (), s32[]{:S(2)}) async-start(), calls=%async_computation.1 | async-start | bytes 2621440 | tf_op jit(solution)/shard_map/all_gather | solution.py:47
  10.1 20.5 %collective-permute-start = (bf16[192,2048]{1,0:T(8,128)(2,1)S(1)}, bf16[192,2048]{1,0:T(8,128)(2,1)S(1)}, u32[]{:S(2)}, u32[]{:S(2)}) collective-permute-start(bf16[192,2048]{1,0:T(8,128)(2,1)S(1)} %copy-done.9), channel_id=1, source_target_pairs={{0,2},{2,0},{1,3},{3,1},{4,6},{6,4},{5,7},{7,5},{8,10},{10,8},{9,1... | collective-permute-start | bytes 2359304 | tf_op jit(solution)/shard_map/ppermute | solution.py:34
  31.0 3.6 %collective-permute-start.1 = (bf16[384,2048]{1,0:T(8,128)(2,1)S(1)}, bf16[384,2048]{1,0:T(8,128)(2,1)}, u32[]{:S(2)}, u32[]{:S(2)}) collective-permute-start(bf16[384,2048]{1,0:T(8,128)(2,1)S(1)} %pad_maximum_fusion), channel_id=1, source_target_pairs={{0,1},{1,0},{2,3},{3,2},{4,5},{5,4},{6,7},{7,6},{8,9},{9,8},{10,11... | collective-permute-start | bytes 4718600 | tf_op jit(solution)/shard_map/ppermute | solution.py:34
  62.0 91.4 %collective-permute-start.2 = (bf16[3072,256]{1,0:T(8,128)(2,1)}, bf16[3072,256]{1,0:T(8,128)(2,1)}, u32[]{:S(2)}, u32[]{:S(2)}) collective-permute-start(bf16[3072,256]{1,0:T(8,128)(2,1)} %slice.28), channel_id=1, source_target_pairs={{0,16},{16,0},{1,17},{17,1},{2,18},{18,2},{3,19},{19,3},{4,20},{20... | collective-permute-start | bytes 4718600 | tf_op jit(solution)/shard_map/ppermute | solution.py:53
  108.4 54.7 %collective-permute-start.9 = (bf16[3072,256]{1,0:T(8,128)(2,1)}, bf16[3072,256]{1,0:T(8,128)(2,1)}, u32[]{:S(2)}, u32[]{:S(2)}) collective-permute-start(bf16[3072,256]{1,0:T(8,128)(2,1)} %slice.29), channel_id=1, source_target_pairs={{0,16},{16,0},{1,17},{17,1},{2,18},{18,2},{3,19},{19,3},{4,20},{20... | collective-permute-start | bytes 4718600 | tf_op jit(solution)/shard_map/ppermute | solution.py:53
  111.2 45.1 %copy-start.5 = (bf16[384,256]{0,1:T(8,128)(2,1)}, bf16[384,256]{0,1:T(8,128)(2,1)S(1)}, u32[]{:S(2)}) copy-start(bf16[384,256]{0,1:T(8,128)(2,1)S(1)} %convolution_convert_fusion.2) | copy-start | bytes 589828
  113.2 40.2 %copy-start.11 = (bf16[1024,256]{1,0:T(8,128)(2,1)S(1)}, bf16[1024,256]{1,0:T(8,128)(2,1)}, u32[]{:S(2)}) copy-start(bf16[1024,256]{1,0:T(8,128)(2,1)} %get-tuple-element.18) | copy-start | bytes 1572868
  156.3 16.2 %collective-permute-start.3 = (bf16[384,512]{0,1:T(8,128)(2,1)S(1)}, bf16[384,512]{0,1:T(8,128)(2,1)S(1)}, u32[]{:S(2)}, u32[]{:S(2)}) collective-permute-start(bf16[384,512]{0,1:T(8,128)(2,1)S(1)} %pad_maximum_fusion.3), channel_id=1, source_target_pairs={{4,0},{8,4},{12,8},{5,1},{9,5},{13,9},{6,2},{10,6},{14,10},{7,3},{... | collective-permute-start | bytes 1179656 | tf_op jit(solution)/shard_map/ppermute | solution.py:22
  157.8 16.0 %collective-permute-start.4 = (bf16[384,512]{0,1:T(8,128)(2,1)S(1)}, bf16[384,512]{0,1:T(8,128)(2,1)}, u32[]{:S(2)}, u32[]{:S(2)}) collective-permute-start(bf16[384,512]{0,1:T(8,128)(2,1)S(1)} %pad_maximum_fusion.3), channel_id=1, source_target_pairs={{0,4},{4,8},{8,12},{1,5},{5,9},{9,13},{2,6},{6,10},{10,14},{3,7},{... | collective-permute-start | bytes 1179656 | tf_op jit(solution)/shard_map/ppermute | solution.py:23
  165.9 14.1 %collective-permute-start.10 = (bf16[384,512]{0,1:T(8,128)(2,1)S(1)}, bf16[384,512]{0,1:T(8,128)(2,1)}, u32[]{:S(2)}, u32[]{:S(2)}) collective-permute-start(bf16[384,512]{0,1:T(8,128)(2,1)S(1)} %pad_maximum_fusion.4), channel_id=1, source_target_pairs={{4,0},{8,4},{12,8},{5,1},{9,5},{13,9},{6,2},{10,6},{14,10},{7,3},{... | collective-permute-start | bytes 1179656 | tf_op jit(solution)/shard_map/ppermute | solution.py:22
  167.2 14.0 %collective-permute-start.11 = (bf16[384,512]{0,1:T(8,128)(2,1)S(1)}, bf16[384,512]{0,1:T(8,128)(2,1)}, u32[]{:S(2)}, u32[]{:S(2)}) collective-permute-start(bf16[384,512]{0,1:T(8,128)(2,1)S(1)} %pad_maximum_fusion.4), channel_id=1, source_target_pairs={{0,4},{4,8},{8,12},{1,5},{5,9},{9,13},{2,6},{6,10},{10,14},{3,7},{... | collective-permute-start | bytes 1179656 | tf_op jit(solution)/shard_map/ppermute | solution.py:23
  172.5 15.9 %collective-permute-start.7 = (bf16[384,512]{0,1:T(8,128)(2,1)S(1)}, bf16[384,512]{0,1:T(8,128)(2,1)}, u32[]{:S(2)}, u32[]{:S(2)}) collective-permute-start(bf16[384,512]{0,1:T(8,128)(2,1)S(1)} %collective-permute-done.3), channel_id=1, source_target_pairs={{4,0},{8,4},{5,1},{9,5},{6,2},{10,6},{7,3},{11,7},{20,16},{24,20},... | collective-permute-start | bytes 1179656 | tf_op jit(solution)/shard_map/ppermute | solution.py:22
  173.8 15.9 %collective-permute-start.5 = (bf16[384,512]{0,1:T(8,128)(2,1)}, bf16[384,512]{0,1:T(8,128)(2,1)S(1)}, u32[]{:S(2)}, u32[]{:S(2)}) collective-permute-start(bf16[384,512]{0,1:T(8,128)(2,1)} %collective-permute-done.4), channel_id=1, source_target_pairs={{4,8},{8,12},{5,9},{9,13},{6,10},{10,14},{7,11},{11,15},{20,24},{2... | collective-permute-start | bytes 1179656 | tf_op jit(solution)/shard_map/ppermute | solution.py:23
  179.9 16.9 %collective-permute-start.14 = (bf16[384,512]{0,1:T(8,128)(2,1)}, bf16[384,512]{0,1:T(8,128)(2,1)}, u32[]{:S(2)}, u32[]{:S(2)}) collective-permute-start(bf16[384,512]{0,1:T(8,128)(2,1)} %collective-permute-done.10), channel_id=1, source_target_pairs={{4,0},{8,4},{5,1},{9,5},{6,2},{10,6},{7,3},{11,7},{20,16},{24,20},... | collective-permute-start | bytes 1179656 | tf_op jit(solution)/shard_map/ppermute | solution.py:22
  181.2 16.8 %collective-permute-start.12 = (bf16[384,512]{0,1:T(8,128)(2,1)}, bf16[384,512]{0,1:T(8,128)(2,1)}, u32[]{:S(2)}, u32[]{:S(2)}) collective-permute-start(bf16[384,512]{0,1:T(8,128)(2,1)} %collective-permute-done.11), channel_id=1, source_target_pairs={{4,8},{8,12},{5,9},{9,13},{6,10},{10,14},{7,11},{11,15},{20,24},{2... | collective-permute-start | bytes 1179656 | tf_op jit(solution)/shard_map/ppermute | solution.py:23
  184.0 33.2 %collective-permute-start.16 = (bf16[3072,256]{1,0:T(8,128)(2,1)}, bf16[3072,256]{1,0:T(8,128)(2,1)}, u32[]{:S(2)}, u32[]{:S(2)}) collective-permute-start(bf16[3072,256]{1,0:T(8,128)(2,1)} %slice.26), channel_id=1, source_target_pairs={{0,16},{16,0},{1,17},{17,1},{2,18},{18,2},{3,19},{19,3},{4,20},{20... | collective-permute-start | bytes 4718600 | tf_op jit(solution)/shard_map/ppermute | solution.py:51
  186.8 25.1 %copy-start.6 = (bf16[384,256]{0,1:T(8,128)(2,1)S(1)}, bf16[384,256]{0,1:T(8,128)(2,1)}, u32[]{:S(2)}) copy-start(bf16[384,256]{0,1:T(8,128)(2,1)} %copy-done.5) | copy-start | bytes 589828
  186.8 25.1 %copy-start.8 = (bf16[384,256]{0,1:T(8,128)(2,1)S(1)}, bf16[384,256]{0,1:T(8,128)(2,1)}, u32[]{:S(2)}) copy-start(bf16[384,256]{0,1:T(8,128)(2,1)} %copy-done.7) | copy-start | bytes 589828
  188.4 16.7 %collective-permute-start.8 = (bf16[384,512]{0,1:T(8,128)(2,1)}, bf16[384,512]{0,1:T(8,128)(2,1)S(1)}, u32[]{:S(2)}, u32[]{:S(2)}) collective-permute-start(bf16[384,512]{0,1:T(8,128)(2,1)} %collective-permute-done.7), channel_id=1, source_target_pairs={{4,0},{5,1},{6,2},{7,3},{20,16},{21,17},{22,18},{23,19}} | collective-permute-start | bytes 1179656 | tf_op jit(solution)/shard_map/ppermute | solution.py:22
  189.7 22.2 %collective-permute-start.6 = (bf16[384,512]{0,1:T(8,128)(2,1)S(1)}, bf16[384,512]{0,1:T(8,128)(2,1)S(1)}, u32[]{:S(2)}, u32[]{:S(2)}) collective-permute-start(bf16[384,512]{0,1:T(8,128)(2,1)S(1)} %collective-permute-done.5), channel_id=1, source_target_pairs={{8,12},{9,13},{10,14},{11,15},{24,28},{25,29},{26,30},{27,31}} | collective-permute-start | bytes 1179656 | tf_op jit(solution)/shard_map/ppermute | solution.py:23
  196.8 15.0 %collective-permute-start.15 = (bf16[384,512]{0,1:T(8,128)(2,1)}, bf16[384,512]{0,1:T(8,128)(2,1)S(1)}, u32[]{:S(2)}, u32[]{:S(2)}) collective-permute-start(bf16[384,512]{0,1:T(8,128)(2,1)} %collective-permute-done.14), channel_id=1, source_target_pairs={{4,0},{5,1},{6,2},{7,3},{20,16},{21,17},{22,18},{23,19}} | collective-permute-start | bytes 1179656 | tf_op jit(solution)/shard_map/ppermute | solution.py:22
  198.1 14.0 %collective-permute-start.13 = (bf16[384,512]{0,1:T(8,128)(2,1)}, bf16[384,512]{0,1:T(8,128)(2,1)S(1)}, u32[]{:S(2)}, u32[]{:S(2)}) collective-permute-start(bf16[384,512]{0,1:T(8,128)(2,1)} %collective-permute-done.12), channel_id=1, source_target_pairs={{8,12},{9,13},{10,14},{11,15},{24,28},{25,29},{26,30},{27,31}} | collective-permute-start | bytes 1179656 | tf_op jit(solution)/shard_map/ppermute | solution.py:23
  (9 other events, 57.8 us)
Sparse Core Ops, SparseCore 0:
  9.1 48.6 all-gather.3
  59.3 44.6 all-gather.7
  105.6 44.6 all-gather.5

commit v17 on v8

--- a/solution.py
+++ b/solution.py
@@ -52,9 +52,25 @@
     return [own, jnp.concatenate([kept, other], axis=0)]
 
 
+def query_columns(weight, after):
+    n = lax.axis_size("seq")
+    rows, half = weight.shape[0], weight.shape[1] // 2
+    group = lax.axis_index("groups")
+    own = lax.dynamic_slice_in_dim(weight, group * half, half, axis=1)
+    kept = lax.dynamic_slice_in_dim(weight, (1 - group) * half, half, axis=1)
+    gathered = lax.all_gather(own, "seq", axis=0, tiled=True)
+    gathered = lax.optimization_barrier((gathered, after))[0]
+    received = []
+    for j in range(n):
+        pairs = [(g * n + i, (1 - g) * n + i) for g in range(2) for i in range(n) if i != j]
+        received.append(lax.ppermute(gathered[j * rows : (j + 1) * rows], ("groups", "seq"), pairs))
+    return gathered, kept, jnp.concatenate(received, axis=0)
+
+
 def per_device(acts, w_query, w_key, w_value):
     block = swap_gather(acts, "row", 0)
     block = swap_gather(block, "col", 1)
+    unrolled = block
     tokens_here = block.shape[0]
     width = w_query.shape[1]
     heads_here = width // HD
@@ -70,7 +86,18 @@
 
     key = jnp.concatenate(project(w_key), axis=1)
     value = jnp.concatenate(project(w_value), axis=1)
-    queries = project(w_query, key)
+    if shared and lax.axis_size("seq") == SPAN:
+        gathered, kept, received = query_columns(w_query, key)
+        rows = kept.shape[0]
+        held = lax.dynamic_slice_in_dim(unrolled, lax.axis_index("seq") * rows, rows, axis=1)
+        early = jnp.dot(held, kept, preferred_element_type=jnp.float32)
+        late = jnp.dot(unrolled, received, preferred_element_type=jnp.float32)
+        queries = [
+            jnp.dot(unrolled, gathered, preferred_element_type=jnp.float32).astype(jnp.bfloat16),
+            (early + late).astype(jnp.bfloat16),
+        ]
+    else:
+        queries = project(w_query, key)
     if lax.axis_size("seq") == SPAN:
         seen = jnp.stack([line_gather(key), line_gather(value)])
     else:

time: 227 us -> 246 us (1.084)
  waiting for transfers between devices: 130 us -> 140 us
  starting transfers between devices: 30.9 us -> 39.7 us
  local copies, waits for them, and re-layouts: 7.56 us -> 11.7 us
  other arithmetic: 25.4 us -> 21.3 us
    all_gather x0 -> x1, waiting for transfers between devices: none -> 14.8 us  [query_columns(): gathered = lax.all_gather(own, 'seq', axis=0, tiled=True)]
    ppermute x6, waiting for transfers between devices: 28.1 us -> 16.4 us  [line_gather(): lax.ppermute(from_right[-1], 'seq', [(j, j - 1) for j in range(1, n - k +...]
    ppermute x0 -> x4, starting transfers between devices: none -> 10.7 us  [query_columns(): lax.ppermute(gathered[j * rows:(j + 1) * rows], ('groups', 'seq'), pairs)]
    ppermute x0 -> x4, waiting for transfers between devices: none -> 10.6 us  [query_columns(): lax.ppermute(gathered[j * rows:(j + 1) * rows], ('groups', 'seq'), pairs)]
    dot_general x0 -> x3, matrix products: none -> 6.93 us  [the longest x1 3.47 us: per_device(): jnp.dot(unrolled, gathered, preferred_element_type=jnp.float32)]
    dot_general x6 -> x4, matrix products: 11.7 us -> 6.65 us  [project(): jnp.dot(block, piece, preferred_element_type=jnp.float32)]
    ppermute x3 -> x2, waiting for transfers between devices: 22.4 us -> 18.9 us  [full_columns(): other = lax.ppermute(own[rows:], 'groups', [(0, 1), (1, 0)])]
    all_gather x3 -> x2, waiting for transfers between devices: 60.7 us -> 57.3 us  [full_columns(): own = lax.all_gather(own, 'seq', axis=0, tiled=True)]
  transfers between devices with their start and end apart: 20 -> 23, of which waited for: 10 -> 11; matrix products, arithmetic and copies ran while one was open for 17% -> 16% of each run, Pallas kernels for 0% -> 0%
where the time goes in v17:
time: 246 us; the launch traced here: 244 us
  waiting for transfers between devices  140 us (57%)
  starting transfers between devices  39.7 us (16%)
  other arithmetic  21.3 us (9%)
  matrix products  17.6 us (7%)
  between operations  13.6 us (6%)
  local copies, waits for them, and re-layouts  11.7 us (5%)
    all_gather x2, waiting for transfers between devices, full_columns(): own = lax.all_gather(own, 'seq', axis=0, tiled=True)  57.3 us
    ppermute x2, waiting for transfers between devices, swap_gather(): other = lax.ppermute(piece, axis, [(0, 1), (1, 0)])  19.3 us
    ppermute x2, waiting for transfers between devices, full_columns(): other = lax.ppermute(own[rows:], 'groups', [(0, 1), (1, 0)])  18.9 us
    ppermute x6, waiting for transfers between devices, line_gather(): lax.ppermute(from_right[-1], 'seq', [(j, j - 1) for j in range(1, n - k +...  16.4 us
    ppermute x6, starting transfers between devices, line_gather(): lax.ppermute(from_left[-1], 'seq', [(j, j + 1) for j in range(k - 1, n -...  14.9 us
    all_gather x1, waiting for transfers between devices, query_columns(): gathered = lax.all_gather(own, 'seq', axis=0, tiled=True)  14.8 us
    ppermute x4, starting transfers between devices, query_columns(): lax.ppermute(gathered[j * rows:(j + 1) * rows], ('groups', 'seq'), pairs)  10.7 us
    ppermute x4, waiting for transfers between devices, query_columns(): lax.ppermute(gathered[j * rows:(j + 1) * rows], ('groups', 'seq'), pairs)  10.6 us
  transfers between devices with their start and end apart: 23, of which 11 were waited for; matrix products, arithmetic and copies ran while one was open for 16% of the time, Pallas kernels for 0%

profile of v17, /device:TPU:0, one launch (start us, length us, event | category | flops | bytes accessed | tf_op | source)
XLA Modules:
  0.0 244.2 jit_solution(13478966323285635752)
XLA Ops:
  6.5 2.4 constant_dynamic-slice_fusion.3
  9.0 3.0 %collective-permute-start = (bf16[192,2048]{1,0:T(8,128)(2,1)}, bf16[192,2048]{1,0:T(8,128)(2,1)}, u32[]{:S(2)}, u32[]{:S(2)}) collective-permute-start(bf16[192,2048]{1,0:T(8,128)(2,1)} %param.6), channel_id=1, source_target_pairs={{0,2},{2,0},{1,3},{3,1},{4,6},{6,4},{5,7},{7,5},{8,10},{10,8},{9,1... | collective-permute-start | bytes 2359304 | tf_op jit(solution)/shard_map/ppermute | solution.py:34
  13.2 16.7 %collective-permute-done = bf16[192,2048]{1,0:T(8,128)(2,1)} collective-permute-done((bf16[192,2048]{1,0:T(8,128)(2,1)}, bf16[192,2048]{1,0:T(8,128)(2,1)}, u32[]{:S(2)}, u32[]{:S(2)}) %collective-permute-start) | collective-permute-done | bytes 786464 | tf_op jit(solution)/shard_map/ppermute | solution.py:34
  33.4 2.6 %collective-permute-done.1 = bf16[384,2048]{1,0:T(8,128)(2,1)} collective-permute-done((bf16[384,2048]{1,0:T(8,128)(2,1)S(1)}, bf16[384,2048]{1,0:T(8,128)(2,1)}, u32[]{:S(2)}, u32[]{:S(2)}) %collective-permute-start.1) | collective-permute-done | bytes 1572896 | tf_op jit(solution)/shard_map/ppermute | solution.py:34
  36.0 3.6 %broadcast_select_fusion = (bf16[384,2048]{1,0:T(8,128)(2,1)S(1)}, bf16[384,2048]{1,0:T(8,128)(2,1)}) fusion(bf16[384,2048]{1,0:T(8,128)(2,1)} %collective-permute-done.1, pred[]{:T(512)S(6)} %eq.12, bf16[192,2048]{1,0:T(8,128)(2,1)} %copy-done.3, bf16[192,2048]{1,0:T(8,128)(2,1)S(1)} %get-tuple-element.14), kind=kLoop, calls=%fused_computation.50 | loop fusion | flops 4718592 | bytes 6291457 | tf_op jit(solution)/shard_map/jit(_where)/select_n | solution.py:36
  39.6 18.1 %all-gather.4.cloned.1.call-done = bf16[4096,256]{1,0:T(8,128)(2,1)} async-done(((bf16[1024,256]{1,0:T(8,128)(2,1)}), bf16[4096,256]{1,0:T(8,128)(2,1)}) %all-gather.4.cloned.1.call-update) | async-done | bytes 2097168 | tf_op jit(solution)/shard_map/all_gather | solution.py:47
  57.7 3.0 %fusion.16 = bf16[4096,256]{1,0:T(8,128)(2,1)S(1)} fusion(s32[]{:T(128)S(6)} %select_n.106, bf16[4096,256]{1,0:T(8,128)(2,1)} %all-gather.4.cloned.1.call-done), kind=kLoop, calls=%fused_computation.29 | loop fusion | flops 4194304 | bytes 4194308 | tf_op jit(solution)/shard_map/jit(_roll_dynamic)/concatenate | solution.py:48
  64.8 39.2 %all-gather.8.cloned.1.call-done = bf16[4096,256]{1,0:T(8,128)(2,1)} async-done(((bf16[1024,256]{1,0:T(8,128)(2,1)}), bf16[4096,256]{1,0:T(8,128)(2,1)}) %all-gather.8.cloned.1.call-update) | async-done | bytes 2097168 | tf_op jit(solution)/shard_map/all_gather | solution.py:47
  104.0 3.1 %fusion.15 = bf16[4096,256]{1,0:T(8,128)(2,1)S(1)} fusion(s32[]{:T(128)S(6)} %select_n.106, bf16[4096,256]{1,0:T(8,128)(2,1)} %all-gather.8.cloned.1.call-done), kind=kLoop, calls=%fused_computation.28 | loop fusion | flops 4194304 | bytes 4194308 | tf_op jit(solution)/shard_map/jit(_roll_dynamic)/concatenate | solution.py:48
  108.8 2.9 %fusion.6 = bf16[384,4096]{1,0:T(8,128)(2,1)S(1)} fusion(s32[]{:T(128)S(6)} %select_n.106, bf16[384,2048]{1,0:T(8,128)(2,1)S(1)} %copy-done.1, bf16[384,2048]{1,0:T(8,128)(2,1)S(1)} %get-tuple-element.8), kind=kLoop, calls=%fused_computation.21 | loop fusion | flops 12582912 | bytes 6291460 | tf_op jit(solution)/shard_map/jit(_roll_dynamic)/concatenate | solution.py:79
  114.3 2.8 %fusion.45 = bf16[384,256]{0,1:T(8,128)(2,1)S(1)} fusion(bf16[384,4096]{1,0:T(8,128)(2,1)S(1)} %fusion.6, bf16[3072,256]{1,0:T(8,128)(2,1)} %collective-permute-done.2, bf16[1024,256]{1,0:T(8,128)(2,1)S(1)} %copy-done.11), kind=kOutput, calls=%fused_computation.58 | convolution fusion | flops 809598976 | bytes 5439488 | tf_op jit(solution)/shard_map/dot_general | solution.py:83
  119.2 5.4 %collective-permute-start.4 = (bf16[384,512]{0,1:T(8,128)(2,1)}, bf16[384,512]{0,1:T(8,128)(2,1)}, u32[]{:S(2)}, u32[]{:S(2)}) collective-permute-start(bf16[384,512]{0,1:T(8,128)(2,1)} %pad_maximum_fusion.8), channel_id=1, source_target_pairs={{0,4},{4,8},{8,12},{1,5},{5,9},{9,13},{2,6},{6,10},{10,14},{3,7},{... | collective-permute-start | bytes 1179656 | tf_op jit(solution)/shard_map/ppermute | solution.py:23
  124.5 18.9 %collective-permute-done.9 = bf16[3072,256]{1,0:T(8,128)(2,1)S(1)} collective-permute-done((bf16[3072,256]{1,0:T(8,128)(2,1)S(1)}, bf16[3072,256]{1,0:T(8,128)(2,1)S(1)}, u32[]{:S(2)}, u32[]{:S(2)}) %collective-permute-start.9) | collective-permute-done | bytes 1572896 | tf_op jit(solution)/shard_map/ppermute | solution.py:51
  147.0 14.8 %all-gather.6.cloned.1.call-done = bf16[4096,256]{1,0:T(8,128)(2,1)} async-done(((bf16[1024,256]{1,0:T(8,128)(2,1)}), bf16[4096,256]{1,0:T(8,128)(2,1)}) %all-gather.6.cloned.1.call-update) | async-done | bytes 2097168 | tf_op jit(solution)/shard_map/all_gather | solution.py:61
  161.8 2.9 %fusion.78 = (bf16[1024,256]{1,0:T(8,128)(2,1)}, bf16[1024,256]{1,0:T(8,128)(2,1)}, bf16[1024,256]{1,0:T(8,128)(2,1)}, bf16[1024,256]{1,0:T(8,128)(2,1)}) fusion(bf16[4096,256]{1,0:T(8,128)(2,1)} %all-gather.6.cloned.1.call-done), kind=kLoop, calls=%fused_computation.101 | loop fusion | bytes 4194304 | tf_op jit(solution)/shard_map/slice | solution.py:66
  164.7 3.4 %collective-permute-start.19 = (bf16[1024,256]{1,0:T(8,128)(2,1)}, bf16[1024,256]{1,0:T(8,128)(2,1)}, u32[]{:S(2)}, u32[]{:S(2)}) collective-permute-start(bf16[1024,256]{1,0:T(8,128)(2,1)} %get-tuple-element.11), channel_id=1, source_target_pairs={{0,16},{4,20},{8,24},{16,0},{20,4},{24,8},{1,17},{5,21},{9,25},{17... | collective-permute-start | bytes 1572872 | tf_op jit(solution)/shard_map/ppermute | solution.py:66
  168.1 2.5 %collective-permute-start.18 = (bf16[1024,256]{1,0:T(8,128)(2,1)}, bf16[1024,256]{1,0:T(8,128)(2,1)}, u32[]{:S(2)}, u32[]{:S(2)}) collective-permute-start(bf16[1024,256]{1,0:T(8,128)(2,1)} %get-tuple-element.12), channel_id=1, source_target_pairs={{0,16},{4,20},{12,28},{16,0},{20,4},{28,12},{1,17},{5,21},{13,29},... | collective-permute-start | bytes 1572872 | tf_op jit(solution)/shard_map/ppermute | solution.py:66
  170.5 3.4 %collective-permute-start.17 = (bf16[1024,256]{1,0:T(8,128)(2,1)}, bf16[1024,256]{1,0:T(8,128)(2,1)}, u32[]{:S(2)}, u32[]{:S(2)}) collective-permute-start(bf16[1024,256]{1,0:T(8,128)(2,1)} %get-tuple-element.13), channel_id=1, source_target_pairs={{0,16},{8,24},{12,28},{16,0},{24,8},{28,12},{1,17},{9,25},{13,29},... | collective-permute-start | bytes 1572872 | tf_op jit(solution)/shard_map/ppermute | solution.py:66
  175.4 6.8 %collective-permute-start.11 = (bf16[384,512]{0,1:T(8,128)(2,1)}, bf16[384,512]{0,1:T(8,128)(2,1)}, u32[]{:S(2)}, u32[]{:S(2)}) collective-permute-start(bf16[384,512]{0,1:T(8,128)(2,1)} %pad_maximum_fusion.9), channel_id=1, source_target_pairs={{0,4},{4,8},{8,12},{1,5},{5,9},{9,13},{2,6},{6,10},{10,14},{3,7},{... | collective-permute-start | bytes 1179656 | tf_op jit(solution)/shard_map/ppermute | solution.py:23
  182.2 3.5 %fusion.41 = bf16[384,256]{0,1:T(8,128)(2,1)S(1)} fusion(bf16[4096,256]{1,0:T(8,128)(2,1)} %all-gather.6.cloned.1.call-done, bf16[384,2048]{1,0:T(8,128)(2,1)S(1)} %get-tuple-element.8, bf16[384,2048]{1,0:T(8,128)(2,1)} %get-tuple-element.9), kind=kOutput, calls=%fused_computation.56 | convolution fusion | flops 811696128 | bytes 5439488 | tf_op jit(solution)/shard_map/dot_general | solution.py:96
  185.7 2.9 %collective-permute-done.11 = bf16[384,512]{0,1:T(8,128)(2,1)} collective-permute-done((bf16[384,512]{0,1:T(8,128)(2,1)}, bf16[384,512]{0,1:T(8,128)(2,1)}, u32[]{:S(2)}, u32[]{:S(2)}) %collective-permute-start.11) | collective-permute-done | bytes 393248 | tf_op jit(solution)/shard_map/ppermute | solution.py:23
  194.3 8.3 %collective-permute-done.17 = bf16[1024,256]{1,0:T(8,128)(2,1)} collective-permute-done((bf16[1024,256]{1,0:T(8,128)(2,1)}, bf16[1024,256]{1,0:T(8,128)(2,1)}, u32[]{:S(2)}, u32[]{:S(2)}) %collective-permute-start.17) | collective-permute-done | bytes 524320 | tf_op jit(solution)/shard_map/ppermute | solution.py:66
  203.2 2.8 %fusion.25 = f32[384,256]{0,1:T(8,128)S(1)} fusion(bf16[1024,256]{1,0:T(8,128)(2,1)} %collective-permute-done.19, bf16[1024,256]{1,0:T(8,128)(2,1)} %collective-permute-done.18, bf16[1024,256]{1,0:T(8,128)(2,1)} %collective-permute-done.17, bf16[1024,256]{1,0:T(8,128)(2,1)} %collective-permute-done.16, bf16[384,2048]{1,0:T(8,128)(2,1)S(1)} %get-tuple-element.8, ...), kind=kOutput, calls=%fused_computation.38 | convolution fusion | flops 819986432 | bytes 5636096 | tf_op jit(solution)/shard_map/dot_general | solution.py:94
  211.5 15.8 %collective-permute-done.15 = bf16[384,512]{0,1:T(8,128)(2,1)S(1)} collective-permute-done((bf16[384,512]{0,1:T(8,128)(2,1)S(1)}, bf16[384,512]{0,1:T(8,128)(2,1)S(1)}, u32[]{:S(2)}, u32[]{:S(2)}) %collective-permute-start.15) | collective-permute-done | bytes 393248 | tf_op jit(solution)/shard_map/ppermute | solution.py:22
  (89 shorter events, 42.0 us)
Async XLA Ops:
  6.5 51.2 %all-gather.4.cloned.1.call-start = ((), (), s32[]{:S(2)}) async-start(), calls=%async_computation | async-start | bytes 2621440 | tf_op jit(solution)/shard_map/all_gather | solution.py:47
  8.9 95.0 %all-gather.8.cloned.1.call-start = ((), (), s32[]{:S(2)}) async-start(), calls=%async_computation.2 | async-start | bytes 2621440 | tf_op jit(solution)/shard_map/all_gather | solution.py:47
  9.0 20.9 %collective-permute-start = (bf16[192,2048]{1,0:T(8,128)(2,1)}, bf16[192,2048]{1,0:T(8,128)(2,1)}, u32[]{:S(2)}, u32[]{:S(2)}) collective-permute-start(bf16[192,2048]{1,0:T(8,128)(2,1)} %param.6), channel_id=1, source_target_pairs={{0,2},{2,0},{1,3},{3,1},{4,6},{6,4},{5,7},{7,5},{8,10},{10,8},{9,1... | collective-permute-start | bytes 2359304 | tf_op jit(solution)/shard_map/ppermute | solution.py:34
  13.1 148.7 %all-gather.6.cloned.1.call-start = ((), (), s32[]{:S(2)}) async-start(), calls=%async_computation.1 | async-start | bytes 2621440 | tf_op jit(solution)/shard_map/all_gather | solution.py:61
  32.4 3.6 %collective-permute-start.1 = (bf16[384,2048]{1,0:T(8,128)(2,1)S(1)}, bf16[384,2048]{1,0:T(8,128)(2,1)}, u32[]{:S(2)}, u32[]{:S(2)}) collective-permute-start(bf16[384,2048]{1,0:T(8,128)(2,1)S(1)} %pad_maximum_fusion.3), channel_id=1, source_target_pairs={{0,1},{1,0},{2,3},{3,2},{4,5},{5,4},{6,7},{7,6},{8,9},{9,8},{10,11... | collective-permute-start | bytes 4718600 | tf_op jit(solution)/shard_map/ppermute | solution.py:34
  63.4 50.9 %collective-permute-start.2 = (bf16[3072,256]{1,0:T(8,128)(2,1)}, bf16[3072,256]{1,0:T(8,128)(2,1)}, u32[]{:S(2)}, u32[]{:S(2)}) collective-permute-start(bf16[3072,256]{1,0:T(8,128)(2,1)} %slice.40), channel_id=1, source_target_pairs={{0,16},{16,0},{1,17},{17,1},{2,18},{18,2},{3,19},{19,3},{4,20},{20... | collective-permute-start | bytes 4718600 | tf_op jit(solution)/shard_map/ppermute | solution.py:51
  107.2 36.2 %collective-permute-start.9 = (bf16[3072,256]{1,0:T(8,128)(2,1)S(1)}, bf16[3072,256]{1,0:T(8,128)(2,1)S(1)}, u32[]{:S(2)}, u32[]{:S(2)}) collective-permute-start(bf16[3072,256]{1,0:T(8,128)(2,1)S(1)} %slice.41), channel_id=1, source_target_pairs={{0,16},{16,0},{1,17},{17,1},{2,18},{18,2},{3,19},{19,3},{4,20},{20... | collective-permute-start | bytes 4718600 | tf_op jit(solution)/shard_map/ppermute | solution.py:51
  117.9 52.7 %collective-permute-start.3 = (bf16[384,512]{0,1:T(8,128)(2,1)}, bf16[384,512]{0,1:T(8,128)(2,1)}, u32[]{:S(2)}, u32[]{:S(2)}) collective-permute-start(bf16[384,512]{0,1:T(8,128)(2,1)} %pad_maximum_fusion.8), channel_id=1, source_target_pairs={{4,0},{8,4},{12,8},{5,1},{9,5},{13,9},{6,2},{10,6},{14,10},{7,3},{... | collective-permute-start | bytes 1179656 | tf_op jit(solution)/shard_map/ppermute | solution.py:22
  119.2 54.8 %collective-permute-start.4 = (bf16[384,512]{0,1:T(8,128)(2,1)}, bf16[384,512]{0,1:T(8,128)(2,1)}, u32[]{:S(2)}, u32[]{:S(2)}) collective-permute-start(bf16[384,512]{0,1:T(8,128)(2,1)} %pad_maximum_fusion.8), channel_id=1, source_target_pairs={{0,4},{4,8},{8,12},{1,5},{5,9},{9,13},{2,6},{6,10},{10,14},{3,7},{... | collective-permute-start | bytes 1179656 | tf_op jit(solution)/shard_map/ppermute | solution.py:23
  144.7 41.0 %copy-start.9 = (bf16[384,256]{0,1:T(8,128)(2,1)}, bf16[384,256]{0,1:T(8,128)(2,1)S(1)}, u32[]{:S(2)}) copy-start(bf16[384,256]{0,1:T(8,128)(2,1)S(1)} %fusion.42) | copy-start | bytes 589828
  145.5 29.9 %collective-permute-start.10 = (bf16[384,512]{0,1:T(8,128)(2,1)}, bf16[384,512]{0,1:T(8,128)(2,1)}, u32[]{:S(2)}, u32[]{:S(2)}) collective-permute-start(bf16[384,512]{0,1:T(8,128)(2,1)} %pad_maximum_fusion.9), channel_id=1, source_target_pairs={{4,0},{8,4},{12,8},{5,1},{9,5},{13,9},{6,2},{10,6},{14,10},{7,3},{... | collective-permute-start | bytes 1179656 | tf_op jit(solution)/shard_map/ppermute | solution.py:22
  164.7 25.2 %collective-permute-start.19 = (bf16[1024,256]{1,0:T(8,128)(2,1)}, bf16[1024,256]{1,0:T(8,128)(2,1)}, u32[]{:S(2)}, u32[]{:S(2)}) collective-permute-start(bf16[1024,256]{1,0:T(8,128)(2,1)} %get-tuple-element.11), channel_id=1, source_target_pairs={{0,16},{4,20},{8,24},{16,0},{20,4},{24,8},{1,17},{5,21},{9,25},{17... | collective-permute-start | bytes 1572872 | tf_op jit(solution)/shard_map/ppermute | solution.py:66
  168.1 24.9 %collective-permute-start.18 = (bf16[1024,256]{1,0:T(8,128)(2,1)}, bf16[1024,256]{1,0:T(8,128)(2,1)}, u32[]{:S(2)}, u32[]{:S(2)}) collective-permute-start(bf16[1024,256]{1,0:T(8,128)(2,1)} %get-tuple-element.12), channel_id=1, source_target_pairs={{0,16},{4,20},{12,28},{16,0},{20,4},{28,12},{1,17},{5,21},{13,29},... | collective-permute-start | bytes 1572872 | tf_op jit(solution)/shard_map/ppermute | solution.py:66
  170.5 32.0 %collective-permute-start.17 = (bf16[1024,256]{1,0:T(8,128)(2,1)}, bf16[1024,256]{1,0:T(8,128)(2,1)}, u32[]{:S(2)}, u32[]{:S(2)}) collective-permute-start(bf16[1024,256]{1,0:T(8,128)(2,1)} %get-tuple-element.13), channel_id=1, source_target_pairs={{0,16},{8,24},{12,28},{16,0},{24,8},{28,12},{1,17},{9,25},{13,29},... | collective-permute-start | bytes 1572872 | tf_op jit(solution)/shard_map/ppermute | solution.py:66
  173.9 29.3 %collective-permute-start.16 = (bf16[1024,256]{1,0:T(8,128)(2,1)}, bf16[1024,256]{1,0:T(8,128)(2,1)}, u32[]{:S(2)}, u32[]{:S(2)}) collective-permute-start(bf16[1024,256]{1,0:T(8,128)(2,1)} %get-tuple-element.10), channel_id=1, source_target_pairs={{4,20},{8,24},{12,28},{20,4},{24,8},{28,12},{5,21},{9,25},{13,29},... | collective-permute-start | bytes 1572872 | tf_op jit(solution)/shard_map/ppermute | solution.py:66
  175.4 13.2 %collective-permute-start.11 = (bf16[384,512]{0,1:T(8,128)(2,1)}, bf16[384,512]{0,1:T(8,128)(2,1)}, u32[]{:S(2)}, u32[]{:S(2)}) collective-permute-start(bf16[384,512]{0,1:T(8,128)(2,1)} %pad_maximum_fusion.9), channel_id=1, source_target_pairs={{0,4},{4,8},{8,12},{1,5},{5,9},{9,13},{2,6},{6,10},{10,14},{3,7},{... | collective-permute-start | bytes 1179656 | tf_op jit(solution)/shard_map/ppermute | solution.py:23
  188.6 18.1 %collective-permute-start.7 = (bf16[384,512]{0,1:T(8,128)(2,1)}, bf16[384,512]{0,1:T(8,128)(2,1)S(1)}, u32[]{:S(2)}, u32[]{:S(2)}) collective-permute-start(bf16[384,512]{0,1:T(8,128)(2,1)} %collective-permute-done.3), channel_id=1, source_target_pairs={{4,0},{8,4},{5,1},{9,5},{6,2},{10,6},{7,3},{11,7},{20,16},{24,20},... | collective-permute-start | bytes 1179656 | tf_op jit(solution)/shard_map/ppermute | solution.py:22
  189.9 18.2 %collective-permute-start.5 = (bf16[384,512]{0,1:T(8,128)(2,1)}, bf16[384,512]{0,1:T(8,128)(2,1)S(1)}, u32[]{:S(2)}, u32[]{:S(2)}) collective-permute-start(bf16[384,512]{0,1:T(8,128)(2,1)} %collective-permute-done.4), channel_id=1, source_target_pairs={{4,8},{8,12},{5,9},{9,13},{6,10},{10,14},{7,11},{11,15},{20,24},{2... | collective-permute-start | bytes 1179656 | tf_op jit(solution)/shard_map/ppermute | solution.py:23
  193.0 16.5 %collective-permute-start.14 = (bf16[384,512]{0,1:T(8,128)(2,1)}, bf16[384,512]{0,1:T(8,128)(2,1)S(1)}, u32[]{:S(2)}, u32[]{:S(2)}) collective-permute-start(bf16[384,512]{0,1:T(8,128)(2,1)} %collective-permute-done.10), channel_id=1, source_target_pairs={{4,0},{8,4},{5,1},{9,5},{6,2},{10,6},{7,3},{11,7},{20,16},{24,20},... | collective-permute-start | bytes 1179656 | tf_op jit(solution)/shard_map/ppermute | solution.py:22
  202.5 8.2 %collective-permute-start.12 = (bf16[384,512]{0,1:T(8,128)(2,1)}, bf16[384,512]{0,1:T(8,128)(2,1)S(1)}, u32[]{:S(2)}, u32[]{:S(2)}) collective-permute-start(bf16[384,512]{0,1:T(8,128)(2,1)} %collective-permute-done.11), channel_id=1, source_target_pairs={{4,8},{8,12},{5,9},{9,13},{6,10},{10,14},{7,11},{11,15},{20,24},{2... | collective-permute-start | bytes 1179656 | tf_op jit(solution)/shard_map/ppermute | solution.py:23
  206.7 22.8 %collective-permute-start.8 = (bf16[384,512]{0,1:T(8,128)(2,1)S(1)}, bf16[384,512]{0,1:T(8,128)(2,1)S(1)}, u32[]{:S(2)}, u32[]{:S(2)}) collective-permute-start(bf16[384,512]{0,1:T(8,128)(2,1)S(1)} %collective-permute-done.7), channel_id=1, source_target_pairs={{4,0},{5,1},{6,2},{7,3},{20,16},{21,17},{22,18},{23,19}} | collective-permute-start | bytes 1179656 | tf_op jit(solution)/shard_map/ppermute | solution.py:22
  208.2 22.3 %collective-permute-start.6 = (bf16[384,512]{0,1:T(8,128)(2,1)S(1)}, bf16[384,512]{0,1:T(8,128)(2,1)S(1)}, u32[]{:S(2)}, u32[]{:S(2)}) collective-permute-start(bf16[384,512]{0,1:T(8,128)(2,1)S(1)} %collective-permute-done.5), channel_id=1, source_target_pairs={{8,12},{9,13},{10,14},{11,15},{24,28},{25,29},{26,30},{27,31}} | collective-permute-start | bytes 1179656 | tf_op jit(solution)/shard_map/ppermute | solution.py:23
  209.4 17.9 %collective-permute-start.15 = (bf16[384,512]{0,1:T(8,128)(2,1)S(1)}, bf16[384,512]{0,1:T(8,128)(2,1)S(1)}, u32[]{:S(2)}, u32[]{:S(2)}) collective-permute-start(bf16[384,512]{0,1:T(8,128)(2,1)S(1)} %collective-permute-done.14), channel_id=1, source_target_pairs={{4,0},{5,1},{6,2},{7,3},{20,16},{21,17},{22,18},{23,19}} | collective-permute-start | bytes 1179656 | tf_op jit(solution)/shard_map/ppermute | solution.py:22
  210.7 16.7 %collective-permute-start.13 = (bf16[384,512]{0,1:T(8,128)(2,1)S(1)}, bf16[384,512]{0,1:T(8,128)(2,1)S(1)}, u32[]{:S(2)}, u32[]{:S(2)}) collective-permute-start(bf16[384,512]{0,1:T(8,128)(2,1)S(1)} %collective-permute-done.12), channel_id=1, source_target_pairs={{8,12},{9,13},{10,14},{11,15},{24,28},{25,29},{26,30},{27,31}} | collective-permute-start | bytes 1179656 | tf_op jit(solution)/shard_map/ppermute | solution.py:23
  (12 other events, 117.2 us)
Sparse Core Ops, SparseCore 0:
  9.1 48.6 all-gather.3
  59.3 44.6 all-gather.7
  105.6 56.1 all-gather.5

commit v18 on v8

--- a/solution.py
+++ b/solution.py
@@ -13,12 +13,14 @@
     return lax.ppermute(block, axis, route)
 
 
-def line_gather(piece):
+def line_gather(piece, gate=None):
     n = lax.axis_size("seq")
     here = lax.axis_index("seq")
     from_right = [piece]
     from_left = [piece]
     for k in range(1, n):
+        if k == 2 and gate is not None:
+            from_right[-1], from_left[-1], _ = lax.optimization_barrier((from_right[-1], from_left[-1], gate))
         from_right.append(lax.ppermute(from_right[-1], "seq", [(j, j - 1) for j in range(1, n - k + 1)]))
         from_left.append(lax.ppermute(from_left[-1], "seq", [(j, j + 1) for j in range(k - 1, n - 1)]))
     slots = [piece]
@@ -70,9 +72,14 @@
 
     key = jnp.concatenate(project(w_key), axis=1)
     value = jnp.concatenate(project(w_value), axis=1)
-    queries = project(w_query, key)
+    query_pieces = full_columns(w_query, shared, key)
+    queries = [
+        jnp.dot(block, piece, preferred_element_type=jnp.float32).astype(jnp.bfloat16)
+        for piece in query_pieces
+    ]
     if lax.axis_size("seq") == SPAN:
-        seen = jnp.stack([line_gather(key), line_gather(value)])
+        gate = query_pieces[0] if shared else None
+        seen = jnp.stack([line_gather(key, gate), line_gather(value, gate)])
     else:
         packed = jnp.stack([key, value])
         blocks_seen = [packed]

time: 227 us -> 231 us (1.018)
  the two profiles are of different devices: /device:TPU:0 before, /device:TPU:8 now
where the time goes in v18:
time: 231 us
  waiting for transfers between devices  131 us (57%)
  starting transfers between devices  36.8 us (16%)
  other arithmetic  24.6 us (11%)
  matrix products  15.8 us (7%)
  between operations  13.6 us (6%)
  local copies, waits for them, and re-layouts  8.21 us (4%)
    all_gather x3, waiting for transfers between devices, full_columns(): own = lax.all_gather(own, 'seq', axis=0, tiled=True)  73.4 us
    ppermute x3, waiting for transfers between devices, full_columns(): other = lax.ppermute(own[rows:], 'groups', [(0, 1), (1, 0)])  28 us
    ppermute x2, waiting for transfers between devices, swap_gather(): other = lax.ppermute(piece, axis, [(0, 1), (1, 0)])  19.2 us
    ppermute x6, starting transfers between devices, line_gather(): lax.ppermute(from_right[-1], 'seq', [(j, j - 1) for j in range(1, n - k +...  15.7 us
    ppermute x6, starting transfers between devices, line_gather(): lax.ppermute(from_left[-1], 'seq', [(j, j + 1) for j in range(k - 1, n -...  14.9 us
    ppermute x6, waiting for transfers between devices, line_gather(): lax.ppermute(from_right[-1], 'seq', [(j, j - 1) for j in range(1, n - k +...  10.8 us
    concatenate x3, other arithmetic, full_columns(): own = jnp.roll(own, -lax.axis_index('seq') * rows, axis=0)  8.93 us
    dot_general x4, matrix products, project(): jnp.dot(block, piece, preferred_element_type=jnp.float32)  6.76 us
  transfers between devices with their start and end apart: 20, of which 10 were waited for; matrix products, arithmetic and copies ran while one was open for 16% of the time, Pallas kernels for 0%

profile of v18, /device:TPU:8, one launch (start us, length us, event | category | flops | bytes accessed | tf_op | source)
XLA Modules:
  0.0 230.5 jit_solution(718438025179803960)
XLA Ops:
  6.5 2.4 %constant_dynamic-slice_fusion.4 = (bf16[1024,256]{1,0:T(8,128)(2,1)}, bf16[1024,256]{1,0:T(8,128)(2,1)}) fusion(bf16[1024,512]{1,0:T(8,128)(2,1)} %param.9, s32[]{:T(128)S(6)} %select_n.105, s32[]{:T(128)S(6)} %select_n.104), kind=kLoop, calls=%fused_computation.84 | loop fusion | bytes 2097160 | tf_op jit(solution)/shard_map/dynamic_slice | solution.py:48
  11.7 16.8 %collective-permute-done = bf16[192,2048]{1,0:T(8,128)(2,1)S(1)} collective-permute-done((bf16[192,2048]{1,0:T(8,128)(2,1)}, bf16[192,2048]{1,0:T(8,128)(2,1)S(1)}, u32[]{:S(2)}, u32[]{:S(2)}) %collective-permute-start) | collective-permute-done | bytes 786464 | tf_op jit(solution)/shard_map/ppermute | solution.py:36
  30.1 2.3 %collective-permute-done.1 = bf16[384,2048]{1,0:T(8,128)(2,1)} collective-permute-done((bf16[384,2048]{1,0:T(8,128)(2,1)S(1)}, bf16[384,2048]{1,0:T(8,128)(2,1)}, u32[]{:S(2)}, u32[]{:S(2)}) %collective-permute-start.1) | collective-permute-done | bytes 1572896 | tf_op jit(solution)/shard_map/ppermute | solution.py:36
  32.4 4.0 %broadcast_select_fusion = (bf16[384,2048]{1,0:T(8,128)(2,1)}, bf16[384,2048]{1,0:T(8,128)(2,1)}) fusion(bf16[384,2048]{1,0:T(8,128)(2,1)} %collective-permute-done.1, pred[]{:T(512)S(6)} %eq.12, bf16[192,2048]{1,0:T(8,128)(2,1)S(1)} %get-tuple-element.19, bf16[192,2048]{1,0:T(8,128)(2,1)S(1)} %get-tuple-element.18), kind=kLoop, calls=%fused_computation.45 | loop fusion | flops 4718592 | bytes 6291457 | tf_op jit(solution)/shard_map/jit(_where)/select_n | solution.py:38
  36.4 18.2 %all-gather.4.cloned.1.call-done = bf16[4096,256]{1,0:T(8,128)(2,1)} async-done(((bf16[1024,256]{1,0:T(8,128)(2,1)}), bf16[4096,256]{1,0:T(8,128)(2,1)}) %all-gather.4.cloned.1.call-update) | async-done | bytes 2097168 | tf_op jit(solution)/shard_map/all_gather | solution.py:49
  54.6 2.9 %fusion.17 = bf16[4096,256]{1,0:T(8,128)(2,1)S(1)} fusion(s32[]{:T(128)S(6)} %select_n.103, bf16[4096,256]{1,0:T(8,128)(2,1)} %all-gather.4.cloned.1.call-done), kind=kLoop, calls=%fused_computation.29 | loop fusion | flops 4194304 | bytes 4194308 | tf_op jit(solution)/shard_map/jit(_roll_dynamic)/concatenate | solution.py:50
  60.2 40.6 %all-gather.8.cloned.1.call-done = bf16[4096,256]{1,0:T(8,128)(2,1)} async-done(((bf16[1024,256]{1,0:T(8,128)(2,1)}), bf16[4096,256]{1,0:T(8,128)(2,1)}) %all-gather.8.cloned.1.call-update) | async-done | bytes 2097168 | tf_op jit(solution)/shard_map/all_gather | solution.py:49
  100.8 3.1 %fusion.15 = bf16[4096,256]{1,0:T(8,128)(2,1)S(1)} fusion(s32[]{:T(128)S(6)} %select_n.103, bf16[4096,256]{1,0:T(8,128)(2,1)} %all-gather.8.cloned.1.call-done), kind=kLoop, calls=%fused_computation.27 | loop fusion | flops 4194304 | bytes 4194308 | tf_op jit(solution)/shard_map/jit(_roll_dynamic)/concatenate | solution.py:50
  105.6 2.9 %fusion.6 = bf16[384,4096]{1,0:T(8,128)(2,1)S(1)} fusion(s32[]{:T(128)S(6)} %select_n.103, bf16[384,2048]{1,0:T(8,128)(2,1)S(1)} %copy-done.1, bf16[384,2048]{1,0:T(8,128)(2,1)S(1)} %copy-done), kind=kLoop, calls=%fused_computation.20 | loop fusion | flops 12582912 | bytes 6291460 | tf_op jit(solution)/shard_map/jit(_roll_dynamic)/concatenate | solution.py:65
  111.1 2.9 %fusion.42 = bf16[384,256]{0,1:T(8,128)(2,1)S(1)} fusion(bf16[384,4096]{1,0:T(8,128)(2,1)S(1)} %fusion.6, bf16[3072,256]{1,0:T(8,128)(2,1)} %collective-permute-done.2, bf16[1024,256]{1,0:T(8,128)(2,1)S(1)} %copy-done.11), kind=kOutput, calls=%fused_computation.51 | convolution fusion | flops 809598976 | bytes 5439488 | tf_op jit(solution)/shard_map/dot_general | solution.py:69
  114.1 4.0 %collective-permute-start.3 = (bf16[384,512]{0,1:T(8,128)(2,1)S(1)}, bf16[384,512]{0,1:T(8,128)(2,1)}, u32[]{:S(2)}, u32[]{:S(2)}) collective-permute-start(bf16[384,512]{0,1:T(8,128)(2,1)S(1)} %pad_maximum_fusion.3), channel_id=1, source_target_pairs={{4,0},{8,4},{12,8},{5,1},{9,5},{13,9},{6,2},{10,6},{14,10},{7,3},{... | collective-permute-start | bytes 1179656 | tf_op jit(solution)/shard_map/ppermute | solution.py:24
  118.1 1.9 collective-permute-start.4
  120.0 19.9 %collective-permute-done.5 = bf16[3072,256]{1,0:T(8,128)(2,1)S(1)} collective-permute-done((bf16[3072,256]{1,0:T(8,128)(2,1)S(1)}, bf16[3072,256]{1,0:T(8,128)(2,1)S(1)}, u32[]{:S(2)}, u32[]{:S(2)}) %collective-permute-start.5) | collective-permute-done | bytes 1572896 | tf_op jit(solution)/shard_map/ppermute | solution.py:53
  142.0 4.4 %collective-permute-start.10 = (bf16[384,512]{0,1:T(8,128)(2,1)S(1)}, bf16[384,512]{0,1:T(8,128)(2,1)}, u32[]{:S(2)}, u32[]{:S(2)}) collective-permute-start(bf16[384,512]{0,1:T(8,128)(2,1)S(1)} %pad_maximum_fusion.4), channel_id=1, source_target_pairs={{4,0},{8,4},{12,8},{5,1},{9,5},{13,9},{6,2},{10,6},{14,10},{7,3},{... | collective-permute-start | bytes 1179656 | tf_op jit(solution)/shard_map/ppermute | solution.py:24
  146.4 2.1 collective-permute-start.11
  148.5 14.7 %all-gather.6.cloned.1.call-done = bf16[4096,256]{1,0:T(8,128)(2,1)} async-done(((bf16[1024,256]{1,0:T(8,128)(2,1)}), bf16[4096,256]{1,0:T(8,128)(2,1)}) %all-gather.6.cloned.1.call-update) | async-done | bytes 2097168 | tf_op jit(solution)/shard_map/all_gather | solution.py:49
  163.2 2.9 %fusion.16 = bf16[4096,256]{1,0:T(8,128)(2,1)S(1)} fusion(s32[]{:T(128)S(6)} %select_n.103, bf16[4096,256]{1,0:T(8,128)(2,1)} %all-gather.6.cloned.1.call-done), kind=kLoop, calls=%fused_computation.28 | loop fusion | flops 4194304 | bytes 4194308 | tf_op jit(solution)/shard_map/jit(_roll_dynamic)/concatenate | solution.py:50
  168.0 4.7 %collective-permute-start.6 = (bf16[384,512]{0,1:T(8,128)(2,1)}, bf16[384,512]{0,1:T(8,128)(2,1)S(1)}, u32[]{:S(2)}, u32[]{:S(2)}) collective-permute-start(bf16[384,512]{0,1:T(8,128)(2,1)} %collective-permute-done.4), channel_id=1, source_target_pairs={{4,8},{8,12},{5,9},{9,13},{6,10},{10,14},{7,11},{11,15},{20,24},{2... | collective-permute-start | bytes 1179656 | tf_op jit(solution)/shard_map/ppermute | solution.py:25
  174.7 4.8 %collective-permute-start.12 = (bf16[384,512]{0,1:T(8,128)(2,1)}, bf16[384,512]{0,1:T(8,128)(2,1)}, u32[]{:S(2)}, u32[]{:S(2)}) collective-permute-start(bf16[384,512]{0,1:T(8,128)(2,1)} %collective-permute-done.11), channel_id=1, source_target_pairs={{4,8},{8,12},{5,9},{9,13},{6,10},{10,14},{7,11},{11,15},{20,24},{2... | collective-permute-start | bytes 1179656 | tf_op jit(solution)/shard_map/ppermute | solution.py:25
  187.5 2.1 collective-permute-start.15
  191.4 3.5 %collective-permute-done.9 = bf16[384,512]{0,1:T(8,128)(2,1)S(1)} collective-permute-done((bf16[384,512]{0,1:T(8,128)(2,1)}, bf16[384,512]{0,1:T(8,128)(2,1)S(1)}, u32[]{:S(2)}, u32[]{:S(2)}) %collective-permute-start.9) | collective-permute-done | bytes 393248 | tf_op jit(solution)/shard_map/ppermute | solution.py:24
  195.9 5.6 %collective-permute-done.15 = bf16[384,512]{0,1:T(8,128)(2,1)S(1)} collective-permute-done((bf16[384,512]{0,1:T(8,128)(2,1)S(1)}, bf16[384,512]{0,1:T(8,128)(2,1)S(1)}, u32[]{:S(2)}, u32[]{:S(2)}) %collective-permute-start.15) | collective-permute-done | bytes 393248 | tf_op jit(solution)/shard_map/ppermute | solution.py:24
  208.1 8.0 %collective-permute-done.16 = bf16[3072,256]{1,0:T(8,128)(2,1)} collective-permute-done((bf16[3072,256]{1,0:T(8,128)(2,1)}, bf16[3072,256]{1,0:T(8,128)(2,1)}, u32[]{:S(2)}, u32[]{:S(2)}) %collective-permute-start.16) | collective-permute-done | bytes 1572896 | tf_op jit(solution)/shard_map/ppermute | solution.py:53
  216.1 3.8 %fusion.36 = bf16[384,256]{0,1:T(8,128)(2,1)S(1)} fusion(bf16[384,4096]{1,0:T(8,128)(2,1)} %copy-done.2, bf16[3072,256]{1,0:T(8,128)(2,1)} %collective-permute-done.16, bf16[1024,256]{1,0:T(8,128)(2,1)} %get-tuple-element.20), kind=kOutput, calls=%fused_computation.49 | convolution fusion | flops 809598976 | bytes 5439488 | tf_op jit(solution)/shard_map/dot_general | solution.py:77
  (83 shorter events, 38.6 us)
Async XLA Ops:
  6.5 22.0 %copy-start.10 = (bf16[192,2048]{1,0:T(8,128)(2,1)S(1)}, bf16[192,2048]{1,0:T(8,128)(2,1)}, u32[]{:S(2)}) copy-start(bf16[192,2048]{1,0:T(8,128)(2,1)} %param.6) | copy-start | bytes 2359300
  6.5 48.0 %all-gather.4.cloned.1.call-start = ((), (), s32[]{:S(2)}) async-start(), calls=%async_computation | async-start | bytes 2621440 | tf_op jit(solution)/shard_map/all_gather | solution.py:49
  8.9 91.9 %all-gather.8.cloned.1.call-start = ((), (), s32[]{:S(2)}) async-start(), calls=%async_computation.2 | async-start | bytes 2621440 | tf_op jit(solution)/shard_map/all_gather | solution.py:49
  9.0 19.6 %collective-permute-start = (bf16[192,2048]{1,0:T(8,128)(2,1)}, bf16[192,2048]{1,0:T(8,128)(2,1)S(1)}, u32[]{:S(2)}, u32[]{:S(2)}) collective-permute-start(bf16[192,2048]{1,0:T(8,128)(2,1)} %param.6), channel_id=1, source_target_pairs={{0,2},{2,0},{1,3},{3,1},{4,6},{6,4},{5,7},{7,5},{8,10},{10,8},{9,1... | collective-permute-start | bytes 2359304 | tf_op jit(solution)/shard_map/ppermute | solution.py:36
  11.6 151.5 %all-gather.6.cloned.1.call-start = ((), (), s32[]{:S(2)}) async-start(), calls=%async_computation.1 | async-start | bytes 2621440 | tf_op jit(solution)/shard_map/all_gather | solution.py:49
  28.8 3.6 %collective-permute-start.1 = (bf16[384,2048]{1,0:T(8,128)(2,1)S(1)}, bf16[384,2048]{1,0:T(8,128)(2,1)}, u32[]{:S(2)}, u32[]{:S(2)}) collective-permute-start(bf16[384,2048]{1,0:T(8,128)(2,1)S(1)} %pad_maximum_fusion), channel_id=1, source_target_pairs={{0,1},{1,0},{2,3},{3,2},{4,5},{5,4},{6,7},{7,6},{8,9},{9,8},{10,11... | collective-permute-start | bytes 4718600 | tf_op jit(solution)/shard_map/ppermute | solution.py:36
  58.7 52.3 %collective-permute-start.2 = (bf16[3072,256]{1,0:T(8,128)(2,1)}, bf16[3072,256]{1,0:T(8,128)(2,1)}, u32[]{:S(2)}, u32[]{:S(2)}) collective-permute-start(bf16[3072,256]{1,0:T(8,128)(2,1)} %slice.28), channel_id=1, source_target_pairs={{0,16},{16,0},{1,17},{17,1},{2,18},{18,2},{3,19},{19,3},{4,20},{20... | collective-permute-start | bytes 4718600 | tf_op jit(solution)/shard_map/ppermute | solution.py:53
  104.0 35.9 %collective-permute-start.5 = (bf16[3072,256]{1,0:T(8,128)(2,1)S(1)}, bf16[3072,256]{1,0:T(8,128)(2,1)S(1)}, u32[]{:S(2)}, u32[]{:S(2)}) collective-permute-start(bf16[3072,256]{1,0:T(8,128)(2,1)S(1)} %slice.29), channel_id=1, source_target_pairs={{0,16},{16,0},{1,17},{17,1},{2,18},{18,2},{3,19},{19,3},{4,20},{20... | collective-permute-start | bytes 4718600 | tf_op jit(solution)/shard_map/ppermute | solution.py:53
  108.5 31.5 %copy-start.2 = (bf16[384,4096]{1,0:T(8,128)(2,1)}, bf16[384,4096]{1,0:T(8,128)(2,1)S(1)}, u32[]{:S(2)}) copy-start(bf16[384,4096]{1,0:T(8,128)(2,1)S(1)} %fusion.6) | copy-start | bytes 9437188
  111.1 28.9 %copy-start.12 = (bf16[1024,256]{1,0:T(8,128)(2,1)S(1)}, bf16[1024,256]{1,0:T(8,128)(2,1)}, u32[]{:S(2)}) copy-start(bf16[1024,256]{1,0:T(8,128)(2,1)} %get-tuple-element.22) | copy-start | bytes 1572868
  114.0 27.3 %copy-start.6 = (bf16[384,256]{0,1:T(8,128)(2,1)}, bf16[384,256]{0,1:T(8,128)(2,1)S(1)}, u32[]{:S(2)}) copy-start(bf16[384,256]{0,1:T(8,128)(2,1)S(1)} %fusion.42) | copy-start | bytes 589828
  114.1 52.0 %collective-permute-start.3 = (bf16[384,512]{0,1:T(8,128)(2,1)S(1)}, bf16[384,512]{0,1:T(8,128)(2,1)}, u32[]{:S(2)}, u32[]{:S(2)}) collective-permute-start(bf16[384,512]{0,1:T(8,128)(2,1)S(1)} %pad_maximum_fusion.3), channel_id=1, source_target_pairs={{4,0},{8,4},{12,8},{5,1},{9,5},{13,9},{6,2},{10,6},{14,10},{7,3},{... | collective-permute-start | bytes 1179656 | tf_op jit(solution)/shard_map/ppermute | solution.py:24
  118.1 48.0 %collective-permute-start.4 = (bf16[384,512]{0,1:T(8,128)(2,1)S(1)}, bf16[384,512]{0,1:T(8,128)(2,1)}, u32[]{:S(2)}, u32[]{:S(2)}) collective-permute-start(bf16[384,512]{0,1:T(8,128)(2,1)S(1)} %pad_maximum_fusion.3), channel_id=1, source_target_pairs={{0,4},{4,8},{8,12},{1,5},{5,9},{9,13},{2,6},{6,10},{10,14},{3,7},{... | collective-permute-start | bytes 1179656 | tf_op jit(solution)/shard_map/ppermute | solution.py:25
  142.0 30.8 %collective-permute-start.10 = (bf16[384,512]{0,1:T(8,128)(2,1)S(1)}, bf16[384,512]{0,1:T(8,128)(2,1)}, u32[]{:S(2)}, u32[]{:S(2)}) collective-permute-start(bf16[384,512]{0,1:T(8,128)(2,1)S(1)} %pad_maximum_fusion.4), channel_id=1, source_target_pairs={{4,0},{8,4},{12,8},{5,1},{9,5},{13,9},{6,2},{10,6},{14,10},{7,3},{... | collective-permute-start | bytes 1179656 | tf_op jit(solution)/shard_map/ppermute | solution.py:24
  146.4 26.4 %collective-permute-start.11 = (bf16[384,512]{0,1:T(8,128)(2,1)S(1)}, bf16[384,512]{0,1:T(8,128)(2,1)}, u32[]{:S(2)}, u32[]{:S(2)}) collective-permute-start(bf16[384,512]{0,1:T(8,128)(2,1)S(1)} %pad_maximum_fusion.4), channel_id=1, source_target_pairs={{0,4},{4,8},{8,12},{1,5},{5,9},{9,13},{2,6},{6,10},{10,14},{3,7},{... | collective-permute-start | bytes 1179656 | tf_op jit(solution)/shard_map/ppermute | solution.py:25
  166.1 17.5 %collective-permute-start.8 = (bf16[384,512]{0,1:T(8,128)(2,1)}, bf16[384,512]{0,1:T(8,128)(2,1)}, u32[]{:S(2)}, u32[]{:S(2)}) collective-permute-start(bf16[384,512]{0,1:T(8,128)(2,1)} %collective-permute-done.3), channel_id=1, source_target_pairs={{4,0},{8,4},{5,1},{9,5},{6,2},{10,6},{7,3},{11,7},{20,16},{24,20},... | collective-permute-start | bytes 1179656 | tf_op jit(solution)/shard_map/ppermute | solution.py:24
  168.0 17.0 %collective-permute-start.6 = (bf16[384,512]{0,1:T(8,128)(2,1)}, bf16[384,512]{0,1:T(8,128)(2,1)S(1)}, u32[]{:S(2)}, u32[]{:S(2)}) collective-permute-start(bf16[384,512]{0,1:T(8,128)(2,1)} %collective-permute-done.4), channel_id=1, source_target_pairs={{4,8},{8,12},{5,9},{9,13},{6,10},{10,14},{7,11},{11,15},{20,24},{2... | collective-permute-start | bytes 1179656 | tf_op jit(solution)/shard_map/ppermute | solution.py:25
  172.8 14.7 %collective-permute-start.14 = (bf16[384,512]{0,1:T(8,128)(2,1)}, bf16[384,512]{0,1:T(8,128)(2,1)S(1)}, u32[]{:S(2)}, u32[]{:S(2)}) collective-permute-start(bf16[384,512]{0,1:T(8,128)(2,1)} %collective-permute-done.10), channel_id=1, source_target_pairs={{4,0},{8,4},{5,1},{9,5},{6,2},{10,6},{7,3},{11,7},{20,16},{24,20},... | collective-permute-start | bytes 1179656 | tf_op jit(solution)/shard_map/ppermute | solution.py:24
  174.7 14.9 %collective-permute-start.12 = (bf16[384,512]{0,1:T(8,128)(2,1)}, bf16[384,512]{0,1:T(8,128)(2,1)}, u32[]{:S(2)}, u32[]{:S(2)}) collective-permute-start(bf16[384,512]{0,1:T(8,128)(2,1)} %collective-permute-done.11), channel_id=1, source_target_pairs={{4,8},{8,12},{5,9},{9,13},{6,10},{10,14},{7,11},{11,15},{20,24},{2... | collective-permute-start | bytes 1179656 | tf_op jit(solution)/shard_map/ppermute | solution.py:25
  180.8 35.3 %collective-permute-start.16 = (bf16[3072,256]{1,0:T(8,128)(2,1)}, bf16[3072,256]{1,0:T(8,128)(2,1)}, u32[]{:S(2)}, u32[]{:S(2)}) collective-permute-start(bf16[3072,256]{1,0:T(8,128)(2,1)} %slice.26), channel_id=1, source_target_pairs={{0,16},{16,0},{1,17},{17,1},{2,18},{18,2},{3,19},{19,3},{4,20},{20... | collective-permute-start | bytes 4718600 | tf_op jit(solution)/shard_map/ppermute | solution.py:53
  183.6 11.3 %collective-permute-start.9 = (bf16[384,512]{0,1:T(8,128)(2,1)}, bf16[384,512]{0,1:T(8,128)(2,1)S(1)}, u32[]{:S(2)}, u32[]{:S(2)}) collective-permute-start(bf16[384,512]{0,1:T(8,128)(2,1)} %collective-permute-done.8), channel_id=1, source_target_pairs={{4,0},{5,1},{6,2},{7,3},{20,16},{21,17},{22,18},{23,19}} | collective-permute-start | bytes 1179656 | tf_op jit(solution)/shard_map/ppermute | solution.py:24
  185.0 17.5 %collective-permute-start.7 = (bf16[384,512]{0,1:T(8,128)(2,1)S(1)}, bf16[384,512]{0,1:T(8,128)(2,1)S(1)}, u32[]{:S(2)}, u32[]{:S(2)}) collective-permute-start(bf16[384,512]{0,1:T(8,128)(2,1)S(1)} %collective-permute-done.6), channel_id=1, source_target_pairs={{8,12},{9,13},{10,14},{11,15},{24,28},{25,29},{26,30},{27,31}} | collective-permute-start | bytes 1179656 | tf_op jit(solution)/shard_map/ppermute | solution.py:25
  187.5 14.0 %collective-permute-start.15 = (bf16[384,512]{0,1:T(8,128)(2,1)S(1)}, bf16[384,512]{0,1:T(8,128)(2,1)S(1)}, u32[]{:S(2)}, u32[]{:S(2)}) collective-permute-start(bf16[384,512]{0,1:T(8,128)(2,1)S(1)} %collective-permute-done.14), channel_id=1, source_target_pairs={{4,0},{5,1},{6,2},{7,3},{20,16},{21,17},{22,18},{23,19}} | collective-permute-start | bytes 1179656 | tf_op jit(solution)/shard_map/ppermute | solution.py:24
  189.6 14.2 %collective-permute-start.13 = (bf16[384,512]{0,1:T(8,128)(2,1)}, bf16[384,512]{0,1:T(8,128)(2,1)S(1)}, u32[]{:S(2)}, u32[]{:S(2)}) collective-permute-start(bf16[384,512]{0,1:T(8,128)(2,1)} %collective-permute-done.12), channel_id=1, source_target_pairs={{8,12},{9,13},{10,14},{11,15},{24,28},{25,29},{26,30},{27,31}} | collective-permute-start | bytes 1179656 | tf_op jit(solution)/shard_map/ppermute | solution.py:25
  (9 other events, 64.5 us)
Sparse Core Ops, SparseCore 0:
  9.0 45.4 all-gather.3
  56.1 44.6 all-gather.7
  102.4 60.7 all-gather.5

commit v19 on v16

--- a/solution.py
+++ b/solution.py
@@ -37,21 +37,29 @@
     return jnp.concatenate([low, high], axis=dim)
 
 
-def full_columns(weight, shared, after=None):
+def full_columns(weight, shared, after=None, gate=None):
     if not shared:
         return [lax.all_gather(weight, "seq", axis=0, tiled=True)]
     rows, half = weight.shape[0], weight.shape[1] // 2
     group = lax.axis_index("groups")
-    own = lax.dynamic_slice_in_dim(weight, group * half, half, axis=1)
-    kept = lax.dynamic_slice_in_dim(weight, (1 - group) * half, half, axis=1)
-    own = lax.all_gather(own, "seq", axis=0, tiled=True)
-    own = jnp.roll(own, -lax.axis_index("seq") * rows, axis=0)
-    if after is not None:
-        own, after = lax.optimization_barrier((own, after))
+    count = 2 if gate is not None and half % (2 * HD) == 0 else 1
+    width = half // count
+    owns, others = [], []
+    for k in range(count):
+        own = lax.dynamic_slice_in_dim(weight, group * half + k * width, width, axis=1)
+        kept = lax.dynamic_slice_in_dim(weight, (1 - group) * half + k * width, width, axis=1)
+        if gate is not None:
+            own, gate = lax.optimization_barrier((own, gate))
+        own = lax.all_gather(own, "seq", axis=0, tiled=True)
+        if others:
+            own, others[-1] = lax.optimization_barrier((own, others[-1]))
+        own = jnp.roll(own, -lax.axis_index("seq") * rows, axis=0)
+        if after is not None:
+            own, after = lax.optimization_barrier((own, after))
         other = lax.ppermute(own[rows:], "groups", [(0, 1), (1, 0)])
-        return [own, jnp.concatenate([kept, other], axis=0)], after
-    other = lax.ppermute(own[rows:], "groups", [(0, 1), (1, 0)])
-    return [own, jnp.concatenate([kept, other], axis=0)]
+        owns.append(own)
+        others.append(jnp.concatenate([kept, other], axis=0))
+    return owns + others
 
 
 def per_device(acts, w_query, w_key, w_value):
@@ -71,12 +79,10 @@
         ]
 
     key = jnp.concatenate(project(full_columns(w_key, shared)), axis=1)
-    value = jnp.concatenate(project(full_columns(w_value, shared)), axis=1)
-    if shared:
-        query_pieces, key = full_columns(w_query, shared, key)
-    else:
-        query_pieces = full_columns(w_query, shared)
-    queries = project(query_pieces)
+    value_pieces = full_columns(w_value, shared)
+    value = jnp.concatenate(project(value_pieces), axis=1)
+    gate = value_pieces[0] if shared else None
+    queries = project(full_columns(w_query, shared, key, gate))
     if lax.axis_size("seq") == SPAN:
         seen = jnp.stack([line_gather(key), line_gather(value)])
     else:

time: 234 us -> 271 us (1.16)
  other arithmetic: 22.4 us -> 35.9 us
  matrix products: 17.9 us -> 31.1 us
  local copies, waits for them, and re-layouts: 8.67 us -> 15.7 us
    ppermute x3 -> x4, waiting for transfers between devices: 0.87 us -> 45.1 us  [full_columns(): other = lax.ppermute(own[rows:], 'groups', [(0, 1), (1, 0)])]
    ppermute x2, waiting for transfers between devices: 19.9 us -> 0.01 us  [swap_gather(): other = lax.ppermute(piece, axis, [(0, 1), (1, 0)])]
    dot_general x2 -> x4, matrix products: 1.81 us -> 18.5 us  [per_device(): jnp.einsum('qhd,khd->hqk', query, part_keys, preferred_element_type=jnp.f...]
    ppermute x6, waiting for transfers between devices: 24.2 us -> 13.3 us  [line_gather(): lax.ppermute(from_right[-1], 'seq', [(j, j - 1) for j in range(1, n - k +...]
    all_gather x3 -> x4, waiting for transfers between devices: 94.4 us -> 83.9 us  [full_columns(): own = lax.all_gather(own, 'seq', axis=0, tiled=True)]
    dot_general x6 -> x4, matrix products: 13.8 us -> 7.3 us  [project(): jnp.dot(block, piece, preferred_element_type=jnp.float32)]
    unnamed x26 -> x49, local copies, waits for them, and re-layouts: 0.05 us -> 5.31 us
    reduce_sum x2 -> x4, other arithmetic: 1.82 us -> 5.33 us  [per_device(): running_total = jnp.sum(expos, axis=-1)]
  transfers between devices with their start and end apart: 20 -> 22, of which waited for: 11 -> 7; matrix products, arithmetic and copies ran while one was open for 17% -> 23% of each run, Pallas kernels for 0% -> 0%
where the time goes in v19:
time: 271 us; the launch traced here: 270 us
  waiting for transfers between devices  142 us (52%)
  other arithmetic  35.9 us (13%)
  starting transfers between devices  31.7 us (12%)
  matrix products  31.1 us (11%)
  local copies, waits for them, and re-layouts  15.7 us (6%)
  between operations  13.5 us (5%)
    all_gather x4, waiting for transfers between devices, full_columns(): own = lax.all_gather(own, 'seq', axis=0, tiled=True)  83.9 us
    ppermute x4, waiting for transfers between devices, full_columns(): other = lax.ppermute(own[rows:], 'groups', [(0, 1), (1, 0)])  45.1 us
    dot_general x4, matrix products, per_device(): jnp.einsum('qhd,khd->hqk', query, part_keys, preferred_element_type=jnp.f...  18.5 us
    ppermute x6, starting transfers between devices, line_gather(): lax.ppermute(from_left[-1], 'seq', [(j, j + 1) for j in range(k - 1, n -...  15.7 us
    ppermute x6, waiting for transfers between devices, line_gather(): lax.ppermute(from_right[-1], 'seq', [(j, j - 1) for j in range(1, n - k +...  13.3 us
    concatenate x4, other arithmetic, full_columns(): own = jnp.roll(own, -lax.axis_index('seq') * rows, axis=0)  11.2 us
    ppermute x6, starting transfers between devices, line_gather(): lax.ppermute(from_right[-1], 'seq', [(j, j - 1) for j in range(1, n - k +...  7.68 us
    dot_general x4, matrix products, project(): jnp.dot(block, piece, preferred_element_type=jnp.float32)  7.3 us
  transfers between devices with their start and end apart: 22, of which 7 were waited for; matrix products, arithmetic and copies ran while one was open for 23% of the time, Pallas kernels for 0%

profile of v19, /device:TPU:0, one launch (start us, length us, event | category | flops | bytes accessed | tf_op | source)
XLA Modules:
  0.0 270.3 jit_solution(14687616093533785308)
XLA Ops:
  6.5 2.4 constant_dynamic-slice_fusion.7
  10.2 3.0 %collective-permute-start = (bf16[192,2048]{1,0:T(8,128)(2,1)S(1)}, bf16[192,2048]{1,0:T(8,128)(2,1)}, u32[]{:S(2)}, u32[]{:S(2)}) collective-permute-start(bf16[192,2048]{1,0:T(8,128)(2,1)S(1)} %copy-done.17), channel_id=1, source_target_pairs={{0,2},{2,0},{1,3},{3,1},{4,6},{6,4},{5,7},{7,5},{8,10},{10,8},{9,1... | collective-permute-start | bytes 2359304 | tf_op jit(solution)/shard_map/ppermute | solution.py:34
  14.2 43.6 %all-gather.5.cloned.1.call-done = bf16[4096,256]{1,0:T(8,128)(2,1)} async-done(((bf16[1024,256]{1,0:T(8,128)(2,1)}), bf16[4096,256]{1,0:T(8,128)(2,1)}) %all-gather.5.cloned.1.call-update) | async-done | bytes 2097168 | tf_op jit(solution)/shard_map/all_gather | solution.py:53
  57.8 4.4 %fusion.4 = bf16[4096,256]{1,0:T(8,128)(2,1)} fusion(s32[]{:T(128)S(6)} %select_n.116, bf16[4096,256]{1,0:T(8,128)(2,1)} %all-gather.5.cloned.1.call-done), kind=kLoop, calls=%fused_computation.20 | loop fusion | flops 4194304 | bytes 4194308 | tf_op jit(solution)/shard_map/jit(_roll_dynamic)/concatenate | solution.py:56
  63.8 40.2 %all-gather.9.cloned.1.call-done = bf16[4096,256]{1,0:T(8,128)(2,1)} async-done(((bf16[1024,256]{1,0:T(8,128)(2,1)}), bf16[4096,256]{1,0:T(8,128)(2,1)}) %all-gather.9.cloned.1.call-update) | async-done | bytes 2097168 | tf_op jit(solution)/shard_map/all_gather | solution.py:53
  104.0 3.0 %fusion.3 = bf16[4096,256]{1,0:T(8,128)(2,1)S(1)} fusion(s32[]{:T(128)S(6)} %select_n.116, bf16[4096,256]{1,0:T(8,128)(2,1)} %all-gather.9.cloned.1.call-done), kind=kLoop, calls=%fused_computation.19 | loop fusion | flops 4194304 | bytes 4194308 | tf_op jit(solution)/shard_map/jit(_roll_dynamic)/concatenate | solution.py:56
  108.7 2.2 broadcast_select_fusion
  110.9 2.9 %fusion.2 = bf16[384,4096]{1,0:T(8,128)(2,1)S(1)} fusion(s32[]{:T(128)S(6)} %select_n.116, bf16[384,2048]{1,0:T(8,128)(2,1)S(1)} %get-tuple-element.16, bf16[384,2048]{1,0:T(8,128)(2,1)S(1)} %get-tuple-element.15), kind=kLoop, calls=%fused_computation.10 | loop fusion | flops 12582912 | bytes 6291460 | tf_op jit(solution)/shard_map/jit(_roll_dynamic)/concatenate | solution.py:73
  119.0 25.5 %collective-permute-done.9 = bf16[3072,256]{1,0:T(8,128)(2,1)S(1)} collective-permute-done((bf16[3072,256]{1,0:T(8,128)(2,1)S(1)}, bf16[3072,256]{1,0:T(8,128)(2,1)S(1)}, u32[]{:S(2)}, u32[]{:S(2)}) %collective-permute-start.9) | collective-permute-done | bytes 1572896 | tf_op jit(solution)/shard_map/ppermute | solution.py:59
  147.9 5.3 %collective-permute-start.11 = (bf16[384,512]{0,1:T(8,128)(2,1)}, bf16[384,512]{0,1:T(8,128)(2,1)}, u32[]{:S(2)}, u32[]{:S(2)}) collective-permute-start(bf16[384,512]{0,1:T(8,128)(2,1)} %pad_maximum_fusion.5), channel_id=1, source_target_pairs={{0,4},{4,8},{8,12},{1,5},{5,9},{9,13},{2,6},{6,10},{10,14},{3,7},{... | collective-permute-start | bytes 1179656 | tf_op jit(solution)/shard_map/ppermute | solution.py:23
  158.6 19.6 %collective-permute-done.2 = bf16[3072,256]{1,0:T(8,128)(2,1)} collective-permute-done((bf16[3072,256]{1,0:T(8,128)(2,1)}, bf16[3072,256]{1,0:T(8,128)(2,1)}, u32[]{:S(2)}, u32[]{:S(2)}) %collective-permute-start.2) | collective-permute-done | bytes 1572896 | tf_op jit(solution)/shard_map/ppermute | solution.py:59
  178.3 2.7 %fusion.36 = bf16[384,256]{0,1:T(8,128)(2,1)S(1)} fusion(bf16[384,4096]{1,0:T(8,128)(2,1)S(1)} %fusion.2, bf16[3072,256]{1,0:T(8,128)(2,1)} %collective-permute-done.2, bf16[1024,256]{1,0:T(8,128)(2,1)S(1)} %copy-done.18), kind=kOutput, calls=%fused_computation.55 | convolution fusion | flops 809598976 | bytes 5439488 | tf_op jit(solution)/shard_map/dot_general | solution.py:77
  183.2 5.3 %collective-permute-start.4 = (bf16[384,512]{0,1:T(8,128)(2,1)}, bf16[384,512]{0,1:T(8,128)(2,1)}, u32[]{:S(2)}, u32[]{:S(2)}) collective-permute-start(bf16[384,512]{0,1:T(8,128)(2,1)} %pad_maximum_fusion.4), channel_id=1, source_target_pairs={{0,4},{4,8},{8,12},{1,5},{5,9},{9,13},{2,6},{6,10},{10,14},{3,7},{... | collective-permute-start | bytes 1179656 | tf_op jit(solution)/shard_map/ppermute | solution.py:23
  191.3 4.0 %collective-permute-done.3 = bf16[384,512]{0,1:T(8,128)(2,1)} collective-permute-done((bf16[384,512]{0,1:T(8,128)(2,1)}, bf16[384,512]{0,1:T(8,128)(2,1)}, u32[]{:S(2)}, u32[]{:S(2)}) %collective-permute-start.3) | collective-permute-done | bytes 393248 | tf_op jit(solution)/shard_map/ppermute | solution.py:22
  198.0 2.2 pad_maximum_fusion.3
  206.5 5.3 %collective-permute-done.7 = bf16[384,512]{0,1:T(8,128)(2,1)} collective-permute-done((bf16[384,512]{0,1:T(8,128)(2,1)}, bf16[384,512]{0,1:T(8,128)(2,1)}, u32[]{:S(2)}, u32[]{:S(2)}) %collective-permute-start.7) | collective-permute-done | bytes 393248 | tf_op jit(solution)/shard_map/ppermute | solution.py:22
  216.7 4.0 %collective-permute-done.15 = bf16[384,512]{0,1:T(8,128)(2,1)S(1)} collective-permute-done((bf16[384,512]{0,1:T(8,128)(2,1)}, bf16[384,512]{0,1:T(8,128)(2,1)S(1)}, u32[]{:S(2)}, u32[]{:S(2)}) %collective-permute-start.15) | collective-permute-done | bytes 393248 | tf_op jit(solution)/shard_map/ppermute | solution.py:22
  223.2 4.6 %fusion.99 = (f32[384]{0:T(512)S(1)}, f32[384,1536]{1,0:T(8,128)}) fusion(bf16[1536,4,128]{0,2,1:T(8,128)(2,1)} %bitcast.103, bf16[384,4096]{1,0:T(8,128)(2,1)S(1)} %fusion.2, bf16[4096,128]{1,0:T(8,128)(2,1)} %copy-done.4), kind=kOutput, calls=%fused_computation.122 | convolution fusion | flops 554876544 | bytes 6948352 | tf_op jit(solution)/shard_map/qhd,khd->hqk/dot_general | solution.py:107
  227.8 2.1 fusion.13
  229.9 4.7 %fusion.100 = (f32[384]{0:T(512)S(1)}, f32[384,1536]{1,0:T(8,128)}) fusion(bf16[1536,4,128]{0,2,1:T(8,128)(2,1)} %bitcast.104, bf16[384,4096]{1,0:T(8,128)(2,1)S(1)} %fusion.2, bf16[4096,128]{1,0:T(8,128)(2,1)} %copy-done.5), kind=kOutput, calls=%fused_computation.123 | convolution fusion | flops 554876544 | bytes 6948352 | tf_op jit(solution)/shard_map/qhd,khd->hqk/dot_general | solution.py:107
  236.4 4.6 %fusion.101 = (f32[384]{0:T(512)S(1)}, f32[384,1536]{1,0:T(8,128)}) fusion(bf16[1536,4,128]{0,2,1:T(8,128)(2,1)} %bitcast.105, bf16[384,4096]{1,0:T(8,128)(2,1)S(1)} %fusion.2, bf16[4096,128]{1,0:T(8,128)(2,1)} %pad_maximum_fusion.3), kind=kOutput, calls=%fused_computation.124 | convolution fusion | flops 554876544 | bytes 6948352 | tf_op jit(solution)/shard_map/qhd,khd->hqk/dot_general | solution.py:107
  249.9 4.6 %fusion.102 = (f32[384]{0:T(512)S(1)}, f32[384,1536]{1,0:T(8,128)}) fusion(bf16[1536,4,128]{0,2,1:T(8,128)(2,1)} %bitcast.106, bf16[384,4096]{1,0:T(8,128)(2,1)S(1)} %fusion.2, bf16[3072,128]{1,0:T(8,128)(2,1)} %collective-permute-done.17, bf16[1024,128]{1,0:T(8,128)(2,1)S(1)} %copy-done.8), kind=kOutput, calls=%fused_computation.125 | convolution fusion | flops 556973696 | bytes 6948352 | tf_op jit(solution)/shard_map/qhd,khd->hqk/dot_general | solution.py:107
  254.5 2.3 fusion.19
  256.9 2.3 constant_dynamic-update-slice_fusion.4
  (118 shorter events, 55.9 us)
Async XLA Ops:
  6.5 51.2 %all-gather.5.cloned.1.call-start = ((), (), s32[]{:S(2)}) async-start(), calls=%async_computation | async-start | bytes 2621440 | tf_op jit(solution)/shard_map/all_gather | solution.py:53
  9.0 95.0 %all-gather.9.cloned.1.call-start = ((), (), s32[]{:S(2)}) async-start(), calls=%async_computation.2 | async-start | bytes 2621440 | tf_op jit(solution)/shard_map/all_gather | solution.py:53
  10.1 143.1 %all-gather.7.cloned.1.call-start = ((), (), s32[]{:S(2)}) async-start(), calls=%async_computation.1 | async-start | bytes 1310720 | tf_op jit(solution)/shard_map/all_gather | solution.py:53
  10.2 52.1 %collective-permute-start = (bf16[192,2048]{1,0:T(8,128)(2,1)S(1)}, bf16[192,2048]{1,0:T(8,128)(2,1)}, u32[]{:S(2)}, u32[]{:S(2)}) collective-permute-start(bf16[192,2048]{1,0:T(8,128)(2,1)S(1)} %copy-done.17), channel_id=1, source_target_pairs={{0,2},{2,0},{1,3},{3,1},{4,6},{6,4},{5,7},{7,5},{8,10},{10,8},{9,1... | collective-permute-start | bytes 2359304 | tf_op jit(solution)/shard_map/ppermute | solution.py:34
  62.2 138.0 %all-gather.11.cloned.1.call-start = ((), (), s32[]{:S(2)}) async-start(), calls=%async_computation.3 | async-start | bytes 1310720 | tf_op jit(solution)/shard_map/all_gather | solution.py:53
  63.6 45.0 %collective-permute-start.1 = (bf16[384,2048]{1,0:T(8,128)(2,1)S(1)}, bf16[384,2048]{1,0:T(8,128)(2,1)}, u32[]{:S(2)}, u32[]{:S(2)}) collective-permute-start(bf16[384,2048]{1,0:T(8,128)(2,1)S(1)} %pad_maximum_fusion), channel_id=1, source_target_pairs={{0,1},{1,0},{2,3},{3,2},{4,5},{5,4},{6,7},{7,6},{8,9},{9,8},{10,11... | collective-permute-start | bytes 4718600 | tf_op jit(solution)/shard_map/ppermute | solution.py:34
  107.1 37.3 %collective-permute-start.9 = (bf16[3072,256]{1,0:T(8,128)(2,1)S(1)}, bf16[3072,256]{1,0:T(8,128)(2,1)S(1)}, u32[]{:S(2)}, u32[]{:S(2)}) collective-permute-start(bf16[3072,256]{1,0:T(8,128)(2,1)S(1)} %slice.50), channel_id=1, source_target_pairs={{0,16},{16,0},{1,17},{17,1},{2,18},{18,2},{3,19},{19,3},{4,20},{20... | collective-permute-start | bytes 4718600 | tf_op jit(solution)/shard_map/ppermute | solution.py:59
  115.2 63.1 %collective-permute-start.2 = (bf16[3072,256]{1,0:T(8,128)(2,1)}, bf16[3072,256]{1,0:T(8,128)(2,1)}, u32[]{:S(2)}, u32[]{:S(2)}) collective-permute-start(bf16[3072,256]{1,0:T(8,128)(2,1)} %slice.48), channel_id=1, source_target_pairs={{0,16},{16,0},{1,17},{17,1},{2,18},{18,2},{3,19},{19,3},{4,20},{20... | collective-permute-start | bytes 4718600 | tf_op jit(solution)/shard_map/ppermute | solution.py:59
  117.0 28.8 %copy-start.12 = (bf16[384,256]{0,1:T(8,128)(2,1)}, bf16[384,256]{0,1:T(8,128)(2,1)S(1)}, u32[]{:S(2)}) copy-start(bf16[384,256]{0,1:T(8,128)(2,1)S(1)} %convolution_convert_fusion) | copy-start | bytes 589828
  117.0 27.5 %copy-start.19 = (bf16[1024,256]{1,0:T(8,128)(2,1)S(1)}, bf16[1024,256]{1,0:T(8,128)(2,1)}, u32[]{:S(2)}) copy-start(bf16[1024,256]{1,0:T(8,128)(2,1)} %get-tuple-element.25) | copy-start | bytes 1572868
  146.6 41.9 %collective-permute-start.10 = (bf16[384,512]{0,1:T(8,128)(2,1)}, bf16[384,512]{0,1:T(8,128)(2,1)}, u32[]{:S(2)}, u32[]{:S(2)}) collective-permute-start(bf16[384,512]{0,1:T(8,128)(2,1)} %pad_maximum_fusion.5), channel_id=1, source_target_pairs={{4,0},{8,4},{12,8},{5,1},{9,5},{13,9},{6,2},{10,6},{14,10},{7,3},{... | collective-permute-start | bytes 1179656 | tf_op jit(solution)/shard_map/ppermute | solution.py:22
  147.9 41.9 %collective-permute-start.11 = (bf16[384,512]{0,1:T(8,128)(2,1)}, bf16[384,512]{0,1:T(8,128)(2,1)}, u32[]{:S(2)}, u32[]{:S(2)}) collective-permute-start(bf16[384,512]{0,1:T(8,128)(2,1)} %pad_maximum_fusion.5), channel_id=1, source_target_pairs={{0,4},{4,8},{8,12},{1,5},{5,9},{9,13},{2,6},{6,10},{10,14},{3,7},{... | collective-permute-start | bytes 1179656 | tf_op jit(solution)/shard_map/ppermute | solution.py:23
  157.1 40.8 %collective-permute-start.16 = (bf16[3072,128]{1,0:T(8,128)(2,1)}, bf16[3072,128]{1,0:T(8,128)(2,1)}, u32[]{:S(2)}, u32[]{:S(2)}) collective-permute-start(bf16[3072,128]{1,0:T(8,128)(2,1)} %slice.41), channel_id=1, source_target_pairs={{0,16},{16,0},{1,17},{17,1},{2,18},{18,2},{3,19},{19,3},{4,20},{20... | collective-permute-start | bytes 2359304 | tf_op jit(solution)/shard_map/ppermute | solution.py:59
  181.9 13.3 %collective-permute-start.3 = (bf16[384,512]{0,1:T(8,128)(2,1)}, bf16[384,512]{0,1:T(8,128)(2,1)}, u32[]{:S(2)}, u32[]{:S(2)}) collective-permute-start(bf16[384,512]{0,1:T(8,128)(2,1)} %pad_maximum_fusion.4), channel_id=1, source_target_pairs={{4,0},{8,4},{12,8},{5,1},{9,5},{13,9},{6,2},{10,6},{14,10},{7,3},{... | collective-permute-start | bytes 1179656 | tf_op jit(solution)/shard_map/ppermute | solution.py:22
  183.2 13.3 %collective-permute-start.4 = (bf16[384,512]{0,1:T(8,128)(2,1)}, bf16[384,512]{0,1:T(8,128)(2,1)}, u32[]{:S(2)}, u32[]{:S(2)}) collective-permute-start(bf16[384,512]{0,1:T(8,128)(2,1)} %pad_maximum_fusion.4), channel_id=1, source_target_pairs={{0,4},{4,8},{8,12},{1,5},{5,9},{9,13},{2,6},{6,10},{10,14},{3,7},{... | collective-permute-start | bytes 1179656 | tf_op jit(solution)/shard_map/ppermute | solution.py:23
  188.5 16.1 %collective-permute-start.14 = (bf16[384,512]{0,1:T(8,128)(2,1)}, bf16[384,512]{0,1:T(8,128)(2,1)}, u32[]{:S(2)}, u32[]{:S(2)}) collective-permute-start(bf16[384,512]{0,1:T(8,128)(2,1)} %collective-permute-done.10), channel_id=1, source_target_pairs={{4,0},{8,4},{5,1},{9,5},{6,2},{10,6},{7,3},{11,7},{20,16},{24,20},... | collective-permute-start | bytes 1179656 | tf_op jit(solution)/shard_map/ppermute | solution.py:22
  189.8 16.0 %collective-permute-start.12 = (bf16[384,512]{0,1:T(8,128)(2,1)}, bf16[384,512]{0,1:T(8,128)(2,1)}, u32[]{:S(2)}, u32[]{:S(2)}) collective-permute-start(bf16[384,512]{0,1:T(8,128)(2,1)} %collective-permute-done.11), channel_id=1, source_target_pairs={{4,8},{8,12},{5,9},{9,13},{6,10},{10,14},{7,11},{11,15},{20,24},{2... | collective-permute-start | bytes 1179656 | tf_op jit(solution)/shard_map/ppermute | solution.py:23
  195.2 16.6 %collective-permute-start.7 = (bf16[384,512]{0,1:T(8,128)(2,1)}, bf16[384,512]{0,1:T(8,128)(2,1)}, u32[]{:S(2)}, u32[]{:S(2)}) collective-permute-start(bf16[384,512]{0,1:T(8,128)(2,1)} %collective-permute-done.3), channel_id=1, source_target_pairs={{4,0},{8,4},{5,1},{9,5},{6,2},{10,6},{7,3},{11,7},{20,16},{24,20},... | collective-permute-start | bytes 1179656 | tf_op jit(solution)/shard_map/ppermute | solution.py:22
  196.5 16.6 %collective-permute-start.5 = (bf16[384,512]{0,1:T(8,128)(2,1)}, bf16[384,512]{0,1:T(8,128)(2,1)}, u32[]{:S(2)}, u32[]{:S(2)}) collective-permute-start(bf16[384,512]{0,1:T(8,128)(2,1)} %collective-permute-done.4), channel_id=1, source_target_pairs={{4,8},{8,12},{5,9},{9,13},{6,10},{10,14},{7,11},{11,15},{20,24},{2... | collective-permute-start | bytes 1179656 | tf_op jit(solution)/shard_map/ppermute | solution.py:23
  203.1 46.9 %collective-permute-start.17 = (bf16[3072,128]{1,0:T(8,128)(2,1)}, bf16[3072,128]{1,0:T(8,128)(2,1)}, u32[]{:S(2)}, u32[]{:S(2)}) collective-permute-start(bf16[3072,128]{1,0:T(8,128)(2,1)} %slice.57), channel_id=1, source_target_pairs={{0,16},{16,0},{1,17},{17,1},{2,18},{18,2},{3,19},{19,3},{4,20},{20... | collective-permute-start | bytes 2359304 | tf_op jit(solution)/shard_map/ppermute | solution.py:59
  204.6 16.1 %collective-permute-start.15 = (bf16[384,512]{0,1:T(8,128)(2,1)}, bf16[384,512]{0,1:T(8,128)(2,1)S(1)}, u32[]{:S(2)}, u32[]{:S(2)}) collective-permute-start(bf16[384,512]{0,1:T(8,128)(2,1)} %collective-permute-done.14), channel_id=1, source_target_pairs={{4,0},{5,1},{6,2},{7,3},{20,16},{21,17},{22,18},{23,19}} | collective-permute-start | bytes 1179656 | tf_op jit(solution)/shard_map/ppermute | solution.py:22
  205.9 14.9 %collective-permute-start.13 = (bf16[384,512]{0,1:T(8,128)(2,1)}, bf16[384,512]{0,1:T(8,128)(2,1)S(1)}, u32[]{:S(2)}, u32[]{:S(2)}) collective-permute-start(bf16[384,512]{0,1:T(8,128)(2,1)} %collective-permute-done.12), channel_id=1, source_target_pairs={{8,12},{9,13},{10,14},{11,15},{24,28},{25,29},{26,30},{27,31}} | collective-permute-start | bytes 1179656 | tf_op jit(solution)/shard_map/ppermute | solution.py:23
  211.9 22.7 %collective-permute-start.8 = (bf16[384,512]{0,1:T(8,128)(2,1)}, bf16[384,512]{0,1:T(8,128)(2,1)}, u32[]{:S(2)}, u32[]{:S(2)}) collective-permute-start(bf16[384,512]{0,1:T(8,128)(2,1)} %collective-permute-done.7), channel_id=1, source_target_pairs={{4,0},{5,1},{6,2},{7,3},{20,16},{21,17},{22,18},{23,19}} | collective-permute-start | bytes 1179656 | tf_op jit(solution)/shard_map/ppermute | solution.py:22
  213.2 27.9 %collective-permute-start.6 = (bf16[384,512]{0,1:T(8,128)(2,1)}, bf16[384,512]{0,1:T(8,128)(2,1)}, u32[]{:S(2)}, u32[]{:S(2)}) collective-permute-start(bf16[384,512]{0,1:T(8,128)(2,1)} %collective-permute-done.5), channel_id=1, source_target_pairs={{8,12},{9,13},{10,14},{11,15},{24,28},{25,29},{26,30},{27,31}} | collective-permute-start | bytes 1179656 | tf_op jit(solution)/shard_map/ppermute | solution.py:23
  (21 other events, 131.6 us)
Sparse Core Ops, SparseCore 0:
  9.1 48.6 all-gather.4
  59.3 44.6 all-gather.8
  105.6 26.6 all-gather.6
  133.7 33.6 all-gather.10

commit v20 on v8

--- a/solution.py
+++ b/solution.py
@@ -72,7 +72,9 @@
     value = jnp.concatenate(project(w_value), axis=1)
     queries = project(w_query, key)
     if lax.axis_size("seq") == SPAN:
-        seen = jnp.stack([line_gather(key), line_gather(value)])
+        values_seen = lax.all_gather(value, "seq", axis=0, tiled=True)
+        values_seen = jnp.roll(values_seen, -lax.axis_index("seq") * value.shape[0], axis=0)
+        seen = jnp.stack([line_gather(key), values_seen])
     else:
         packed = jnp.stack([key, value])
         blocks_seen = [packed]

time: 227 us -> 241 us (1.062)
  waiting for transfers between devices: 130 us -> 155 us
  starting transfers between devices: 30.9 us -> 15.9 us
  local copies, waits for them, and re-layouts: 7.56 us -> 12.1 us
  matrix products: 15.7 us -> 19.3 us
    all_gather x3, waiting for transfers between devices: 60.7 us -> 102 us  [full_columns(): own = lax.all_gather(own, 'seq', axis=0, tiled=True)]
    ppermute x6 -> x3, waiting for transfers between devices: 28.1 us -> 7.64 us  [line_gather(): lax.ppermute(from_right[-1], 'seq', [(j, j - 1) for j in range(1, n - k +...]
    ppermute x6 -> x3, starting transfers between devices: 15.1 us -> 4.02 us  [line_gather(): lax.ppermute(from_left[-1], 'seq', [(j, j + 1) for j in range(k - 1, n -...]
    dot_general x2, matrix products: 2.22 us -> 6.82 us  [per_device(): jnp.einsum('hqk,khd->qhd', expos.astype(jnp.bfloat16), part_values, prefe...]
    unnamed x26, local copies, waits for them, and re-layouts: 0.05 us -> 4.62 us
    ppermute x6 -> x3, starting transfers between devices: 8.09 us -> 4.03 us  [line_gather(): lax.ppermute(from_right[-1], 'seq', [(j, j - 1) for j in range(1, n - k +...]
    ppermute x6 -> x3, waiting for transfers between devices: 0.02 us -> 3.29 us  [line_gather(): lax.ppermute(from_left[-1], 'seq', [(j, j + 1) for j in range(k - 1, n -...]
    select_n x6 -> x3, other arithmetic: 4.37 us -> 1.18 us  [line_gather(): slots.append(jnp.where(here + m < n, from_right[m], from_left[n - m]))]
  transfers between devices with their start and end apart: 20 -> 15, of which waited for: 10 -> 8; matrix products, arithmetic and copies ran while one was open for 17% -> 16% of each run, Pallas kernels for 0% -> 0%
where the time goes in v20:
time: 241 us; the launch traced here: 239 us
  waiting for transfers between devices  155 us (64%)
  other arithmetic  23.8 us (10%)
  matrix products  19.3 us (8%)
  starting transfers between devices  15.9 us (7%)
  between operations  13.5 us (6%)
  local copies, waits for them, and re-layouts  12.1 us (5%)
    all_gather x3, waiting for transfers between devices, full_columns(): own = lax.all_gather(own, 'seq', axis=0, tiled=True)  102 us
    ppermute x3, waiting for transfers between devices, full_columns(): other = lax.ppermute(own[rows:], 'groups', [(0, 1), (1, 0)])  23.7 us
    ppermute x2, waiting for transfers between devices, swap_gather(): other = lax.ppermute(piece, axis, [(0, 1), (1, 0)])  17.5 us
    dot_general x6, matrix products, project(): jnp.dot(block, piece, preferred_element_type=jnp.float32)  10.6 us
    concatenate x3, other arithmetic, full_columns(): own = jnp.roll(own, -lax.axis_index('seq') * rows, axis=0)  9.31 us
    ppermute x3, waiting for transfers between devices, line_gather(): lax.ppermute(from_right[-1], 'seq', [(j, j - 1) for j in range(1, n - k +...  7.64 us
    dot_general x2, matrix products, per_device(): jnp.einsum('hqk,khd->qhd', expos.astype(jnp.bfloat16), part_values, prefe...  6.82 us
  transfers between devices with their start and end apart: 15, of which 8 were waited for; matrix products, arithmetic and copies ran while one was open for 16% of the time, Pallas kernels for 0%

profile of v20, /device:TPU:0, one launch (start us, length us, event | category | flops | bytes accessed | tf_op | source)
XLA Modules:
  0.0 239.4 jit_solution(3842386260519391743)
XLA Ops:
  6.5 2.4 %constant_dynamic-slice_fusion.1 = (bf16[1024,256]{1,0:T(8,128)(2,1)}, bf16[1024,256]{1,0:T(8,128)(2,1)}) fusion(bf16[1024,512]{1,0:T(8,128)(2,1)} %param.8, s32[]{:T(128)S(6)} %select_n.103, s32[]{:T(128)S(6)} %select_n.102), kind=kLoop, calls=%fused_computation.80 | loop fusion | bytes 2097160 | tf_op jit(solution)/shard_map/dynamic_slice | solution.py:46
  10.2 3.0 %collective-permute-start = (bf16[192,2048]{1,0:T(8,128)(2,1)S(1)}, bf16[192,2048]{1,0:T(8,128)(2,1)S(1)}, u32[]{:S(2)}, u32[]{:S(2)}) collective-permute-start(bf16[192,2048]{1,0:T(8,128)(2,1)S(1)} %copy-done.9), channel_id=1, source_target_pairs={{0,2},{2,0},{1,3},{3,1},{4,6},{6,4},{5,7},{7,5},{8,10},{10,8},{9,1... | collective-permute-start | bytes 2359304 | tf_op jit(solution)/shard_map/ppermute | solution.py:34
  13.2 17.5 %collective-permute-done = bf16[192,2048]{1,0:T(8,128)(2,1)S(1)} collective-permute-done((bf16[192,2048]{1,0:T(8,128)(2,1)S(1)}, bf16[192,2048]{1,0:T(8,128)(2,1)S(1)}, u32[]{:S(2)}, u32[]{:S(2)}) %collective-permute-start) | collective-permute-done | bytes 786464 | tf_op jit(solution)/shard_map/ppermute | solution.py:34
  32.3 25.5 %all-gather.11.cloned.1.call-done = bf16[4096,256]{1,0:T(8,128)(2,1)} async-done(((bf16[1024,256]{1,0:T(8,128)(2,1)}), bf16[4096,256]{1,0:T(8,128)(2,1)}) %all-gather.11.cloned.1.call-update) | async-done | bytes 2097168 | tf_op jit(solution)/shard_map/all_gather | solution.py:47
  57.8 3.0 %fusion.15 = bf16[4096,256]{1,0:T(8,128)(2,1)S(1)} fusion(s32[]{:T(128)S(6)} %select_n.101, bf16[4096,256]{1,0:T(8,128)(2,1)} %all-gather.11.cloned.1.call-done), kind=kLoop, calls=%fused_computation.29 | loop fusion | flops 4194304 | bytes 4194308 | tf_op jit(solution)/shard_map/jit(_roll_dynamic)/concatenate | solution.py:48
  63.6 2.3 broadcast_select_fusion
  66.0 4.0 %fusion.6 = bf16[384,4096]{1,0:T(8,128)(2,1)} fusion(s32[]{:T(128)S(6)} %select_n.101, bf16[384,2048]{1,0:T(8,128)(2,1)S(1)} %get-tuple-element.9, bf16[384,2048]{1,0:T(8,128)(2,1)S(1)} %get-tuple-element.8), kind=kLoop, calls=%fused_computation.20 | loop fusion | flops 12582912 | bytes 6291460 | tf_op jit(solution)/shard_map/jit(_roll_dynamic)/concatenate | solution.py:63
  70.0 34.0 %all-gather.5.cloned.1.call-done = bf16[4096,256]{1,0:T(8,128)(2,1)} async-done(((bf16[1024,256]{1,0:T(8,128)(2,1)}), bf16[4096,256]{1,0:T(8,128)(2,1)}) %all-gather.5.cloned.1.call-update) | async-done | bytes 2097168 | tf_op jit(solution)/shard_map/all_gather | solution.py:47
  104.0 3.2 %fusion.17 = bf16[4096,256]{1,0:T(8,128)(2,1)S(1)} fusion(s32[]{:T(128)S(6)} %select_n.101, bf16[4096,256]{1,0:T(8,128)(2,1)} %all-gather.5.cloned.1.call-done), kind=kLoop, calls=%fused_computation.31 | loop fusion | flops 4194304 | bytes 4194308 | tf_op jit(solution)/shard_map/jit(_roll_dynamic)/concatenate | solution.py:48
  108.4 1.7 collective-permute-start.2
  111.5 2.8 %fusion.40 = bf16[384,256]{0,1:T(8,128)(2,1)S(1)} fusion(bf16[384,4096]{1,0:T(8,128)(2,1)S(1)} %copy-done.4, bf16[3072,256]{1,0:T(8,128)(2,1)} %collective-permute-done.3, bf16[1024,256]{1,0:T(8,128)(2,1)S(1)} %copy-done.12), kind=kOutput, calls=%fused_computation.52 | convolution fusion | flops 809598976 | bytes 5439488 | tf_op jit(solution)/shard_map/dot_general | solution.py:67
  115.6 43.0 %all-gather.9.cloned.1.call-done = bf16[4096,256]{1,0:T(8,128)(2,1)} async-done(((bf16[1024,256]{1,0:T(8,128)(2,1)}), bf16[4096,256]{1,0:T(8,128)(2,1)}) %all-gather.9.cloned.1.call-update) | async-done | bytes 2097168 | tf_op jit(solution)/shard_map/all_gather | solution.py:47
  158.6 3.2 %fusion.16 = bf16[4096,256]{1,0:T(8,128)(2,1)S(1)} fusion(s32[]{:T(128)S(6)} %select_n.101, bf16[4096,256]{1,0:T(8,128)(2,1)} %all-gather.9.cloned.1.call-done), kind=kLoop, calls=%fused_computation.30 | loop fusion | flops 4194304 | bytes 4194308 | tf_op jit(solution)/shard_map/jit(_roll_dynamic)/concatenate | solution.py:48
  161.7 2.7 %collective-permute-start.5 = (bf16[384,512]{0,1:T(8,128)(2,1)S(1)}, bf16[384,512]{0,1:T(8,128)(2,1)}, u32[]{:S(2)}, u32[]{:S(2)}) collective-permute-start(bf16[384,512]{0,1:T(8,128)(2,1)S(1)} %pad_maximum_fusion.3), channel_id=1, source_target_pairs={{0,4},{4,8},{8,12},{1,5},{5,9},{9,13},{2,6},{6,10},{10,14},{3,7},{... | collective-permute-start | bytes 1179656 | tf_op jit(solution)/shard_map/ppermute | solution.py:23
  168.5 3.3 %collective-permute-done.5 = bf16[384,512]{0,1:T(8,128)(2,1)} collective-permute-done((bf16[384,512]{0,1:T(8,128)(2,1)S(1)}, bf16[384,512]{0,1:T(8,128)(2,1)}, u32[]{:S(2)}, u32[]{:S(2)}) %collective-permute-start.5) | collective-permute-done | bytes 393248 | tf_op jit(solution)/shard_map/ppermute | solution.py:23
  172.5 4.3 %collective-permute-done.8 = bf16[384,512]{0,1:T(8,128)(2,1)} collective-permute-done((bf16[384,512]{0,1:T(8,128)(2,1)S(1)}, bf16[384,512]{0,1:T(8,128)(2,1)}, u32[]{:S(2)}, u32[]{:S(2)}) %collective-permute-start.8) | collective-permute-done | bytes 393248 | tf_op jit(solution)/shard_map/ppermute | solution.py:22
  178.1 2.7 %fusion.43 = bf16[384,256]{0,1:T(8,128)(2,1)S(1)} fusion(bf16[384,4096]{1,0:T(8,128)(2,1)S(1)} %copy-done.5, bf16[3072,256]{1,0:T(8,128)(2,1)} %collective-permute-done.2, bf16[1024,256]{1,0:T(8,128)(2,1)S(1)} %copy-done.11), kind=kOutput, calls=%fused_computation.53 | convolution fusion | flops 809598976 | bytes 5439488 | tf_op jit(solution)/shard_map/dot_general | solution.py:67
  184.9 3.4 %collective-permute-done.9 = bf16[384,512]{0,1:T(8,128)(2,1)S(1)} collective-permute-done((bf16[384,512]{0,1:T(8,128)(2,1)}, bf16[384,512]{0,1:T(8,128)(2,1)S(1)}, u32[]{:S(2)}, u32[]{:S(2)}) %collective-permute-start.9) | collective-permute-done | bytes 393248 | tf_op jit(solution)/shard_map/ppermute | solution.py:22
  189.5 2.4 %copy-done = f32[2,384,1536]{2,1,0:T(8,128)} copy-done((f32[2,384,1536]{2,1,0:T(8,128)}, f32[2,384,1536]{2,1,0:T(8,128)S(1)}, u32[]{:S(2)}) %copy-start) | copy-done | bytes 4718616
  192.8 23.7 %collective-permute-done.10 = bf16[3072,256]{1,0:T(8,128)(2,1)S(1)} collective-permute-done((bf16[3072,256]{1,0:T(8,128)(2,1)S(1)}, bf16[3072,256]{1,0:T(8,128)(2,1)S(1)}, u32[]{:S(2)}, u32[]{:S(2)}) %collective-permute-start.10) | collective-permute-done | bytes 1572896 | tf_op jit(solution)/shard_map/ppermute | solution.py:51
  218.7 2.2 copy-done.1
  221.8 2.8 %fusion.30 = bf16[1536,512]{0,1:T(8,128)(2,1)S(1)} fusion(s32[]{:T(128)S(6)} %select_n.105, bf16[1536,512]{0,1:T(8,128)(2,1)} %all-gather.7.cloned.1.call-done), kind=kLoop, calls=%fused_computation.44 | loop fusion | flops 3145728 | bytes 3145732 | tf_op jit(solution)/shard_map/jit(_roll_dynamic)/concatenate | solution.py:76
  224.7 3.4 %fusion.55 = bf16[384,2,128]{0,2,1:T(8,128)(2,1)S(1)} fusion(bf16[1536,4,128]{0,2,1:T(8,128)(2,1)S(1)} %bitcast.35, f32[2,384,1536]{2,1,0:T(8,128)} %copy-done, f32[2,384]{1,0:T(2,128)S(1)} %get-tuple-element.18, f32[384,2]{0,1:T(2,128)S(1)} %bitcast.41), kind=kOutput, calls=%fused_computation.60 | convolution fusion | flops 305725440 | bytes 6494208 | tf_op jit(solution)/shard_map/hqk,khd->qhd/dot_general | solution.py:101
  228.2 3.4 %fusion.49 = bf16[384,2,128]{0,2,1:T(8,128)(2,1)S(1)} fusion(bf16[1536,4,128]{0,2,1:T(8,128)(2,1)S(1)} %bitcast.36, f32[2,384,1536]{2,1,0:T(8,128)} %copy-done.1, f32[2,384]{1,0:T(2,128)S(1)} %get-tuple-element.20, f32[384,2]{0,1:T(2,128)S(1)} %bitcast.42), kind=kOutput, calls=%fused_computation.58 | convolution fusion | flops 305725440 | bytes 6494208 | tf_op jit(solution)/shard_map/hqk,khd->qhd/dot_general | solution.py:101
  (71 shorter events, 26.0 us)
Async XLA Ops:
  6.5 3.6 %copy-start.9 = (bf16[192,2048]{1,0:T(8,128)(2,1)S(1)}, bf16[192,2048]{1,0:T(8,128)(2,1)}, u32[]{:S(2)}) copy-start(bf16[192,2048]{1,0:T(8,128)(2,1)} %param.6) | copy-start | bytes 2359300
  6.5 51.2 %all-gather.11.cloned.1.call-start = ((), (), s32[]{:S(2)}) async-start(), calls=%async_computation.3 | async-start | bytes 2621440 | tf_op jit(solution)/shard_map/all_gather | solution.py:47
  9.0 95.0 %all-gather.5.cloned.1.call-start = ((), (), s32[]{:S(2)}) async-start(), calls=%async_computation | async-start | bytes 2621440 | tf_op jit(solution)/shard_map/all_gather | solution.py:47
  10.1 148.5 %all-gather.9.cloned.1.call-start = ((), (), s32[]{:S(2)}) async-start(), calls=%async_computation.2 | async-start | bytes 2621440 | tf_op jit(solution)/shard_map/all_gather | solution.py:47
  10.2 20.5 %collective-permute-start = (bf16[192,2048]{1,0:T(8,128)(2,1)S(1)}, bf16[192,2048]{1,0:T(8,128)(2,1)S(1)}, u32[]{:S(2)}, u32[]{:S(2)}) collective-permute-start(bf16[192,2048]{1,0:T(8,128)(2,1)S(1)} %copy-done.9), channel_id=1, source_target_pairs={{0,2},{2,0},{1,3},{3,1},{4,6},{6,4},{5,7},{7,5},{8,10},{10,8},{9,1... | collective-permute-start | bytes 2359304 | tf_op jit(solution)/shard_map/ppermute | solution.py:34
  13.2 17.9 %copy-start.8 = (bf16[1024,512]{1,0:T(8,128)(2,1)S(1)}, bf16[1024,512]{1,0:T(8,128)(2,1)}, u32[]{:S(2)}) copy-start(bf16[1024,512]{1,0:T(8,128)(2,1)} %param.7) | copy-start | bytes 3145732
  31.0 32.6 %collective-permute-start.1 = (bf16[384,2048]{1,0:T(8,128)(2,1)S(1)}, bf16[384,2048]{1,0:T(8,128)(2,1)}, u32[]{:S(2)}, u32[]{:S(2)}) collective-permute-start(bf16[384,2048]{1,0:T(8,128)(2,1)S(1)} %pad_maximum_fusion), channel_id=1, source_target_pairs={{0,1},{1,0},{2,3},{3,2},{4,5},{5,4},{6,7},{7,6},{8,9},{9,8},{10,11... | collective-permute-start | bytes 4718600 | tf_op jit(solution)/shard_map/ppermute | solution.py:34
  32.2 189.6 %all-gather.7.cloned.1.call-start = ((), (), s32[]{:S(2)}) async-start(), calls=%async_computation.1 | async-start | bytes 1966080 | tf_op jit(solution)/shard_map/all_gather | solution.py:75
  60.8 5.2 %copy-start.2 = (bf16[4096,256]{1,0:T(8,128)(2,1)}, bf16[4096,256]{1,0:T(8,128)(2,1)S(1)}, u32[]{:S(2)}) copy-start(bf16[4096,256]{1,0:T(8,128)(2,1)S(1)} %fusion.15) | copy-start | bytes 6291460
  62.1 49.3 %collective-permute-start.3 = (bf16[3072,256]{1,0:T(8,128)(2,1)}, bf16[3072,256]{1,0:T(8,128)(2,1)}, u32[]{:S(2)}, u32[]{:S(2)}) collective-permute-start(bf16[3072,256]{1,0:T(8,128)(2,1)} %slice.29), channel_id=1, source_target_pairs={{0,16},{16,0},{1,17},{17,1},{2,18},{18,2},{3,19},{19,3},{4,20},{20... | collective-permute-start | bytes 4718600 | tf_op jit(solution)/shard_map/ppermute | solution.py:51
  104.0 6.1 %copy-start.3 = (bf16[4096,256]{1,0:T(8,128)(2,1)S(1)}, bf16[4096,256]{1,0:T(8,128)(2,1)}, u32[]{:S(2)}) copy-start(bf16[4096,256]{1,0:T(8,128)(2,1)} %copy-done.2) | copy-start | bytes 6291460
  104.0 6.1 %copy-start.4 = (bf16[384,4096]{1,0:T(8,128)(2,1)S(1)}, bf16[384,4096]{1,0:T(8,128)(2,1)}, u32[]{:S(2)}) copy-start(bf16[384,4096]{1,0:T(8,128)(2,1)} %fusion.6) | copy-start | bytes 9437188
  108.4 69.6 %collective-permute-start.2 = (bf16[3072,256]{1,0:T(8,128)(2,1)}, bf16[3072,256]{1,0:T(8,128)(2,1)}, u32[]{:S(2)}, u32[]{:S(2)}) collective-permute-start(bf16[3072,256]{1,0:T(8,128)(2,1)} %slice.28), channel_id=1, source_target_pairs={{0,16},{16,0},{1,17},{17,1},{2,18},{18,2},{3,19},{19,3},{4,20},{20... | collective-permute-start | bytes 4718600 | tf_op jit(solution)/shard_map/ppermute | solution.py:51
  114.3 50.1 %collective-permute-start.4 = (bf16[384,512]{0,1:T(8,128)(2,1)S(1)}, bf16[384,512]{0,1:T(8,128)(2,1)S(1)}, u32[]{:S(2)}, u32[]{:S(2)}) collective-permute-start(bf16[384,512]{0,1:T(8,128)(2,1)S(1)} %pad_maximum_fusion.3), channel_id=1, source_target_pairs={{4,0},{8,4},{12,8},{5,1},{9,5},{13,9},{6,2},{10,6},{14,10},{7,3},{... | collective-permute-start | bytes 1179656 | tf_op jit(solution)/shard_map/ppermute | solution.py:22
  158.6 7.3 %copy-start.5 = (bf16[384,4096]{1,0:T(8,128)(2,1)S(1)}, bf16[384,4096]{1,0:T(8,128)(2,1)}, u32[]{:S(2)}) copy-start(bf16[384,4096]{1,0:T(8,128)(2,1)} %fusion.6) | copy-start | bytes 9437188
  161.7 10.0 %collective-permute-start.5 = (bf16[384,512]{0,1:T(8,128)(2,1)S(1)}, bf16[384,512]{0,1:T(8,128)(2,1)}, u32[]{:S(2)}, u32[]{:S(2)}) collective-permute-start(bf16[384,512]{0,1:T(8,128)(2,1)S(1)} %pad_maximum_fusion.3), channel_id=1, source_target_pairs={{0,4},{4,8},{8,12},{1,5},{5,9},{9,13},{2,6},{6,10},{10,14},{3,7},{... | collective-permute-start | bytes 1179656 | tf_op jit(solution)/shard_map/ppermute | solution.py:23
  164.4 12.3 %collective-permute-start.8 = (bf16[384,512]{0,1:T(8,128)(2,1)S(1)}, bf16[384,512]{0,1:T(8,128)(2,1)}, u32[]{:S(2)}, u32[]{:S(2)}) collective-permute-start(bf16[384,512]{0,1:T(8,128)(2,1)S(1)} %collective-permute-done.4), channel_id=1, source_target_pairs={{4,0},{8,4},{5,1},{9,5},{6,2},{10,6},{7,3},{11,7},{20,16},{24,20},... | collective-permute-start | bytes 1179656 | tf_op jit(solution)/shard_map/ppermute | solution.py:22
  167.2 10.9 %copy-start.11 = (bf16[1024,256]{1,0:T(8,128)(2,1)S(1)}, bf16[1024,256]{1,0:T(8,128)(2,1)}, u32[]{:S(2)}) copy-start(bf16[1024,256]{1,0:T(8,128)(2,1)} %get-tuple-element.16) | copy-start | bytes 1572868
  171.8 11.4 %collective-permute-start.6 = (bf16[384,512]{0,1:T(8,128)(2,1)}, bf16[384,512]{0,1:T(8,128)(2,1)S(1)}, u32[]{:S(2)}, u32[]{:S(2)}) collective-permute-start(bf16[384,512]{0,1:T(8,128)(2,1)} %collective-permute-done.5), channel_id=1, source_target_pairs={{4,8},{8,12},{5,9},{9,13},{6,10},{10,14},{7,11},{11,15},{20,24},{2... | collective-permute-start | bytes 1179656 | tf_op jit(solution)/shard_map/ppermute | solution.py:23
  176.8 11.5 %collective-permute-start.9 = (bf16[384,512]{0,1:T(8,128)(2,1)}, bf16[384,512]{0,1:T(8,128)(2,1)S(1)}, u32[]{:S(2)}, u32[]{:S(2)}) collective-permute-start(bf16[384,512]{0,1:T(8,128)(2,1)} %collective-permute-done.8), channel_id=1, source_target_pairs={{4,0},{5,1},{6,2},{7,3},{20,16},{21,17},{22,18},{23,19}} | collective-permute-start | bytes 1179656 | tf_op jit(solution)/shard_map/ppermute | solution.py:22
  181.7 34.8 %collective-permute-start.10 = (bf16[3072,256]{1,0:T(8,128)(2,1)S(1)}, bf16[3072,256]{1,0:T(8,128)(2,1)S(1)}, u32[]{:S(2)}, u32[]{:S(2)}) collective-permute-start(bf16[3072,256]{1,0:T(8,128)(2,1)S(1)} %slice.26), channel_id=1, source_target_pairs={{0,16},{16,0},{1,17},{17,1},{2,18},{18,2},{3,19},{19,3},{4,20},{20... | collective-permute-start | bytes 4718600 | tf_op jit(solution)/shard_map/ppermute | solution.py:51
  183.2 5.2 %collective-permute-start.7 = (bf16[384,512]{0,1:T(8,128)(2,1)S(1)}, bf16[384,512]{0,1:T(8,128)(2,1)S(1)}, u32[]{:S(2)}, u32[]{:S(2)}) collective-permute-start(bf16[384,512]{0,1:T(8,128)(2,1)S(1)} %collective-permute-done.6), channel_id=1, source_target_pairs={{8,12},{9,13},{10,14},{11,15},{24,28},{25,29},{26,30},{27,31}} | collective-permute-start | bytes 1179656 | tf_op jit(solution)/shard_map/ppermute | solution.py:23
  189.5 27.0 %copy-start.6 = (bf16[384,4096]{1,0:T(8,128)(2,1)S(1)}, bf16[384,4096]{1,0:T(8,128)(2,1)}, u32[]{:S(2)}) copy-start(bf16[384,4096]{1,0:T(8,128)(2,1)} %fusion.6) | copy-start | bytes 9437188
  189.5 27.0 %copy-start.10 = (bf16[1024,256]{1,0:T(8,128)(2,1)S(1)}, bf16[1024,256]{1,0:T(8,128)(2,1)}, u32[]{:S(2)}) copy-start(bf16[1024,256]{1,0:T(8,128)(2,1)} %get-tuple-element.12) | copy-start | bytes 1572868
  (4 other events, 10.1 us)
Sparse Core Ops, SparseCore 0:
  9.1 48.6 all-gather.10
  59.3 44.6 all-gather.4
  105.6 52.9 all-gather.8
  181.8 36.1 all-gather.6

commit v21 on v8

--- a/solution.py
+++ b/solution.py
@@ -52,6 +52,17 @@
     return [own, jnp.concatenate([kept, other], axis=0)]
 
 
+def query_columns(weight, after):
+    rows, quarter = weight.shape[0], weight.shape[1] // 4
+    group = lax.axis_index("groups")
+    ordered = jnp.roll(weight, -group * 2 * quarter, axis=1)
+    own = lax.all_gather(ordered[:, : 3 * quarter], "seq", axis=0, tiled=True)
+    own = jnp.roll(own, -lax.axis_index("seq") * rows, axis=0)
+    own = lax.optimization_barrier((own, after))[0]
+    other = lax.ppermute(own[rows:, quarter : 2 * quarter], "groups", [(0, 1), (1, 0)])
+    return [own, jnp.concatenate([ordered[:, 3 * quarter :], other], axis=0)]
+
+
 def per_device(acts, w_query, w_key, w_value):
     block = swap_gather(acts, "row", 0)
     block = swap_gather(block, "col", 1)
@@ -70,7 +81,13 @@
 
     key = jnp.concatenate(project(w_key), axis=1)
     value = jnp.concatenate(project(w_value), axis=1)
-    queries = project(w_query, key)
+    if shared and width % (4 * HD) == 0:
+        queries = [
+            jnp.dot(block, piece, preferred_element_type=jnp.float32).astype(jnp.bfloat16)
+            for piece in query_columns(w_query, key)
+        ]
+    else:
+        queries = project(w_query, key)
     if lax.axis_size("seq") == SPAN:
         seen = jnp.stack([line_gather(key), line_gather(value)])
     else:

time: 227 us -> 246 us (1.084); the launches traced: 223 us -> 246 us
  waiting for transfers between devices: 130 us -> 148 us
  starting transfers between devices: 30.9 us -> 24.7 us
  other arithmetic: 25.4 us -> 31.2 us
    all_gather x0 -> x1, waiting for transfers between devices: none -> 35.2 us  [query_columns(): own = lax.all_gather(ordered[:, :3 * quarter], 'seq', axis=0, tiled=True)]
    ppermute x6, waiting for transfers between devices: 28.1 us -> 16.8 us  [line_gather(): lax.ppermute(from_right[-1], 'seq', [(j, j - 1) for j in range(1, n - k +...]
    ppermute x6, starting transfers between devices: 15.1 us -> 9.27 us  [line_gather(): lax.ppermute(from_left[-1], 'seq', [(j, j + 1) for j in range(k - 1, n -...]
    concatenate x0 -> x2, other arithmetic: none -> 5.84 us  [the longest x1 4.23 us: query_columns(): own = jnp.roll(own, -lax.axis_index('seq') * rows, axis=0)]
    dot_general x6 -> x4, matrix products: 11.7 us -> 6.64 us  [project(): jnp.dot(block, piece, preferred_element_type=jnp.float32)]
    dot_general x2, matrix products: 1.82 us -> 6.63 us  [per_device(): jnp.einsum('qhd,khd->hqk', query, part_keys, preferred_element_type=jnp.f...]
    all_gather x3 -> x2, waiting for transfers between devices: 60.7 us -> 57 us  [full_columns(): own = lax.all_gather(own, 'seq', axis=0, tiled=True)]
    unnamed x26 -> x32, local copies, waits for them, and re-layouts: 0.05 us -> 3.47 us
  transfers between devices with their start and end apart: 20 -> 20, of which waited for: 10 -> 9; matrix products, arithmetic and copies ran while one was open for 17% -> 18% of each run, Pallas kernels for 0% -> 0%
where the time goes in v21:
time: 246 us
  waiting for transfers between devices  148 us (60%)
  other arithmetic  31.2 us (13%)
  starting transfers between devices  24.7 us (10%)
  matrix products  18 us (7%)
  between operations  13.6 us (6%)
  local copies, waits for them, and re-layouts  9.78 us (4%)
    all_gather x2, waiting for transfers between devices, full_columns(): own = lax.all_gather(own, 'seq', axis=0, tiled=True)  57 us
    all_gather x1, waiting for transfers between devices, query_columns(): own = lax.all_gather(ordered[:, :3 * quarter], 'seq', axis=0, tiled=True)  35.2 us
    ppermute x2, waiting for transfers between devices, full_columns(): other = lax.ppermute(own[rows:], 'groups', [(0, 1), (1, 0)])  20.7 us
    ppermute x2, waiting for transfers between devices, swap_gather(): other = lax.ppermute(piece, axis, [(0, 1), (1, 0)])  18.5 us
    ppermute x6, waiting for transfers between devices, line_gather(): lax.ppermute(from_right[-1], 'seq', [(j, j - 1) for j in range(1, n - k +...  16.8 us
    ppermute x6, starting transfers between devices, line_gather(): lax.ppermute(from_left[-1], 'seq', [(j, j + 1) for j in range(k - 1, n -...  9.27 us
    ppermute x6, starting transfers between devices, line_gather(): lax.ppermute(from_right[-1], 'seq', [(j, j - 1) for j in range(1, n - k +...  7.71 us
    dot_general x4, matrix products, project(): jnp.dot(block, piece, preferred_element_type=jnp.float32)  6.64 us
  transfers between devices with their start and end apart: 20, of which 9 were waited for; matrix products, arithmetic and copies ran while one was open for 18% of the time, Pallas kernels for 0%

profile of v21, /device:TPU:0, one launch (start us, length us, event | category | flops | bytes accessed | tf_op | source)
XLA Modules:
  0.0 245.5 jit_solution(17243227021728378633)
XLA Ops:
  6.5 2.4 constant_dynamic-slice_fusion
  10.2 3.0 %collective-permute-start = (bf16[192,2048]{1,0:T(8,128)(2,1)S(1)}, bf16[192,2048]{1,0:T(8,128)(2,1)S(1)}, u32[]{:S(2)}, u32[]{:S(2)}) collective-permute-start(bf16[192,2048]{1,0:T(8,128)(2,1)S(1)} %copy-done.12), channel_id=1, source_target_pairs={{0,2},{2,0},{1,3},{3,1},{4,6},{6,4},{5,7},{7,5},{8,10},{10,8},{9,1... | collective-permute-start | bytes 2359304 | tf_op jit(solution)/shard_map/ppermute | solution.py:34
  13.2 17.5 %collective-permute-done = bf16[192,2048]{1,0:T(8,128)(2,1)S(1)} collective-permute-done((bf16[192,2048]{1,0:T(8,128)(2,1)S(1)}, bf16[192,2048]{1,0:T(8,128)(2,1)S(1)}, u32[]{:S(2)}, u32[]{:S(2)}) %collective-permute-start) | collective-permute-done | bytes 786464 | tf_op jit(solution)/shard_map/ppermute | solution.py:34
  32.2 1.6 fusion.54
  35.9 4.0 %broadcast_select_fusion = (bf16[384,2048]{1,0:T(8,128)(2,1)}, bf16[384,2048]{1,0:T(8,128)(2,1)}) fusion(bf16[384,2048]{1,0:T(8,128)(2,1)} %collective-permute-done.1, pred[]{:T(512)S(6)} %eq.16, bf16[192,2048]{1,0:T(8,128)(2,1)S(1)} %get-tuple-element.11, bf16[192,2048]{1,0:T(8,128)(2,1)S(1)} %get-tuple-element.10), kind=kLoop, calls=%fused_computation.40 | loop fusion | flops 4718592 | bytes 6291457 | tf_op jit(solution)/shard_map/jit(_where)/select_n | solution.py:36
  39.9 17.8 %all-gather.8.cloned.1.call-done = bf16[4096,256]{1,0:T(8,128)(2,1)} async-done(((bf16[1024,256]{1,0:T(8,128)(2,1)}), bf16[4096,256]{1,0:T(8,128)(2,1)}) %all-gather.8.cloned.1.call-update) | async-done | bytes 2097168 | tf_op jit(solution)/shard_map/all_gather | solution.py:47
  57.8 3.0 %fusion.10 = bf16[4096,256]{1,0:T(8,128)(2,1)S(1)} fusion(s32[]{:T(128)S(6)} %select_n.117, bf16[4096,256]{1,0:T(8,128)(2,1)} %all-gather.8.cloned.1.call-done), kind=kLoop, calls=%fused_computation.23 | loop fusion | flops 4194304 | bytes 4194308 | tf_op jit(solution)/shard_map/jit(_roll_dynamic)/concatenate | solution.py:48
  64.9 39.2 %all-gather.4.cloned.1.call-done = bf16[4096,256]{1,0:T(8,128)(2,1)} async-done(((bf16[1024,256]{1,0:T(8,128)(2,1)}), bf16[4096,256]{1,0:T(8,128)(2,1)}) %all-gather.4.cloned.1.call-update) | async-done | bytes 2097168 | tf_op jit(solution)/shard_map/all_gather | solution.py:47
  104.0 3.0 %fusion.11 = bf16[4096,256]{1,0:T(8,128)(2,1)S(1)} fusion(s32[]{:T(128)S(6)} %select_n.117, bf16[4096,256]{1,0:T(8,128)(2,1)} %all-gather.4.cloned.1.call-done), kind=kLoop, calls=%fused_computation.24 | loop fusion | flops 4194304 | bytes 4194308 | tf_op jit(solution)/shard_map/jit(_roll_dynamic)/concatenate | solution.py:48
  107.1 1.5 collective-permute-start.2
  108.7 3.7 %fusion.9 = bf16[384,4096]{1,0:T(8,128)(2,1)S(1)} fusion(s32[]{:T(128)S(6)} %select_n.117, bf16[384,2048]{1,0:T(8,128)(2,1)} %get-tuple-element.9, bf16[384,2048]{1,0:T(8,128)(2,1)} %get-tuple-element.8), kind=kLoop, calls=%fused_computation.20 | loop fusion | flops 12582912 | bytes 6291460 | tf_op jit(solution)/shard_map/jit(_roll_dynamic)/concatenate | solution.py:74
  115.1 2.8 %fusion.36 = bf16[384,256]{0,1:T(8,128)(2,1)S(1)} fusion(bf16[384,4096]{1,0:T(8,128)(2,1)S(1)} %fusion.9, bf16[3072,256]{1,0:T(8,128)(2,1)} %collective-permute-done.9, bf16[1024,256]{1,0:T(8,128)(2,1)S(1)} %copy-done.14), kind=kOutput, calls=%fused_computation.50 | convolution fusion | flops 809598976 | bytes 5439488 | tf_op jit(solution)/shard_map/dot_general | solution.py:78
  118.7 2.6 %collective-permute-start.11 = (bf16[384,512]{0,1:T(8,128)(2,1)}, bf16[384,512]{0,1:T(8,128)(2,1)}, u32[]{:S(2)}, u32[]{:S(2)}) collective-permute-start(bf16[384,512]{0,1:T(8,128)(2,1)} %pad_maximum_fusion.4), channel_id=1, source_target_pairs={{0,4},{4,8},{8,12},{1,5},{5,9},{9,13},{2,6},{6,10},{10,14},{3,7},{... | collective-permute-start | bytes 1179656 | tf_op jit(solution)/shard_map/ppermute | solution.py:23
  122.6 20.7 %collective-permute-done.2 = bf16[3072,256]{1,0:T(8,128)(2,1)S(1)} collective-permute-done((bf16[3072,256]{1,0:T(8,128)(2,1)S(1)}, bf16[3072,256]{1,0:T(8,128)(2,1)S(1)}, u32[]{:S(2)}, u32[]{:S(2)}) %collective-permute-start.2) | collective-permute-done | bytes 1572896 | tf_op jit(solution)/shard_map/ppermute | solution.py:51
  145.4 2.4 collective-permute-start.4
  149.1 35.2 %all-gather.6.cloned.1.call-done = bf16[4096,384]{1,0:T(8,128)(2,1)} async-done(((bf16[1024,384]{1,0:T(8,128)(2,1)}), bf16[4096,384]{1,0:T(8,128)(2,1)}) %all-gather.6.cloned.1.call-update) | async-done | bytes 3145744 | tf_op jit(solution)/shard_map/all_gather | solution.py:59
  184.3 4.2 %fusion.6 = bf16[4096,384]{1,0:T(8,128)(2,1)S(1)} fusion(s32[]{:T(128)S(6)} %select_n.117, bf16[4096,384]{1,0:T(8,128)(2,1)} %all-gather.6.cloned.1.call-done), kind=kLoop, calls=%fused_computation.17 | loop fusion | flops 6291456 | bytes 6291460 | tf_op jit(solution)/shard_map/jit(_roll_dynamic)/concatenate | solution.py:60
  193.2 2.6 %convolution_convert_fusion = bf16[384,384]{0,1:T(8,128)(2,1)} fusion(bf16[384,4096]{1,0:T(8,128)(2,1)S(1)} %fusion.9, bf16[4096,384]{1,0:T(8,128)(2,1)S(1)} %fusion.6), kind=kOutput, calls=%fused_computation.43 | convolution fusion | flops 1208107008 | bytes 6586368 | tf_op jit(solution)/shard_map/dot_general | solution.py:86
  195.9 1.6 collective-permute-start.16
  198.2 6.2 %collective-permute-done.14 = bf16[384,512]{0,1:T(8,128)(2,1)S(1)} collective-permute-done((bf16[384,512]{0,1:T(8,128)(2,1)}, bf16[384,512]{0,1:T(8,128)(2,1)S(1)}, u32[]{:S(2)}, u32[]{:S(2)}) %collective-permute-start.14) | collective-permute-done | bytes 393248 | tf_op jit(solution)/shard_map/ppermute | solution.py:22
  207.2 5.7 %collective-permute-done.7 = bf16[384,512]{0,1:T(8,128)(2,1)} collective-permute-done((bf16[384,512]{0,1:T(8,128)(2,1)}, bf16[384,512]{0,1:T(8,128)(2,1)}, u32[]{:S(2)}, u32[]{:S(2)}) %collective-permute-start.7) | collective-permute-done | bytes 393248 | tf_op jit(solution)/shard_map/ppermute | solution.py:22
  216.4 4.9 %collective-permute-done.15 = bf16[384,512]{0,1:T(8,128)(2,1)S(1)} collective-permute-done((bf16[384,512]{0,1:T(8,128)(2,1)S(1)}, bf16[384,512]{0,1:T(8,128)(2,1)S(1)}, u32[]{:S(2)}, u32[]{:S(2)}) %collective-permute-start.15) | collective-permute-done | bytes 393248 | tf_op jit(solution)/shard_map/ppermute | solution.py:22
  223.5 4.2 %fusion.69 = (f32[384]{0:T(512)S(1)}, f32[384,1536]{1,0:T(8,128)S(1)}) fusion(bf16[1536,4,128]{0,2,1:T(8,128)(2,1)} %bitcast.42, bf16[384,4096]{1,0:T(8,128)(2,1)} %copy-done, bf16[3072,128]{1,0:T(8,128)(2,1)} %copy-done.7, bf16[1024,128]{1,0:T(8,128)(2,1)S(1)} %slice-done), kind=kOutput, calls=%fused_computation.90 | convolution fusion | flops 556973696 | bytes 6948352 | tf_op jit(solution)/shard_map/qhd,khd->hqk/dot_general | solution.py:112
  232.3 2.5 %multiply_reduce_fusion = (f32[3,384]{1,0:T(4,128)S(1)}, f32[3,384,1536]{2,1,0:T(8,128)S(1)}) fusion(bf16[384,3,128]{0,2,1:T(8,128)(2,1)S(1)} %bitcast.46, bf16[1536,4,128]{0,2,1:T(8,128)(2,1)} %bitcast.43), kind=kOutput, calls=%fused_computation.1 | convolution fusion | flops 456522624 | bytes 8557056 | tf_op jit(solution)/shard_map/qhd,khd->hqk/dot_general | solution.py:112
  (91 shorter events, 39.6 us)
Async XLA Ops:
  6.5 51.2 %all-gather.8.cloned.1.call-start = ((), (), s32[]{:S(2)}) async-start(), calls=%async_computation.2 | async-start | bytes 2621440 | tf_op jit(solution)/shard_map/all_gather | solution.py:47
  9.0 95.0 %all-gather.4.cloned.1.call-start = ((), (), s32[]{:S(2)}) async-start(), calls=%async_computation | async-start | bytes 2621440 | tf_op jit(solution)/shard_map/all_gather | solution.py:47
  10.1 174.2 %all-gather.6.cloned.1.call-start = ((), (), s32[]{:S(2)}) async-start(), calls=%async_computation.1 | async-start | bytes 3932160 | tf_op jit(solution)/shard_map/all_gather | solution.py:59
  10.2 20.5 %collective-permute-start = (bf16[192,2048]{1,0:T(8,128)(2,1)S(1)}, bf16[192,2048]{1,0:T(8,128)(2,1)S(1)}, u32[]{:S(2)}, u32[]{:S(2)}) collective-permute-start(bf16[192,2048]{1,0:T(8,128)(2,1)S(1)} %copy-done.12), channel_id=1, source_target_pairs={{0,2},{2,0},{1,3},{3,1},{4,6},{6,4},{5,7},{7,5},{8,10},{10,8},{9,1... | collective-permute-start | bytes 2359304 | tf_op jit(solution)/shard_map/ppermute | solution.py:34
  32.2 3.8 %collective-permute-start.1 = (bf16[384,2048]{1,0:T(8,128)(2,1)}, bf16[384,2048]{1,0:T(8,128)(2,1)}, u32[]{:S(2)}, u32[]{:S(2)}) collective-permute-start(bf16[384,2048]{1,0:T(8,128)(2,1)} %pad_maximum_fusion), channel_id=1, source_target_pairs={{0,1},{1,0},{2,3},{3,2},{4,5},{5,4},{6,7},{7,6},{8,9},{9,8},{10,11... | collective-permute-start | bytes 4718600 | tf_op jit(solution)/shard_map/ppermute | solution.py:34
  63.4 51.7 %collective-permute-start.9 = (bf16[3072,256]{1,0:T(8,128)(2,1)}, bf16[3072,256]{1,0:T(8,128)(2,1)}, u32[]{:S(2)}, u32[]{:S(2)}) collective-permute-start(bf16[3072,256]{1,0:T(8,128)(2,1)} %slice.38), channel_id=1, source_target_pairs={{0,16},{16,0},{1,17},{17,1},{2,18},{18,2},{3,19},{19,3},{4,20},{20... | collective-permute-start | bytes 4718600 | tf_op jit(solution)/shard_map/ppermute | solution.py:51
  107.1 36.2 %collective-permute-start.2 = (bf16[3072,256]{1,0:T(8,128)(2,1)S(1)}, bf16[3072,256]{1,0:T(8,128)(2,1)S(1)}, u32[]{:S(2)}, u32[]{:S(2)}) collective-permute-start(bf16[3072,256]{1,0:T(8,128)(2,1)S(1)} %slice.36), channel_id=1, source_target_pairs={{0,16},{16,0},{1,17},{17,1},{2,18},{18,2},{3,19},{19,3},{4,20},{20... | collective-permute-start | bytes 4718600 | tf_op jit(solution)/shard_map/ppermute | solution.py:51
  112.4 80.8 %copy-start = (bf16[384,4096]{1,0:T(8,128)(2,1)}, bf16[384,4096]{1,0:T(8,128)(2,1)S(1)}, u32[]{:S(2)}) copy-start(bf16[384,4096]{1,0:T(8,128)(2,1)S(1)} %fusion.9) | copy-start | bytes 9437188
  115.1 28.3 %copy-start.13 = (bf16[1024,256]{1,0:T(8,128)(2,1)S(1)}, bf16[1024,256]{1,0:T(8,128)(2,1)}, u32[]{:S(2)}) copy-start(bf16[1024,256]{1,0:T(8,128)(2,1)} %get-tuple-element.14) | copy-start | bytes 1572868
  117.8 26.8 %copy-start.10 = (bf16[384,256]{0,1:T(8,128)(2,1)}, bf16[384,256]{0,1:T(8,128)(2,1)S(1)}, u32[]{:S(2)}) copy-start(bf16[384,256]{0,1:T(8,128)(2,1)S(1)} %fusion.36) | copy-start | bytes 589828
  118.7 69.8 %collective-permute-start.11 = (bf16[384,512]{0,1:T(8,128)(2,1)}, bf16[384,512]{0,1:T(8,128)(2,1)}, u32[]{:S(2)}, u32[]{:S(2)}) collective-permute-start(bf16[384,512]{0,1:T(8,128)(2,1)} %pad_maximum_fusion.4), channel_id=1, source_target_pairs={{0,4},{4,8},{8,12},{1,5},{5,9},{9,13},{2,6},{6,10},{10,14},{3,7},{... | collective-permute-start | bytes 1179656 | tf_op jit(solution)/shard_map/ppermute | solution.py:23
  121.3 67.9 %collective-permute-start.10 = (bf16[384,512]{0,1:T(8,128)(2,1)}, bf16[384,512]{0,1:T(8,128)(2,1)}, u32[]{:S(2)}, u32[]{:S(2)}) collective-permute-start(bf16[384,512]{0,1:T(8,128)(2,1)} %pad_maximum_fusion.4), channel_id=1, source_target_pairs={{4,0},{8,4},{12,8},{5,1},{9,5},{13,9},{6,2},{10,6},{14,10},{7,3},{... | collective-permute-start | bytes 1179656 | tf_op jit(solution)/shard_map/ppermute | solution.py:22
  145.4 45.1 %collective-permute-start.4 = (bf16[384,512]{0,1:T(8,128)(2,1)}, bf16[384,512]{0,1:T(8,128)(2,1)}, u32[]{:S(2)}, u32[]{:S(2)}) collective-permute-start(bf16[384,512]{0,1:T(8,128)(2,1)} %pad_maximum_fusion.3), channel_id=1, source_target_pairs={{0,4},{4,8},{8,12},{1,5},{5,9},{9,13},{2,6},{6,10},{10,14},{3,7},{... | collective-permute-start | bytes 1179656 | tf_op jit(solution)/shard_map/ppermute | solution.py:23
  147.8 44.1 %collective-permute-start.3 = (bf16[384,512]{0,1:T(8,128)(2,1)}, bf16[384,512]{0,1:T(8,128)(2,1)}, u32[]{:S(2)}, u32[]{:S(2)}) collective-permute-start(bf16[384,512]{0,1:T(8,128)(2,1)} %pad_maximum_fusion.3), channel_id=1, source_target_pairs={{4,0},{8,4},{12,8},{5,1},{9,5},{13,9},{6,2},{10,6},{14,10},{7,3},{... | collective-permute-start | bytes 1179656 | tf_op jit(solution)/shard_map/ppermute | solution.py:22
  188.5 9.0 %collective-permute-start.12 = (bf16[384,512]{0,1:T(8,128)(2,1)}, bf16[384,512]{0,1:T(8,128)(2,1)S(1)}, u32[]{:S(2)}, u32[]{:S(2)}) collective-permute-start(bf16[384,512]{0,1:T(8,128)(2,1)} %collective-permute-done.11), channel_id=1, source_target_pairs={{4,8},{8,12},{5,9},{9,13},{6,10},{10,14},{7,11},{11,15},{20,24},{2... | collective-permute-start | bytes 1179656 | tf_op jit(solution)/shard_map/ppermute | solution.py:23
  189.2 15.2 %collective-permute-start.14 = (bf16[384,512]{0,1:T(8,128)(2,1)}, bf16[384,512]{0,1:T(8,128)(2,1)S(1)}, u32[]{:S(2)}, u32[]{:S(2)}) collective-permute-start(bf16[384,512]{0,1:T(8,128)(2,1)} %collective-permute-done.10), channel_id=1, source_target_pairs={{4,0},{8,4},{5,1},{9,5},{6,2},{10,6},{7,3},{11,7},{20,16},{24,20},... | collective-permute-start | bytes 1179656 | tf_op jit(solution)/shard_map/ppermute | solution.py:22
  190.5 15.2 %collective-permute-start.5 = (bf16[384,512]{0,1:T(8,128)(2,1)}, bf16[384,512]{0,1:T(8,128)(2,1)}, u32[]{:S(2)}, u32[]{:S(2)}) collective-permute-start(bf16[384,512]{0,1:T(8,128)(2,1)} %collective-permute-done.4), channel_id=1, source_target_pairs={{4,8},{8,12},{5,9},{9,13},{6,10},{10,14},{7,11},{11,15},{20,24},{2... | collective-permute-start | bytes 1179656 | tf_op jit(solution)/shard_map/ppermute | solution.py:23
  191.9 21.0 %collective-permute-start.7 = (bf16[384,512]{0,1:T(8,128)(2,1)}, bf16[384,512]{0,1:T(8,128)(2,1)}, u32[]{:S(2)}, u32[]{:S(2)}) collective-permute-start(bf16[384,512]{0,1:T(8,128)(2,1)} %collective-permute-done.3), channel_id=1, source_target_pairs={{4,0},{8,4},{5,1},{9,5},{6,2},{10,6},{7,3},{11,7},{20,16},{24,20},... | collective-permute-start | bytes 1179656 | tf_op jit(solution)/shard_map/ppermute | solution.py:22
  195.8 25.5 %copy-start.11 = (bf16[384,256]{0,1:T(8,128)(2,1)S(1)}, bf16[384,256]{0,1:T(8,128)(2,1)}, u32[]{:S(2)}) copy-start(bf16[384,256]{0,1:T(8,128)(2,1)} %copy-done.10) | copy-start | bytes 589828
  195.9 26.7 %collective-permute-start.16 = (bf16[3072,128]{1,0:T(8,128)(2,1)S(1)}, bf16[3072,128]{1,0:T(8,128)(2,1)S(1)}, u32[]{:S(2)}, u32[]{:S(2)}) collective-permute-start(bf16[3072,128]{1,0:T(8,128)(2,1)S(1)} %slice.34), channel_id=1, source_target_pairs={{0,16},{16,0},{1,17},{17,1},{2,18},{18,2},{3,19},{19,3},{4,20},{20... | collective-permute-start | bytes 2359304 | tf_op jit(solution)/shard_map/ppermute | solution.py:62
  197.5 17.8 %collective-permute-start.13 = (bf16[384,512]{0,1:T(8,128)(2,1)S(1)}, bf16[384,512]{0,1:T(8,128)(2,1)S(1)}, u32[]{:S(2)}, u32[]{:S(2)}) collective-permute-start(bf16[384,512]{0,1:T(8,128)(2,1)S(1)} %collective-permute-done.12), channel_id=1, source_target_pairs={{8,12},{9,13},{10,14},{11,15},{24,28},{25,29},{26,30},{27,31}} | collective-permute-start | bytes 1179656 | tf_op jit(solution)/shard_map/ppermute | solution.py:23
  204.4 16.9 %collective-permute-start.15 = (bf16[384,512]{0,1:T(8,128)(2,1)S(1)}, bf16[384,512]{0,1:T(8,128)(2,1)S(1)}, u32[]{:S(2)}, u32[]{:S(2)}) collective-permute-start(bf16[384,512]{0,1:T(8,128)(2,1)S(1)} %collective-permute-done.14), channel_id=1, source_target_pairs={{4,0},{5,1},{6,2},{7,3},{20,16},{21,17},{22,18},{23,19}} | collective-permute-start | bytes 1179656 | tf_op jit(solution)/shard_map/ppermute | solution.py:22
  205.7 22.5 %collective-permute-start.6 = (bf16[384,512]{0,1:T(8,128)(2,1)}, bf16[384,512]{0,1:T(8,128)(2,1)}, u32[]{:S(2)}, u32[]{:S(2)}) collective-permute-start(bf16[384,512]{0,1:T(8,128)(2,1)} %collective-permute-done.5), channel_id=1, source_target_pairs={{8,12},{9,13},{10,14},{11,15},{24,28},{25,29},{26,30},{27,31}} | collective-permute-start | bytes 1179656 | tf_op jit(solution)/shard_map/ppermute | solution.py:23
  214.0 15.3 %collective-permute-start.8 = (bf16[384,512]{0,1:T(8,128)(2,1)}, bf16[384,512]{0,1:T(8,128)(2,1)}, u32[]{:S(2)}, u32[]{:S(2)}) collective-permute-start(bf16[384,512]{0,1:T(8,128)(2,1)} %collective-permute-done.7), channel_id=1, source_target_pairs={{4,0},{5,1},{6,2},{7,3},{20,16},{21,17},{22,18},{23,19}} | collective-permute-start | bytes 1179656 | tf_op jit(solution)/shard_map/ppermute | solution.py:22
  (13 other events, 69.9 us)
Sparse Core Ops, SparseCore 0:
  9.1 48.6 all-gather.7
  59.3 44.6 all-gather.3
  105.6 78.6 all-gather.5

commit v22 on v8

--- a/solution.py
+++ b/solution.py
@@ -13,7 +13,7 @@
     return lax.ppermute(block, axis, route)
 
 
-def line_gather(piece):
+def line_gather(piece, axis=0):
     n = lax.axis_size("seq")
     here = lax.axis_index("seq")
     from_right = [piece]
@@ -24,7 +24,7 @@
     slots = [piece]
     for m in range(1, n):
         slots.append(jnp.where(here + m < n, from_right[m], from_left[n - m]))
-    return jnp.concatenate(slots, axis=0)
+    return jnp.concatenate(slots, axis=axis)
 
 
 def swap_gather(piece, axis, dim):
@@ -72,7 +72,7 @@
     value = jnp.concatenate(project(w_value), axis=1)
     queries = project(w_query, key)
     if lax.axis_size("seq") == SPAN:
-        seen = jnp.stack([line_gather(key), line_gather(value)])
+        seen = line_gather(jnp.stack([key, value]), axis=1)
     else:
         packed = jnp.stack([key, value])
         blocks_seen = [packed]

time: 227 us -> 231 us (1.018); the launches traced: 223 us -> 231 us
  waiting for transfers between devices: 130 us -> 152 us
  starting transfers between devices: 30.9 us -> 16.3 us
    ppermute x6 -> x3, starting transfers between devices: 15.1 us -> 4.78 us  [line_gather(): lax.ppermute(from_left[-1], 'seq', [(j, j + 1) for j in range(k - 1, n -...]
    ppermute x6 -> x3, waiting for transfers between devices: 28.1 us -> 37.4 us  [line_gather(): lax.ppermute(from_right[-1], 'seq', [(j, j - 1) for j in range(1, n - k +...]
    ppermute x6 -> x3, waiting for transfers between devices: 0.02 us -> 6.43 us  [line_gather(): lax.ppermute(from_left[-1], 'seq', [(j, j + 1) for j in range(k - 1, n -...]
    ppermute x6 -> x3, starting transfers between devices: 8.09 us -> 3.85 us  [line_gather(): lax.ppermute(from_right[-1], 'seq', [(j, j - 1) for j in range(1, n - k +...]
    ppermute x3, waiting for transfers between devices: 22.4 us -> 26.3 us  [full_columns(): other = lax.ppermute(own[rows:], 'groups', [(0, 1), (1, 0)])]
  transfers between devices with their start and end apart: 20 -> 14, of which waited for: 10 -> 10; matrix products, arithmetic and copies ran while one was open for 17% -> 16% of each run, Pallas kernels for 0% -> 0%
where the time goes in v22:
time: 231 us
  waiting for transfers between devices  152 us (66%)
  other arithmetic  23.2 us (10%)
  matrix products  17.5 us (8%)
  starting transfers between devices  16.3 us (7%)
  between operations  13.5 us (6%)
  local copies, waits for them, and re-layouts  8.59 us (4%)
    all_gather x3, waiting for transfers between devices, full_columns(): own = lax.all_gather(own, 'seq', axis=0, tiled=True)  62.7 us
    ppermute x3, waiting for transfers between devices, line_gather(): lax.ppermute(from_right[-1], 'seq', [(j, j - 1) for j in range(1, n - k +...  37.4 us
    ppermute x3, waiting for transfers between devices, full_columns(): other = lax.ppermute(own[rows:], 'groups', [(0, 1), (1, 0)])  26.3 us
    ppermute x2, waiting for transfers between devices, swap_gather(): other = lax.ppermute(piece, axis, [(0, 1), (1, 0)])  19 us
    dot_general x6, matrix products, project(): jnp.dot(block, piece, preferred_element_type=jnp.float32)  12.8 us
    concatenate x3, other arithmetic, full_columns(): own = jnp.roll(own, -lax.axis_index('seq') * rows, axis=0)  9.16 us
    ppermute x3, waiting for transfers between devices, line_gather(): lax.ppermute(from_left[-1], 'seq', [(j, j + 1) for j in range(k - 1, n -...  6.43 us
    ppermute x3, starting transfers between devices, line_gather(): lax.ppermute(from_left[-1], 'seq', [(j, j + 1) for j in range(k - 1, n -...  4.78 us
  transfers between devices with their start and end apart: 14, of which 10 were waited for; matrix products, arithmetic and copies ran while one was open for 16% of the time, Pallas kernels for 0%

profile of v22, /device:TPU:0, one launch (start us, length us, event | category | flops | bytes accessed | tf_op | source)
XLA Modules:
  0.0 230.9 jit_solution(11217017781878119466)
XLA Ops:
  6.5 2.4 %constant_dynamic-slice_fusion.4 = (bf16[1024,256]{1,0:T(8,128)(2,1)}, bf16[1024,256]{1,0:T(8,128)(2,1)}) fusion(bf16[1024,512]{1,0:T(8,128)(2,1)} %param.8, s32[]{:T(128)S(6)} %select_n.93, s32[]{:T(128)S(6)} %select_n.92), kind=kLoop, calls=%fused_computation.81 | loop fusion | bytes 2097160 | tf_op jit(solution)/shard_map/dynamic_slice | solution.py:46
  9.0 3.0 %collective-permute-start = (bf16[192,2048]{1,0:T(8,128)(2,1)}, bf16[192,2048]{1,0:T(8,128)(2,1)S(1)}, u32[]{:S(2)}, u32[]{:S(2)}) collective-permute-start(bf16[192,2048]{1,0:T(8,128)(2,1)} %param.6), channel_id=1, source_target_pairs={{0,2},{2,0},{1,3},{3,1},{4,6},{6,4},{5,7},{7,5},{8,10},{10,8},{9,1... | collective-permute-start | bytes 2359304 | tf_op jit(solution)/shard_map/ppermute | solution.py:34
  13.1 16.6 %collective-permute-done = bf16[192,2048]{1,0:T(8,128)(2,1)S(1)} collective-permute-done((bf16[192,2048]{1,0:T(8,128)(2,1)}, bf16[192,2048]{1,0:T(8,128)(2,1)S(1)}, u32[]{:S(2)}, u32[]{:S(2)}) %collective-permute-start) | collective-permute-done | bytes 786464 | tf_op jit(solution)/shard_map/ppermute | solution.py:34
  31.3 2.4 %collective-permute-done.1 = bf16[384,2048]{1,0:T(8,128)(2,1)} collective-permute-done((bf16[384,2048]{1,0:T(8,128)(2,1)S(1)}, bf16[384,2048]{1,0:T(8,128)(2,1)}, u32[]{:S(2)}, u32[]{:S(2)}) %collective-permute-start.1) | collective-permute-done | bytes 1572896 | tf_op jit(solution)/shard_map/ppermute | solution.py:34
  33.6 4.0 %broadcast_select_fusion = (bf16[384,2048]{1,0:T(8,128)(2,1)}, bf16[384,2048]{1,0:T(8,128)(2,1)}) fusion(bf16[384,2048]{1,0:T(8,128)(2,1)} %collective-permute-done.1, pred[]{:T(512)S(6)} %eq.12, bf16[192,2048]{1,0:T(8,128)(2,1)S(1)} %get-tuple-element.13, bf16[192,2048]{1,0:T(8,128)(2,1)S(1)} %get-tuple-element.12), kind=kLoop, calls=%fused_computation.44 | loop fusion | flops 4718592 | bytes 6291457 | tf_op jit(solution)/shard_map/jit(_where)/select_n | solution.py:36
  37.6 20.1 %all-gather.4.cloned.1.call-done = bf16[4096,256]{1,0:T(8,128)(2,1)} async-done(((bf16[1024,256]{1,0:T(8,128)(2,1)}), bf16[4096,256]{1,0:T(8,128)(2,1)}) %all-gather.4.cloned.1.call-update) | async-done | bytes 2097168 | tf_op jit(solution)/shard_map/all_gather | solution.py:47
  57.7 3.0 %fusion.17 = bf16[4096,256]{1,0:T(8,128)(2,1)S(1)} fusion(s32[]{:T(128)S(6)} %select_n.91, bf16[4096,256]{1,0:T(8,128)(2,1)} %all-gather.4.cloned.1.call-done), kind=kLoop, calls=%fused_computation.30 | loop fusion | flops 4194304 | bytes 4194308 | tf_op jit(solution)/shard_map/jit(_roll_dynamic)/concatenate | solution.py:48
  63.4 40.5 %all-gather.6.cloned.1.call-done = bf16[4096,256]{1,0:T(8,128)(2,1)} async-done(((bf16[1024,256]{1,0:T(8,128)(2,1)}), bf16[4096,256]{1,0:T(8,128)(2,1)}) %all-gather.6.cloned.1.call-update) | async-done | bytes 2097168 | tf_op jit(solution)/shard_map/all_gather | solution.py:47
  104.0 3.2 %fusion.16 = bf16[4096,256]{1,0:T(8,128)(2,1)S(1)} fusion(s32[]{:T(128)S(6)} %select_n.91, bf16[4096,256]{1,0:T(8,128)(2,1)} %all-gather.6.cloned.1.call-done), kind=kLoop, calls=%fused_computation.29 | loop fusion | flops 4194304 | bytes 4194308 | tf_op jit(solution)/shard_map/jit(_roll_dynamic)/concatenate | solution.py:48
  107.3 1.5 collective-permute-start.3
  108.8 2.9 %fusion.6 = bf16[384,4096]{1,0:T(8,128)(2,1)S(1)} fusion(s32[]{:T(128)S(6)} %select_n.91, bf16[384,2048]{1,0:T(8,128)(2,1)S(1)} %copy-done.1, bf16[384,2048]{1,0:T(8,128)(2,1)S(1)} %copy-done), kind=kLoop, calls=%fused_computation.20 | loop fusion | flops 12582912 | bytes 6291460 | tf_op jit(solution)/shard_map/jit(_roll_dynamic)/concatenate | solution.py:63
  114.4 2.8 %fusion.42 = bf16[384,256]{0,1:T(8,128)(2,1)S(1)} fusion(bf16[384,4096]{1,0:T(8,128)(2,1)S(1)} %fusion.6, bf16[3072,256]{1,0:T(8,128)(2,1)} %collective-permute-done.2, bf16[1024,256]{1,0:T(8,128)(2,1)S(1)} %copy-done.8), kind=kOutput, calls=%fused_computation.50 | convolution fusion | flops 809598976 | bytes 5439488 | tf_op jit(solution)/shard_map/dot_general | solution.py:67
  117.2 26.3 %collective-permute-done.3 = bf16[3072,256]{1,0:T(8,128)(2,1)S(1)} collective-permute-done((bf16[3072,256]{1,0:T(8,128)(2,1)S(1)}, bf16[3072,256]{1,0:T(8,128)(2,1)S(1)}, u32[]{:S(2)}, u32[]{:S(2)}) %collective-permute-start.3) | collective-permute-done | bytes 1572896 | tf_op jit(solution)/shard_map/ppermute | solution.py:51
  145.9 2.3 %collective-permute-start.5 = (bf16[2,384,512]{1,2,0:T(8,128)(2,1)}, bf16[2,384,512]{1,2,0:T(8,128)(2,1)}, u32[]{:S(2)}, u32[]{:S(2)}) collective-permute-start(bf16[2,384,512]{1,2,0:T(8,128)(2,1)} %pad_maximum_fusion.2), channel_id=1, source_target_pairs={{0,4},{4,8},{8,12},{1,5},{5,9},{9,13},{2,6},{6,10},{10,14},{3,7},{... | collective-permute-start | bytes 2359304 | tf_op jit(solution)/shard_map/ppermute | solution.py:23
  148.2 2.0 all-gather.8.cloned.1.call-done
  150.3 3.0 %fusion.15 = bf16[4096,256]{1,0:T(8,128)(2,1)S(1)} fusion(s32[]{:T(128)S(6)} %select_n.91, bf16[4096,256]{1,0:T(8,128)(2,1)} %all-gather.8.cloned.1.call-done), kind=kLoop, calls=%fused_computation.28 | loop fusion | flops 4194304 | bytes 4194308 | tf_op jit(solution)/shard_map/jit(_roll_dynamic)/concatenate | solution.py:48
  157.3 6.4 %collective-permute-done.5 = bf16[2,384,512]{1,2,0:T(8,128)(2,1)} collective-permute-done((bf16[2,384,512]{1,2,0:T(8,128)(2,1)}, bf16[2,384,512]{1,2,0:T(8,128)(2,1)}, u32[]{:S(2)}, u32[]{:S(2)}) %collective-permute-start.5) | collective-permute-done | bytes 786464 | tf_op jit(solution)/shard_map/ppermute | solution.py:23
  163.8 1.6 collective-permute-start.6
  165.4 9.4 %collective-permute-done.4 = bf16[2,384,512]{1,2,0:T(8,128)(2,1)} collective-permute-done((bf16[2,384,512]{1,2,0:T(8,128)(2,1)}, bf16[2,384,512]{1,2,0:T(8,128)(2,1)}, u32[]{:S(2)}, u32[]{:S(2)}) %collective-permute-start.4) | collective-permute-done | bytes 786464 | tf_op jit(solution)/shard_map/ppermute | solution.py:22
  176.9 3.4 %convolution_convert_fusion = bf16[384,256]{0,1:T(8,128)(2,1)S(1)} fusion(bf16[384,4096]{1,0:T(8,128)(2,1)} %copy-done.2, bf16[4096,256]{1,0:T(8,128)(2,1)S(1)} %fusion.15), kind=kOutput, calls=%fused_computation.51 | convolution fusion | flops 805404672 | bytes 5439488 | tf_op jit(solution)/shard_map/dot_general | solution.py:67
  180.4 15.0 %collective-permute-done.8 = bf16[2,384,512]{1,2,0:T(8,128)(2,1)} collective-permute-done((bf16[2,384,512]{1,2,0:T(8,128)(2,1)}, bf16[2,384,512]{1,2,0:T(8,128)(2,1)}, u32[]{:S(2)}, u32[]{:S(2)}) %collective-permute-start.8) | collective-permute-done | bytes 786464 | tf_op jit(solution)/shard_map/ppermute | solution.py:22
  196.7 2.7 %fusion.36 = bf16[384,256]{0,1:T(8,128)(2,1)S(1)} fusion(bf16[384,4096]{1,0:T(8,128)(2,1)S(1)} %copy-done.3, bf16[3072,256]{1,0:T(8,128)(2,1)} %collective-permute-done.10, bf16[1024,256]{1,0:T(8,128)(2,1)S(1)} %copy-done.7), kind=kOutput, calls=%fused_computation.48 | convolution fusion | flops 809598976 | bytes 5439488 | tf_op jit(solution)/shard_map/dot_general | solution.py:67
  201.9 13.1 %collective-permute-done.9 = bf16[2,384,512]{1,2,0:T(8,128)(2,1)S(1)} collective-permute-done((bf16[2,384,512]{1,2,0:T(8,128)(2,1)}, bf16[2,384,512]{1,2,0:T(8,128)(2,1)S(1)}, u32[]{:S(2)}, u32[]{:S(2)}) %collective-permute-start.9) | collective-permute-done | bytes 786464 | tf_op jit(solution)/shard_map/ppermute | solution.py:22
  217.4 1.8 fusion.48
  (63 shorter events, 28.0 us)
Async XLA Ops:
  6.5 23.2 %copy-start.6 = (bf16[192,2048]{1,0:T(8,128)(2,1)S(1)}, bf16[192,2048]{1,0:T(8,128)(2,1)}, u32[]{:S(2)}) copy-start(bf16[192,2048]{1,0:T(8,128)(2,1)} %param.6) | copy-start | bytes 2359300
  6.5 5.5 %copy-start.4 = (bf16[1024,512]{1,0:T(8,128)(2,1)S(1)}, bf16[1024,512]{1,0:T(8,128)(2,1)}, u32[]{:S(2)}) copy-start(bf16[1024,512]{1,0:T(8,128)(2,1)} %param.9) | copy-start | bytes 3145732
  6.5 51.2 %all-gather.4.cloned.1.call-start = ((), (), s32[]{:S(2)}) async-start(), calls=%async_computation | async-start | bytes 2621440 | tf_op jit(solution)/shard_map/all_gather | solution.py:47
  8.9 95.0 %all-gather.6.cloned.1.call-start = ((), (), s32[]{:S(2)}) async-start(), calls=%async_computation.1 | async-start | bytes 2621440 | tf_op jit(solution)/shard_map/all_gather | solution.py:47
  9.0 20.8 %collective-permute-start = (bf16[192,2048]{1,0:T(8,128)(2,1)}, bf16[192,2048]{1,0:T(8,128)(2,1)S(1)}, u32[]{:S(2)}, u32[]{:S(2)}) collective-permute-start(bf16[192,2048]{1,0:T(8,128)(2,1)} %param.6), channel_id=1, source_target_pairs={{0,2},{2,0},{1,3},{3,1},{4,6},{6,4},{5,7},{7,5},{8,10},{10,8},{9,1... | collective-permute-start | bytes 2359304 | tf_op jit(solution)/shard_map/ppermute | solution.py:34
  13.1 137.2 %all-gather.8.cloned.1.call-start = ((), (), s32[]{:S(2)}) async-start(), calls=%async_computation.2 | async-start | bytes 2621440 | tf_op jit(solution)/shard_map/all_gather | solution.py:47
  13.1 17.0 %copy-start.5 = (bf16[1024,512]{1,0:T(8,128)(2,1)S(1)}, bf16[1024,512]{1,0:T(8,128)(2,1)}, u32[]{:S(2)}) copy-start(bf16[1024,512]{1,0:T(8,128)(2,1)} %param.7) | copy-start | bytes 3145732
  30.0 3.6 %collective-permute-start.1 = (bf16[384,2048]{1,0:T(8,128)(2,1)S(1)}, bf16[384,2048]{1,0:T(8,128)(2,1)}, u32[]{:S(2)}, u32[]{:S(2)}) collective-permute-start(bf16[384,2048]{1,0:T(8,128)(2,1)S(1)} %pad_maximum_fusion.1), channel_id=1, source_target_pairs={{0,1},{1,0},{2,3},{3,2},{4,5},{5,4},{6,7},{7,6},{8,9},{9,8},{10,11... | collective-permute-start | bytes 4718600 | tf_op jit(solution)/shard_map/ppermute | solution.py:34
  62.0 52.4 %collective-permute-start.2 = (bf16[3072,256]{1,0:T(8,128)(2,1)}, bf16[3072,256]{1,0:T(8,128)(2,1)}, u32[]{:S(2)}, u32[]{:S(2)}) collective-permute-start(bf16[3072,256]{1,0:T(8,128)(2,1)} %slice.36), channel_id=1, source_target_pairs={{0,16},{16,0},{1,17},{17,1},{2,18},{18,2},{3,19},{19,3},{4,20},{20... | collective-permute-start | bytes 4718600 | tf_op jit(solution)/shard_map/ppermute | solution.py:51
  104.0 4.8 %copy-start = (bf16[384,2048]{1,0:T(8,128)(2,1)S(1)}, bf16[384,2048]{1,0:T(8,128)(2,1)}, u32[]{:S(2)}) copy-start(bf16[384,2048]{1,0:T(8,128)(2,1)} %get-tuple-element.10) | copy-start | bytes 4718596
  104.0 4.8 %copy-start.1 = (bf16[384,2048]{1,0:T(8,128)(2,1)S(1)}, bf16[384,2048]{1,0:T(8,128)(2,1)}, u32[]{:S(2)}) copy-start(bf16[384,2048]{1,0:T(8,128)(2,1)} %get-tuple-element.11) | copy-start | bytes 4718596
  107.3 36.2 %collective-permute-start.3 = (bf16[3072,256]{1,0:T(8,128)(2,1)S(1)}, bf16[3072,256]{1,0:T(8,128)(2,1)S(1)}, u32[]{:S(2)}, u32[]{:S(2)}) collective-permute-start(bf16[3072,256]{1,0:T(8,128)(2,1)S(1)} %slice.37), channel_id=1, source_target_pairs={{0,16},{16,0},{1,17},{17,1},{2,18},{18,2},{3,19},{19,3},{4,20},{20... | collective-permute-start | bytes 4718600 | tf_op jit(solution)/shard_map/ppermute | solution.py:51
  111.7 31.8 %copy-start.2 = (bf16[384,4096]{1,0:T(8,128)(2,1)}, bf16[384,4096]{1,0:T(8,128)(2,1)S(1)}, u32[]{:S(2)}) copy-start(bf16[384,4096]{1,0:T(8,128)(2,1)S(1)} %fusion.6) | copy-start | bytes 9437188
  113.0 1.3 copy-start.8
  114.3 29.1 %copy-start.9 = (bf16[1024,256]{1,0:T(8,128)(2,1)S(1)}, bf16[1024,256]{1,0:T(8,128)(2,1)}, u32[]{:S(2)}) copy-start(bf16[1024,256]{1,0:T(8,128)(2,1)} %get-tuple-element.18) | copy-start | bytes 1572868
  145.9 17.9 %collective-permute-start.5 = (bf16[2,384,512]{1,2,0:T(8,128)(2,1)}, bf16[2,384,512]{1,2,0:T(8,128)(2,1)}, u32[]{:S(2)}, u32[]{:S(2)}) collective-permute-start(bf16[2,384,512]{1,2,0:T(8,128)(2,1)} %pad_maximum_fusion.2), channel_id=1, source_target_pairs={{0,4},{4,8},{8,12},{1,5},{5,9},{9,13},{2,6},{6,10},{10,14},{3,7},{... | collective-permute-start | bytes 2359304 | tf_op jit(solution)/shard_map/ppermute | solution.py:23
  153.3 21.5 %collective-permute-start.4 = (bf16[2,384,512]{1,2,0:T(8,128)(2,1)}, bf16[2,384,512]{1,2,0:T(8,128)(2,1)}, u32[]{:S(2)}, u32[]{:S(2)}) collective-permute-start(bf16[2,384,512]{1,2,0:T(8,128)(2,1)} %pad_maximum_fusion.2), channel_id=1, source_target_pairs={{4,0},{8,4},{12,8},{5,1},{9,5},{13,9},{6,2},{10,6},{14,10},{7,3},{... | collective-permute-start | bytes 2359304 | tf_op jit(solution)/shard_map/ppermute | solution.py:22
  155.9 40.8 %collective-permute-start.10 = (bf16[3072,256]{1,0:T(8,128)(2,1)}, bf16[3072,256]{1,0:T(8,128)(2,1)}, u32[]{:S(2)}, u32[]{:S(2)}) collective-permute-start(bf16[3072,256]{1,0:T(8,128)(2,1)} %slice.34), channel_id=1, source_target_pairs={{0,16},{16,0},{1,17},{17,1},{2,18},{18,2},{3,19},{19,3},{4,20},{20... | collective-permute-start | bytes 4718600 | tf_op jit(solution)/shard_map/ppermute | solution.py:51
  163.8 12.3 %collective-permute-start.6 = (bf16[2,384,512]{1,2,0:T(8,128)(2,1)}, bf16[2,384,512]{1,2,0:T(8,128)(2,1)}, u32[]{:S(2)}, u32[]{:S(2)}) collective-permute-start(bf16[2,384,512]{1,2,0:T(8,128)(2,1)} %collective-permute-done.5), channel_id=1, source_target_pairs={{4,8},{8,12},{5,9},{9,13},{6,10},{10,14},{7,11},{11,15},{20,24},{2... | collective-permute-start | bytes 2359304 | tf_op jit(solution)/shard_map/ppermute | solution.py:23
  174.8 20.6 %collective-permute-start.8 = (bf16[2,384,512]{1,2,0:T(8,128)(2,1)}, bf16[2,384,512]{1,2,0:T(8,128)(2,1)}, u32[]{:S(2)}, u32[]{:S(2)}) collective-permute-start(bf16[2,384,512]{1,2,0:T(8,128)(2,1)} %collective-permute-done.4), channel_id=1, source_target_pairs={{4,0},{8,4},{5,1},{9,5},{6,2},{10,6},{7,3},{11,7},{20,16},{24,20},... | collective-permute-start | bytes 2359304 | tf_op jit(solution)/shard_map/ppermute | solution.py:22
  176.1 20.6 %copy-start.3 = (bf16[384,4096]{1,0:T(8,128)(2,1)S(1)}, bf16[384,4096]{1,0:T(8,128)(2,1)}, u32[]{:S(2)}) copy-start(bf16[384,4096]{1,0:T(8,128)(2,1)} %copy-done.2) | copy-start | bytes 9437188
  176.1 20.6 %copy-start.7 = (bf16[1024,256]{1,0:T(8,128)(2,1)S(1)}, bf16[1024,256]{1,0:T(8,128)(2,1)}, u32[]{:S(2)}) copy-start(bf16[1024,256]{1,0:T(8,128)(2,1)} %get-tuple-element.14) | copy-start | bytes 1572868
  176.1 24.5 %collective-permute-start.7 = (bf16[2,384,512]{1,2,0:T(8,128)(2,1)}, bf16[2,384,512]{1,2,0:T(8,128)(2,1)S(1)}, u32[]{:S(2)}, u32[]{:S(2)}) collective-permute-start(bf16[2,384,512]{1,2,0:T(8,128)(2,1)} %collective-permute-done.6), channel_id=1, source_target_pairs={{8,12},{9,13},{10,14},{11,15},{24,28},{25,29},{26,30},{27,31}} | collective-permute-start | bytes 2359304 | tf_op jit(solution)/shard_map/ppermute | solution.py:23
  195.4 19.6 %collective-permute-start.9 = (bf16[2,384,512]{1,2,0:T(8,128)(2,1)}, bf16[2,384,512]{1,2,0:T(8,128)(2,1)S(1)}, u32[]{:S(2)}, u32[]{:S(2)}) collective-permute-start(bf16[2,384,512]{1,2,0:T(8,128)(2,1)} %collective-permute-done.8), channel_id=1, source_target_pairs={{4,0},{5,1},{6,2},{7,3},{20,16},{21,17},{22,18},{23,19}} | collective-permute-start | bytes 2359304 | tf_op jit(solution)/shard_map/ppermute | solution.py:22
Sparse Core Ops, SparseCore 0:
  9.1 48.6 all-gather.3
  59.3 44.6 all-gather.5
  105.6 44.6 all-gather.7

commit v23 on v8

--- a/solution.py
+++ b/solution.py
@@ -101,10 +101,14 @@
         )
         attended = summed / jnp.transpose(running_total)[:, :, None]
         outputs.append(attended.astype(jnp.bfloat16).reshape(tokens_here, count * HD))
-    attended = jnp.concatenate(outputs, axis=1)
     if shared:
-        attended = jnp.roll(attended, lax.axis_index("groups") * (width // 2), axis=1)
-    return attended
+        first_group = lax.axis_index("groups") == 0
+        return jnp.where(
+            first_group,
+            jnp.concatenate(outputs, axis=1),
+            jnp.concatenate(outputs[::-1], axis=1),
+        )
+    return jnp.concatenate(outputs, axis=1)
 
 
 def solution(mesh):

time: 227 us -> 226 us (level)
  no operation moved by 1% of the time
where the time goes in v23:
time: 226 us; the launch traced here: 223 us
  waiting for transfers between devices  130 us (58%)
  starting transfers between devices  30.9 us (14%)
  other arithmetic  25.2 us (11%)
  matrix products  15.7 us (7%)
  between operations  13.5 us (6%)
  local copies, waits for them, and re-layouts  7.56 us (3%)
    all_gather x3, waiting for transfers between devices, full_columns(): own = lax.all_gather(own, 'seq', axis=0, tiled=True)  60.7 us
    ppermute x6, waiting for transfers between devices, line_gather(): lax.ppermute(from_right[-1], 'seq', [(j, j - 1) for j in range(1, n - k +...  28.1 us
    ppermute x3, waiting for transfers between devices, full_columns(): other = lax.ppermute(own[rows:], 'groups', [(0, 1), (1, 0)])  22.4 us
    ppermute x2, waiting for transfers between devices, swap_gather(): other = lax.ppermute(piece, axis, [(0, 1), (1, 0)])  18.9 us
    ppermute x6, starting transfers between devices, line_gather(): lax.ppermute(from_left[-1], 'seq', [(j, j + 1) for j in range(k - 1, n -...  15.1 us
    dot_general x6, matrix products, project(): jnp.dot(block, piece, preferred_element_type=jnp.float32)  11.7 us
    concatenate x3, other arithmetic, full_columns(): own = jnp.roll(own, -lax.axis_index('seq') * rows, axis=0)  9.16 us
    ppermute x6, starting transfers between devices, line_gather(): lax.ppermute(from_right[-1], 'seq', [(j, j - 1) for j in range(1, n - k +...  8.09 us
  transfers between devices with their start and end apart: 20, of which 10 were waited for; matrix products, arithmetic and copies ran while one was open for 17% of the time, Pallas kernels for 0%

profile of v23, /device:TPU:0, one launch (start us, length us, event | category | flops | bytes accessed | tf_op | source)
XLA Modules:
  0.0 223.1 jit_solution(5482720395283816545)
XLA Ops:
  6.5 2.4 %constant_dynamic-slice_fusion.4 = (bf16[1024,256]{1,0:T(8,128)(2,1)}, bf16[1024,256]{1,0:T(8,128)(2,1)}) fusion(bf16[1024,512]{1,0:T(8,128)(2,1)} %param.9, s32[]{:T(128)S(6)} %select_n.102, s32[]{:T(128)S(6)} %select_n.101), kind=kLoop, calls=%fused_computation.78 | loop fusion | bytes 2097160 | tf_op jit(solution)/shard_map/dynamic_slice | solution.py:46
  9.0 3.0 %collective-permute-start = (bf16[192,2048]{1,0:T(8,128)(2,1)}, bf16[192,2048]{1,0:T(8,128)(2,1)S(1)}, u32[]{:S(2)}, u32[]{:S(2)}) collective-permute-start(bf16[192,2048]{1,0:T(8,128)(2,1)} %param.6), channel_id=1, source_target_pairs={{0,2},{2,0},{1,3},{3,1},{4,6},{6,4},{5,7},{7,5},{8,10},{10,8},{9,1... | collective-permute-start | bytes 2359304 | tf_op jit(solution)/shard_map/ppermute | solution.py:34
  13.2 16.6 %collective-permute-done = bf16[192,2048]{1,0:T(8,128)(2,1)S(1)} collective-permute-done((bf16[192,2048]{1,0:T(8,128)(2,1)}, bf16[192,2048]{1,0:T(8,128)(2,1)S(1)}, u32[]{:S(2)}, u32[]{:S(2)}) %collective-permute-start) | collective-permute-done | bytes 786464 | tf_op jit(solution)/shard_map/ppermute | solution.py:34
  31.3 2.3 %collective-permute-done.1 = bf16[384,2048]{1,0:T(8,128)(2,1)} collective-permute-done((bf16[384,2048]{1,0:T(8,128)(2,1)S(1)}, bf16[384,2048]{1,0:T(8,128)(2,1)}, u32[]{:S(2)}, u32[]{:S(2)}) %collective-permute-start.1) | collective-permute-done | bytes 1572896 | tf_op jit(solution)/shard_map/ppermute | solution.py:34
  33.6 4.0 %broadcast_select_fusion = (bf16[384,2048]{1,0:T(8,128)(2,1)}, bf16[384,2048]{1,0:T(8,128)(2,1)}) fusion(bf16[384,2048]{1,0:T(8,128)(2,1)} %collective-permute-done.1, pred[]{:T(512)S(6)} %eq.14, bf16[192,2048]{1,0:T(8,128)(2,1)S(1)} %get-tuple-element.11, bf16[192,2048]{1,0:T(8,128)(2,1)S(1)} %get-tuple-element.10), kind=kLoop, calls=%fused_computation.45 | loop fusion | flops 4718592 | bytes 6291457 | tf_op jit(solution)/shard_map/jit(_where)/select_n | solution.py:36
  37.6 20.1 %all-gather.4.cloned.1.call-done = bf16[4096,256]{1,0:T(8,128)(2,1)} async-done(((bf16[1024,256]{1,0:T(8,128)(2,1)}), bf16[4096,256]{1,0:T(8,128)(2,1)}) %all-gather.4.cloned.1.call-update) | async-done | bytes 2097168 | tf_op jit(solution)/shard_map/all_gather | solution.py:47
  57.7 3.0 %fusion.17 = bf16[4096,256]{1,0:T(8,128)(2,1)S(1)} fusion(s32[]{:T(128)S(6)} %select_n.100, bf16[4096,256]{1,0:T(8,128)(2,1)} %all-gather.4.cloned.1.call-done), kind=kLoop, calls=%fused_computation.29 | loop fusion | flops 4194304 | bytes 4194308 | tf_op jit(solution)/shard_map/jit(_roll_dynamic)/concatenate | solution.py:48
  63.4 40.5 %all-gather.8.cloned.1.call-done = bf16[4096,256]{1,0:T(8,128)(2,1)} async-done(((bf16[1024,256]{1,0:T(8,128)(2,1)}), bf16[4096,256]{1,0:T(8,128)(2,1)}) %all-gather.8.cloned.1.call-update) | async-done | bytes 2097168 | tf_op jit(solution)/shard_map/all_gather | solution.py:47
  104.0 3.2 %fusion.15 = bf16[4096,256]{1,0:T(8,128)(2,1)S(1)} fusion(s32[]{:T(128)S(6)} %select_n.100, bf16[4096,256]{1,0:T(8,128)(2,1)} %all-gather.8.cloned.1.call-done), kind=kLoop, calls=%fused_computation.27 | loop fusion | flops 4194304 | bytes 4194308 | tf_op jit(solution)/shard_map/jit(_roll_dynamic)/concatenate | solution.py:48
  107.2 1.5 collective-permute-start.9
  108.8 2.9 %fusion.6 = bf16[384,4096]{1,0:T(8,128)(2,1)S(1)} fusion(s32[]{:T(128)S(6)} %select_n.100, bf16[384,2048]{1,0:T(8,128)(2,1)S(1)} %copy-done.1, bf16[384,2048]{1,0:T(8,128)(2,1)S(1)} %copy-done), kind=kLoop, calls=%fused_computation.20 | loop fusion | flops 12582912 | bytes 6291460 | tf_op jit(solution)/shard_map/jit(_roll_dynamic)/concatenate | solution.py:63
  114.3 2.8 %fusion.42 = bf16[384,256]{0,1:T(8,128)(2,1)S(1)} fusion(bf16[384,4096]{1,0:T(8,128)(2,1)S(1)} %fusion.6, bf16[3072,256]{1,0:T(8,128)(2,1)} %collective-permute-done.2, bf16[1024,256]{1,0:T(8,128)(2,1)S(1)} %copy-done.11), kind=kOutput, calls=%fused_computation.51 | convolution fusion | flops 809598976 | bytes 5439488 | tf_op jit(solution)/shard_map/dot_general | solution.py:67
  119.2 5.3 %collective-permute-start.4 = (bf16[384,512]{0,1:T(8,128)(2,1)}, bf16[384,512]{0,1:T(8,128)(2,1)}, u32[]{:S(2)}, u32[]{:S(2)}) collective-permute-start(bf16[384,512]{0,1:T(8,128)(2,1)} %pad_maximum_fusion.3), channel_id=1, source_target_pairs={{0,4},{4,8},{8,12},{1,5},{5,9},{9,13},{2,6},{6,10},{10,14},{3,7},{... | collective-permute-start | bytes 1179656 | tf_op jit(solution)/shard_map/ppermute | solution.py:23
  124.5 18.9 %collective-permute-done.9 = bf16[3072,256]{1,0:T(8,128)(2,1)S(1)} collective-permute-done((bf16[3072,256]{1,0:T(8,128)(2,1)S(1)}, bf16[3072,256]{1,0:T(8,128)(2,1)S(1)}, u32[]{:S(2)}, u32[]{:S(2)}) %collective-permute-start.9) | collective-permute-done | bytes 1572896 | tf_op jit(solution)/shard_map/ppermute | solution.py:51
  146.9 5.5 %collective-permute-start.11 = (bf16[384,512]{0,1:T(8,128)(2,1)}, bf16[384,512]{0,1:T(8,128)(2,1)}, u32[]{:S(2)}, u32[]{:S(2)}) collective-permute-start(bf16[384,512]{0,1:T(8,128)(2,1)} %pad_maximum_fusion.4), channel_id=1, source_target_pairs={{0,4},{4,8},{8,12},{1,5},{5,9},{9,13},{2,6},{6,10},{10,14},{3,7},{... | collective-permute-start | bytes 1179656 | tf_op jit(solution)/shard_map/ppermute | solution.py:23
  152.4 1.5 collective-permute-start.7
  154.0 1.5 collective-permute-start.5
  155.5 10.2 %collective-permute-done.10 = bf16[384,512]{0,1:T(8,128)(2,1)} collective-permute-done((bf16[384,512]{0,1:T(8,128)(2,1)}, bf16[384,512]{0,1:T(8,128)(2,1)}, u32[]{:S(2)}, u32[]{:S(2)}) %collective-permute-start.10) | collective-permute-done | bytes 393248 | tf_op jit(solution)/shard_map/ppermute | solution.py:22
  168.4 3.0 %fusion.16 = bf16[4096,256]{1,0:T(8,128)(2,1)S(1)} fusion(s32[]{:T(128)S(6)} %select_n.100, bf16[4096,256]{1,0:T(8,128)(2,1)} %all-gather.6.cloned.1.call-done), kind=kLoop, calls=%fused_computation.28 | loop fusion | flops 4194304 | bytes 4194308 | tf_op jit(solution)/shard_map/jit(_roll_dynamic)/concatenate | solution.py:48
  177.7 4.5 %collective-permute-done.14 = bf16[384,512]{0,1:T(8,128)(2,1)} collective-permute-done((bf16[384,512]{0,1:T(8,128)(2,1)}, bf16[384,512]{0,1:T(8,128)(2,1)}, u32[]{:S(2)}, u32[]{:S(2)}) %collective-permute-start.14) | collective-permute-done | bytes 393248 | tf_op jit(solution)/shard_map/ppermute | solution.py:22
  186.3 7.3 %collective-permute-done.8 = bf16[384,512]{0,1:T(8,128)(2,1)S(1)} collective-permute-done((bf16[384,512]{0,1:T(8,128)(2,1)}, bf16[384,512]{0,1:T(8,128)(2,1)S(1)}, u32[]{:S(2)}, u32[]{:S(2)}) %collective-permute-start.8) | collective-permute-done | bytes 393248 | tf_op jit(solution)/shard_map/ppermute | solution.py:22
  193.7 6.1 %collective-permute-done.15 = bf16[384,512]{0,1:T(8,128)(2,1)S(1)} collective-permute-done((bf16[384,512]{0,1:T(8,128)(2,1)}, bf16[384,512]{0,1:T(8,128)(2,1)S(1)}, u32[]{:S(2)}, u32[]{:S(2)}) %collective-permute-start.15) | collective-permute-done | bytes 393248 | tf_op jit(solution)/shard_map/ppermute | solution.py:22
  205.4 3.5 %collective-permute-done.16 = bf16[3072,256]{1,0:T(8,128)(2,1)} collective-permute-done((bf16[3072,256]{1,0:T(8,128)(2,1)}, bf16[3072,256]{1,0:T(8,128)(2,1)}, u32[]{:S(2)}, u32[]{:S(2)}) %collective-permute-start.16) | collective-permute-done | bytes 1572896 | tf_op jit(solution)/shard_map/ppermute | solution.py:51
  208.9 3.8 %fusion.36 = bf16[384,256]{0,1:T(8,128)(2,1)S(1)} fusion(bf16[384,4096]{1,0:T(8,128)(2,1)} %copy-done.2, bf16[3072,256]{1,0:T(8,128)(2,1)} %collective-permute-done.16, bf16[1024,256]{1,0:T(8,128)(2,1)} %get-tuple-element.12), kind=kOutput, calls=%fused_computation.49 | convolution fusion | flops 809598976 | bytes 5439488 | tf_op jit(solution)/shard_map/dot_general | solution.py:67
  (83 shorter events, 36.2 us)
Async XLA Ops:
  6.5 51.2 %all-gather.4.cloned.1.call-start = ((), (), s32[]{:S(2)}) async-start(), calls=%async_computation | async-start | bytes 2621440 | tf_op jit(solution)/shard_map/all_gather | solution.py:47
  8.9 95.0 %all-gather.8.cloned.1.call-start = ((), (), s32[]{:S(2)}) async-start(), calls=%async_computation.2 | async-start | bytes 2621440 | tf_op jit(solution)/shard_map/all_gather | solution.py:47
  9.0 20.8 %collective-permute-start = (bf16[192,2048]{1,0:T(8,128)(2,1)}, bf16[192,2048]{1,0:T(8,128)(2,1)S(1)}, u32[]{:S(2)}, u32[]{:S(2)}) collective-permute-start(bf16[192,2048]{1,0:T(8,128)(2,1)} %param.6), channel_id=1, source_target_pairs={{0,2},{2,0},{1,3},{3,1},{4,6},{6,4},{5,7},{7,5},{8,10},{10,8},{9,1... | collective-permute-start | bytes 2359304 | tf_op jit(solution)/shard_map/ppermute | solution.py:34
  13.1 155.3 %all-gather.6.cloned.1.call-start = ((), (), s32[]{:S(2)}) async-start(), calls=%async_computation.1 | async-start | bytes 2621440 | tf_op jit(solution)/shard_map/all_gather | solution.py:47
  30.0 3.6 %collective-permute-start.1 = (bf16[384,2048]{1,0:T(8,128)(2,1)S(1)}, bf16[384,2048]{1,0:T(8,128)(2,1)}, u32[]{:S(2)}, u32[]{:S(2)}) collective-permute-start(bf16[384,2048]{1,0:T(8,128)(2,1)S(1)} %pad_maximum_fusion), channel_id=1, source_target_pairs={{0,1},{1,0},{2,3},{3,2},{4,5},{5,4},{6,7},{7,6},{8,9},{9,8},{10,11... | collective-permute-start | bytes 4718600 | tf_op jit(solution)/shard_map/ppermute | solution.py:34
  62.0 52.3 %collective-permute-start.2 = (bf16[3072,256]{1,0:T(8,128)(2,1)}, bf16[3072,256]{1,0:T(8,128)(2,1)}, u32[]{:S(2)}, u32[]{:S(2)}) collective-permute-start(bf16[3072,256]{1,0:T(8,128)(2,1)} %slice.28), channel_id=1, source_target_pairs={{0,16},{16,0},{1,17},{17,1},{2,18},{18,2},{3,19},{19,3},{4,20},{20... | collective-permute-start | bytes 4718600 | tf_op jit(solution)/shard_map/ppermute | solution.py:51
  107.2 36.2 %collective-permute-start.9 = (bf16[3072,256]{1,0:T(8,128)(2,1)S(1)}, bf16[3072,256]{1,0:T(8,128)(2,1)S(1)}, u32[]{:S(2)}, u32[]{:S(2)}) collective-permute-start(bf16[3072,256]{1,0:T(8,128)(2,1)S(1)} %slice.29), channel_id=1, source_target_pairs={{0,16},{16,0},{1,17},{17,1},{2,18},{18,2},{3,19},{19,3},{4,20},{20... | collective-permute-start | bytes 4718600 | tf_op jit(solution)/shard_map/ppermute | solution.py:51
  111.7 31.8 %copy-start.2 = (bf16[384,4096]{1,0:T(8,128)(2,1)}, bf16[384,4096]{1,0:T(8,128)(2,1)S(1)}, u32[]{:S(2)}) copy-start(bf16[384,4096]{1,0:T(8,128)(2,1)S(1)} %fusion.6) | copy-start | bytes 9437188
  114.3 29.1 %copy-start.12 = (bf16[1024,256]{1,0:T(8,128)(2,1)S(1)}, bf16[1024,256]{1,0:T(8,128)(2,1)}, u32[]{:S(2)}) copy-start(bf16[1024,256]{1,0:T(8,128)(2,1)} %get-tuple-element.14) | copy-start | bytes 1572868
  117.1 27.6 %copy-start.6 = (bf16[384,256]{0,1:T(8,128)(2,1)}, bf16[384,256]{0,1:T(8,128)(2,1)S(1)}, u32[]{:S(2)}) copy-start(bf16[384,256]{0,1:T(8,128)(2,1)S(1)} %fusion.42) | copy-start | bytes 589828
  117.9 34.5 %collective-permute-start.3 = (bf16[384,512]{0,1:T(8,128)(2,1)}, bf16[384,512]{0,1:T(8,128)(2,1)}, u32[]{:S(2)}, u32[]{:S(2)}) collective-permute-start(bf16[384,512]{0,1:T(8,128)(2,1)} %pad_maximum_fusion.3), channel_id=1, source_target_pairs={{4,0},{8,4},{12,8},{5,1},{9,5},{13,9},{6,2},{10,6},{14,10},{7,3},{... | collective-permute-start | bytes 1179656 | tf_op jit(solution)/shard_map/ppermute | solution.py:22
  119.2 34.8 %collective-permute-start.4 = (bf16[384,512]{0,1:T(8,128)(2,1)}, bf16[384,512]{0,1:T(8,128)(2,1)}, u32[]{:S(2)}, u32[]{:S(2)}) collective-permute-start(bf16[384,512]{0,1:T(8,128)(2,1)} %pad_maximum_fusion.3), channel_id=1, source_target_pairs={{0,4},{4,8},{8,12},{1,5},{5,9},{9,13},{2,6},{6,10},{10,14},{3,7},{... | collective-permute-start | bytes 1179656 | tf_op jit(solution)/shard_map/ppermute | solution.py:23
  145.6 20.1 %collective-permute-start.10 = (bf16[384,512]{0,1:T(8,128)(2,1)}, bf16[384,512]{0,1:T(8,128)(2,1)}, u32[]{:S(2)}, u32[]{:S(2)}) collective-permute-start(bf16[384,512]{0,1:T(8,128)(2,1)} %pad_maximum_fusion.4), channel_id=1, source_target_pairs={{4,0},{8,4},{12,8},{5,1},{9,5},{13,9},{6,2},{10,6},{14,10},{7,3},{... | collective-permute-start | bytes 1179656 | tf_op jit(solution)/shard_map/ppermute | solution.py:22
  146.9 20.1 %collective-permute-start.11 = (bf16[384,512]{0,1:T(8,128)(2,1)}, bf16[384,512]{0,1:T(8,128)(2,1)}, u32[]{:S(2)}, u32[]{:S(2)}) collective-permute-start(bf16[384,512]{0,1:T(8,128)(2,1)} %pad_maximum_fusion.4), channel_id=1, source_target_pairs={{0,4},{4,8},{8,12},{1,5},{5,9},{9,13},{2,6},{6,10},{10,14},{3,7},{... | collective-permute-start | bytes 1179656 | tf_op jit(solution)/shard_map/ppermute | solution.py:23
  152.4 23.1 %collective-permute-start.7 = (bf16[384,512]{0,1:T(8,128)(2,1)}, bf16[384,512]{0,1:T(8,128)(2,1)}, u32[]{:S(2)}, u32[]{:S(2)}) collective-permute-start(bf16[384,512]{0,1:T(8,128)(2,1)} %collective-permute-done.3), channel_id=1, source_target_pairs={{4,0},{8,4},{5,1},{9,5},{6,2},{10,6},{7,3},{11,7},{20,16},{24,20},... | collective-permute-start | bytes 1179656 | tf_op jit(solution)/shard_map/ppermute | solution.py:22
  154.0 23.0 %collective-permute-start.5 = (bf16[384,512]{0,1:T(8,128)(2,1)}, bf16[384,512]{0,1:T(8,128)(2,1)}, u32[]{:S(2)}, u32[]{:S(2)}) collective-permute-start(bf16[384,512]{0,1:T(8,128)(2,1)} %collective-permute-done.4), channel_id=1, source_target_pairs={{4,8},{8,12},{5,9},{9,13},{6,10},{10,14},{7,11},{11,15},{20,24},{2... | collective-permute-start | bytes 1179656 | tf_op jit(solution)/shard_map/ppermute | solution.py:23
  165.7 16.6 %collective-permute-start.14 = (bf16[384,512]{0,1:T(8,128)(2,1)}, bf16[384,512]{0,1:T(8,128)(2,1)}, u32[]{:S(2)}, u32[]{:S(2)}) collective-permute-start(bf16[384,512]{0,1:T(8,128)(2,1)} %collective-permute-done.10), channel_id=1, source_target_pairs={{4,0},{8,4},{5,1},{9,5},{6,2},{10,6},{7,3},{11,7},{20,16},{24,20},... | collective-permute-start | bytes 1179656 | tf_op jit(solution)/shard_map/ppermute | solution.py:22
  167.0 16.5 %collective-permute-start.12 = (bf16[384,512]{0,1:T(8,128)(2,1)}, bf16[384,512]{0,1:T(8,128)(2,1)}, u32[]{:S(2)}, u32[]{:S(2)}) collective-permute-start(bf16[384,512]{0,1:T(8,128)(2,1)} %collective-permute-done.11), channel_id=1, source_target_pairs={{4,8},{8,12},{5,9},{9,13},{6,10},{10,14},{7,11},{11,15},{20,24},{2... | collective-permute-start | bytes 1179656 | tf_op jit(solution)/shard_map/ppermute | solution.py:23
  172.8 36.1 %collective-permute-start.16 = (bf16[3072,256]{1,0:T(8,128)(2,1)}, bf16[3072,256]{1,0:T(8,128)(2,1)}, u32[]{:S(2)}, u32[]{:S(2)}) collective-permute-start(bf16[3072,256]{1,0:T(8,128)(2,1)} %slice.26), channel_id=1, source_target_pairs={{0,16},{16,0},{1,17},{17,1},{2,18},{18,2},{3,19},{19,3},{4,20},{20... | collective-permute-start | bytes 4718600 | tf_op jit(solution)/shard_map/ppermute | solution.py:51
  175.5 25.4 %copy-start.7 = (bf16[384,256]{0,1:T(8,128)(2,1)S(1)}, bf16[384,256]{0,1:T(8,128)(2,1)}, u32[]{:S(2)}) copy-start(bf16[384,256]{0,1:T(8,128)(2,1)} %copy-done.6) | copy-start | bytes 589828
  175.5 18.1 %collective-permute-start.8 = (bf16[384,512]{0,1:T(8,128)(2,1)}, bf16[384,512]{0,1:T(8,128)(2,1)S(1)}, u32[]{:S(2)}, u32[]{:S(2)}) collective-permute-start(bf16[384,512]{0,1:T(8,128)(2,1)} %collective-permute-done.7), channel_id=1, source_target_pairs={{4,0},{5,1},{6,2},{7,3},{20,16},{21,17},{22,18},{23,19}} | collective-permute-start | bytes 1179656 | tf_op jit(solution)/shard_map/ppermute | solution.py:22
  177.0 22.9 %collective-permute-start.6 = (bf16[384,512]{0,1:T(8,128)(2,1)}, bf16[384,512]{0,1:T(8,128)(2,1)S(1)}, u32[]{:S(2)}, u32[]{:S(2)}) collective-permute-start(bf16[384,512]{0,1:T(8,128)(2,1)} %collective-permute-done.5), channel_id=1, source_target_pairs={{8,12},{9,13},{10,14},{11,15},{24,28},{25,29},{26,30},{27,31}} | collective-permute-start | bytes 1179656 | tf_op jit(solution)/shard_map/ppermute | solution.py:23
  182.2 17.6 %collective-permute-start.15 = (bf16[384,512]{0,1:T(8,128)(2,1)}, bf16[384,512]{0,1:T(8,128)(2,1)S(1)}, u32[]{:S(2)}, u32[]{:S(2)}) collective-permute-start(bf16[384,512]{0,1:T(8,128)(2,1)} %collective-permute-done.14), channel_id=1, source_target_pairs={{4,0},{5,1},{6,2},{7,3},{20,16},{21,17},{22,18},{23,19}} | collective-permute-start | bytes 1179656 | tf_op jit(solution)/shard_map/ppermute | solution.py:22
  183.5 17.6 %collective-permute-start.13 = (bf16[384,512]{0,1:T(8,128)(2,1)}, bf16[384,512]{0,1:T(8,128)(2,1)S(1)}, u32[]{:S(2)}, u32[]{:S(2)}) collective-permute-start(bf16[384,512]{0,1:T(8,128)(2,1)} %collective-permute-done.12), channel_id=1, source_target_pairs={{8,12},{9,13},{10,14},{11,15},{24,28},{25,29},{26,30},{27,31}} | collective-permute-start | bytes 1179656 | tf_op jit(solution)/shard_map/ppermute | solution.py:23
  (9 other events, 87.7 us)
Sparse Core Ops, SparseCore 0:
  9.0 48.6 all-gather.3
  59.3 44.6 all-gather.7
  105.6 56.1 all-gather.5

commit v24 on v8

--- a/solution.py
+++ b/solution.py
@@ -42,8 +42,9 @@
         return [lax.all_gather(weight, "seq", axis=0, tiled=True)]
     rows, half = weight.shape[0], weight.shape[1] // 2
     group = lax.axis_index("groups")
-    own = lax.dynamic_slice_in_dim(weight, group * half, half, axis=1)
-    kept = lax.dynamic_slice_in_dim(weight, (1 - group) * half, half, axis=1)
+    first = group == 0
+    own = jnp.where(first, weight[:, :half], weight[:, half:])
+    kept = jnp.where(first, weight[:, half:], weight[:, :half])
     own = lax.all_gather(own, "seq", axis=0, tiled=True)
     own = jnp.roll(own, -lax.axis_index("seq") * rows, axis=0)
     if after is not None:

time: 227 us -> 227 us (level)
  other arithmetic: 25.4 us -> 30 us
  local copies, waits for them, and re-layouts: 7.56 us -> 3 us
    select_n x0 -> x3, other arithmetic: none -> 4.56 us  [full_columns(): kept = jnp.where(first, weight[:, half:], weight[:, :half])]
    dynamic_slice x3 -> x0, local copies, waits for them, and re-layouts: 4.56 us -> none  [full_columns(): kept = lax.dynamic_slice_in_dim(weight, (1 - group) * half, half, axis=1)]
where the time goes in v24:
time: 227 us; the launch traced here: 223 us
  waiting for transfers between devices  130 us (57%)
  starting transfers between devices  30.7 us (14%)
  other arithmetic  30 us (13%)
  matrix products  15.7 us (7%)
  between operations  13.5 us (6%)
  local copies, waits for them, and re-layouts  3 us (1%)
    all_gather x3, waiting for transfers between devices, full_columns(): own = lax.all_gather(own, 'seq', axis=0, tiled=True)  60.6 us
    ppermute x6, waiting for transfers between devices, line_gather(): lax.ppermute(from_right[-1], 'seq', [(j, j - 1) for j in range(1, n - k +...  28.3 us
    ppermute x3, waiting for transfers between devices, full_columns(): other = lax.ppermute(own[rows:], 'groups', [(0, 1), (1, 0)])  22.4 us
    ppermute x2, waiting for transfers between devices, swap_gather(): other = lax.ppermute(piece, axis, [(0, 1), (1, 0)])  18.9 us
    ppermute x6, starting transfers between devices, line_gather(): lax.ppermute(from_left[-1], 'seq', [(j, j + 1) for j in range(k - 1, n -...  15 us
    dot_general x6, matrix products, project(): jnp.dot(block, piece, preferred_element_type=jnp.float32)  11.7 us
    concatenate x3, other arithmetic, full_columns(): own = jnp.roll(own, -lax.axis_index('seq') * rows, axis=0)  9.16 us
    ppermute x6, starting transfers between devices, line_gather(): lax.ppermute(from_right[-1], 'seq', [(j, j - 1) for j in range(1, n - k +...  8.09 us
  transfers between devices with their start and end apart: 20, of which 10 were waited for; matrix products, arithmetic and copies ran while one was open for 17% of the time, Pallas kernels for 0%

profile of v24, /device:TPU:0, one launch (start us, length us, event | category | flops | bytes accessed | tf_op | source)
XLA Modules:
  0.0 223.3 jit_solution(13073176551306748440)
XLA Ops:
  6.5 2.4 %broadcast_select_fusion.8 = (bf16[1024,256]{1,0:T(8,128)(2,1)}, bf16[1024,256]{1,0:T(8,128)(2,1)}) fusion(pred[]{:T(512)S(6)} %eq.19, bf16[1024,512]{1,0:T(8,128)(2,1)} %param.9), kind=kLoop, calls=%fused_computation.73 | loop fusion | flops 524288 | bytes 2097153 | tf_op jit(solution)/shard_map/jit(_where)/select_n | solution.py:47
  9.0 3.0 %collective-permute-start = (bf16[192,2048]{1,0:T(8,128)(2,1)}, bf16[192,2048]{1,0:T(8,128)(2,1)S(1)}, u32[]{:S(2)}, u32[]{:S(2)}) collective-permute-start(bf16[192,2048]{1,0:T(8,128)(2,1)} %param.6), channel_id=1, source_target_pairs={{0,2},{2,0},{1,3},{3,1},{4,6},{6,4},{5,7},{7,5},{8,10},{10,8},{9,1... | collective-permute-start | bytes 2359304 | tf_op jit(solution)/shard_map/ppermute | solution.py:34
  13.2 16.6 %collective-permute-done = bf16[192,2048]{1,0:T(8,128)(2,1)S(1)} collective-permute-done((bf16[192,2048]{1,0:T(8,128)(2,1)}, bf16[192,2048]{1,0:T(8,128)(2,1)S(1)}, u32[]{:S(2)}, u32[]{:S(2)}) %collective-permute-start) | collective-permute-done | bytes 786464 | tf_op jit(solution)/shard_map/ppermute | solution.py:34
  31.3 2.4 %collective-permute-done.1 = bf16[384,2048]{1,0:T(8,128)(2,1)} collective-permute-done((bf16[384,2048]{1,0:T(8,128)(2,1)S(1)}, bf16[384,2048]{1,0:T(8,128)(2,1)}, u32[]{:S(2)}, u32[]{:S(2)}) %collective-permute-start.1) | collective-permute-done | bytes 1572896 | tf_op jit(solution)/shard_map/ppermute | solution.py:34
  33.6 4.0 %broadcast_select_fusion = (bf16[384,2048]{1,0:T(8,128)(2,1)}, bf16[384,2048]{1,0:T(8,128)(2,1)}) fusion(bf16[384,2048]{1,0:T(8,128)(2,1)} %collective-permute-done.1, pred[]{:T(512)S(6)} %eq.17, bf16[192,2048]{1,0:T(8,128)(2,1)S(1)} %get-tuple-element.11, bf16[192,2048]{1,0:T(8,128)(2,1)S(1)} %get-tuple-element.10), kind=kLoop, calls=%fused_computation.45 | loop fusion | flops 4718592 | bytes 6291457 | tf_op jit(solution)/shard_map/jit(_where)/select_n | solution.py:36
  37.6 20.1 %all-gather.4.cloned.1.call-done = bf16[4096,256]{1,0:T(8,128)(2,1)} async-done(((bf16[1024,256]{1,0:T(8,128)(2,1)}), bf16[4096,256]{1,0:T(8,128)(2,1)}) %all-gather.4.cloned.1.call-update) | async-done | bytes 2097168 | tf_op jit(solution)/shard_map/all_gather | solution.py:48
  57.7 3.0 %fusion.17 = bf16[4096,256]{1,0:T(8,128)(2,1)S(1)} fusion(s32[]{:T(128)S(6)} %select_n.121, bf16[4096,256]{1,0:T(8,128)(2,1)} %all-gather.4.cloned.1.call-done), kind=kLoop, calls=%fused_computation.29 | loop fusion | flops 4194304 | bytes 4194308 | tf_op jit(solution)/shard_map/jit(_roll_dynamic)/concatenate | solution.py:49
  63.4 40.5 %all-gather.8.cloned.1.call-done = bf16[4096,256]{1,0:T(8,128)(2,1)} async-done(((bf16[1024,256]{1,0:T(8,128)(2,1)}), bf16[4096,256]{1,0:T(8,128)(2,1)}) %all-gather.8.cloned.1.call-update) | async-done | bytes 2097168 | tf_op jit(solution)/shard_map/all_gather | solution.py:48
  104.0 3.2 %fusion.15 = bf16[4096,256]{1,0:T(8,128)(2,1)S(1)} fusion(s32[]{:T(128)S(6)} %select_n.121, bf16[4096,256]{1,0:T(8,128)(2,1)} %all-gather.8.cloned.1.call-done), kind=kLoop, calls=%fused_computation.27 | loop fusion | flops 4194304 | bytes 4194308 | tf_op jit(solution)/shard_map/jit(_roll_dynamic)/concatenate | solution.py:49
  107.3 1.5 collective-permute-start.9
  108.8 2.9 %fusion.6 = bf16[384,4096]{1,0:T(8,128)(2,1)S(1)} fusion(s32[]{:T(128)S(6)} %select_n.121, bf16[384,2048]{1,0:T(8,128)(2,1)S(1)} %copy-done.1, bf16[384,2048]{1,0:T(8,128)(2,1)S(1)} %copy-done), kind=kLoop, calls=%fused_computation.20 | loop fusion | flops 12582912 | bytes 6291460 | tf_op jit(solution)/shard_map/jit(_roll_dynamic)/concatenate | solution.py:64
  114.3 2.8 %fusion.42 = bf16[384,256]{0,1:T(8,128)(2,1)S(1)} fusion(bf16[384,4096]{1,0:T(8,128)(2,1)S(1)} %fusion.6, bf16[3072,256]{1,0:T(8,128)(2,1)} %collective-permute-done.2, bf16[1024,256]{1,0:T(8,128)(2,1)S(1)} %copy-done.11), kind=kOutput, calls=%fused_computation.51 | convolution fusion | flops 809598976 | bytes 5439488 | tf_op jit(solution)/shard_map/dot_general | solution.py:68
  119.2 5.3 %collective-permute-start.4 = (bf16[384,512]{0,1:T(8,128)(2,1)}, bf16[384,512]{0,1:T(8,128)(2,1)}, u32[]{:S(2)}, u32[]{:S(2)}) collective-permute-start(bf16[384,512]{0,1:T(8,128)(2,1)} %pad_maximum_fusion.3), channel_id=1, source_target_pairs={{0,4},{4,8},{8,12},{1,5},{5,9},{9,13},{2,6},{6,10},{10,14},{3,7},{... | collective-permute-start | bytes 1179656 | tf_op jit(solution)/shard_map/ppermute | solution.py:23
  124.5 18.9 %collective-permute-done.9 = bf16[3072,256]{1,0:T(8,128)(2,1)S(1)} collective-permute-done((bf16[3072,256]{1,0:T(8,128)(2,1)S(1)}, bf16[3072,256]{1,0:T(8,128)(2,1)S(1)}, u32[]{:S(2)}, u32[]{:S(2)}) %collective-permute-start.9) | collective-permute-done | bytes 1572896 | tf_op jit(solution)/shard_map/ppermute | solution.py:52
  146.9 5.3 %collective-permute-start.11 = (bf16[384,512]{0,1:T(8,128)(2,1)}, bf16[384,512]{0,1:T(8,128)(2,1)}, u32[]{:S(2)}, u32[]{:S(2)}) collective-permute-start(bf16[384,512]{0,1:T(8,128)(2,1)} %pad_maximum_fusion.4), channel_id=1, source_target_pairs={{0,4},{4,8},{8,12},{1,5},{5,9},{9,13},{2,6},{6,10},{10,14},{3,7},{... | collective-permute-start | bytes 1179656 | tf_op jit(solution)/shard_map/ppermute | solution.py:23
  152.2 1.5 collective-permute-start.7
  153.8 1.5 collective-permute-start.5
  155.3 10.4 %collective-permute-done.10 = bf16[384,512]{0,1:T(8,128)(2,1)} collective-permute-done((bf16[384,512]{0,1:T(8,128)(2,1)}, bf16[384,512]{0,1:T(8,128)(2,1)}, u32[]{:S(2)}, u32[]{:S(2)}) %collective-permute-start.10) | collective-permute-done | bytes 393248 | tf_op jit(solution)/shard_map/ppermute | solution.py:22
  168.4 3.0 %fusion.16 = bf16[4096,256]{1,0:T(8,128)(2,1)S(1)} fusion(s32[]{:T(128)S(6)} %select_n.121, bf16[4096,256]{1,0:T(8,128)(2,1)} %all-gather.6.cloned.1.call-done), kind=kLoop, calls=%fused_computation.28 | loop fusion | flops 4194304 | bytes 4194308 | tf_op jit(solution)/shard_map/jit(_roll_dynamic)/concatenate | solution.py:49
  177.7 4.5 %collective-permute-done.14 = bf16[384,512]{0,1:T(8,128)(2,1)} collective-permute-done((bf16[384,512]{0,1:T(8,128)(2,1)}, bf16[384,512]{0,1:T(8,128)(2,1)}, u32[]{:S(2)}, u32[]{:S(2)}) %collective-permute-start.14) | collective-permute-done | bytes 393248 | tf_op jit(solution)/shard_map/ppermute | solution.py:22
  186.3 7.3 %collective-permute-done.8 = bf16[384,512]{0,1:T(8,128)(2,1)S(1)} collective-permute-done((bf16[384,512]{0,1:T(8,128)(2,1)}, bf16[384,512]{0,1:T(8,128)(2,1)S(1)}, u32[]{:S(2)}, u32[]{:S(2)}) %collective-permute-start.8) | collective-permute-done | bytes 393248 | tf_op jit(solution)/shard_map/ppermute | solution.py:22
  193.7 6.1 %collective-permute-done.15 = bf16[384,512]{0,1:T(8,128)(2,1)S(1)} collective-permute-done((bf16[384,512]{0,1:T(8,128)(2,1)}, bf16[384,512]{0,1:T(8,128)(2,1)S(1)}, u32[]{:S(2)}, u32[]{:S(2)}) %collective-permute-start.15) | collective-permute-done | bytes 393248 | tf_op jit(solution)/shard_map/ppermute | solution.py:22
  205.4 3.5 %collective-permute-done.16 = bf16[3072,256]{1,0:T(8,128)(2,1)} collective-permute-done((bf16[3072,256]{1,0:T(8,128)(2,1)}, bf16[3072,256]{1,0:T(8,128)(2,1)}, u32[]{:S(2)}, u32[]{:S(2)}) %collective-permute-start.16) | collective-permute-done | bytes 1572896 | tf_op jit(solution)/shard_map/ppermute | solution.py:52
  208.9 3.8 %fusion.36 = bf16[384,256]{0,1:T(8,128)(2,1)S(1)} fusion(bf16[384,4096]{1,0:T(8,128)(2,1)} %copy-done.2, bf16[3072,256]{1,0:T(8,128)(2,1)} %collective-permute-done.16, bf16[1024,256]{1,0:T(8,128)(2,1)} %get-tuple-element.12), kind=kOutput, calls=%fused_computation.49 | convolution fusion | flops 809598976 | bytes 5439488 | tf_op jit(solution)/shard_map/dot_general | solution.py:68
  (83 shorter events, 36.3 us)
Async XLA Ops:
  6.5 51.2 %all-gather.4.cloned.1.call-start = ((), (), s32[]{:S(2)}) async-start(), calls=%async_computation | async-start | bytes 2621440 | tf_op jit(solution)/shard_map/all_gather | solution.py:48
  8.9 95.0 %all-gather.8.cloned.1.call-start = ((), (), s32[]{:S(2)}) async-start(), calls=%async_computation.2 | async-start | bytes 2621440 | tf_op jit(solution)/shard_map/all_gather | solution.py:48
  9.0 20.8 %collective-permute-start = (bf16[192,2048]{1,0:T(8,128)(2,1)}, bf16[192,2048]{1,0:T(8,128)(2,1)S(1)}, u32[]{:S(2)}, u32[]{:S(2)}) collective-permute-start(bf16[192,2048]{1,0:T(8,128)(2,1)} %param.6), channel_id=1, source_target_pairs={{0,2},{2,0},{1,3},{3,1},{4,6},{6,4},{5,7},{7,5},{8,10},{10,8},{9,1... | collective-permute-start | bytes 2359304 | tf_op jit(solution)/shard_map/ppermute | solution.py:34
  13.1 155.3 %all-gather.6.cloned.1.call-start = ((), (), s32[]{:S(2)}) async-start(), calls=%async_computation.1 | async-start | bytes 2621440 | tf_op jit(solution)/shard_map/all_gather | solution.py:48
  30.0 3.6 %collective-permute-start.1 = (bf16[384,2048]{1,0:T(8,128)(2,1)S(1)}, bf16[384,2048]{1,0:T(8,128)(2,1)}, u32[]{:S(2)}, u32[]{:S(2)}) collective-permute-start(bf16[384,2048]{1,0:T(8,128)(2,1)S(1)} %pad_maximum_fusion), channel_id=1, source_target_pairs={{0,1},{1,0},{2,3},{3,2},{4,5},{5,4},{6,7},{7,6},{8,9},{9,8},{10,11... | collective-permute-start | bytes 4718600 | tf_op jit(solution)/shard_map/ppermute | solution.py:34
  62.0 52.3 %collective-permute-start.2 = (bf16[3072,256]{1,0:T(8,128)(2,1)}, bf16[3072,256]{1,0:T(8,128)(2,1)}, u32[]{:S(2)}, u32[]{:S(2)}) collective-permute-start(bf16[3072,256]{1,0:T(8,128)(2,1)} %slice.58), channel_id=1, source_target_pairs={{0,16},{16,0},{1,17},{17,1},{2,18},{18,2},{3,19},{19,3},{4,20},{20... | collective-permute-start | bytes 4718600 | tf_op jit(solution)/shard_map/ppermute | solution.py:52
  107.3 36.2 %collective-permute-start.9 = (bf16[3072,256]{1,0:T(8,128)(2,1)S(1)}, bf16[3072,256]{1,0:T(8,128)(2,1)S(1)}, u32[]{:S(2)}, u32[]{:S(2)}) collective-permute-start(bf16[3072,256]{1,0:T(8,128)(2,1)S(1)} %slice.59), channel_id=1, source_target_pairs={{0,16},{16,0},{1,17},{17,1},{2,18},{18,2},{3,19},{19,3},{4,20},{20... | collective-permute-start | bytes 4718600 | tf_op jit(solution)/shard_map/ppermute | solution.py:52
  111.7 31.8 %copy-start.2 = (bf16[384,4096]{1,0:T(8,128)(2,1)}, bf16[384,4096]{1,0:T(8,128)(2,1)S(1)}, u32[]{:S(2)}) copy-start(bf16[384,4096]{1,0:T(8,128)(2,1)S(1)} %fusion.6) | copy-start | bytes 9437188
  114.3 29.1 %copy-start.12 = (bf16[1024,256]{1,0:T(8,128)(2,1)S(1)}, bf16[1024,256]{1,0:T(8,128)(2,1)}, u32[]{:S(2)}) copy-start(bf16[1024,256]{1,0:T(8,128)(2,1)} %get-tuple-element.14) | copy-start | bytes 1572868
  117.1 27.6 %copy-start.6 = (bf16[384,256]{0,1:T(8,128)(2,1)}, bf16[384,256]{0,1:T(8,128)(2,1)S(1)}, u32[]{:S(2)}) copy-start(bf16[384,256]{0,1:T(8,128)(2,1)S(1)} %fusion.42) | copy-start | bytes 589828
  117.9 34.3 %collective-permute-start.3 = (bf16[384,512]{0,1:T(8,128)(2,1)}, bf16[384,512]{0,1:T(8,128)(2,1)}, u32[]{:S(2)}, u32[]{:S(2)}) collective-permute-start(bf16[384,512]{0,1:T(8,128)(2,1)} %pad_maximum_fusion.3), channel_id=1, source_target_pairs={{4,0},{8,4},{12,8},{5,1},{9,5},{13,9},{6,2},{10,6},{14,10},{7,3},{... | collective-permute-start | bytes 1179656 | tf_op jit(solution)/shard_map/ppermute | solution.py:22
  119.2 34.6 %collective-permute-start.4 = (bf16[384,512]{0,1:T(8,128)(2,1)}, bf16[384,512]{0,1:T(8,128)(2,1)}, u32[]{:S(2)}, u32[]{:S(2)}) collective-permute-start(bf16[384,512]{0,1:T(8,128)(2,1)} %pad_maximum_fusion.3), channel_id=1, source_target_pairs={{0,4},{4,8},{8,12},{1,5},{5,9},{9,13},{2,6},{6,10},{10,14},{3,7},{... | collective-permute-start | bytes 1179656 | tf_op jit(solution)/shard_map/ppermute | solution.py:23
  145.6 20.1 %collective-permute-start.10 = (bf16[384,512]{0,1:T(8,128)(2,1)}, bf16[384,512]{0,1:T(8,128)(2,1)}, u32[]{:S(2)}, u32[]{:S(2)}) collective-permute-start(bf16[384,512]{0,1:T(8,128)(2,1)} %pad_maximum_fusion.4), channel_id=1, source_target_pairs={{4,0},{8,4},{12,8},{5,1},{9,5},{13,9},{6,2},{10,6},{14,10},{7,3},{... | collective-permute-start | bytes 1179656 | tf_op jit(solution)/shard_map/ppermute | solution.py:22
  146.9 20.1 %collective-permute-start.11 = (bf16[384,512]{0,1:T(8,128)(2,1)}, bf16[384,512]{0,1:T(8,128)(2,1)}, u32[]{:S(2)}, u32[]{:S(2)}) collective-permute-start(bf16[384,512]{0,1:T(8,128)(2,1)} %pad_maximum_fusion.4), channel_id=1, source_target_pairs={{0,4},{4,8},{8,12},{1,5},{5,9},{9,13},{2,6},{6,10},{10,14},{3,7},{... | collective-permute-start | bytes 1179656 | tf_op jit(solution)/shard_map/ppermute | solution.py:23
  152.2 23.3 %collective-permute-start.7 = (bf16[384,512]{0,1:T(8,128)(2,1)}, bf16[384,512]{0,1:T(8,128)(2,1)}, u32[]{:S(2)}, u32[]{:S(2)}) collective-permute-start(bf16[384,512]{0,1:T(8,128)(2,1)} %collective-permute-done.3), channel_id=1, source_target_pairs={{4,0},{8,4},{5,1},{9,5},{6,2},{10,6},{7,3},{11,7},{20,16},{24,20},... | collective-permute-start | bytes 1179656 | tf_op jit(solution)/shard_map/ppermute | solution.py:22
  153.8 23.2 %collective-permute-start.5 = (bf16[384,512]{0,1:T(8,128)(2,1)}, bf16[384,512]{0,1:T(8,128)(2,1)}, u32[]{:S(2)}, u32[]{:S(2)}) collective-permute-start(bf16[384,512]{0,1:T(8,128)(2,1)} %collective-permute-done.4), channel_id=1, source_target_pairs={{4,8},{8,12},{5,9},{9,13},{6,10},{10,14},{7,11},{11,15},{20,24},{2... | collective-permute-start | bytes 1179656 | tf_op jit(solution)/shard_map/ppermute | solution.py:23
  165.7 16.6 %collective-permute-start.14 = (bf16[384,512]{0,1:T(8,128)(2,1)}, bf16[384,512]{0,1:T(8,128)(2,1)}, u32[]{:S(2)}, u32[]{:S(2)}) collective-permute-start(bf16[384,512]{0,1:T(8,128)(2,1)} %collective-permute-done.10), channel_id=1, source_target_pairs={{4,0},{8,4},{5,1},{9,5},{6,2},{10,6},{7,3},{11,7},{20,16},{24,20},... | collective-permute-start | bytes 1179656 | tf_op jit(solution)/shard_map/ppermute | solution.py:22
  167.0 16.5 %collective-permute-start.12 = (bf16[384,512]{0,1:T(8,128)(2,1)}, bf16[384,512]{0,1:T(8,128)(2,1)}, u32[]{:S(2)}, u32[]{:S(2)}) collective-permute-start(bf16[384,512]{0,1:T(8,128)(2,1)} %collective-permute-done.11), channel_id=1, source_target_pairs={{4,8},{8,12},{5,9},{9,13},{6,10},{10,14},{7,11},{11,15},{20,24},{2... | collective-permute-start | bytes 1179656 | tf_op jit(solution)/shard_map/ppermute | solution.py:23
  172.8 36.1 %collective-permute-start.16 = (bf16[3072,256]{1,0:T(8,128)(2,1)}, bf16[3072,256]{1,0:T(8,128)(2,1)}, u32[]{:S(2)}, u32[]{:S(2)}) collective-permute-start(bf16[3072,256]{1,0:T(8,128)(2,1)} %slice.56), channel_id=1, source_target_pairs={{0,16},{16,0},{1,17},{17,1},{2,18},{18,2},{3,19},{19,3},{4,20},{20... | collective-permute-start | bytes 4718600 | tf_op jit(solution)/shard_map/ppermute | solution.py:52
  175.5 25.4 %copy-start.7 = (bf16[384,256]{0,1:T(8,128)(2,1)S(1)}, bf16[384,256]{0,1:T(8,128)(2,1)}, u32[]{:S(2)}) copy-start(bf16[384,256]{0,1:T(8,128)(2,1)} %copy-done.6) | copy-start | bytes 589828
  175.6 18.1 %collective-permute-start.8 = (bf16[384,512]{0,1:T(8,128)(2,1)}, bf16[384,512]{0,1:T(8,128)(2,1)S(1)}, u32[]{:S(2)}, u32[]{:S(2)}) collective-permute-start(bf16[384,512]{0,1:T(8,128)(2,1)} %collective-permute-done.7), channel_id=1, source_target_pairs={{4,0},{5,1},{6,2},{7,3},{20,16},{21,17},{22,18},{23,19}} | collective-permute-start | bytes 1179656 | tf_op jit(solution)/shard_map/ppermute | solution.py:22
  177.0 22.9 %collective-permute-start.6 = (bf16[384,512]{0,1:T(8,128)(2,1)}, bf16[384,512]{0,1:T(8,128)(2,1)S(1)}, u32[]{:S(2)}, u32[]{:S(2)}) collective-permute-start(bf16[384,512]{0,1:T(8,128)(2,1)} %collective-permute-done.5), channel_id=1, source_target_pairs={{8,12},{9,13},{10,14},{11,15},{24,28},{25,29},{26,30},{27,31}} | collective-permute-start | bytes 1179656 | tf_op jit(solution)/shard_map/ppermute | solution.py:23
  182.2 17.6 %collective-permute-start.15 = (bf16[384,512]{0,1:T(8,128)(2,1)}, bf16[384,512]{0,1:T(8,128)(2,1)S(1)}, u32[]{:S(2)}, u32[]{:S(2)}) collective-permute-start(bf16[384,512]{0,1:T(8,128)(2,1)} %collective-permute-done.14), channel_id=1, source_target_pairs={{4,0},{5,1},{6,2},{7,3},{20,16},{21,17},{22,18},{23,19}} | collective-permute-start | bytes 1179656 | tf_op jit(solution)/shard_map/ppermute | solution.py:22
  183.5 17.6 %collective-permute-start.13 = (bf16[384,512]{0,1:T(8,128)(2,1)}, bf16[384,512]{0,1:T(8,128)(2,1)S(1)}, u32[]{:S(2)}, u32[]{:S(2)}) collective-permute-start(bf16[384,512]{0,1:T(8,128)(2,1)} %collective-permute-done.12), channel_id=1, source_target_pairs={{8,12},{9,13},{10,14},{11,15},{24,28},{25,29},{26,30},{27,31}} | collective-permute-start | bytes 1179656 | tf_op jit(solution)/shard_map/ppermute | solution.py:23
  (9 other events, 87.9 us)
Sparse Core Ops, SparseCore 0:
  9.1 48.6 all-gather.3
  59.3 44.6 all-gather.7
  105.6 56.1 all-gather.5

commit v25 on v10

--- a/solution.py
+++ b/solution.py
@@ -42,8 +42,9 @@
         return [lax.all_gather(weight, "seq", axis=0, tiled=True)]
     rows, half = weight.shape[0], weight.shape[1] // 2
     group = lax.axis_index("groups")
-    own = lax.dynamic_slice_in_dim(weight, group * half, half, axis=1)
-    kept = lax.dynamic_slice_in_dim(weight, (1 - group) * half, half, axis=1)
+    first = group == 0
+    own = jnp.where(first, weight[:, :half], weight[:, half:])
+    kept = jnp.where(first, weight[:, half:], weight[:, :half])
     own = lax.all_gather(own, "seq", axis=0, tiled=True)
     own = jnp.roll(own, -lax.axis_index("seq") * rows, axis=0)
     if after is not None:
@@ -106,10 +107,14 @@
         )
         attended = summed / jnp.transpose(running_total)[:, :, None]
         outputs.append(attended.astype(jnp.bfloat16).reshape(tokens_here, count * HD))
-    attended = jnp.concatenate(outputs, axis=1)
     if shared:
-        attended = jnp.roll(attended, lax.axis_index("groups") * (width // 2), axis=1)
-    return attended
+        first_group = lax.axis_index("groups") == 0
+        return jnp.where(
+            first_group,
+            jnp.concatenate(outputs, axis=1),
+            jnp.concatenate(outputs[::-1], axis=1),
+        )
+    return jnp.concatenate(outputs, axis=1)
 
 
 def solution(mesh):

time: 228 us -> 227 us (level)
  local copies, waits for them, and re-layouts: 8.29 us -> 3.03 us
  other arithmetic: 26 us -> 30.3 us
    select_n x0 -> x4, other arithmetic: none -> 5.9 us  [the longest x3 5.06 us: full_columns(): own = jnp.where(first, weight[:, :half], weight[:, half:])]
    dynamic_slice x3 -> x0, local copies, waits for them, and re-layouts: 3.57 us -> none  [full_columns(): own = lax.dynamic_slice_in_dim(weight, group * half, half, axis=1)]
    all_gather x3, waiting for transfers between devices: 58.3 us -> 60.7 us  [full_columns(): own = lax.all_gather(own, 'seq', axis=0, tiled=True)]
where the time goes in v25:
time: 227 us; the launch traced here: 224 us
  waiting for transfers between devices  129 us (57%)
  starting transfers between devices  30.6 us (13%)
  other arithmetic  30.3 us (13%)
  matrix products  17.2 us (8%)
  between operations  13.6 us (6%)
  local copies, waits for them, and re-layouts  3.03 us (1%)
    all_gather x3, waiting for transfers between devices, full_columns(): own = lax.all_gather(own, 'seq', axis=0, tiled=True)  60.7 us
    ppermute x6, waiting for transfers between devices, line_gather(): lax.ppermute(from_right[-1], 'seq', [(j, j - 1) for j in range(1, n - k +...  28.1 us
    ppermute x3, waiting for transfers between devices, full_columns(): other = lax.ppermute(own[rows:], 'groups', [(0, 1), (1, 0)])  22.1 us
    ppermute x2, waiting for transfers between devices, swap_gather(): other = lax.ppermute(piece, axis, [(0, 1), (1, 0)])  18.2 us
    ppermute x6, starting transfers between devices, line_gather(): lax.ppermute(from_left[-1], 'seq', [(j, j + 1) for j in range(k - 1, n -...  14.9 us
    concatenate x3, other arithmetic, full_columns(): own = jnp.roll(own, -lax.axis_index('seq') * rows, axis=0)  9.16 us
    ppermute x6, starting transfers between devices, line_gather(): lax.ppermute(from_right[-1], 'seq', [(j, j - 1) for j in range(1, n - k +...  8.09 us
    dot_general x3, matrix products, product(): jnp.dot(block[:, rows:], other, preferred_element_type=jnp.float32)  6.67 us
  transfers between devices with their start and end apart: 20, of which 10 were waited for; matrix products, arithmetic and copies ran while one was open for 18% of the time, Pallas kernels for 0%

profile of v25, /device:TPU:0, one launch (start us, length us, event | category | flops | bytes accessed | tf_op | source)
XLA Modules:
  0.0 223.9 jit_solution(16806193722740713319)
XLA Ops:
  6.5 2.1 broadcast_select_fusion.6
  8.7 3.0 %collective-permute-start = (bf16[192,2048]{1,0:T(8,128)(2,1)}, bf16[192,2048]{1,0:T(8,128)(2,1)S(1)}, u32[]{:S(2)}, u32[]{:S(2)}) collective-permute-start(bf16[192,2048]{1,0:T(8,128)(2,1)} %param.6), channel_id=1, source_target_pairs={{0,2},{2,0},{1,3},{3,1},{4,6},{6,4},{5,7},{7,5},{8,10},{10,8},{9,1... | collective-permute-start | bytes 2359304 | tf_op jit(solution)/shard_map/ppermute | solution.py:34
  11.7 2.1 broadcast_select_fusion.4
  13.9 15.6 %collective-permute-done = bf16[192,2048]{1,0:T(8,128)(2,1)S(1)} collective-permute-done((bf16[192,2048]{1,0:T(8,128)(2,1)}, bf16[192,2048]{1,0:T(8,128)(2,1)S(1)}, u32[]{:S(2)}, u32[]{:S(2)}) %collective-permute-start) | collective-permute-done | bytes 786464 | tf_op jit(solution)/shard_map/ppermute | solution.py:34
  30.8 2.6 %collective-permute-done.1 = bf16[384,2048]{1,0:T(8,128)(2,1)} collective-permute-done((bf16[384,2048]{1,0:T(8,128)(2,1)S(1)}, bf16[384,2048]{1,0:T(8,128)(2,1)}, u32[]{:S(2)}, u32[]{:S(2)}) %collective-permute-start.1) | collective-permute-done | bytes 1572896 | tf_op jit(solution)/shard_map/ppermute | solution.py:34
  33.4 4.0 %broadcast_select_fusion = (bf16[384,2048]{1,0:T(8,128)(2,1)}, bf16[384,2048]{1,0:T(8,128)(2,1)}) fusion(bf16[384,2048]{1,0:T(8,128)(2,1)} %collective-permute-done.1, pred[]{:T(512)S(6)} %eq.17, bf16[192,2048]{1,0:T(8,128)(2,1)S(1)} %get-tuple-element.11, bf16[192,2048]{1,0:T(8,128)(2,1)S(1)} %get-tuple-element.10), kind=kLoop, calls=%fused_computation.39 | loop fusion | flops 4718592 | bytes 6291457 | tf_op jit(solution)/shard_map/jit(_where)/select_n | solution.py:36
  37.4 20.2 %all-gather.4.cloned.1.call-done = bf16[4096,256]{1,0:T(8,128)(2,1)} async-done(((bf16[1024,256]{1,0:T(8,128)(2,1)}), bf16[4096,256]{1,0:T(8,128)(2,1)}) %all-gather.4.cloned.1.call-update) | async-done | bytes 2097168 | tf_op jit(solution)/shard_map/all_gather | solution.py:48
  57.6 3.0 %fusion.17 = bf16[4096,256]{1,0:T(8,128)(2,1)S(1)} fusion(s32[]{:T(128)S(6)} %select_n.118, bf16[4096,256]{1,0:T(8,128)(2,1)} %all-gather.4.cloned.1.call-done), kind=kLoop, calls=%fused_computation.29 | loop fusion | flops 4194304 | bytes 4194308 | tf_op jit(solution)/shard_map/jit(_roll_dynamic)/concatenate | solution.py:49
  63.4 40.5 %all-gather.8.cloned.1.call-done = bf16[4096,256]{1,0:T(8,128)(2,1)} async-done(((bf16[1024,256]{1,0:T(8,128)(2,1)}), bf16[4096,256]{1,0:T(8,128)(2,1)}) %all-gather.8.cloned.1.call-update) | async-done | bytes 2097168 | tf_op jit(solution)/shard_map/all_gather | solution.py:48
  103.9 3.2 %fusion.15 = bf16[4096,256]{1,0:T(8,128)(2,1)S(1)} fusion(s32[]{:T(128)S(6)} %select_n.118, bf16[4096,256]{1,0:T(8,128)(2,1)} %all-gather.8.cloned.1.call-done), kind=kLoop, calls=%fused_computation.27 | loop fusion | flops 4194304 | bytes 4194308 | tf_op jit(solution)/shard_map/jit(_roll_dynamic)/concatenate | solution.py:49
  108.7 2.9 %fusion.6 = bf16[384,4096]{1,0:T(8,128)(2,1)S(1)} fusion(s32[]{:T(128)S(6)} %select_n.118, bf16[384,2048]{1,0:T(8,128)(2,1)S(1)} %copy-done.1, bf16[384,2048]{1,0:T(8,128)(2,1)S(1)} %copy-done), kind=kLoop, calls=%fused_computation.20 | loop fusion | flops 12582912 | bytes 6291460 | tf_op jit(solution)/shard_map/jit(_roll_dynamic)/concatenate | solution.py:64
  114.2 2.5 %fusion.22 = f32[384,256]{0,1:T(8,128)S(1)} fusion(bf16[3072,256]{1,0:T(8,128)(2,1)} %collective-permute-done.2, bf16[384,4096]{1,0:T(8,128)(2,1)S(1)} %fusion.6), kind=kOutput, calls=%fused_computation.34 | convolution fusion | flops 603979776 | bytes 4325376 | tf_op jit(solution)/shard_map/dot_general | solution.py:71
  119.3 5.3 %collective-permute-start.4 = (bf16[384,512]{0,1:T(8,128)(2,1)}, bf16[384,512]{0,1:T(8,128)(2,1)}, u32[]{:S(2)}, u32[]{:S(2)}) collective-permute-start(bf16[384,512]{0,1:T(8,128)(2,1)} %pad_maximum_fusion.3), channel_id=1, source_target_pairs={{0,4},{4,8},{8,12},{1,5},{5,9},{9,13},{2,6},{6,10},{10,14},{3,7},{... | collective-permute-start | bytes 1179656 | tf_op jit(solution)/shard_map/ppermute | solution.py:23
  124.6 18.7 %collective-permute-done.9 = bf16[3072,256]{1,0:T(8,128)(2,1)S(1)} collective-permute-done((bf16[3072,256]{1,0:T(8,128)(2,1)S(1)}, bf16[3072,256]{1,0:T(8,128)(2,1)S(1)}, u32[]{:S(2)}, u32[]{:S(2)}) %collective-permute-start.9) | collective-permute-done | bytes 1572896 | tf_op jit(solution)/shard_map/ppermute | solution.py:52
  147.0 5.3 %collective-permute-start.11 = (bf16[384,512]{0,1:T(8,128)(2,1)}, bf16[384,512]{0,1:T(8,128)(2,1)}, u32[]{:S(2)}, u32[]{:S(2)}) collective-permute-start(bf16[384,512]{0,1:T(8,128)(2,1)} %pad_maximum_fusion.4), channel_id=1, source_target_pairs={{0,4},{4,8},{8,12},{1,5},{5,9},{9,13},{2,6},{6,10},{10,14},{3,7},{... | collective-permute-start | bytes 1179656 | tf_op jit(solution)/shard_map/ppermute | solution.py:23
  152.4 1.5 collective-permute-start.7
  155.4 10.2 %collective-permute-done.10 = bf16[384,512]{0,1:T(8,128)(2,1)} collective-permute-done((bf16[384,512]{0,1:T(8,128)(2,1)}, bf16[384,512]{0,1:T(8,128)(2,1)}, u32[]{:S(2)}, u32[]{:S(2)}) %collective-permute-start.10) | collective-permute-done | bytes 393248 | tf_op jit(solution)/shard_map/ppermute | solution.py:22
  168.4 3.0 %fusion.16 = bf16[4096,256]{1,0:T(8,128)(2,1)S(1)} fusion(s32[]{:T(128)S(6)} %select_n.118, bf16[4096,256]{1,0:T(8,128)(2,1)} %all-gather.6.cloned.1.call-done), kind=kLoop, calls=%fused_computation.28 | loop fusion | flops 4194304 | bytes 4194308 | tf_op jit(solution)/shard_map/jit(_roll_dynamic)/concatenate | solution.py:49
  177.6 4.5 %collective-permute-done.14 = bf16[384,512]{0,1:T(8,128)(2,1)} collective-permute-done((bf16[384,512]{0,1:T(8,128)(2,1)}, bf16[384,512]{0,1:T(8,128)(2,1)}, u32[]{:S(2)}, u32[]{:S(2)}) %collective-permute-start.14) | collective-permute-done | bytes 393248 | tf_op jit(solution)/shard_map/ppermute | solution.py:22
  186.2 7.3 %collective-permute-done.8 = bf16[384,512]{0,1:T(8,128)(2,1)S(1)} collective-permute-done((bf16[384,512]{0,1:T(8,128)(2,1)}, bf16[384,512]{0,1:T(8,128)(2,1)S(1)}, u32[]{:S(2)}, u32[]{:S(2)}) %collective-permute-start.8) | collective-permute-done | bytes 393248 | tf_op jit(solution)/shard_map/ppermute | solution.py:22
  193.6 6.0 %collective-permute-done.15 = bf16[384,512]{0,1:T(8,128)(2,1)S(1)} collective-permute-done((bf16[384,512]{0,1:T(8,128)(2,1)}, bf16[384,512]{0,1:T(8,128)(2,1)S(1)}, u32[]{:S(2)}, u32[]{:S(2)}) %collective-permute-start.15) | collective-permute-done | bytes 393248 | tf_op jit(solution)/shard_map/ppermute | solution.py:22
  205.2 3.4 %collective-permute-done.16 = bf16[3072,256]{1,0:T(8,128)(2,1)} collective-permute-done((bf16[3072,256]{1,0:T(8,128)(2,1)}, bf16[3072,256]{1,0:T(8,128)(2,1)}, u32[]{:S(2)}, u32[]{:S(2)}) %collective-permute-start.16) | collective-permute-done | bytes 1572896 | tf_op jit(solution)/shard_map/ppermute | solution.py:52
  208.6 3.1 %fusion.18 = f32[384,256]{0,1:T(8,128)S(1)} fusion(bf16[3072,256]{1,0:T(8,128)(2,1)} %collective-permute-done.16, bf16[384,4096]{1,0:T(8,128)(2,1)} %copy-done.2), kind=kOutput, calls=%fused_computation.30 | convolution fusion | flops 603979776 | bytes 4325376 | tf_op jit(solution)/shard_map/dot_general | solution.py:71
  211.8 1.6 fusion.61
  (86 shorter events, 38.6 us)
Async XLA Ops:
  6.5 51.1 %all-gather.4.cloned.1.call-start = ((), (), s32[]{:S(2)}) async-start(), calls=%async_computation | async-start | bytes 2621440 | tf_op jit(solution)/shard_map/all_gather | solution.py:48
  8.7 95.2 %all-gather.8.cloned.1.call-start = ((), (), s32[]{:S(2)}) async-start(), calls=%async_computation.2 | async-start | bytes 2621440 | tf_op jit(solution)/shard_map/all_gather | solution.py:48
  8.7 20.8 %collective-permute-start = (bf16[192,2048]{1,0:T(8,128)(2,1)}, bf16[192,2048]{1,0:T(8,128)(2,1)S(1)}, u32[]{:S(2)}, u32[]{:S(2)}) collective-permute-start(bf16[192,2048]{1,0:T(8,128)(2,1)} %param.6), channel_id=1, source_target_pairs={{0,2},{2,0},{1,3},{3,1},{4,6},{6,4},{5,7},{7,5},{8,10},{10,8},{9,1... | collective-permute-start | bytes 2359304 | tf_op jit(solution)/shard_map/ppermute | solution.py:34
  13.8 154.5 %all-gather.6.cloned.1.call-start = ((), (), s32[]{:S(2)}) async-start(), calls=%async_computation.1 | async-start | bytes 2621440 | tf_op jit(solution)/shard_map/all_gather | solution.py:48
  29.8 3.6 %collective-permute-start.1 = (bf16[384,2048]{1,0:T(8,128)(2,1)S(1)}, bf16[384,2048]{1,0:T(8,128)(2,1)}, u32[]{:S(2)}, u32[]{:S(2)}) collective-permute-start(bf16[384,2048]{1,0:T(8,128)(2,1)S(1)} %pad_maximum_fusion), channel_id=1, source_target_pairs={{0,1},{1,0},{2,3},{3,2},{4,5},{5,4},{6,7},{7,6},{8,9},{9,8},{10,11... | collective-permute-start | bytes 4718600 | tf_op jit(solution)/shard_map/ppermute | solution.py:34
  61.9 52.3 %collective-permute-start.2 = (bf16[3072,256]{1,0:T(8,128)(2,1)}, bf16[3072,256]{1,0:T(8,128)(2,1)}, u32[]{:S(2)}, u32[]{:S(2)}) collective-permute-start(bf16[3072,256]{1,0:T(8,128)(2,1)} %slice.72), channel_id=1, source_target_pairs={{0,16},{16,0},{1,17},{17,1},{2,18},{18,2},{3,19},{19,3},{4,20},{20... | collective-permute-start | bytes 4718600 | tf_op jit(solution)/shard_map/ppermute | solution.py:52
  107.1 36.2 %collective-permute-start.9 = (bf16[3072,256]{1,0:T(8,128)(2,1)S(1)}, bf16[3072,256]{1,0:T(8,128)(2,1)S(1)}, u32[]{:S(2)}, u32[]{:S(2)}) collective-permute-start(bf16[3072,256]{1,0:T(8,128)(2,1)S(1)} %slice.73), channel_id=1, source_target_pairs={{0,16},{16,0},{1,17},{17,1},{2,18},{18,2},{3,19},{19,3},{4,20},{20... | collective-permute-start | bytes 4718600 | tf_op jit(solution)/shard_map/ppermute | solution.py:52
  111.6 32.8 %copy-start.2 = (bf16[384,4096]{1,0:T(8,128)(2,1)}, bf16[384,4096]{1,0:T(8,128)(2,1)S(1)}, u32[]{:S(2)}) copy-start(bf16[384,4096]{1,0:T(8,128)(2,1)S(1)} %fusion.6) | copy-start | bytes 9437188
  117.2 27.6 %copy-start.8 = (bf16[384,256]{0,1:T(8,128)(2,1)}, bf16[384,256]{0,1:T(8,128)(2,1)S(1)}, u32[]{:S(2)}) copy-start(bf16[384,256]{0,1:T(8,128)(2,1)S(1)} %fusion.67) | copy-start | bytes 589828
  117.2 27.1 %copy-start.5 = (bf16[1024,512]{1,0:T(8,128)(2,1)S(1)}, bf16[1024,512]{1,0:T(8,128)(2,1)}, u32[]{:S(2)}) copy-start(bf16[1024,512]{1,0:T(8,128)(2,1)} %param.8) | copy-start | bytes 3145732
  118.0 34.3 %collective-permute-start.3 = (bf16[384,512]{0,1:T(8,128)(2,1)}, bf16[384,512]{0,1:T(8,128)(2,1)}, u32[]{:S(2)}, u32[]{:S(2)}) collective-permute-start(bf16[384,512]{0,1:T(8,128)(2,1)} %pad_maximum_fusion.3), channel_id=1, source_target_pairs={{4,0},{8,4},{12,8},{5,1},{9,5},{13,9},{6,2},{10,6},{14,10},{7,3},{... | collective-permute-start | bytes 1179656 | tf_op jit(solution)/shard_map/ppermute | solution.py:22
  119.3 34.6 %collective-permute-start.4 = (bf16[384,512]{0,1:T(8,128)(2,1)}, bf16[384,512]{0,1:T(8,128)(2,1)}, u32[]{:S(2)}, u32[]{:S(2)}) collective-permute-start(bf16[384,512]{0,1:T(8,128)(2,1)} %pad_maximum_fusion.3), channel_id=1, source_target_pairs={{0,4},{4,8},{8,12},{1,5},{5,9},{9,13},{2,6},{6,10},{10,14},{3,7},{... | collective-permute-start | bytes 1179656 | tf_op jit(solution)/shard_map/ppermute | solution.py:23
  145.7 19.9 %collective-permute-start.10 = (bf16[384,512]{0,1:T(8,128)(2,1)}, bf16[384,512]{0,1:T(8,128)(2,1)}, u32[]{:S(2)}, u32[]{:S(2)}) collective-permute-start(bf16[384,512]{0,1:T(8,128)(2,1)} %pad_maximum_fusion.4), channel_id=1, source_target_pairs={{4,0},{8,4},{12,8},{5,1},{9,5},{13,9},{6,2},{10,6},{14,10},{7,3},{... | collective-permute-start | bytes 1179656 | tf_op jit(solution)/shard_map/ppermute | solution.py:22
  147.0 19.9 %collective-permute-start.11 = (bf16[384,512]{0,1:T(8,128)(2,1)}, bf16[384,512]{0,1:T(8,128)(2,1)}, u32[]{:S(2)}, u32[]{:S(2)}) collective-permute-start(bf16[384,512]{0,1:T(8,128)(2,1)} %pad_maximum_fusion.4), channel_id=1, source_target_pairs={{0,4},{4,8},{8,12},{1,5},{5,9},{9,13},{2,6},{6,10},{10,14},{3,7},{... | collective-permute-start | bytes 1179656 | tf_op jit(solution)/shard_map/ppermute | solution.py:23
  152.4 23.1 %collective-permute-start.7 = (bf16[384,512]{0,1:T(8,128)(2,1)}, bf16[384,512]{0,1:T(8,128)(2,1)}, u32[]{:S(2)}, u32[]{:S(2)}) collective-permute-start(bf16[384,512]{0,1:T(8,128)(2,1)} %collective-permute-done.3), channel_id=1, source_target_pairs={{4,0},{8,4},{5,1},{9,5},{6,2},{10,6},{7,3},{11,7},{20,16},{24,20},... | collective-permute-start | bytes 1179656 | tf_op jit(solution)/shard_map/ppermute | solution.py:22
  153.9 23.0 %collective-permute-start.5 = (bf16[384,512]{0,1:T(8,128)(2,1)}, bf16[384,512]{0,1:T(8,128)(2,1)}, u32[]{:S(2)}, u32[]{:S(2)}) collective-permute-start(bf16[384,512]{0,1:T(8,128)(2,1)} %collective-permute-done.4), channel_id=1, source_target_pairs={{4,8},{8,12},{5,9},{9,13},{6,10},{10,14},{7,11},{11,15},{20,24},{2... | collective-permute-start | bytes 1179656 | tf_op jit(solution)/shard_map/ppermute | solution.py:23
  165.6 16.5 %collective-permute-start.14 = (bf16[384,512]{0,1:T(8,128)(2,1)}, bf16[384,512]{0,1:T(8,128)(2,1)}, u32[]{:S(2)}, u32[]{:S(2)}) collective-permute-start(bf16[384,512]{0,1:T(8,128)(2,1)} %collective-permute-done.10), channel_id=1, source_target_pairs={{4,0},{8,4},{5,1},{9,5},{6,2},{10,6},{7,3},{11,7},{20,16},{24,20},... | collective-permute-start | bytes 1179656 | tf_op jit(solution)/shard_map/ppermute | solution.py:22
  166.9 16.5 %collective-permute-start.12 = (bf16[384,512]{0,1:T(8,128)(2,1)}, bf16[384,512]{0,1:T(8,128)(2,1)}, u32[]{:S(2)}, u32[]{:S(2)}) collective-permute-start(bf16[384,512]{0,1:T(8,128)(2,1)} %collective-permute-done.11), channel_id=1, source_target_pairs={{4,8},{8,12},{5,9},{9,13},{6,10},{10,14},{7,11},{11,15},{20,24},{2... | collective-permute-start | bytes 1179656 | tf_op jit(solution)/shard_map/ppermute | solution.py:23
  172.7 36.0 %collective-permute-start.16 = (bf16[3072,256]{1,0:T(8,128)(2,1)}, bf16[3072,256]{1,0:T(8,128)(2,1)}, u32[]{:S(2)}, u32[]{:S(2)}) collective-permute-start(bf16[3072,256]{1,0:T(8,128)(2,1)} %slice.68), channel_id=1, source_target_pairs={{0,16},{16,0},{1,17},{17,1},{2,18},{18,2},{3,19},{19,3},{4,20},{20... | collective-permute-start | bytes 4718600 | tf_op jit(solution)/shard_map/ppermute | solution.py:52
  175.4 25.3 %copy-start.9 = (bf16[384,256]{0,1:T(8,128)(2,1)S(1)}, bf16[384,256]{0,1:T(8,128)(2,1)}, u32[]{:S(2)}) copy-start(bf16[384,256]{0,1:T(8,128)(2,1)} %copy-done.8) | copy-start | bytes 589828
  175.5 18.1 %collective-permute-start.8 = (bf16[384,512]{0,1:T(8,128)(2,1)}, bf16[384,512]{0,1:T(8,128)(2,1)S(1)}, u32[]{:S(2)}, u32[]{:S(2)}) collective-permute-start(bf16[384,512]{0,1:T(8,128)(2,1)} %collective-permute-done.7), channel_id=1, source_target_pairs={{4,0},{5,1},{6,2},{7,3},{20,16},{21,17},{22,18},{23,19}} | collective-permute-start | bytes 1179656 | tf_op jit(solution)/shard_map/ppermute | solution.py:22
  176.9 22.8 %collective-permute-start.6 = (bf16[384,512]{0,1:T(8,128)(2,1)}, bf16[384,512]{0,1:T(8,128)(2,1)S(1)}, u32[]{:S(2)}, u32[]{:S(2)}) collective-permute-start(bf16[384,512]{0,1:T(8,128)(2,1)} %collective-permute-done.5), channel_id=1, source_target_pairs={{8,12},{9,13},{10,14},{11,15},{24,28},{25,29},{26,30},{27,31}} | collective-permute-start | bytes 1179656 | tf_op jit(solution)/shard_map/ppermute | solution.py:23
  182.1 17.5 %collective-permute-start.15 = (bf16[384,512]{0,1:T(8,128)(2,1)}, bf16[384,512]{0,1:T(8,128)(2,1)S(1)}, u32[]{:S(2)}, u32[]{:S(2)}) collective-permute-start(bf16[384,512]{0,1:T(8,128)(2,1)} %collective-permute-done.14), channel_id=1, source_target_pairs={{4,0},{5,1},{6,2},{7,3},{20,16},{21,17},{22,18},{23,19}} | collective-permute-start | bytes 1179656 | tf_op jit(solution)/shard_map/ppermute | solution.py:22
  183.4 17.5 %collective-permute-start.13 = (bf16[384,512]{0,1:T(8,128)(2,1)}, bf16[384,512]{0,1:T(8,128)(2,1)S(1)}, u32[]{:S(2)}, u32[]{:S(2)}) collective-permute-start(bf16[384,512]{0,1:T(8,128)(2,1)} %collective-permute-done.12), channel_id=1, source_target_pairs={{8,12},{9,13},{10,14},{11,15},{24,28},{25,29},{26,30},{27,31}} | collective-permute-start | bytes 1179656 | tf_op jit(solution)/shard_map/ppermute | solution.py:23
  (9 other events, 88.7 us)
Sparse Core Ops, SparseCore 0:
  8.9 48.6 all-gather.3
  59.2 44.6 all-gather.7
  105.4 56.1 all-gather.5
